TPU v7x, 32 devices: a whole 2x2x4 slice. The times are simulated.
32 devices in a mesh: probe: 2 (over x), space: 16 (over z, y, core).
Axes of the slice: x: 2, y: 2, z: 4, core: 2. Of those that a mesh axis runs over, the one named last changes fastest.
Arguments:
- cos_polar: float32 [4, 64, 128], P(None, 'space', 'probe'), may hold values from -1 to 1
- azimuth: float32 [4, 64, 128], P(None, 'space', 'probe'), may hold values from -3.140625 to 3.140625
- bond_class: int32 [3, 4, 64, 128], P(None, None, 'space', 'probe'), may hold values from 0 to 7
- exchange: float32 [8], replicated, may hold values from -1 to 1
- probe_wave: int32 [16, 3], P('probe'), may hold values from 0 to 63
Outputs:
- relaxed: float32 [3, 4, 64, 128], P(None, None, 'space', 'probe')
- cheb_last: bfloat16 [16, 2, 3, 4, 64, 128], P('probe', None, None, None, 'space')
- moments: float32 [16, 4], P('probe')
All inputs are finite; a program needn't handle non-finite values.
Results may differ from a plain program's by a relative error of at most 0.001.
Values sent between devices are 32-bit elements; how exact they have to be, the bound alone decides.
No kernel may reach another device: no remote copies, remote signals or barrier semaphores. Data moves between devices by JAX's collectives and lax.ppermute only.
A program may use at most 128 MiB of HBM per device.

v0:
```python
import math

import jax
import jax.numpy as jnp
from jax import lax
from jax.sharding import PartitionSpec as P

LZ = 4
SWEEPS = 2
CHEB = 4


relax_rate = 0.15
precess_scale = 1.0 / 6.0


def extended(array, sides, width):
    for axis, dim in sides:
        size, length = (lax.axis_size(axis), array.shape[dim])
        up = [(i, (i + 1) % size) for i in range(size)]
        down = [(j, i) for i, j in up]
        last = lax.slice_in_dim(array, length - width, length, axis=dim)
        leading = lax.slice_in_dim(array, 0, width, axis=dim)
        before = lax.ppermute(last, axis, up)
        after = lax.ppermute(leading, axis, down)
        array = jnp.concatenate([before, array, after], axis=dim)
    return array


def spin_field(cos_polar, azimuth):
    radial = jnp.sqrt(1.0 - cos_polar * cos_polar)
    return jnp.stack([radial * jnp.cos(azimuth), radial * jnp.sin(azimuth), cos_polar], 0)


def bond_strengths(bond_class, exchange):
    strengths = jnp.zeros(bond_class.shape, exchange.dtype)
    for class_index in range(exchange.shape[0]):
        strengths = strengths + jnp.where(bond_class == class_index, exchange[class_index], 0.0)
    return strengths


def cross_product(spin_core, vector):
    spin_a, spin_b, spin_c = (spin_core[0], spin_core[1], spin_core[2])
    vec_a = vector[..., 0, :, :, :]
    vec_b = vector[..., 1, :, :, :]
    vec_c = vector[..., 2, :, :, :]
    return jnp.stack(
        [
            spin_b * vec_c - spin_c * vec_b,
            spin_c * vec_a - spin_a * vec_c,
            spin_a * vec_b - spin_b * vec_a,
        ],
        axis=-4,
    )


def interior(array, ext_y):
    cut = array[..., 1:-1, :]
    return cut[..., 1:-1] if ext_y else cut


def ahead_x(array, ext_y):
    cut = array[..., 2:, :]
    return cut[..., 1:-1] if ext_y else cut


def behind_x(array, ext_y):
    cut = array[..., :-2, :]
    return cut[..., 1:-1] if ext_y else cut


def ahead_y(array, ext_y):
    cut = array[..., 1:-1, :]
    return cut[..., 2:] if ext_y else jnp.roll(cut, -1, -1)


def behind_y(array, ext_y):
    cut = array[..., 1:-1, :]
    return cut[..., :-2] if ext_y else jnp.roll(cut, 1, -1)


def neighbour_ext(vector, bonds, ext_y):
    along_x, along_y, along_z = (bonds[0], bonds[1], bonds[2])
    total = interior(along_x, ext_y) * ahead_x(vector, ext_y) + behind_x(along_x, ext_y) * behind_x(
        vector, ext_y
    )
    total = (
        total
        + interior(along_y, ext_y) * ahead_y(vector, ext_y)
        + behind_y(along_y, ext_y) * behind_y(vector, ext_y)
    )
    centre = interior(vector, ext_y)
    bond_z = interior(along_z, ext_y)
    total = (
        total
        + bond_z * jnp.roll(centre, -1, -3)
        + jnp.roll(bond_z, 1, -3) * jnp.roll(centre, 1, -3)
    )
    return total


def relax_update(spins, field):
    turned = cross_product(spins, field)
    twice = cross_product(spins, turned)
    moved = spins - relax_rate * twice
    length = jnp.sqrt(jnp.sum(moved * moved, axis=0))
    return moved / length


def relax_ext(spins_ext, bonds_ext):
    field = neighbour_ext(spins_ext, bonds_ext, True)
    return relax_update(interior(spins_ext, True), field)


def precess_ext(vector_ext, spin_ext, bond_ext):
    field = neighbour_ext(vector_ext, bond_ext, False)
    return cross_product(interior(spin_ext, False), field) * -precess_scale


def make_probes(probe_wave, probe_ids, x_coords, total_x, total_y, depth_z):
    wave_x = probe_wave[:, 0][:, None]
    wave_y = probe_wave[:, 1][:, None]
    wave_z = probe_wave[:, 2][:, None]
    phase_x = wave_x * x_coords[None, :] % total_x
    phase_y = wave_y * jnp.arange(total_y, dtype=jnp.int32)[None, :] % total_y
    phase_z = wave_z * jnp.arange(depth_z, dtype=jnp.int32)[None, :] % depth_z
    fraction = (
        phase_z[:, :, None, None].astype(jnp.float32) / depth_z
        + phase_x[:, None, :, None].astype(jnp.float32) / total_x
        + phase_y[:, None, None, :].astype(jnp.float32) / total_y
    )
    angle = 2.0 * math.pi * fraction
    ramp = jnp.sqrt(1.0 + 2.0 * x_coords.astype(jnp.float32) / total_x)[None, None, :, None]
    waves = jnp.stack([jnp.cos(angle) * ramp, jnp.sin(angle) * ramp], 1)
    polar = ((probe_ids % 3)[:, None] == jnp.arange(3, dtype=jnp.int32)[None, :]).astype(
        jnp.float32
    )
    return waves[:, :, None] * polar[:, None, :, None, None, None]


def shards(cos_polar, azimuth, bond_class, exchange, probe_wave):
    spins = spin_field(cos_polar, azimuth)
    bonds = bond_strengths(bond_class, exchange)
    slab_rows = spins.shape[2]
    for sweep_index in range(SWEEPS):
        spins_ext, bonds_ext = (
            extended(spins, (("probe", 3), ("space", 2)), 1),
            extended(bonds, (("probe", 3), ("space", 2)), 1),
        )
        spins = relax_ext(spins_ext, bonds_ext)
    slab_spins, slab_bonds = (
        lax.all_gather(spins, "probe", axis=3, tiled=True),
        lax.all_gather(bonds, "probe", axis=3, tiled=True),
    )
    total_x = slab_rows * lax.axis_size("space")
    total_y = slab_spins.shape[3]
    site_count = total_x * total_y * LZ
    group_size = probe_wave.shape[0]
    probe_ids = lax.axis_index("probe") * group_size + jnp.arange(group_size, dtype=jnp.int32)
    x_coords = lax.axis_index("space") * slab_rows + jnp.arange(slab_rows, dtype=jnp.int32)
    start = make_probes(probe_wave, probe_ids, x_coords, total_x, total_y, LZ)
    background = jnp.stack([slab_spins, slab_bonds], 0)[:, None]
    summed_terms = []

    def record(vector):
        local = jnp.sum(vector * vector, axis=(1, 2, 3, 4, 5))
        summed_terms.append(lax.psum(local, "space"))

    previous = start
    current = start
    for order in range(CHEB):
        vector_ext, back_ext = (
            extended(current, (("space", 4),), 1),
            extended(background, (("space", 4),), 1),
        )
        advanced = precess_ext(vector_ext, back_ext[0, 0], back_ext[1, 0])
        if order > 0:
            advanced = 2.0 * advanced - previous
        previous, current = (current, advanced)
        record(current)
    moment_rows = jnp.stack(summed_terms, 1)
    moment_rows = moment_rows / site_count
    return (spins, current.astype(jnp.bfloat16), moment_rows)


def solution(mesh):
    return jax.shard_map(
        shards,
        mesh=mesh,
        in_specs=(
            P(None, "space", "probe"),
            P(None, "space", "probe"),
            P(None, None, "space", "probe"),
            P(),
            P("probe", None),
        ),
        out_specs=(
            P(None, None, "space", "probe"),
            P("probe", None, None, None, "space", None),
            P("probe", None),
        ),
        check_vma=False,
    )
```

profile of v0, /device:TPU:0, one launch (start us, length us, event | category | flops | bytes accessed | tf_op | source)
XLA Modules:
  0.0 147.4 jit_solution(15678469411058019290)
XLA Ops:
  2.3 5.9 %select_add_fusion = f32[3,4,4,64]{3,2,1,0:T(4,128)S(1)} fusion(s32[3,4,4,64]{3,2,1,0:T(4,128)} %param.7, f32[]{:T(128)} %bitcast.10, f32[]{:T(128)} %bitcast.9, f32[]{:T(128)} %bitcast.8, f32[]{:T(128)} %bitcast.7, f32[]{:T(128)} %bitcast.6, f32[]{:T(128)} %bitcast.5, f32[]{:T(128)} %bitcast.4, f32[]{:T(128)} %bitcast.3), kind=kLoop, calls=%fused_computation.138 | loop fusion | flops 70656 | bytes 24608 | tf_op jit(solution)/shard_map/add | solution.py:38
  8.3 3.0 %collective-permute-start = (f32[3,4,4,1]{3,2,1,0:T(4,128)S(1)}, f32[3,4,4,1]{3,2,1,0:T(4,128)S(1)}, u32[]{:S(2)}, u32[]{:S(2)}) collective-permute-start(f32[3,4,4,1]{3,2,1,0:T(4,128)S(1)} %get-tuple-element.109), channel_id=1, source_target_pairs={{0,16},{16,0},{1,17},{17,1},{2,18},{18,2},{3,19},{19,3},{4,20},{20... | collective-permute-start | bytes 584 | tf_op jit(solution)/shard_map/ppermute | solution.py:24
  12.9 2.0 %collective-permute-start.4 = (f32[3,4,4,1]{3,2,1,0:T(4,128)S(1)}, f32[3,4,4,1]{3,2,1,0:T(4,128)S(1)}, u32[]{:S(2)}, u32[]{:S(2)}) collective-permute-start(f32[3,4,4,1]{3,2,1,0:T(4,128)S(1)} %get-tuple-element.116), channel_id=1, source_target_pairs={{0,16},{16,0},{1,17},{17,1},{2,18},{18,2},{3,19},{19,3},{4,20},{20... | collective-permute-start | bytes 584 | tf_op jit(solution)/shard_map/ppermute | solution.py:24
  18.3 3.3 %collective-permute-start.14 = (f32[8,2,3,4,1,128]{5,4,3,2,1,0:T(1,128)}, f32[8,2,3,4,1,128]{5,4,3,2,1,0:T(1,128)}, u32[]{:S(2)}, u32[]{:S(2)}) collective-permute-start(f32[8,2,3,4,1,128]{5,4,3,2,1,0:T(1,128)} %get-tuple-element.83), channel_id=1, source_target_pairs={{1,0},{2,1},{3,2},{4,3},{5,4},{6,5},{7,6},{8,7},{9,8},{10,9},{11,1... | collective-permute-start | bytes 294920 | tf_op jit(solution)/shard_map/ppermute | solution.py:25
  25.0 9.1 %all_gather.7 = f32[3,4,4,128]{2,1,0,3:T(4,128)S(1)} all-gather(f32[3,4,4,64]{2,1,0,3:T(4,128)S(1)} %copy.499), channel_id=1, replica_groups=mesh['probe'=2,'space'=16] {'probe'}, dimensions={3}, use_global_device_ids=true | all-gather | bytes 36864 | tf_op jit(solution)/shard_map/all_gather | solution.py:153
  34.2 1.9 %collective-permute-start.2 = (f32[3,4,1,66]{3,2,1,0:T(1,128)S(1)}, f32[3,4,1,66]{3,2,1,0:T(1,128)S(1)}, u32[]{:S(2)}, u32[]{:S(2)}) collective-permute-start(f32[3,4,1,66]{3,2,1,0:T(1,128)S(1)} %get-tuple-element.107), channel_id=1, source_target_pairs={{0,1},{1,2},{2,3},{3,4},{4,5},{5,6},{6,7},{7,8},{8,9},{9,10},{10,1... | collective-permute-start | bytes 9512 | tf_op jit(solution)/shard_map/ppermute | solution.py:24
  36.2 2.6 %collective-permute-start.3 = (f32[3,4,1,66]{3,2,1,0:T(1,128)S(1)}, f32[3,4,1,66]{3,2,1,0:T(1,128)S(1)}, u32[]{:S(2)}, u32[]{:S(2)}) collective-permute-start(f32[3,4,1,66]{3,2,1,0:T(1,128)S(1)} %get-tuple-element.108), channel_id=1, source_target_pairs={{1,0},{2,1},{3,2},{4,3},{5,4},{6,5},{7,6},{8,7},{9,8},{10,9},{11,1... | collective-permute-start | bytes 9512 | tf_op jit(solution)/shard_map/ppermute | solution.py:25
  39.5 1.7 %collective-permute-done.2 = f32[3,4,1,66]{3,2,1,0:T(1,128)S(1)} collective-permute-done((f32[3,4,1,66]{3,2,1,0:T(1,128)S(1)}, f32[3,4,1,66]{3,2,1,0:T(1,128)S(1)}, u32[]{:S(2)}, u32[]{:S(2)}) %collective-permute-start.2) | collective-permute-done | bytes 3200 | tf_op jit(solution)/shard_map/ppermute | solution.py:24
  41.6 5.3 %collective-permute-done.7 = f32[3,4,1,66]{3,2,1,0:T(1,128)S(1)} collective-permute-done((f32[3,4,1,66]{3,2,1,0:T(1,128)S(1)}, f32[3,4,1,66]{3,2,1,0:T(1,128)S(1)}, u32[]{:S(2)}, u32[]{:S(2)}) %collective-permute-start.7) | collective-permute-done | bytes 3200 | tf_op jit(solution)/shard_map/ppermute | solution.py:24
  47.4 1.7 %collective-permute-start.8 = (f32[3,4,4,1]{3,2,1,0:T(4,128)S(1)}, f32[3,4,4,1]{3,2,1,0:T(4,128)S(1)}, u32[]{:S(2)}, u32[]{:S(2)}) collective-permute-start(f32[3,4,4,1]{3,2,1,0:T(4,128)S(1)} %get-tuple-element.106), channel_id=1, source_target_pairs={{0,16},{16,0},{1,17},{17,1},{2,18},{18,2},{3,19},{19,3},{4,20},{20... | collective-permute-start | bytes 584 | tf_op jit(solution)/shard_map/ppermute | solution.py:24
  49.5 1.8 %collective-permute-done.8 = f32[3,4,4,1]{3,2,1,0:T(4,128)S(1)} collective-permute-done((f32[3,4,4,1]{3,2,1,0:T(4,128)S(1)}, f32[3,4,4,1]{3,2,1,0:T(4,128)S(1)}, u32[]{:S(2)}, u32[]{:S(2)}) %collective-permute-start.8) | collective-permute-done | bytes 224 | tf_op jit(solution)/shard_map/ppermute | solution.py:24
  54.5 4.5 %collective-permute-done.11 = f32[3,4,1,66]{3,2,1,0:T(1,128)S(1)} collective-permute-done((f32[3,4,1,66]{3,2,1,0:T(1,128)S(1)}, f32[3,4,1,66]{3,2,1,0:T(1,128)S(1)}, u32[]{:S(2)}, u32[]{:S(2)}) %collective-permute-start.11) | collective-permute-done | bytes 3200 | tf_op jit(solution)/shard_map/ppermute | solution.py:24
  59.5 8.5 %all_gather.6 = f32[3,4,4,128]{2,1,0,3:T(4,128)S(1)} all-gather(f32[3,4,4,64]{2,1,0,3:T(4,128)S(1)} %copy.498), channel_id=1, replica_groups=mesh['probe'=2,'space'=16] {'probe'}, dimensions={3}, use_global_device_ids=true | all-gather | bytes 36864 | tf_op jit(solution)/shard_map/all_gather | solution.py:152
  68.4 2.2 %fusion.71 = (f32[2,1,3,4,1,128]{4,3,2,5,0,1:T(4,128)}, f32[2,1,3,4,1,128]{4,3,2,5,0,1:T(4,128)S(1)}) fusion(f32[2,1,3,4,4,128]{4,3,2,5,0,1:T(4,128)S(1)} %maximum_bitcast_fusion), kind=kLoop, calls=%fused_computation.218 | loop fusion | bytes 49152 | tf_op jit(solution)/shard_map/slice | solution.py:22
  70.6 2.3 %copy.500 = f32[2,1,3,4,1,128]{5,3,4,2,1,0:T(4,128)} copy(f32[2,1,3,4,1,128]{4,3,2,5,0,1:T(4,128)} %get-tuple-element.30) | data formatting | bytes 24576 | tf_op jit(solution)/shard_map/slice | solution.py:22
  74.2 4.5 %collective-permute-start.13 = (f32[2,1,3,4,1,128]{5,3,4,2,1,0:T(4,128)}, f32[2,1,3,4,1,128]{5,3,4,2,1,0:T(4,128)}, u32[]{:S(2)}, u32[]{:S(2)}) collective-permute-start(f32[2,1,3,4,1,128]{5,3,4,2,1,0:T(4,128)} %copy.501), channel_id=1, source_target_pairs={{1,0},{2,1},{3,2},{4,3},{5,4},{6,5},{7,6},{8,7},{9,8},{10,9},{11,1... | collective-permute-start | bytes 36872 | tf_op jit(solution)/shard_map/ppermute | solution.py:25
  82.6 2.2 %fusion.26 = f32[8,2,3,4,4,128]{5,4,3,2,1,0:T(4,128)S(1)} fusion(f32[8,2,3,4,4,128]{5,4,3,2,1,0:T(4,128)S(1)} %broadcast_multiply_fusion, f32[8,2,3,4,1,128]{5,4,3,2,1,0:T(1,128)} %collective-permute-done.15, f32[8,2,3,4,1,128]{5,4,3,2,1,0:T(1,128)} %collective-permute-done.14, f32[8,2,3,4,4,1]{5,4,3,2,1,0:T(4,128)S(1)} %copy-done.3, ...), kind=kLoop, calls=%fused_computation.34 | loop fusion | flops 1671168 | bytes 2605056 | tf_op jit(solution)/shard_map/add | solution.py:95
  86.0 4.2 %collective-permute-start.16 = (f32[8,2,3,4,1,128]{5,4,3,2,1,0:T(1,128)S(1)}, f32[8,2,3,4,1,128]{5,4,3,2,1,0:T(1,128)S(1)}, u32[]{:S(2)}, u32[]{:S(2)}) collective-permute-start(f32[8,2,3,4,1,128]{5,4,3,2,1,0:T(1,128)S(1)} %get-tuple-element.73), channel_id=1, source_target_pairs={{1,0},{2,1},{3,2},{4,3},{5,4},{6,5},{7,6},{8,7},{9,8},{10,9},{11,1... | collective-permute-start | bytes 294920 | tf_op jit(solution)/shard_map/ppermute | solution.py:25
  90.2 2.2 %collective-permute-done.16 = f32[8,2,3,4,1,128]{5,4,3,2,1,0:T(1,128)S(1)} collective-permute-done((f32[8,2,3,4,1,128]{5,4,3,2,1,0:T(1,128)S(1)}, f32[8,2,3,4,1,128]{5,4,3,2,1,0:T(1,128)S(1)}, u32[]{:S(2)}, u32[]{:S(2)}) %collective-permute-start.16) | collective-permute-done | bytes 98336 | tf_op jit(solution)/shard_map/ppermute | solution.py:25
  92.4 4.5 %collective-permute-done.17 = f32[8,2,3,4,1,128]{5,4,3,2,1,0:T(1,128)S(1)} collective-permute-done((f32[8,2,3,4,1,128]{5,4,3,2,1,0:T(1,128)S(1)}, f32[8,2,3,4,1,128]{5,4,3,2,1,0:T(1,128)S(1)}, u32[]{:S(2)}, u32[]{:S(2)}) %collective-permute-start.17) | collective-permute-done | bytes 98336 | tf_op jit(solution)/shard_map/ppermute | solution.py:24
  99.7 1.7 %collective-permute-done.18 = f32[8,2,3,4,1,128]{5,4,3,2,1,0:T(1,128)S(1)} collective-permute-done((f32[8,2,3,4,1,128]{5,4,3,2,1,0:T(1,128)S(1)}, f32[8,2,3,4,1,128]{5,4,3,2,1,0:T(1,128)S(1)}, u32[]{:S(2)}, u32[]{:S(2)}) %collective-permute-start.18) | collective-permute-done | bytes 98336 | tf_op jit(solution)/shard_map/ppermute | solution.py:25
  101.4 4.7 %collective-permute-done.19 = f32[8,2,3,4,1,128]{5,4,3,2,1,0:T(1,128)S(1)} collective-permute-done((f32[8,2,3,4,1,128]{5,4,3,2,1,0:T(1,128)S(1)}, f32[8,2,3,4,1,128]{5,4,3,2,1,0:T(1,128)S(1)}, u32[]{:S(2)}, u32[]{:S(2)}) %collective-permute-start.19) | collective-permute-done | bytes 98336 | tf_op jit(solution)/shard_map/ppermute | solution.py:24
  110.5 4.6 %collective-permute-done.21 = f32[8,2,3,4,1,128]{5,4,3,2,1,0:T(1,128)S(1)} collective-permute-done((f32[8,2,3,4,1,128]{5,4,3,2,1,0:T(1,128)S(1)}, f32[8,2,3,4,1,128]{5,4,3,2,1,0:T(1,128)S(1)}, u32[]{:S(2)}, u32[]{:S(2)}) %collective-permute-start.21) | collective-permute-done | bytes 98336 | tf_op jit(solution)/shard_map/ppermute | solution.py:24
  117.3 29.5 %all-reduce = (f32[8,1]{0,1:T(1,128)S(1)}, f32[8,1]{0,1:T(1,128)S(1)}, f32[8,1]{0,1:T(1,128)S(1)}, f32[8,1]{0,1:T(1,128)S(1)}) all-reduce(f32[8,1]{0,1:T(1,128)S(1)} %bitcast.111, f32[8,1]{0,1:T(1,128)S(1)} %bitcast.112, f32[8,1]{0,1:T(1,128)S(1)} %bitcast.110, f32[8,1]{0,1:T(1,128)S(1)} %bitcast.113), channel_id=1, replica_groups=mesh['probe'=2,'space'=16] {'space'}, use_global_device_ids=true, to_apply=%region_9.10 | all-reduce | flops 32 | bytes 256 | tf_op jit(solution)/shard_map/psum | solution.py:167
  (156 shorter events, 32.3 us)
Async XLA Ops:
  8.3 25.8 %collective-permute-start = (f32[3,4,4,1]{3,2,1,0:T(4,128)S(1)}, f32[3,4,4,1]{3,2,1,0:T(4,128)S(1)}, u32[]{:S(2)}, u32[]{:S(2)}) collective-permute-start(f32[3,4,4,1]{3,2,1,0:T(4,128)S(1)} %get-tuple-element.109), channel_id=1, source_target_pairs={{0,16},{16,0},{1,17},{17,1},{2,18},{18,2},{3,19},{19,3},{4,20},{20... | collective-permute-start | bytes 584 | tf_op jit(solution)/shard_map/ppermute | solution.py:24
  11.2 22.9 %collective-permute-start.1 = (f32[3,4,4,1]{3,2,1,0:T(4,128)S(1)}, f32[3,4,4,1]{3,2,1,0:T(4,128)S(1)}, u32[]{:S(2)}, u32[]{:S(2)}) collective-permute-start(f32[3,4,4,1]{3,2,1,0:T(4,128)S(1)} %get-tuple-element.110), channel_id=1, source_target_pairs={{16,0},{0,16},{17,1},{1,17},{18,2},{2,18},{19,3},{3,19},{20,4},{4,... | collective-permute-start | bytes 584 | tf_op jit(solution)/shard_map/ppermute | solution.py:25
  12.9 23.3 %collective-permute-start.4 = (f32[3,4,4,1]{3,2,1,0:T(4,128)S(1)}, f32[3,4,4,1]{3,2,1,0:T(4,128)S(1)}, u32[]{:S(2)}, u32[]{:S(2)}) collective-permute-start(f32[3,4,4,1]{3,2,1,0:T(4,128)S(1)} %get-tuple-element.116), channel_id=1, source_target_pairs={{0,16},{16,0},{1,17},{17,1},{2,18},{18,2},{3,19},{19,3},{4,20},{20... | collective-permute-start | bytes 584 | tf_op jit(solution)/shard_map/ppermute | solution.py:24
  14.8 24.0 %collective-permute-start.5 = (f32[3,4,4,1]{3,2,1,0:T(4,128)S(1)}, f32[3,4,4,1]{3,2,1,0:T(4,128)S(1)}, u32[]{:S(2)}, u32[]{:S(2)}) collective-permute-start(f32[3,4,4,1]{3,2,1,0:T(4,128)S(1)} %get-tuple-element.115), channel_id=1, source_target_pairs={{16,0},{0,16},{17,1},{1,17},{18,2},{2,18},{19,3},{3,19},{20,4},{4,... | collective-permute-start | bytes 584 | tf_op jit(solution)/shard_map/ppermute | solution.py:25
  18.3 64.2 %collective-permute-start.14 = (f32[8,2,3,4,1,128]{5,4,3,2,1,0:T(1,128)}, f32[8,2,3,4,1,128]{5,4,3,2,1,0:T(1,128)}, u32[]{:S(2)}, u32[]{:S(2)}) collective-permute-start(f32[8,2,3,4,1,128]{5,4,3,2,1,0:T(1,128)} %get-tuple-element.83), channel_id=1, source_target_pairs={{1,0},{2,1},{3,2},{4,3},{5,4},{6,5},{7,6},{8,7},{9,8},{10,9},{11,1... | collective-permute-start | bytes 294920 | tf_op jit(solution)/shard_map/ppermute | solution.py:25
  24.1 14.7 %copy-start.6 = (f32[4,4,64]{2,1,0:T(4,128)S(1)}, f32[4,4,64]{2,1,0:T(4,128)}, u32[]{:S(2)}) copy-start(f32[4,4,64]{2,1,0:T(4,128)} %param.5) | copy-start | bytes 12292
  24.1 23.0 %copy-start.8 = (f32[4,4,64]{2,1,0:T(4,128)S(1)}, f32[4,4,64]{2,1,0:T(4,128)}, u32[]{:S(2)}) copy-start(f32[4,4,64]{2,1,0:T(4,128)} %param.6) | copy-start | bytes 12292
  34.1 48.5 %collective-permute-start.15 = (f32[8,2,3,4,1,128]{5,4,3,2,1,0:T(1,128)}, f32[8,2,3,4,1,128]{5,4,3,2,1,0:T(1,128)}, u32[]{:S(2)}, u32[]{:S(2)}) collective-permute-start(f32[8,2,3,4,1,128]{5,4,3,2,1,0:T(1,128)} %get-tuple-element.84), channel_id=1, source_target_pairs={{0,1},{1,2},{2,3},{3,4},{4,5},{5,6},{6,7},{7,8},{8,9},{9,10},{10,1... | collective-permute-start | bytes 294920 | tf_op jit(solution)/shard_map/ppermute | solution.py:24
  34.2 7.0 %collective-permute-start.2 = (f32[3,4,1,66]{3,2,1,0:T(1,128)S(1)}, f32[3,4,1,66]{3,2,1,0:T(1,128)S(1)}, u32[]{:S(2)}, u32[]{:S(2)}) collective-permute-start(f32[3,4,1,66]{3,2,1,0:T(1,128)S(1)} %get-tuple-element.107), channel_id=1, source_target_pairs={{0,1},{1,2},{2,3},{3,4},{4,5},{5,6},{6,7},{7,8},{8,9},{9,10},{10,1... | collective-permute-start | bytes 9512 | tf_op jit(solution)/shard_map/ppermute | solution.py:24
  36.2 5.1 %collective-permute-start.3 = (f32[3,4,1,66]{3,2,1,0:T(1,128)S(1)}, f32[3,4,1,66]{3,2,1,0:T(1,128)S(1)}, u32[]{:S(2)}, u32[]{:S(2)}) collective-permute-start(f32[3,4,1,66]{3,2,1,0:T(1,128)S(1)} %get-tuple-element.108), channel_id=1, source_target_pairs={{1,0},{2,1},{3,2},{4,3},{5,4},{6,5},{7,6},{8,7},{9,8},{10,9},{11,1... | collective-permute-start | bytes 9512 | tf_op jit(solution)/shard_map/ppermute | solution.py:25
  38.9 2.7 %collective-permute-start.6 = (f32[3,4,1,66]{3,2,1,0:T(1,128)S(1)}, f32[3,4,1,66]{3,2,1,0:T(1,128)S(1)}, u32[]{:S(2)}, u32[]{:S(2)}) collective-permute-start(f32[3,4,1,66]{3,2,1,0:T(1,128)S(1)} %get-tuple-element.90), channel_id=1, source_target_pairs={{1,0},{2,1},{3,2},{4,3},{5,4},{6,5},{7,6},{8,7},{9,8},{10,9},{11,1... | collective-permute-start | bytes 9512 | tf_op jit(solution)/shard_map/ppermute | solution.py:25
  41.2 5.8 %collective-permute-start.7 = (f32[3,4,1,66]{3,2,1,0:T(1,128)S(1)}, f32[3,4,1,66]{3,2,1,0:T(1,128)S(1)}, u32[]{:S(2)}, u32[]{:S(2)}) collective-permute-start(f32[3,4,1,66]{3,2,1,0:T(1,128)S(1)} %get-tuple-element.91), channel_id=1, source_target_pairs={{0,1},{1,2},{2,3},{3,4},{4,5},{5,6},{6,7},{7,8},{8,9},{9,10},{10,1... | collective-permute-start | bytes 9512 | tf_op jit(solution)/shard_map/ppermute | solution.py:24
  47.4 3.8 %collective-permute-start.8 = (f32[3,4,4,1]{3,2,1,0:T(4,128)S(1)}, f32[3,4,4,1]{3,2,1,0:T(4,128)S(1)}, u32[]{:S(2)}, u32[]{:S(2)}) collective-permute-start(f32[3,4,4,1]{3,2,1,0:T(4,128)S(1)} %get-tuple-element.106), channel_id=1, source_target_pairs={{0,16},{16,0},{1,17},{17,1},{2,18},{18,2},{3,19},{19,3},{4,20},{20... | collective-permute-start | bytes 584 | tf_op jit(solution)/shard_map/ppermute | solution.py:24
  49.1 3.8 %collective-permute-start.9 = (f32[3,4,4,1]{3,2,1,0:T(4,128)S(1)}, f32[3,4,4,1]{3,2,1,0:T(4,128)S(1)}, u32[]{:S(2)}, u32[]{:S(2)}) collective-permute-start(f32[3,4,4,1]{3,2,1,0:T(4,128)S(1)} %get-tuple-element.105), channel_id=1, source_target_pairs={{16,0},{0,16},{17,1},{1,17},{18,2},{2,18},{19,3},{3,19},{20,4},{4,... | collective-permute-start | bytes 584 | tf_op jit(solution)/shard_map/ppermute | solution.py:25
  53.1 1.4 collective-permute-start.10
  53.1 5.8 %collective-permute-start.11 = (f32[3,4,1,66]{3,2,1,0:T(1,128)S(1)}, f32[3,4,1,66]{3,2,1,0:T(1,128)S(1)}, u32[]{:S(2)}, u32[]{:S(2)}) collective-permute-start(f32[3,4,1,66]{3,2,1,0:T(1,128)S(1)} %get-tuple-element.89), channel_id=1, source_target_pairs={{0,1},{1,2},{2,3},{3,4},{4,5},{5,6},{6,7},{7,8},{8,9},{9,10},{10,1... | collective-permute-start | bytes 9512 | tf_op jit(solution)/shard_map/ppermute | solution.py:24
  72.9 7.7 %collective-permute-start.12 = (f32[2,1,3,4,1,128]{5,3,4,2,1,0:T(4,128)}, f32[2,1,3,4,1,128]{5,3,4,2,1,0:T(4,128)S(1)}, u32[]{:S(2)}, u32[]{:S(2)}) collective-permute-start(f32[2,1,3,4,1,128]{5,3,4,2,1,0:T(4,128)} %copy.500), channel_id=1, source_target_pairs={{0,1},{1,2},{2,3},{3,4},{4,5},{5,6},{6,7},{7,8},{8,9},{9,10},{10,1... | collective-permute-start | bytes 36872 | tf_op jit(solution)/shard_map/ppermute | solution.py:24
  74.2 6.5 %collective-permute-start.13 = (f32[2,1,3,4,1,128]{5,3,4,2,1,0:T(4,128)}, f32[2,1,3,4,1,128]{5,3,4,2,1,0:T(4,128)}, u32[]{:S(2)}, u32[]{:S(2)}) collective-permute-start(f32[2,1,3,4,1,128]{5,3,4,2,1,0:T(4,128)} %copy.501), channel_id=1, source_target_pairs={{1,0},{2,1},{3,2},{4,3},{5,4},{6,5},{7,6},{8,7},{9,8},{10,9},{11,1... | collective-permute-start | bytes 36872 | tf_op jit(solution)/shard_map/ppermute | solution.py:25
  86.0 6.4 %collective-permute-start.16 = (f32[8,2,3,4,1,128]{5,4,3,2,1,0:T(1,128)S(1)}, f32[8,2,3,4,1,128]{5,4,3,2,1,0:T(1,128)S(1)}, u32[]{:S(2)}, u32[]{:S(2)}) collective-permute-start(f32[8,2,3,4,1,128]{5,4,3,2,1,0:T(1,128)S(1)} %get-tuple-element.73), channel_id=1, source_target_pairs={{1,0},{2,1},{3,2},{4,3},{5,4},{6,5},{7,6},{8,7},{9,8},{10,9},{11,1... | collective-permute-start | bytes 294920 | tf_op jit(solution)/shard_map/ppermute | solution.py:25
  90.2 6.7 %collective-permute-start.17 = (f32[8,2,3,4,1,128]{5,4,3,2,1,0:T(1,128)S(1)}, f32[8,2,3,4,1,128]{5,4,3,2,1,0:T(1,128)S(1)}, u32[]{:S(2)}, u32[]{:S(2)}) collective-permute-start(f32[8,2,3,4,1,128]{5,4,3,2,1,0:T(1,128)S(1)} %get-tuple-element.74), channel_id=1, source_target_pairs={{0,1},{1,2},{2,3},{3,4},{4,5},{5,6},{6,7},{7,8},{8,9},{9,10},{10,1... | collective-permute-start | bytes 294920 | tf_op jit(solution)/shard_map/ppermute | solution.py:24
  99.1 2.3 %collective-permute-start.18 = (f32[8,2,3,4,1,128]{5,4,3,2,1,0:T(1,128)S(1)}, f32[8,2,3,4,1,128]{5,4,3,2,1,0:T(1,128)S(1)}, u32[]{:S(2)}, u32[]{:S(2)}) collective-permute-start(f32[8,2,3,4,1,128]{5,4,3,2,1,0:T(1,128)S(1)} %get-tuple-element.63), channel_id=1, source_target_pairs={{1,0},{2,1},{3,2},{4,3},{5,4},{6,5},{7,6},{8,7},{9,8},{10,9},{11,1... | collective-permute-start | bytes 294920 | tf_op jit(solution)/shard_map/ppermute | solution.py:25
  99.2 6.9 %collective-permute-start.19 = (f32[8,2,3,4,1,128]{5,4,3,2,1,0:T(1,128)S(1)}, f32[8,2,3,4,1,128]{5,4,3,2,1,0:T(1,128)S(1)}, u32[]{:S(2)}, u32[]{:S(2)}) collective-permute-start(f32[8,2,3,4,1,128]{5,4,3,2,1,0:T(1,128)S(1)} %get-tuple-element.64), channel_id=1, source_target_pairs={{0,1},{1,2},{2,3},{3,4},{4,5},{5,6},{6,7},{7,8},{8,9},{9,10},{10,1... | collective-permute-start | bytes 294920 | tf_op jit(solution)/shard_map/ppermute | solution.py:24
  108.3 2.3 %collective-permute-start.20 = (f32[8,2,3,4,1,128]{5,4,3,2,1,0:T(1,128)S(1)}, f32[8,2,3,4,1,128]{5,4,3,2,1,0:T(1,128)S(1)}, u32[]{:S(2)}, u32[]{:S(2)}) collective-permute-start(f32[8,2,3,4,1,128]{5,4,3,2,1,0:T(1,128)S(1)} %get-tuple-element.53), channel_id=1, source_target_pairs={{1,0},{2,1},{3,2},{4,3},{5,4},{6,5},{7,6},{8,7},{9,8},{10,9},{11,1... | collective-permute-start | bytes 294920 | tf_op jit(solution)/shard_map/ppermute | solution.py:25
  108.3 6.8 %collective-permute-start.21 = (f32[8,2,3,4,1,128]{5,4,3,2,1,0:T(1,128)S(1)}, f32[8,2,3,4,1,128]{5,4,3,2,1,0:T(1,128)S(1)}, u32[]{:S(2)}, u32[]{:S(2)}) collective-permute-start(f32[8,2,3,4,1,128]{5,4,3,2,1,0:T(1,128)S(1)} %get-tuple-element.54), channel_id=1, source_target_pairs={{0,1},{1,2},{2,3},{3,4},{4,5},{5,6},{6,7},{7,8},{8,9},{9,10},{10,1... | collective-permute-start | bytes 294920 | tf_op jit(solution)/shard_map/ppermute | solution.py:24
  (7 other events, 44.2 us)
where the time goes:
time: 148 us; the launch traced here: 147 us
  blocking collectives  47 us (32%)
  waiting for transfers between devices  35.3 us (24%)
  starting transfers between devices  25.9 us (18%)
  other arithmetic  19.5 us (13%)
  local copies, waits for them, and re-layouts  18.5 us (12%)
    psum x1, blocking collectives, record(): summed_terms.append(lax.psum(local, 'space'))  29.5 us
    ppermute x11, waiting for transfers between devices, extended(): before = lax.ppermute(last, axis, up)  27.2 us
    ppermute x11, starting transfers between devices, extended(): after = lax.ppermute(leading, axis, down)  15.9 us
    ppermute x11, starting transfers between devices, extended(): before = lax.ppermute(last, axis, up)  9.99 us
    all_gather x1, blocking collectives, shards(): lax.all_gather(bonds, 'probe', axis=3, tiled=True)  9.06 us
    all_gather x1, blocking collectives, shards(): lax.all_gather(spins, 'probe', axis=3, tiled=True)  8.45 us
    ppermute x11, waiting for transfers between devices, extended(): after = lax.ppermute(leading, axis, down)  8.1 us
    add x1, other arithmetic, bond_strengths(): strengths + jnp.where(bond_class == class_index, exchange[class_index], 0.0)  5.92 us
  transfers between devices with their start and end apart: 22, of which 12 were waited for; matrix products, arithmetic and copies ran while one was open for 13% of the time, Pallas kernels for 0%

commit v1 on v0

v1 whole, which is shorter than its diff:
```python
import math

import jax
import jax.numpy as jnp
from jax import lax
from jax.sharding import PartitionSpec as P

LZ = 4
SWEEPS = 2
CHEB = 4
HALO_SLABS = 2


relax_rate = 0.15
precess_scale = 1.0 / 6.0


def shifted(array, axis, shift):
    size = lax.axis_size(axis)
    if shift % size == 0:
        return array
    return lax.ppermute(array, axis, [(i, (i - shift) % size) for i in range(size)])


def bond_strengths(bond_class, exchange):
    strengths = jnp.zeros(bond_class.shape, exchange.dtype)
    for class_index in range(exchange.shape[0]):
        strengths = strengths + jnp.where(bond_class == class_index, exchange[class_index], 0.0)
    return strengths


def cross_product(spin_core, vector):
    spin_a, spin_b, spin_c = (spin_core[0], spin_core[1], spin_core[2])
    vec_a = vector[..., 0, :, :, :]
    vec_b = vector[..., 1, :, :, :]
    vec_c = vector[..., 2, :, :, :]
    return jnp.stack(
        [
            spin_b * vec_c - spin_c * vec_b,
            spin_c * vec_a - spin_a * vec_c,
            spin_a * vec_b - spin_b * vec_a,
        ],
        axis=-4,
    )


def rows(array, start, stop):
    return lax.slice_in_dim(array, start, stop, axis=array.ndim - 2)


def neighbour_window(vector, bonds):
    n = vector.shape[-2]
    along_x, along_y, along_z = (bonds[0], bonds[1], bonds[2])
    total = rows(along_x, 1, n - 1) * rows(vector, 2, n) + rows(along_x, 0, n - 2) * rows(vector, 0, n - 2)
    centre = rows(vector, 1, n - 1)
    bond_y = rows(along_y, 1, n - 1)
    total = total + bond_y * jnp.roll(centre, -1, -1) + jnp.roll(bond_y, 1, -1) * jnp.roll(centre, 1, -1)
    bond_z = rows(along_z, 1, n - 1)
    total = total + bond_z * jnp.roll(centre, -1, -3) + jnp.roll(bond_z, 1, -3) * jnp.roll(centre, 1, -3)
    return total


def relax_update(spins, field):
    turned = cross_product(spins, field)
    twice = cross_product(spins, turned)
    moved = spins - relax_rate * twice
    length = jnp.sqrt(jnp.sum(moved * moved, axis=0))
    return moved / length


def make_probes(probe_wave, probe_ids, x_coords, y_coords, total_x, total_y, depth_z):
    wave_x = probe_wave[:, 0][:, None]
    wave_y = probe_wave[:, 1][:, None]
    wave_z = probe_wave[:, 2][:, None]
    phase_x = wave_x * x_coords[None, :] % total_x
    phase_y = wave_y * y_coords[None, :] % total_y
    phase_z = wave_z * jnp.arange(depth_z, dtype=jnp.int32)[None, :] % depth_z
    fraction = (
        phase_z[:, :, None, None].astype(jnp.float32) / depth_z
        + phase_x[:, None, :, None].astype(jnp.float32) / total_x
        + phase_y[:, None, None, :].astype(jnp.float32) / total_y
    )
    angle = 2.0 * math.pi * fraction
    ramp = jnp.sqrt(1.0 + 2.0 * x_coords.astype(jnp.float32) / total_x)[None, None, :, None]
    waves = jnp.stack([jnp.cos(angle) * ramp, jnp.sin(angle) * ramp], 1)
    polar = ((probe_ids % 3)[:, None] == jnp.arange(3, dtype=jnp.int32)[None, :]).astype(
        jnp.float32
    )
    return waves[:, :, None] * polar[:, None, :, None, None, None]


def butterfly_sum(value, axis):
    size = lax.axis_size(axis)
    if size & (size - 1):
        return lax.psum(value, axis)
    step = 1
    while step < size:
        value = value + lax.ppermute(value, axis, [(i, i ^ step) for i in range(size)])
        step *= 2
    return value


def shards(cos_polar, azimuth, bond_class, exchange, probe_wave):
    groups = lax.axis_size("probe")
    slabs = lax.axis_size("space")
    group = lax.axis_index("probe")
    slab = lax.axis_index("space")
    slab_rows = cos_polar.shape[1]
    block_y = cos_polar.shape[2]
    total_x = slab_rows * slabs
    total_y = block_y * groups
    site_count = total_x * total_y * LZ

    bonds = bond_strengths(bond_class, exchange)
    local = jnp.concatenate([cos_polar[None], azimuth[None], bonds], 0)

    pieces = [shifted(local, "probe", k) for k in range(groups)]
    rotated = jnp.concatenate(pieces, -1)
    full_y = jnp.roll(rotated, group * block_y, -1) if groups > 1 else rotated

    window = jnp.concatenate(
        [shifted(full_y, "space", k) for k in range(-HALO_SLABS, HALO_SLABS + 1)], -2
    )
    halo = HALO_SLABS * slab_rows
    cos_w, az_w, bonds_w = window[0], window[1], window[2:]

    radial = jnp.sqrt(1.0 - cos_w * cos_w)
    spins = jnp.stack([radial * jnp.cos(az_w), radial * jnp.sin(az_w), cos_w], 0)
    sweep_bonds = bonds_w
    for sweep_index in range(SWEEPS):
        n = spins.shape[-2]
        field = neighbour_window(spins, sweep_bonds)
        spins = relax_update(rows(spins, 1, n - 1), field)
        sweep_bonds = rows(sweep_bonds, 1, n - 1)
    own = halo - SWEEPS
    relaxed_own = lax.dynamic_slice_in_dim(rows(spins, own, own + slab_rows), group * block_y, block_y, -1)

    reach = CHEB
    first = halo - reach
    width = slab_rows + 2 * reach
    x_coords = (slab * slab_rows - reach + jnp.arange(width, dtype=jnp.int32)) % total_x
    y_coords = jnp.arange(total_y, dtype=jnp.int32)
    group_size = probe_wave.shape[0]
    probe_ids = group * group_size + jnp.arange(group_size, dtype=jnp.int32)
    start = make_probes(probe_wave, probe_ids, x_coords, y_coords, total_x, total_y, LZ)

    def precess(vector, lo):
        n = vector.shape[-2]
        field = neighbour_window(vector, rows(bonds_w, lo, lo + n))
        spin_rows = rows(spins, lo + 1 - SWEEPS, lo + n - 1 - SWEEPS)
        return cross_product(spin_rows, field) * -precess_scale

    terms = []
    previous, current, lo = start, start, first
    for order in range(CHEB):
        advanced = precess(current, lo)
        n = current.shape[-2]
        if order > 0:
            advanced = 2.0 * advanced - rows(previous, 2, n)
        previous, current, lo = current, advanced, lo + 1
        keep = halo - lo
        mine = rows(current, keep, keep + slab_rows)
        terms.append(jnp.sum(mine * mine, axis=(1, 2, 3, 4, 5)))
    moment_rows = butterfly_sum(jnp.stack(terms, 1), "space") / site_count
    return (relaxed_own, current.astype(jnp.bfloat16), moment_rows)


def solution(mesh):
    return jax.shard_map(
        shards,
        mesh=mesh,
        in_specs=(
            P(None, "space", "probe"),
            P(None, "space", "probe"),
            P(None, None, "space", "probe"),
            P(),
            P("probe", None),
        ),
        out_specs=(
            P(None, None, "space", "probe"),
            P("probe", None, None, None, "space", None),
            P("probe", None),
        ),
        check_vma=False,
    )
```

time: 148 us -> 58.7 us (0.40)
  blocking collectives: 47 us -> 0 us
  waiting for transfers between devices: 35.3 us -> 13.8 us
  starting transfers between devices: 25.9 us -> 10.5 us
  other arithmetic: 19.5 us -> 16.4 us
  local copies, waits for them, and re-layouts: 18.5 us -> 16.1 us
    psum x1 -> x0, blocking collectives: 29.5 us -> none  [record(): summed_terms.append(lax.psum(local, 'space'))]
    ppermute x22 -> x9, waiting for transfers between devices: 35.3 us -> 13.8 us  [the longest x4 11.3 us: butterfly_sum(): lax.ppermute(value, axis, [(i, i ^ step) for i in range(size)])]
    all_gather x2 -> x0, blocking collectives: 17.5 us -> none  [the longest x1 9.06 us: shards(): lax.all_gather(bonds, 'probe', axis=3, tiled=True)]
    ppermute x22 -> x9, starting transfers between devices: 25.9 us -> 10.5 us  [the longest x5 9.52 us: shifted(): lax.ppermute(array, axis, [(i, (i - shift) % size) for i in range(size)])]
    slice x54 -> x67, local copies, waits for them, and re-layouts: 13.6 us -> 9.97 us  [the longest x12 6.16 us: neighbour_window(): jnp.roll(centre, 1, -1)]
    add x7 -> x8, other arithmetic: 5.46 us -> 3.08 us  [the longest x5 3.05 us: neighbour_window(): total + bond_z * jnp.roll(centre, -1, -3)]
    another operation x3 -> x2, other arithmetic: 1.59 us -> 0.03 us  [the longest x1 0.01 us: shards(): jnp.stack([radial * jnp.cos(az_w), radial * jnp.sin(az_w), cos_w], 0)]
  transfers between devices with their start and end apart: 22 -> 9, of which waited for: 12 -> 6; matrix products, arithmetic and copies ran while one was open for 13% -> 17% of each run, Pallas kernels for 0% -> 0%
where the time goes in v1:
time: 58.7 us; the launch traced here: 58.3 us
  other arithmetic  16.4 us (28%)
  local copies, waits for them, and re-layouts  16.1 us (27%)
  waiting for transfers between devices  13.8 us (24%)
  starting transfers between devices  10.5 us (18%)
  between operations  1.4 us (2%)
    ppermute x4, waiting for transfers between devices, butterfly_sum(): lax.ppermute(value, axis, [(i, i ^ step) for i in range(size)])  11.3 us
    ppermute x5, starting transfers between devices, shifted(): lax.ppermute(array, axis, [(i, (i - shift) % size) for i in range(size)])  9.52 us
    slice x12, local copies, waits for them, and re-layouts, neighbour_window(): jnp.roll(centre, 1, -1)  6.16 us
    add x1, other arithmetic, bond_strengths(): strengths + jnp.where(bond_class == class_index, exchange[class_index], 0.0)  5.75 us
    slice x12, local copies, waits for them, and re-layouts, neighbour_window(): jnp.roll(centre, 1, -3)  3.15 us
    add x5, other arithmetic, neighbour_window(): total + bond_z * jnp.roll(centre, -1, -3)  3.05 us
    ppermute x5, waiting for transfers between devices, shifted(): lax.ppermute(array, axis, [(i, (i - shift) % size) for i in range(size)])  2.54 us
    reduce_sum x3, other arithmetic, shards(): terms.append(jnp.sum(mine * mine, axis=(1, 2, 3, 4, 5)))  2.18 us
  transfers between devices with their start and end apart: 9, of which 6 were waited for; matrix products, arithmetic and copies ran while one was open for 17% of the time, Pallas kernels for 0%

profile of v1, /device:TPU:0, one launch (start us, length us, event | category | flops | bytes accessed | tf_op | source)
XLA Modules:
  0.0 58.3 jit_solution(5325308511113303790)
XLA Ops:
  0.6 1.6 %fusion.89 = (f32[1]{0:T(128)}, f32[1]{0:T(128)}, f32[1]{0:T(128)}, f32[1]{0:T(128)}, f32[1]{0:T(128)}, /*index=5*/f32[1]{0:T(128)}, f32[1]{0:T(128)}, f32[1]{0:T(128)}) fusion(f32[8]{0:T(128)} %param.8), kind=kLoop, calls=%fused_computation.252 | loop fusion | bytes 64 | tf_op jit(solution)/shard_map/slice | solution.py:28
  2.2 5.8 %select_add_fusion = f32[3,4,4,64]{3,2,1,0:T(4,128)S(1)} fusion(s32[3,4,4,64]{3,2,1,0:T(4,128)} %param.7, f32[]{:T(128)} %bitcast.9, f32[]{:T(128)} %bitcast.8, f32[]{:T(128)} %bitcast.7, f32[]{:T(128)} %bitcast.6, f32[]{:T(128)} %bitcast.5, f32[]{:T(128)} %bitcast.4, f32[]{:T(128)} %bitcast.3, f32[]{:T(128)} %bitcast.2), kind=kLoop, calls=%fused_computation.158 | loop fusion | flops 70656 | bytes 24608 | tf_op jit(solution)/shard_map/add | solution.py:28
  8.0 0.7 %pad_maximum_fusion.5 = f32[5,4,4,64]{3,2,1,0:T(4,128)S(1)} fusion(f32[3,4,4,64]{3,2,1,0:T(4,128)S(1)} %select_add_fusion, f32[1,4,4,64]{3,2,1,0:T(4,128)} %bitcast.82, f32[1,4,4,64]{3,2,1,0:T(4,128)} %bitcast.80), kind=kLoop, calls=%fused_computation.138 | loop fusion | flops 10240 | bytes 40960 | tf_op jit(solution)/shard_map/concatenate | solution.py:115
  8.7 3.0 %collective-permute-start = (f32[5,4,4,64]{3,2,1,0:T(4,128)S(1)}, f32[5,4,4,64]{3,2,1,0:T(4,128)S(1)}, u32[]{:S(2)}, u32[]{:S(2)}) collective-permute-start(f32[5,4,4,64]{3,2,1,0:T(4,128)S(1)} %pad_maximum_fusion.5), channel_id=1, source_target_pairs={{0,16},{16,0},{1,17},{17,1},{2,18},{18,2},{3,19},{19,3},{4,20},{20... | collective-permute-start | bytes 61448 | tf_op jit(solution)/shard_map/ppermute | solution.py:22
  11.9 0.8 %slice_bitcast_fusion.32 = (s32[8]{0:T(128)S(1)}, s32[8]{0:T(128)S(1)}, s32[8]{0:T(128)S(1)}) fusion(s32[8,3]{0,1:T(4,128)} %param.9), kind=kLoop, calls=%fused_computation.220 | loop fusion | bytes 192 | tf_op jit(solution)/shard_map/slice | solution.py:74
  13.0 1.1 %cosine_multiply_fusion = (f32[8,1,4,12,128]{4,3,2,1,0:T(8,128)S(1)}, f32[8,1,4,12,128]{4,3,2,1,0:T(8,128)S(1)}) fusion(f32[12]{0:T(128)S(1)} %add_sqrt_fusion, f32[8,128]{1,0:T(8,128)S(1)} %fusion.47, f32[8,4,12]{2,1,0:T(4,128)S(1)} %broadcast_add_fusion), kind=kLoop, calls=%fused_computation.69 | loop fusion | flops 196608 | bytes 398896 | tf_op jit(solution)/shard_map/mul | solution.py:85
  14.3 1.8 %fusion.65 = (f32[8,2,3,4,10,1]{5,4,3,2,1,0:T(8,128)S(1)}, f32[8,2,3,4,10,1]{5,4,3,2,1,0:T(8,128)}) fusion(f32[8,2,3,4,12,128]{5,4,3,2,1,0:T(8,128)S(1)} %broadcast_multiply_fusion), kind=kLoop, calls=%fused_computation.228 | loop fusion | bytes 30720 | tf_op jit(solution)/shard_map/jit(_roll_static)/slice | solution.py:57
  16.1 2.2 %fusion.66 = (f32[8,2,3,4,10,127]{5,4,3,2,1,0:T(8,128)}, f32[8,2,3,4,10,127]{5,4,3,2,1,0:T(8,128)}) fusion(f32[8,2,3,4,12,128]{5,4,3,2,1,0:T(8,128)S(1)} %broadcast_multiply_fusion), kind=kLoop, calls=%fused_computation.229 | loop fusion | bytes 3901440 | tf_op jit(solution)/shard_map/jit(_roll_static)/slice | solution.py:57
  18.3 1.6 %fusion.64 = (f32[8,2,3,3,10,128]{5,4,3,2,1,0:T(8,128)}, f32[8,2,3,3,10,128]{5,4,3,2,1,0:T(8,128)}) fusion(f32[8,2,3,4,12,128]{5,4,3,2,1,0:T(8,128)S(1)} %broadcast_multiply_fusion), kind=kLoop, calls=%fused_computation.227 | loop fusion | bytes 2949120 | tf_op jit(solution)/shard_map/jit(_roll_static)/slice | solution.py:59
  20.0 1.6 %collective-permute-start.1 = (f32[5,4,4,128]{3,2,1,0:T(4,128)S(1)}, f32[5,4,4,128]{3,2,1,0:T(4,128)S(1)}, u32[]{:S(2)}, u32[]{:S(2)}) collective-permute-start(f32[5,4,4,128]{3,2,1,0:T(4,128)S(1)} %fusion.37), channel_id=1, source_target_pairs={{0,2},{1,3},{2,4},{3,5},{4,6},{5,7},{6,8},{7,9},{8,10},{9,11},{10,... | collective-permute-start | bytes 122888 | tf_op jit(solution)/shard_map/ppermute | solution.py:22
  21.6 4.4 %collective-permute-start.3 = (f32[5,4,4,128]{3,2,1,0:T(4,128)S(1)}, f32[5,4,4,128]{3,2,1,0:T(4,128)S(1)}, u32[]{:S(2)}, u32[]{:S(2)}) collective-permute-start(f32[5,4,4,128]{3,2,1,0:T(4,128)S(1)} %fusion.37), channel_id=1, source_target_pairs={{0,15},{1,0},{2,1},{3,2},{4,3},{5,4},{6,5},{7,6},{8,7},{9,8},{10,9... | collective-permute-start | bytes 122888 | tf_op jit(solution)/shard_map/ppermute | solution.py:22
  26.6 1.1 %fusion.63 = (f32[8,2,3,1,10,128]{5,4,3,2,1,0:T(8,128)}, f32[8,2,3,1,10,128]{5,4,3,2,1,0:T(8,128)}) fusion(f32[8,2,3,4,12,128]{5,4,3,2,1,0:T(8,128)S(1)} %broadcast_multiply_fusion), kind=kLoop, calls=%fused_computation.226 | loop fusion | bytes 983040 | tf_op jit(solution)/shard_map/jit(_roll_static)/slice | solution.py:59
  27.7 2.4 %collective-permute-done.4 = f32[5,4,4,128]{3,2,1,0:T(4,128)} collective-permute-done((f32[5,4,4,128]{3,2,1,0:T(4,128)S(1)}, f32[5,4,4,128]{3,2,1,0:T(4,128)}, u32[]{:S(2)}, u32[]{:S(2)}) %collective-permute-start.4) | collective-permute-done | bytes 40992 | tf_op jit(solution)/shard_map/ppermute | solution.py:22
  30.2 0.9 %concatenate.168 = f32[5,4,20,128]{3,2,1,0:T(8,128)S(1)} concatenate(f32[5,4,4,128]{3,2,1,0:T(4,128)S(1)} %collective-permute-done.1, f32[5,4,4,128]{3,2,1,0:T(4,128)S(1)} %collective-permute-done.2, f32[5,4,4,128]{3,2,1,0:T(4,128)S(1)} %fusion.37, f32[5,4,4,128]{3,2,1,0:T(4,128)S(1)} %collective-permute-done.3, f32[5,4,4,128]{3,2,1,0:T(4,128)} %collective-permute-done.4), dimensions={2} | concatenate | bytes 409600 | tf_op jit(solution)/shard_map/concatenate | solution.py:121
  35.5 1.4 %fusion.4 = f32[8,2,3,4,10,128]{5,4,3,2,1,0:T(8,128)S(1)} fusion(f32[8,2,3,4,12,128]{5,4,3,2,1,0:T(8,128)S(1)} %broadcast_multiply_fusion, f32[8,2,3,4,10,1]{5,4,3,2,1,0:T(8,128)S(1)} %copy-done, f32[8,2,3,4,10,127]{5,4,3,2,1,0:T(8,128)S(1)} %copy-done.2, f32[8,2,3,4,10,127]{5,4,3,2,1,0:T(8,128)S(1)} %copy-done.1, ...), kind=kLoop, calls=%fused_computation.5 | loop fusion | flops 3686400 | bytes 7004160 | tf_op jit(solution)/shard_map/add | solution.py:59
  40.3 0.7 %fusion.9 = f32[8,2,3,4,6,128]{5,4,3,2,1,0:T(8,128)S(1)} fusion(f32[8,2,3,4,8,128]{5,4,3,2,1,0:T(8,128)S(1)} %slice_subtract_fusion.1, f32[8,2,3,4,6,1]{5,4,3,2,1,0:T(8,128)S(1)} %get-tuple-element.56, f32[8,2,3,4,6,127]{5,4,3,2,1,0:T(8,128)S(1)} %get-tuple-element.58, f32[8,2,3,4,6,127]{5,4,3,2,1,0:T(8,128)S(1)} %get-tuple-element.57, ...), kind=kLoop, calls=%fused_computation.18 | loop fusion | flops 2211840 | bytes 4202496 | tf_op jit(solution)/shard_map/add | solution.py:59
  42.6 0.9 %fusion.15 = (f32[8]{0:T(128)S(1)}, f32[8,2,3,4,4,128]{5,4,3,2,1,0:T(4,128)S(1)}) fusion(f32[8,2,3,4,6,128]{5,4,3,2,1,0:T(8,128)S(1)} %slice_subtract_fusion, f32[8,2,3,3,4,128]{5,4,3,2,1,0:T(4,128)S(1)} %get-tuple-element.45, f32[8,2,3,1,4,128]{5,4,3,2,1,0:T(4,128)S(1)} %get-tuple-element.43, f32[4,4,128]{2,1,0:T(4,128)S(1)} %get-tuple-element.145, ...), kind=kLoop, calls=%fused_computation.44 | loop fusion | flops 1671160 | bytes 3194912 | tf_op jit(solution)/shard_map/reduce_sum | solution.py:163
  43.6 1.1 %multiply_reduce_fusion = (f32[8]{0:T(128)S(1)}, bf16[8,2,3,4,4,128]{5,4,3,2,1,0:T(4,128)(2,1)}, f32[8]{0:T(128)S(1)}) fusion(f32[8,2,3,4,8,128]{5,4,3,2,1,0:T(8,128)S(1)} %slice_subtract_fusion.1, f32[8,2,1,4,4,128]{5,4,3,2,1,0:T(4,128)S(1)} %get-tuple-element.61, f32[8,2,1,4,4,128]{5,4,3,2,1,0:T(4,128)S(1)} %get-tuple-element.60, ...), kind=kLoop, calls=%fused_computation.60 | loop fusion | flops 884720 | bytes 983104 | tf_op jit(solution)/shard_map/reduce_sum | solution.py:163
  44.8 1.1 %collective-permute-done.5 = f32[8,4]{0,1:T(4,128)S(1)} collective-permute-done((f32[8,4]{0,1:T(4,128)S(1)}, f32[8,4]{0,1:T(4,128)S(1)}, u32[]{:S(2)}, u32[]{:S(2)}) %collective-permute-start.5) | collective-permute-done | bytes 160 | tf_op jit(solution)/shard_map/ppermute | solution.py:98
  46.0 3.6 %collective-permute-done.6 = f32[8,4]{0,1:T(4,128)S(1)} collective-permute-done((f32[8,4]{0,1:T(4,128)S(1)}, f32[8,4]{0,1:T(4,128)S(1)}, u32[]{:S(2)}, u32[]{:S(2)}) %collective-permute-start.6) | collective-permute-done | bytes 160 | tf_op jit(solution)/shard_map/ppermute | solution.py:98
  49.7 3.6 %collective-permute-done.7 = f32[8,4]{0,1:T(4,128)S(1)} collective-permute-done((f32[8,4]{0,1:T(4,128)S(1)}, f32[8,4]{0,1:T(4,128)S(1)}, u32[]{:S(2)}, u32[]{:S(2)}) %collective-permute-start.7) | collective-permute-done | bytes 160 | tf_op jit(solution)/shard_map/ppermute | solution.py:98
  53.2 0.8 %collective-permute-start.8 = (f32[8,4]{0,1:T(4,128)S(1)}, f32[8,4]{0,1:T(4,128)S(1)}, u32[]{:S(2)}, u32[]{:S(2)}) collective-permute-start(f32[8,4]{0,1:T(4,128)S(1)} %add.322), channel_id=1, source_target_pairs={{0,8},{1,9},{2,10},{3,11},{4,12},{5,13},{6,14},{7,15},{8,0},{9,1},... | collective-permute-start | bytes 392 | tf_op jit(solution)/shard_map/ppermute | solution.py:98
  54.0 0.7 %constant_dynamic-slice_fusion = f32[3,4,4,64]{3,2,1,0:T(4,128)} fusion(f32[3,4,4,128]{3,2,1,0:T(4,128)S(1)} %slice.1013, s32[]{:T(128)S(6)} %select_n.105), kind=kLoop, calls=%fused_computation.209 | loop fusion | bytes 24580 | tf_op jit(solution)/shard_map/dynamic_slice | solution.py:136
  54.7 3.0 %collective-permute-done.8 = f32[8,4]{0,1:T(4,128)S(1)} collective-permute-done((f32[8,4]{0,1:T(4,128)S(1)}, f32[8,4]{0,1:T(4,128)S(1)}, u32[]{:S(2)}, u32[]{:S(2)}) %collective-permute-start.8) | collective-permute-done | bytes 160 | tf_op jit(solution)/shard_map/ppermute | solution.py:98
  (147 shorter events, 11.2 us)
Async XLA Ops:
  8.7 11.1 %collective-permute-start = (f32[5,4,4,64]{3,2,1,0:T(4,128)S(1)}, f32[5,4,4,64]{3,2,1,0:T(4,128)S(1)}, u32[]{:S(2)}, u32[]{:S(2)}) collective-permute-start(f32[5,4,4,64]{3,2,1,0:T(4,128)S(1)} %pad_maximum_fusion.5), channel_id=1, source_target_pairs={{0,16},{16,0},{1,17},{17,1},{2,18},{18,2},{3,19},{19,3},{4,20},{20... | collective-permute-start | bytes 61448 | tf_op jit(solution)/shard_map/ppermute | solution.py:22
  18.3 1.6 %copy-start.7 = (f32[4,4,64]{2,1,0:T(4,128)S(1)}, f32[4,4,64]{2,1,0:T(4,128)}, u32[]{:S(2)}) copy-start(f32[4,4,64]{2,1,0:T(4,128)} %param.5) | copy-start | bytes 12292
  18.3 1.6 %copy-start.8 = (f32[4,4,64]{2,1,0:T(4,128)S(1)}, f32[4,4,64]{2,1,0:T(4,128)}, u32[]{:S(2)}) copy-start(f32[4,4,64]{2,1,0:T(4,128)} %param.6) | copy-start | bytes 12292
  20.0 7.6 %collective-permute-start.1 = (f32[5,4,4,128]{3,2,1,0:T(4,128)S(1)}, f32[5,4,4,128]{3,2,1,0:T(4,128)S(1)}, u32[]{:S(2)}, u32[]{:S(2)}) collective-permute-start(f32[5,4,4,128]{3,2,1,0:T(4,128)S(1)} %fusion.37), channel_id=1, source_target_pairs={{0,2},{1,3},{2,4},{3,5},{4,6},{5,7},{6,8},{7,9},{8,10},{9,11},{10,... | collective-permute-start | bytes 122888 | tf_op jit(solution)/shard_map/ppermute | solution.py:22
  21.6 6.1 %collective-permute-start.2 = (f32[5,4,4,128]{3,2,1,0:T(4,128)S(1)}, f32[5,4,4,128]{3,2,1,0:T(4,128)S(1)}, u32[]{:S(2)}, u32[]{:S(2)}) collective-permute-start(f32[5,4,4,128]{3,2,1,0:T(4,128)S(1)} %fusion.37), channel_id=1, source_target_pairs={{0,1},{1,2},{2,3},{3,4},{4,5},{5,6},{6,7},{7,8},{8,9},{9,10},{10,1... | collective-permute-start | bytes 122888 | tf_op jit(solution)/shard_map/ppermute | solution.py:22
  21.6 6.1 %collective-permute-start.3 = (f32[5,4,4,128]{3,2,1,0:T(4,128)S(1)}, f32[5,4,4,128]{3,2,1,0:T(4,128)S(1)}, u32[]{:S(2)}, u32[]{:S(2)}) collective-permute-start(f32[5,4,4,128]{3,2,1,0:T(4,128)S(1)} %fusion.37), channel_id=1, source_target_pairs={{0,15},{1,0},{2,1},{3,2},{4,3},{5,4},{6,5},{7,6},{8,7},{9,8},{10,9... | collective-permute-start | bytes 122888 | tf_op jit(solution)/shard_map/ppermute | solution.py:22
  26.1 4.1 %collective-permute-start.4 = (f32[5,4,4,128]{3,2,1,0:T(4,128)S(1)}, f32[5,4,4,128]{3,2,1,0:T(4,128)}, u32[]{:S(2)}, u32[]{:S(2)}) collective-permute-start(f32[5,4,4,128]{3,2,1,0:T(4,128)S(1)} %fusion.37), channel_id=1, source_target_pairs={{0,14},{1,15},{2,0},{3,1},{4,2},{5,3},{6,4},{7,5},{8,6},{9,7},{10,... | collective-permute-start | bytes 122888 | tf_op jit(solution)/shard_map/ppermute | solution.py:22
  32.0 1.4 %copy-start.5 = (f32[8,2,3,1,10,128]{5,4,3,2,1,0:T(8,128)S(1)}, f32[8,2,3,1,10,128]{5,4,3,2,1,0:T(8,128)}, u32[]{:S(2)}) copy-start(f32[8,2,3,1,10,128]{5,4,3,2,1,0:T(8,128)} %get-tuple-element.26) | copy-start | bytes 737284
  32.0 1.4 %copy-start.6 = (f32[8,2,3,1,10,128]{5,4,3,2,1,0:T(8,128)S(1)}, f32[8,2,3,1,10,128]{5,4,3,2,1,0:T(8,128)}, u32[]{:S(2)}) copy-start(f32[8,2,3,1,10,128]{5,4,3,2,1,0:T(8,128)} %get-tuple-element.27) | copy-start | bytes 737284
  32.0 1.5 %copy-start.4 = (f32[8,2,3,3,10,128]{5,4,3,2,1,0:T(8,128)S(1)}, f32[8,2,3,3,10,128]{5,4,3,2,1,0:T(8,128)}, u32[]{:S(2)}) copy-start(f32[8,2,3,3,10,128]{5,4,3,2,1,0:T(8,128)} %get-tuple-element.29) | copy-start | bytes 2211844
  32.2 1.7 %copy-start.3 = (f32[8,2,3,3,10,128]{5,4,3,2,1,0:T(8,128)S(1)}, f32[8,2,3,3,10,128]{5,4,3,2,1,0:T(8,128)}, u32[]{:S(2)}) copy-start(f32[8,2,3,3,10,128]{5,4,3,2,1,0:T(8,128)} %get-tuple-element.28) | copy-start | bytes 2211844
  32.4 2.0 %copy-start.2 = (f32[8,2,3,4,10,127]{5,4,3,2,1,0:T(8,128)S(1)}, f32[8,2,3,4,10,127]{5,4,3,2,1,0:T(8,128)}, u32[]{:S(2)}) copy-start(f32[8,2,3,4,10,127]{5,4,3,2,1,0:T(8,128)} %get-tuple-element.33) | copy-start | bytes 2926084
  32.8 2.2 %copy-start.1 = (f32[8,2,3,4,10,127]{5,4,3,2,1,0:T(8,128)S(1)}, f32[8,2,3,4,10,127]{5,4,3,2,1,0:T(8,128)}, u32[]{:S(2)}) copy-start(f32[8,2,3,4,10,127]{5,4,3,2,1,0:T(8,128)} %get-tuple-element.32) | copy-start | bytes 2926084
  32.8 2.6 %copy-start = (f32[8,2,3,4,10,1]{5,4,3,2,1,0:T(8,128)S(1)}, f32[8,2,3,4,10,1]{5,4,3,2,1,0:T(8,128)}, u32[]{:S(2)}) copy-start(f32[8,2,3,4,10,1]{5,4,3,2,1,0:T(8,128)} %get-tuple-element.31) | copy-start | bytes 23044
  44.7 1.2 %collective-permute-start.5 = (f32[8,4]{0,1:T(4,128)S(1)}, f32[8,4]{0,1:T(4,128)S(1)}, u32[]{:S(2)}, u32[]{:S(2)}) collective-permute-start(f32[8,4]{0,1:T(4,128)S(1)} %pad_maximum_fusion.16), channel_id=1, source_target_pairs={{0,1},{1,0},{2,3},{3,2},{4,5},{5,4},{6,7},{7,6},{8,9},{9,8},{10,11... | collective-permute-start | bytes 392 | tf_op jit(solution)/shard_map/ppermute | solution.py:98
  45.9 3.7 %collective-permute-start.6 = (f32[8,4]{0,1:T(4,128)S(1)}, f32[8,4]{0,1:T(4,128)S(1)}, u32[]{:S(2)}, u32[]{:S(2)}) collective-permute-start(f32[8,4]{0,1:T(4,128)S(1)} %fusion.57), channel_id=1, source_target_pairs={{0,2},{1,3},{2,0},{3,1},{4,6},{5,7},{6,4},{7,5},{8,10},{9,11},{10,... | collective-permute-start | bytes 392 | tf_op jit(solution)/shard_map/ppermute | solution.py:98
  49.6 3.7 %collective-permute-start.7 = (f32[8,4]{0,1:T(4,128)S(1)}, f32[8,4]{0,1:T(4,128)S(1)}, u32[]{:S(2)}, u32[]{:S(2)}) collective-permute-start(f32[8,4]{0,1:T(4,128)S(1)} %fusion.90), channel_id=1, source_target_pairs={{0,4},{1,5},{2,6},{3,7},{4,0},{5,1},{6,2},{7,3},{8,12},{9,13},{10,... | collective-permute-start | bytes 392 | tf_op jit(solution)/shard_map/ppermute | solution.py:98
  53.2 4.5 %collective-permute-start.8 = (f32[8,4]{0,1:T(4,128)S(1)}, f32[8,4]{0,1:T(4,128)S(1)}, u32[]{:S(2)}, u32[]{:S(2)}) collective-permute-start(f32[8,4]{0,1:T(4,128)S(1)} %add.322), channel_id=1, source_target_pairs={{0,8},{1,9},{2,10},{3,11},{4,12},{5,13},{6,14},{7,15},{8,0},{9,1},... | collective-permute-start | bytes 392 | tf_op jit(solution)/shard_map/ppermute | solution.py:98

commit v2 on v1

--- a/solution.py
+++ b/solution.py
@@ -23,10 +23,9 @@
 
 
 def bond_strengths(bond_class, exchange):
-    strengths = jnp.zeros(bond_class.shape, exchange.dtype)
-    for class_index in range(exchange.shape[0]):
-        strengths = strengths + jnp.where(bond_class == class_index, exchange[class_index], 0.0)
-    return strengths
+    classes = jnp.arange(exchange.shape[0], dtype=bond_class.dtype)
+    picked = jnp.where(bond_class[..., None] == classes, exchange, 0.0)
+    return jnp.sum(picked, axis=-1)
 
 
 def cross_product(spin_core, vector):

time: 58.7 us -> 52.1 us (0.89)
  other arithmetic: 16.4 us -> 11.6 us
  local copies, waits for them, and re-layouts: 16.1 us -> 14.5 us
    add x1 -> x0, other arithmetic: 5.75 us -> none  [bond_strengths(): strengths + jnp.where(bond_class == class_index, exchange[class_index], 0.0)]
    slice x1 -> x0, local copies, waits for them, and re-layouts: 1.6 us -> none  [bond_strengths(): exchange[class_index]]
    reduce_sum x0 -> x1, other arithmetic: none -> 0.89 us  [bond_strengths(): return jnp.sum(picked, axis=-1)]
  transfers between devices with their start and end apart: 9 -> 9, of which waited for: 6 -> 6; matrix products, arithmetic and copies ran while one was open for 17% -> 19% of each run, Pallas kernels for 0% -> 0%
where the time goes in v2:
time: 52.1 us; the launch traced here: 51.8 us
  local copies, waits for them, and re-layouts  14.5 us (28%)
  waiting for transfers between devices  13.8 us (26%)
  other arithmetic  11.6 us (22%)
  starting transfers between devices  10.5 us (20%)
  between operations  1.4 us (3%)
    ppermute x4, waiting for transfers between devices, butterfly_sum(): lax.ppermute(value, axis, [(i, i ^ step) for i in range(size)])  11.3 us
    ppermute x5, starting transfers between devices, shifted(): lax.ppermute(array, axis, [(i, (i - shift) % size) for i in range(size)])  9.52 us
    slice x12, local copies, waits for them, and re-layouts, neighbour_window(): jnp.roll(centre, 1, -1)  6.14 us
    slice x12, local copies, waits for them, and re-layouts, neighbour_window(): jnp.roll(centre, 1, -3)  3.13 us
    add x5, other arithmetic, neighbour_window(): total + bond_z * jnp.roll(centre, -1, -3)  3.05 us
    ppermute x5, waiting for transfers between devices, shifted(): lax.ppermute(array, axis, [(i, (i - shift) % size) for i in range(size)])  2.54 us
    reduce_sum x3, other arithmetic, shards(): terms.append(jnp.sum(mine * mine, axis=(1, 2, 3, 4, 5)))  2.18 us
    unnamed x18, local copies, waits for them, and re-layouts  2.1 us
  transfers between devices with their start and end apart: 9, of which 6 were waited for; matrix products, arithmetic and copies ran while one was open for 19% of the time, Pallas kernels for 0%

profile of v2, /device:TPU:0, one launch (start us, length us, event | category | flops | bytes accessed | tf_op | source)
XLA Modules:
  0.0 51.8 jit_solution(8755528941986670680)
XLA Ops:
  0.6 0.9 %select_reduce_fusion = f32[3,4,4,64]{3,2,1,0:T(4,128)S(1)} fusion(f32[8]{0:T(128)} %param.8, s32[3,4,4,64]{3,2,1,0:T(4,128)} %param.7), kind=kLoop, calls=%fused_computation.71 | loop fusion | flops 70656 | bytes 24608 | tf_op jit(solution)/shard_map/reduce_sum | solution.py:28
  1.5 0.7 %pad_maximum_fusion.5 = f32[5,4,4,64]{3,2,1,0:T(4,128)S(1)} fusion(f32[3,4,4,64]{3,2,1,0:T(4,128)S(1)} %select_reduce_fusion, f32[1,4,4,64]{3,2,1,0:T(4,128)} %bitcast.74, f32[1,4,4,64]{3,2,1,0:T(4,128)} %bitcast.72), kind=kLoop, calls=%fused_computation.140 | loop fusion | flops 10240 | bytes 40960 | tf_op jit(solution)/shard_map/concatenate | solution.py:114
  2.3 3.0 %collective-permute-start = (f32[5,4,4,64]{3,2,1,0:T(4,128)S(1)}, f32[5,4,4,64]{3,2,1,0:T(4,128)S(1)}, u32[]{:S(2)}, u32[]{:S(2)}) collective-permute-start(f32[5,4,4,64]{3,2,1,0:T(4,128)S(1)} %pad_maximum_fusion.5), channel_id=1, source_target_pairs={{0,16},{16,0},{1,17},{17,1},{2,18},{18,2},{3,19},{19,3},{4,20},{20... | collective-permute-start | bytes 61448 | tf_op jit(solution)/shard_map/ppermute | solution.py:22
  5.4 0.8 %slice_bitcast_fusion.32 = (s32[8]{0:T(128)S(1)}, s32[8]{0:T(128)S(1)}, s32[8]{0:T(128)S(1)}) fusion(s32[8,3]{0,1:T(4,128)} %param.9), kind=kLoop, calls=%fused_computation.221 | loop fusion | bytes 192 | tf_op jit(solution)/shard_map/slice | solution.py:73
  6.5 1.1 %cosine_multiply_fusion = (f32[8,1,4,12,128]{4,3,2,1,0:T(8,128)S(1)}, f32[8,1,4,12,128]{4,3,2,1,0:T(8,128)S(1)}) fusion(f32[12]{0:T(128)S(1)} %add_sqrt_fusion, f32[8,128]{1,0:T(8,128)S(1)} %fusion.47, f32[8,4,12]{2,1,0:T(4,128)S(1)} %broadcast_add_fusion), kind=kLoop, calls=%fused_computation.69 | loop fusion | flops 196608 | bytes 398896 | tf_op jit(solution)/shard_map/mul | solution.py:84
  7.9 1.7 %fusion.65 = (f32[8,2,3,4,10,1]{5,4,3,2,1,0:T(8,128)S(1)}, f32[8,2,3,4,10,1]{5,4,3,2,1,0:T(8,128)}) fusion(f32[8,2,3,4,12,128]{5,4,3,2,1,0:T(8,128)S(1)} %broadcast_multiply_fusion), kind=kLoop, calls=%fused_computation.229 | loop fusion | bytes 30720 | tf_op jit(solution)/shard_map/jit(_roll_static)/slice | solution.py:56
  9.6 2.2 %fusion.66 = (f32[8,2,3,4,10,127]{5,4,3,2,1,0:T(8,128)}, f32[8,2,3,4,10,127]{5,4,3,2,1,0:T(8,128)}) fusion(f32[8,2,3,4,12,128]{5,4,3,2,1,0:T(8,128)S(1)} %broadcast_multiply_fusion), kind=kLoop, calls=%fused_computation.230 | loop fusion | bytes 3901440 | tf_op jit(solution)/shard_map/jit(_roll_static)/slice | solution.py:56
  11.8 1.6 %fusion.64 = (f32[8,2,3,3,10,128]{5,4,3,2,1,0:T(8,128)}, f32[8,2,3,3,10,128]{5,4,3,2,1,0:T(8,128)}) fusion(f32[8,2,3,4,12,128]{5,4,3,2,1,0:T(8,128)S(1)} %broadcast_multiply_fusion), kind=kLoop, calls=%fused_computation.228 | loop fusion | bytes 2949120 | tf_op jit(solution)/shard_map/jit(_roll_static)/slice | solution.py:58
  13.6 1.6 %collective-permute-start.1 = (f32[5,4,4,128]{3,2,1,0:T(4,128)S(1)}, f32[5,4,4,128]{3,2,1,0:T(4,128)S(1)}, u32[]{:S(2)}, u32[]{:S(2)}) collective-permute-start(f32[5,4,4,128]{3,2,1,0:T(4,128)S(1)} %fusion.37), channel_id=1, source_target_pairs={{0,2},{1,3},{2,4},{3,5},{4,6},{5,7},{6,8},{7,9},{8,10},{9,11},{10,... | collective-permute-start | bytes 122888 | tf_op jit(solution)/shard_map/ppermute | solution.py:22
  15.1 4.4 %collective-permute-start.3 = (f32[5,4,4,128]{3,2,1,0:T(4,128)S(1)}, f32[5,4,4,128]{3,2,1,0:T(4,128)S(1)}, u32[]{:S(2)}, u32[]{:S(2)}) collective-permute-start(f32[5,4,4,128]{3,2,1,0:T(4,128)S(1)} %fusion.37), channel_id=1, source_target_pairs={{0,15},{1,0},{2,1},{3,2},{4,3},{5,4},{6,5},{7,6},{8,7},{9,8},{10,9... | collective-permute-start | bytes 122888 | tf_op jit(solution)/shard_map/ppermute | solution.py:22
  20.1 1.1 %fusion.63 = (f32[8,2,3,1,10,128]{5,4,3,2,1,0:T(8,128)}, f32[8,2,3,1,10,128]{5,4,3,2,1,0:T(8,128)}) fusion(f32[8,2,3,4,12,128]{5,4,3,2,1,0:T(8,128)S(1)} %broadcast_multiply_fusion), kind=kLoop, calls=%fused_computation.227 | loop fusion | bytes 983040 | tf_op jit(solution)/shard_map/jit(_roll_static)/slice | solution.py:58
  21.3 2.4 %collective-permute-done.4 = f32[5,4,4,128]{3,2,1,0:T(4,128)} collective-permute-done((f32[5,4,4,128]{3,2,1,0:T(4,128)S(1)}, f32[5,4,4,128]{3,2,1,0:T(4,128)}, u32[]{:S(2)}, u32[]{:S(2)}) %collective-permute-start.4) | collective-permute-done | bytes 40992 | tf_op jit(solution)/shard_map/ppermute | solution.py:22
  23.7 0.9 %concatenate.168 = f32[5,4,20,128]{3,2,1,0:T(8,128)S(1)} concatenate(f32[5,4,4,128]{3,2,1,0:T(4,128)S(1)} %collective-permute-done.1, f32[5,4,4,128]{3,2,1,0:T(4,128)S(1)} %collective-permute-done.2, f32[5,4,4,128]{3,2,1,0:T(4,128)S(1)} %fusion.37, f32[5,4,4,128]{3,2,1,0:T(4,128)S(1)} %collective-permute-done.3, f32[5,4,4,128]{3,2,1,0:T(4,128)} %collective-permute-done.4), dimensions={2} | concatenate | bytes 409600 | tf_op jit(solution)/shard_map/concatenate | solution.py:120
  29.0 1.4 %fusion.4 = f32[8,2,3,4,10,128]{5,4,3,2,1,0:T(8,128)S(1)} fusion(f32[8,2,3,4,12,128]{5,4,3,2,1,0:T(8,128)S(1)} %broadcast_multiply_fusion, f32[8,2,3,4,10,1]{5,4,3,2,1,0:T(8,128)S(1)} %copy-done, f32[8,2,3,4,10,127]{5,4,3,2,1,0:T(8,128)S(1)} %copy-done.2, f32[8,2,3,4,10,127]{5,4,3,2,1,0:T(8,128)S(1)} %copy-done.1, ...), kind=kLoop, calls=%fused_computation.5 | loop fusion | flops 3686400 | bytes 7004160 | tf_op jit(solution)/shard_map/add | solution.py:58
  31.8 0.6 %fusion.14 = f32[8,2,3,4,8,128]{5,4,3,2,1,0:T(8,128)S(1)} fusion(f32[8,2,3,4,10,128]{5,4,3,2,1,0:T(8,128)S(1)} %maximum_multiply_fusion.4, f32[8,2,3,4,8,1]{5,4,3,2,1,0:T(8,128)S(1)} %get-tuple-element.23, f32[8,2,3,4,8,127]{5,4,3,2,1,0:T(8,128)S(1)} %get-tuple-element.25, f32[8,2,3,4,8,127]{5,4,3,2,1,0:T(8,128)S(1)} %get-tuple-element.24, ...), kind=kLoop, calls=%fused_computation.26 | loop fusion | flops 2949120 | bytes 5603328 | tf_op jit(solution)/shard_map/add | solution.py:58
  33.8 0.7 %fusion.9 = f32[8,2,3,4,6,128]{5,4,3,2,1,0:T(8,128)S(1)} fusion(f32[8,2,3,4,8,128]{5,4,3,2,1,0:T(8,128)S(1)} %slice_subtract_fusion.1, f32[8,2,3,4,6,1]{5,4,3,2,1,0:T(8,128)S(1)} %get-tuple-element.56, f32[8,2,3,4,6,127]{5,4,3,2,1,0:T(8,128)S(1)} %get-tuple-element.58, f32[8,2,3,4,6,127]{5,4,3,2,1,0:T(8,128)S(1)} %get-tuple-element.57, ...), kind=kLoop, calls=%fused_computation.18 | loop fusion | flops 2211840 | bytes 4202496 | tf_op jit(solution)/shard_map/add | solution.py:58
  36.1 0.9 %fusion.15 = (f32[8]{0:T(128)S(1)}, f32[8,2,3,4,4,128]{5,4,3,2,1,0:T(4,128)S(1)}) fusion(f32[8,2,3,4,6,128]{5,4,3,2,1,0:T(8,128)S(1)} %slice_subtract_fusion, f32[8,2,3,3,4,128]{5,4,3,2,1,0:T(4,128)S(1)} %get-tuple-element.45, f32[8,2,3,1,4,128]{5,4,3,2,1,0:T(4,128)S(1)} %get-tuple-element.43, f32[4,4,128]{2,1,0:T(4,128)S(1)} %get-tuple-element.137, ...), kind=kLoop, calls=%fused_computation.44 | loop fusion | flops 1671160 | bytes 3194912 | tf_op jit(solution)/shard_map/reduce_sum | solution.py:162
  37.1 1.1 %multiply_reduce_fusion = (f32[8]{0:T(128)S(1)}, bf16[8,2,3,4,4,128]{5,4,3,2,1,0:T(4,128)(2,1)}, f32[8]{0:T(128)S(1)}) fusion(f32[8,2,3,4,8,128]{5,4,3,2,1,0:T(8,128)S(1)} %slice_subtract_fusion.1, f32[8,2,1,4,4,128]{5,4,3,2,1,0:T(4,128)S(1)} %get-tuple-element.61, f32[8,2,1,4,4,128]{5,4,3,2,1,0:T(4,128)S(1)} %get-tuple-element.60, ...), kind=kLoop, calls=%fused_computation.60 | loop fusion | flops 884720 | bytes 983104 | tf_op jit(solution)/shard_map/reduce_sum | solution.py:162
  38.3 1.1 %collective-permute-done.5 = f32[8,4]{0,1:T(4,128)S(1)} collective-permute-done((f32[8,4]{0,1:T(4,128)S(1)}, f32[8,4]{0,1:T(4,128)S(1)}, u32[]{:S(2)}, u32[]{:S(2)}) %collective-permute-start.5) | collective-permute-done | bytes 160 | tf_op jit(solution)/shard_map/ppermute | solution.py:97
  39.5 3.6 %collective-permute-done.6 = f32[8,4]{0,1:T(4,128)S(1)} collective-permute-done((f32[8,4]{0,1:T(4,128)S(1)}, f32[8,4]{0,1:T(4,128)S(1)}, u32[]{:S(2)}, u32[]{:S(2)}) %collective-permute-start.6) | collective-permute-done | bytes 160 | tf_op jit(solution)/shard_map/ppermute | solution.py:97
  43.2 3.6 %collective-permute-done.7 = f32[8,4]{0,1:T(4,128)S(1)} collective-permute-done((f32[8,4]{0,1:T(4,128)S(1)}, f32[8,4]{0,1:T(4,128)S(1)}, u32[]{:S(2)}, u32[]{:S(2)}) %collective-permute-start.7) | collective-permute-done | bytes 160 | tf_op jit(solution)/shard_map/ppermute | solution.py:97
  46.7 0.8 %collective-permute-start.8 = (f32[8,4]{0,1:T(4,128)S(1)}, f32[8,4]{0,1:T(4,128)S(1)}, u32[]{:S(2)}, u32[]{:S(2)}) collective-permute-start(f32[8,4]{0,1:T(4,128)S(1)} %add.294), channel_id=1, source_target_pairs={{0,8},{1,9},{2,10},{3,11},{4,12},{5,13},{6,14},{7,15},{8,0},{9,1},... | collective-permute-start | bytes 392 | tf_op jit(solution)/shard_map/ppermute | solution.py:97
  47.5 0.7 %constant_dynamic-slice_fusion = f32[3,4,4,64]{3,2,1,0:T(4,128)} fusion(f32[3,4,4,128]{3,2,1,0:T(4,128)S(1)} %slice.981, s32[]{:T(128)S(6)} %select_n.77), kind=kLoop, calls=%fused_computation.210 | loop fusion | bytes 24580 | tf_op jit(solution)/shard_map/dynamic_slice | solution.py:135
  48.2 3.0 %collective-permute-done.8 = f32[8,4]{0,1:T(4,128)S(1)} collective-permute-done((f32[8,4]{0,1:T(4,128)S(1)}, f32[8,4]{0,1:T(4,128)S(1)}, u32[]{:S(2)}, u32[]{:S(2)}) %collective-permute-start.8) | collective-permute-done | bytes 160 | tf_op jit(solution)/shard_map/ppermute | solution.py:97
  (146 shorter events, 10.6 us)
Async XLA Ops:
  2.3 11.1 %collective-permute-start = (f32[5,4,4,64]{3,2,1,0:T(4,128)S(1)}, f32[5,4,4,64]{3,2,1,0:T(4,128)S(1)}, u32[]{:S(2)}, u32[]{:S(2)}) collective-permute-start(f32[5,4,4,64]{3,2,1,0:T(4,128)S(1)} %pad_maximum_fusion.5), channel_id=1, source_target_pairs={{0,16},{16,0},{1,17},{17,1},{2,18},{18,2},{3,19},{19,3},{4,20},{20... | collective-permute-start | bytes 61448 | tf_op jit(solution)/shard_map/ppermute | solution.py:22
  11.8 1.6 %copy-start.7 = (f32[4,4,64]{2,1,0:T(4,128)S(1)}, f32[4,4,64]{2,1,0:T(4,128)}, u32[]{:S(2)}) copy-start(f32[4,4,64]{2,1,0:T(4,128)} %param.5) | copy-start | bytes 12292
  11.8 1.6 %copy-start.8 = (f32[4,4,64]{2,1,0:T(4,128)S(1)}, f32[4,4,64]{2,1,0:T(4,128)}, u32[]{:S(2)}) copy-start(f32[4,4,64]{2,1,0:T(4,128)} %param.6) | copy-start | bytes 12292
  13.6 7.6 %collective-permute-start.1 = (f32[5,4,4,128]{3,2,1,0:T(4,128)S(1)}, f32[5,4,4,128]{3,2,1,0:T(4,128)S(1)}, u32[]{:S(2)}, u32[]{:S(2)}) collective-permute-start(f32[5,4,4,128]{3,2,1,0:T(4,128)S(1)} %fusion.37), channel_id=1, source_target_pairs={{0,2},{1,3},{2,4},{3,5},{4,6},{5,7},{6,8},{7,9},{8,10},{9,11},{10,... | collective-permute-start | bytes 122888 | tf_op jit(solution)/shard_map/ppermute | solution.py:22
  15.1 6.1 %collective-permute-start.2 = (f32[5,4,4,128]{3,2,1,0:T(4,128)S(1)}, f32[5,4,4,128]{3,2,1,0:T(4,128)S(1)}, u32[]{:S(2)}, u32[]{:S(2)}) collective-permute-start(f32[5,4,4,128]{3,2,1,0:T(4,128)S(1)} %fusion.37), channel_id=1, source_target_pairs={{0,1},{1,2},{2,3},{3,4},{4,5},{5,6},{6,7},{7,8},{8,9},{9,10},{10,1... | collective-permute-start | bytes 122888 | tf_op jit(solution)/shard_map/ppermute | solution.py:22
  15.1 6.1 %collective-permute-start.3 = (f32[5,4,4,128]{3,2,1,0:T(4,128)S(1)}, f32[5,4,4,128]{3,2,1,0:T(4,128)S(1)}, u32[]{:S(2)}, u32[]{:S(2)}) collective-permute-start(f32[5,4,4,128]{3,2,1,0:T(4,128)S(1)} %fusion.37), channel_id=1, source_target_pairs={{0,15},{1,0},{2,1},{3,2},{4,3},{5,4},{6,5},{7,6},{8,7},{9,8},{10,9... | collective-permute-start | bytes 122888 | tf_op jit(solution)/shard_map/ppermute | solution.py:22
  19.6 4.1 %collective-permute-start.4 = (f32[5,4,4,128]{3,2,1,0:T(4,128)S(1)}, f32[5,4,4,128]{3,2,1,0:T(4,128)}, u32[]{:S(2)}, u32[]{:S(2)}) collective-permute-start(f32[5,4,4,128]{3,2,1,0:T(4,128)S(1)} %fusion.37), channel_id=1, source_target_pairs={{0,14},{1,15},{2,0},{3,1},{4,2},{5,3},{6,4},{7,5},{8,6},{9,7},{10,... | collective-permute-start | bytes 122888 | tf_op jit(solution)/shard_map/ppermute | solution.py:22
  25.5 1.4 %copy-start.5 = (f32[8,2,3,1,10,128]{5,4,3,2,1,0:T(8,128)S(1)}, f32[8,2,3,1,10,128]{5,4,3,2,1,0:T(8,128)}, u32[]{:S(2)}) copy-start(f32[8,2,3,1,10,128]{5,4,3,2,1,0:T(8,128)} %get-tuple-element.26) | copy-start | bytes 737284
  25.5 1.4 %copy-start.6 = (f32[8,2,3,1,10,128]{5,4,3,2,1,0:T(8,128)S(1)}, f32[8,2,3,1,10,128]{5,4,3,2,1,0:T(8,128)}, u32[]{:S(2)}) copy-start(f32[8,2,3,1,10,128]{5,4,3,2,1,0:T(8,128)} %get-tuple-element.27) | copy-start | bytes 737284
  25.5 1.5 %copy-start.4 = (f32[8,2,3,3,10,128]{5,4,3,2,1,0:T(8,128)S(1)}, f32[8,2,3,3,10,128]{5,4,3,2,1,0:T(8,128)}, u32[]{:S(2)}) copy-start(f32[8,2,3,3,10,128]{5,4,3,2,1,0:T(8,128)} %get-tuple-element.29) | copy-start | bytes 2211844
  25.7 1.7 %copy-start.3 = (f32[8,2,3,3,10,128]{5,4,3,2,1,0:T(8,128)S(1)}, f32[8,2,3,3,10,128]{5,4,3,2,1,0:T(8,128)}, u32[]{:S(2)}) copy-start(f32[8,2,3,3,10,128]{5,4,3,2,1,0:T(8,128)} %get-tuple-element.28) | copy-start | bytes 2211844
  25.9 2.0 %copy-start.2 = (f32[8,2,3,4,10,127]{5,4,3,2,1,0:T(8,128)S(1)}, f32[8,2,3,4,10,127]{5,4,3,2,1,0:T(8,128)}, u32[]{:S(2)}) copy-start(f32[8,2,3,4,10,127]{5,4,3,2,1,0:T(8,128)} %get-tuple-element.33) | copy-start | bytes 2926084
  26.3 2.2 %copy-start.1 = (f32[8,2,3,4,10,127]{5,4,3,2,1,0:T(8,128)S(1)}, f32[8,2,3,4,10,127]{5,4,3,2,1,0:T(8,128)}, u32[]{:S(2)}) copy-start(f32[8,2,3,4,10,127]{5,4,3,2,1,0:T(8,128)} %get-tuple-element.32) | copy-start | bytes 2926084
  26.4 2.6 %copy-start = (f32[8,2,3,4,10,1]{5,4,3,2,1,0:T(8,128)S(1)}, f32[8,2,3,4,10,1]{5,4,3,2,1,0:T(8,128)}, u32[]{:S(2)}) copy-start(f32[8,2,3,4,10,1]{5,4,3,2,1,0:T(8,128)} %get-tuple-element.31) | copy-start | bytes 23044
  38.2 1.2 %collective-permute-start.5 = (f32[8,4]{0,1:T(4,128)S(1)}, f32[8,4]{0,1:T(4,128)S(1)}, u32[]{:S(2)}, u32[]{:S(2)}) collective-permute-start(f32[8,4]{0,1:T(4,128)S(1)} %pad_maximum_fusion.16), channel_id=1, source_target_pairs={{0,1},{1,0},{2,3},{3,2},{4,5},{5,4},{6,7},{7,6},{8,9},{9,8},{10,11... | collective-permute-start | bytes 392 | tf_op jit(solution)/shard_map/ppermute | solution.py:97
  39.4 3.7 %collective-permute-start.6 = (f32[8,4]{0,1:T(4,128)S(1)}, f32[8,4]{0,1:T(4,128)S(1)}, u32[]{:S(2)}, u32[]{:S(2)}) collective-permute-start(f32[8,4]{0,1:T(4,128)S(1)} %fusion.57), channel_id=1, source_target_pairs={{0,2},{1,3},{2,0},{3,1},{4,6},{5,7},{6,4},{7,5},{8,10},{9,11},{10,... | collective-permute-start | bytes 392 | tf_op jit(solution)/shard_map/ppermute | solution.py:97
  43.1 3.7 %collective-permute-start.7 = (f32[8,4]{0,1:T(4,128)S(1)}, f32[8,4]{0,1:T(4,128)S(1)}, u32[]{:S(2)}, u32[]{:S(2)}) collective-permute-start(f32[8,4]{0,1:T(4,128)S(1)} %fusion.89), channel_id=1, source_target_pairs={{0,4},{1,5},{2,6},{3,7},{4,0},{5,1},{6,2},{7,3},{8,12},{9,13},{10,... | collective-permute-start | bytes 392 | tf_op jit(solution)/shard_map/ppermute | solution.py:97
  46.7 4.5 %collective-permute-start.8 = (f32[8,4]{0,1:T(4,128)S(1)}, f32[8,4]{0,1:T(4,128)S(1)}, u32[]{:S(2)}, u32[]{:S(2)}) collective-permute-start(f32[8,4]{0,1:T(4,128)S(1)} %add.294), channel_id=1, source_target_pairs={{0,8},{1,9},{2,10},{3,11},{4,12},{5,13},{6,14},{7,15},{8,0},{9,1},... | collective-permute-start | bytes 392 | tf_op jit(solution)/shard_map/ppermute | solution.py:97

commit v3 on v2

--- a/solution.py
+++ b/solution.py
@@ -3,6 +3,8 @@
 import jax
 import jax.numpy as jnp
 from jax import lax
+from jax.experimental import pallas as pl
+from jax.experimental.pallas import tpu as pltpu
 from jax.sharding import PartitionSpec as P
 
 LZ = 4
@@ -99,6 +101,115 @@
     return value
 
 
+def y_roll(x, shift):
+    return pltpu.roll(x, shift % x.shape[-1], x.ndim - 1)
+
+
+def z_roll(x, shift):
+    axis = x.ndim - 3
+    n = x.shape[axis]
+    s = shift % n
+    if s == 0:
+        return x
+    return jnp.concatenate(
+        [lax.slice_in_dim(x, n - s, n, axis=axis), lax.slice_in_dim(x, 0, n - s, axis=axis)], axis
+    )
+
+
+def field_rows(vector, bond, lo, n):
+    up = vector(lo + 2, lo + n)
+    down = vector(lo, lo + n - 2)
+    centre = vector(lo + 1, lo + n - 1)
+    total = bond(0, lo + 1, lo + n - 1) * up + bond(0, lo, lo + n - 2) * down
+    bond_y = bond(1, lo + 1, lo + n - 1)
+    total = total + bond_y * y_roll(centre, -1) + y_roll(bond_y, 1) * y_roll(centre, 1)
+    bond_z = bond(2, lo + 1, lo + n - 1)
+    total = total + bond_z * z_roll(centre, -1) + z_roll(bond_z, 1) * z_roll(centre, 1)
+    return total
+
+
+def local_kernel(halo, slab_rows, win_ref, start_ref, relaxed_ref, last_ref, sq_ref, sweep_a, sweep_b, t_refs):
+    width = win_ref.shape[2]
+
+    def bond(d, a, b):
+        return win_ref[3 + d, :, a:b, :]
+
+    def from_window(a, b):
+        return win_ref[0:3, :, a:b, :]
+
+    def from_a(a, b):
+        return sweep_a[:, :, a - 1:b - 1, :]
+
+    rows_a = width - 2
+    sweep_a[:, :, 0:rows_a, :] = relax_update(win_ref[0:3, :, 1:width - 1, :], field_rows(from_window, bond, 0, width))
+    rows_b = width - 4
+    sweep_b[:, :, 0:rows_b, :] = relax_update(sweep_a[:, :, 1:rows_a - 1, :], field_rows(from_a, bond, 1, width - 2))
+    relaxed_ref[...] = sweep_b[:, :, halo - SWEEPS:halo - SWEEPS + slab_rows, :]
+
+    first = halo - CHEB
+    n_start = slab_rows + 2 * CHEB
+
+    def one_vector(q, carry):
+        def from_start(a, b):
+            return start_ref[q, :, :, a - first:b - first, :]
+
+        loaders = [from_start]
+        for order in range(CHEB):
+            lo = first + order
+            n = n_start - 2 * order
+            spin_rows = sweep_b[:, :, lo + 1 - SWEEPS:lo + n - 1 - SWEEPS, :]
+            advanced = cross_product(spin_rows, field_rows(loaders[-1], bond, lo, n)) * -precess_scale
+            if order > 0:
+                advanced = 2.0 * advanced - loaders[-2](lo + 1, lo + n - 1)
+            mine = advanced[:, :, halo - lo - 1:halo - lo - 1 + slab_rows, :]
+            squares = mine * mine
+            total = squares[0] + squares[1] + squares[2]
+            sq_ref[order, q] = total[0] + total[1] + total[2] + total[3]
+            if order == CHEB - 1:
+                last_ref[q] = advanced
+            else:
+                t_ref = t_refs[order]
+                t_ref[:, :, 0:n - 2, :] = advanced
+
+                def from_t(a, b, t_ref=t_ref, base=lo + 1):
+                    return t_ref[:, :, a - base:b - base, :]
+
+                loaders.append(from_t)
+        return carry
+
+    lax.fori_loop(0, start_ref.shape[0], one_vector, 0)
+
+
+def run_local(window, start, halo, slab_rows):
+    width = window.shape[2]
+    vectors = start.shape[0]
+    depth, lanes = window.shape[1], window.shape[3]
+    spin_shape = (3, depth, width, lanes)
+    vector_rows = start.shape[3]
+
+    def body(win_ref, start_ref, relaxed_ref, last_ref, sq_ref, sweep_a, sweep_b, t1, t2, t3):
+        local_kernel(halo, slab_rows, win_ref, start_ref, relaxed_ref, last_ref, sq_ref, sweep_a, sweep_b, (t1, t2, t3))
+
+    sites = vectors * 3 * depth * vector_rows * lanes
+    return pl.pallas_call(
+        body,
+        out_shape=(
+            jax.ShapeDtypeStruct((3, depth, slab_rows, lanes), jnp.float32),
+            jax.ShapeDtypeStruct((vectors, 3, depth, slab_rows, lanes), jnp.float32),
+            jax.ShapeDtypeStruct((CHEB, vectors, slab_rows, lanes), jnp.float32),
+        ),
+        in_specs=[pl.BlockSpec(memory_space=pltpu.VMEM)] * 2,
+        out_specs=[pl.BlockSpec(memory_space=pltpu.VMEM)] * 3,
+        scratch_shapes=[pltpu.VMEM(spin_shape, jnp.float32)] * 2
+        + [pltpu.VMEM((3, depth, vector_rows, lanes), jnp.float32)] * (CHEB - 1),
+        cost_estimate=pl.CostEstimate(
+            flops=40 * CHEB * sites + 200 * 3 * depth * width * lanes,
+            transcendentals=0,
+            bytes_accessed=4 * (window.size + start.size + sites // 2),
+        ),
+    )(window, start)
+
+
 def shards(cos_polar, azimuth, bond_class, exchange, probe_wave):
     groups = lax.axis_size("probe")
     slabs = lax.axis_size("space")
@@ -111,7 +222,9 @@
     site_count = total_x * total_y * LZ
 
     bonds = bond_strengths(bond_class, exchange)
-    local = jnp.concatenate([cos_polar[None], azimuth[None], bonds], 0)
+    radial = jnp.sqrt(1.0 - cos_polar * cos_polar)
+    spins0 = jnp.stack([radial * jnp.cos(azimuth), radial * jnp.sin(azimuth), cos_polar], 0)
+    local = jnp.concatenate([spins0, bonds], 0)
 
     pieces = [shifted(local, "probe", k) for k in range(groups)]
     rotated = jnp.concatenate(pieces, -1)
@@ -121,47 +234,21 @@
         [shifted(full_y, "space", k) for k in range(-HALO_SLABS, HALO_SLABS + 1)], -2
     )
     halo = HALO_SLABS * slab_rows
-    cos_w, az_w, bonds_w = window[0], window[1], window[2:]
-
-    radial = jnp.sqrt(1.0 - cos_w * cos_w)
-    spins = jnp.stack([radial * jnp.cos(az_w), radial * jnp.sin(az_w), cos_w], 0)
-    sweep_bonds = bonds_w
-    for sweep_index in range(SWEEPS):
-        n = spins.shape[-2]
-        field = neighbour_window(spins, sweep_bonds)
-        spins = relax_update(rows(spins, 1, n - 1), field)
-        sweep_bonds = rows(sweep_bonds, 1, n - 1)
-    own = halo - SWEEPS
-    relaxed_own = lax.dynamic_slice_in_dim(rows(spins, own, own + slab_rows), group * block_y, block_y, -1)
-
-    reach = CHEB
-    first = halo - reach
-    width = slab_rows + 2 * reach
-    x_coords = (slab * slab_rows - reach + jnp.arange(width, dtype=jnp.int32)) % total_x
+
+    width = slab_rows + 2 * CHEB
+    x_coords = (slab * slab_rows - CHEB + jnp.arange(width, dtype=jnp.int32)) % total_x
     y_coords = jnp.arange(total_y, dtype=jnp.int32)
     group_size = probe_wave.shape[0]
     probe_ids = group * group_size + jnp.arange(group_size, dtype=jnp.int32)
     start = make_probes(probe_wave, probe_ids, x_coords, y_coords, total_x, total_y, LZ)
-
-    def precess(vector, lo):
-        n = vector.shape[-2]
-        field = neighbour_window(vector, rows(bonds_w, lo, lo + n))
-        spin_rows = rows(spins, lo + 1 - SWEEPS, lo + n - 1 - SWEEPS)
-        return cross_product(spin_rows, field) * -precess_scale
-
-    terms = []
-    previous, current, lo = start, start, first
-    for order in range(CHEB):
-        advanced = precess(current, lo)
-        n = current.shape[-2]
-        if order > 0:
-            advanced = 2.0 * advanced - rows(previous, 2, n)
-        previous, current, lo = current, advanced, lo + 1
-        keep = halo - lo
-        mine = rows(current, keep, keep + slab_rows)
-        terms.append(jnp.sum(mine * mine, axis=(1, 2, 3, 4, 5)))
-    moment_rows = butterfly_sum(jnp.stack(terms, 1), "space") / site_count
-    return (relaxed_own, current.astype(jnp.bfloat16), moment_rows)
+    start = start.reshape((group_size * 2,) + start.shape[2:])
+
+    relaxed, last, squares = run_local(window, start, halo, slab_rows)
+    relaxed_own = lax.dynamic_slice_in_dim(relaxed, group * block_y, block_y, -1)
+    last = last.reshape((group_size, 2) + last.shape[1:]).astype(jnp.bfloat16)
+    terms = squares.reshape((CHEB, group_size, 2 * slab_rows * total_y)).sum(-1)
+    moment_rows = butterfly_sum(terms.T, "space") / site_count
+    return (relaxed_own, last, moment_rows)
 
 
 def solution(mesh):

time: 52.1 us -> 48 us (0.921)
  Pallas kernels: 0 us -> 9.83 us
  local copies, waits for them, and re-layouts: 14.5 us -> 5.1 us
  other arithmetic: 11.6 us -> 8.42 us
  starting transfers between devices: 10.5 us -> 8.63 us
  waiting for transfers between devices: 13.8 us -> 14.9 us
  between operations: 1.4 us -> 0.74 us
    slice x67 -> x0, local copies, waits for them, and re-layouts: 9.92 us -> none  [the longest x12 6.14 us: neighbour_window(): jnp.roll(centre, 1, -1)]
    pallas_call x0 -> x1, Pallas kernels: none -> 9.83 us  [run_local(): pl.pallas_call(body, out_shape=(jax.ShapeDtypeStruct((3, depth, slab_rows...]
    add x5 -> x0, other arithmetic: 3.05 us -> none  [neighbour_window(): total + bond_z * jnp.roll(centre, -1, -3)]
    ppermute x5, waiting for transfers between devices: 2.54 us -> 5.17 us  [shifted(): lax.ppermute(array, axis, [(i, (i - shift) % size) for i in range(size)])]
    convert_element_type x0 -> x1, other arithmetic: none -> 1.74 us  [shards(): last = last.reshape((group_size, 2) + last.shape[1:]).astype(jnp.bfloat16)]
    ppermute x4, waiting for transfers between devices: 11.3 us -> 9.7 us  [butterfly_sum(): lax.ppermute(value, axis, [(i, i ^ step) for i in range(size)])]
    unnamed x18 -> x4, local copies, waits for them, and re-layouts: 2.1 us -> 0.74 us
    concatenate x1, local copies, waits for them, and re-layouts: 0.88 us -> 2.05 us  [shards(): jnp.concatenate([shifted(full_y, 'space', k) for k in range(-HALO_SLABS,...]
  transfers between devices with their start and end apart: 9 -> 9, of which waited for: 6 -> 7; matrix products, arithmetic and copies ran while one was open for 19% -> 15% of each run, Pallas kernels for 0% -> 0%
where the time goes in v3:
time: 48 us; the launch traced here: 47.6 us
  waiting for transfers between devices  14.9 us (31%)
  Pallas kernels  9.83 us (20%)
  starting transfers between devices  8.63 us (18%)
  other arithmetic  8.42 us (18%)
  local copies, waits for them, and re-layouts  5.1 us (11%)
  between operations  0.74 us (2%)
    pallas_call x1, Pallas kernels, run_local(): pl.pallas_call(body, out_shape=(jax.ShapeDtypeStruct((3, depth, slab_rows...  9.83 us
    ppermute x4, waiting for transfers between devices, butterfly_sum(): lax.ppermute(value, axis, [(i, i ^ step) for i in range(size)])  9.7 us
    ppermute x5, starting transfers between devices, shifted(): lax.ppermute(array, axis, [(i, (i - shift) % size) for i in range(size)])  8.55 us
    ppermute x5, waiting for transfers between devices, shifted(): lax.ppermute(array, axis, [(i, (i - shift) % size) for i in range(size)])  5.17 us
    concatenate x1, local copies, waits for them, and re-layouts, shards(): jnp.concatenate([shifted(full_y, 'space', k) for k in range(-HALO_SLABS,...  2.05 us
    convert_element_type x1, other arithmetic, shards(): last = last.reshape((group_size, 2) + last.shape[1:]).astype(jnp.bfloat16)  1.74 us
    dynamic_slice x1, local copies, waits for them, and re-layouts, shards(): lax.dynamic_slice_in_dim(relaxed, group * block_y, block_y, -1)  1.43 us
    mul x1, other arithmetic, make_probes(): return waves[:, :, None] * polar[:, None, :, None, None, None]  1.35 us
  transfers between devices with their start and end apart: 9, of which 7 were waited for; matrix products, arithmetic and copies ran while one was open for 15% of the time, Pallas kernels for 0%

profile of v3, /device:TPU:0, one launch (start us, length us, event | category | flops | bytes accessed | tf_op | source)
XLA Modules:
  0.0 47.6 jit_solution(8386495194195518068)
XLA Ops:
  0.6 0.8 %multiply_bitcast_fusion = (f32[1,4,4,64]{3,2,1,0:T(4,128)S(1)}, f32[1,4,4,64]{3,2,1,0:T(4,128)S(1)}) fusion(f32[4,4,64]{2,1,0:T(4,128)} %param.6, f32[4,4,64]{2,1,0:T(4,128)} %param.5), kind=kLoop, calls=%fused_computation.28 | loop fusion | flops 4096 | bytes 16384 | tf_op jit(solution)/shard_map/stack | solution.py:226
  1.5 0.9 %select_reduce_fusion = f32[3,4,4,64]{3,2,1,0:T(4,128)S(1)} fusion(f32[8]{0:T(128)} %param.8, s32[3,4,4,64]{3,2,1,0:T(4,128)} %param.7), kind=kLoop, calls=%fused_computation.5 | loop fusion | flops 70656 | bytes 24608 | tf_op jit(solution)/shard_map/reduce_sum | solution.py:30
  2.4 0.7 %pad_maximum_fusion.1 = f32[6,4,4,64]{3,2,1,0:T(4,128)S(1)} fusion(f32[3,4,4,64]{3,2,1,0:T(4,128)S(1)} %select_reduce_fusion, f32[1,4,4,64]{3,2,1,0:T(4,128)} %bitcast.19, f32[1,4,4,64]{3,2,1,0:T(4,128)S(1)} %get-tuple-element.17, f32[1,4,4,64]{3,2,1,0:T(4,128)S(1)} %get-tuple-element.18), kind=kLoop, calls=%fused_computation.26 | loop fusion | flops 18432 | bytes 49152 | tf_op jit(solution)/shard_map/concatenate | solution.py:227
  3.1 3.0 %collective-permute-start = (f32[6,4,4,64]{3,2,1,0:T(4,128)S(1)}, f32[6,4,4,64]{3,2,1,0:T(4,128)S(1)}, u32[]{:S(2)}, u32[]{:S(2)}) collective-permute-start(f32[6,4,4,64]{3,2,1,0:T(4,128)S(1)} %pad_maximum_fusion.1), channel_id=1, source_target_pairs={{0,16},{16,0},{1,17},{17,1},{2,18},{18,2},{3,19},{19,3},{4,20},{20... | collective-permute-start | bytes 73736 | tf_op jit(solution)/shard_map/ppermute | solution.py:24
  6.2 0.8 %slice_bitcast_fusion.2 = (s32[8]{0:T(128)S(1)}, s32[8]{0:T(128)S(1)}, s32[8]{0:T(128)S(1)}) fusion(s32[8,3]{0,1:T(4,128)} %param.9), kind=kLoop, calls=%fused_computation.69 | loop fusion | bytes 192 | tf_op jit(solution)/shard_map/slice | solution.py:75
  7.3 1.1 %cosine_multiply_fusion = (f32[8,1,4,12,128]{4,3,2,1,0:T(8,128)S(1)}, f32[8,1,4,12,128]{4,3,2,1,0:T(8,128)S(1)}) fusion(f32[12]{0:T(128)S(1)} %add_sqrt_fusion, f32[8,128]{1,0:T(8,128)S(1)} %fusion.16, f32[8,4,12]{2,1,0:T(4,128)S(1)} %broadcast_add_fusion), kind=kLoop, calls=%fused_computation.3 | loop fusion | flops 196608 | bytes 398896 | tf_op jit(solution)/shard_map/mul | solution.py:86
  8.6 0.2 fusion.5
  8.8 4.8 %collective-permute-start.4 = (f32[6,4,4,128]{3,2,1,0:T(4,128)S(1)}, f32[6,4,4,128]{3,2,1,0:T(4,128)S(1)}, u32[]{:S(2)}, u32[]{:S(2)}) collective-permute-start(f32[6,4,4,128]{3,2,1,0:T(4,128)S(1)} %fusion.5), channel_id=1, source_target_pairs={{0,14},{1,15},{2,0},{3,1},{4,2},{5,3},{6,4},{7,5},{8,6},{9,7},{10,... | collective-permute-start | bytes 147464 | tf_op jit(solution)/shard_map/ppermute | solution.py:24
  13.6 0.5 %collective-permute-start.2 = (f32[6,4,4,128]{3,2,1,0:T(4,128)S(1)}, f32[6,4,4,128]{3,2,1,0:T(4,128)S(1)}, u32[]{:S(2)}, u32[]{:S(2)}) collective-permute-start(f32[6,4,4,128]{3,2,1,0:T(4,128)S(1)} %fusion.5), channel_id=1, source_target_pairs={{0,1},{1,2},{2,3},{3,4},{4,5},{5,6},{6,7},{7,8},{8,9},{9,10},{10,1... | collective-permute-start | bytes 147464 | tf_op jit(solution)/shard_map/ppermute | solution.py:24
  14.1 0.3 collective-permute-start.1
  14.4 1.3 %broadcast_multiply_fusion.start_ref = f32[16,3,4,12,128]{4,3,2,1,0:T(8,128)} fusion(f32[16,3]{1,0:T(8,128)S(1)} %bitcast.21, f32[16,4,12,128]{3,2,1,0:T(8,128)S(1)} %bitcast.17), kind=kLoop, calls=%fused_computation | loop fusion | flops 294912 | bytes 1573056 | tf_op jit(solution)/shard_map/mul | solution.py:90
  15.8 4.0 %collective-permute-done.2 = f32[6,4,4,128]{3,2,1,0:T(4,128)S(1)} collective-permute-done((f32[6,4,4,128]{3,2,1,0:T(4,128)S(1)}, f32[6,4,4,128]{3,2,1,0:T(4,128)S(1)}, u32[]{:S(2)}, u32[]{:S(2)}) %collective-permute-start.2) | collective-permute-done | bytes 49184 | tf_op jit(solution)/shard_map/ppermute | solution.py:24
  19.8 1.1 %collective-permute-done.1 = f32[6,4,4,128]{3,2,1,0:T(4,128)S(1)} collective-permute-done((f32[6,4,4,128]{3,2,1,0:T(4,128)S(1)}, f32[6,4,4,128]{3,2,1,0:T(4,128)S(1)}, u32[]{:S(2)}, u32[]{:S(2)}) %collective-permute-start.1) | collective-permute-done | bytes 49184 | tf_op jit(solution)/shard_map/ppermute | solution.py:24
  20.9 2.0 %concatenate.14.win_ref = f32[6,4,20,128]{3,2,1,0:T(8,128)} concatenate(f32[6,4,4,128]{3,2,1,0:T(4,128)S(1)} %collective-permute-done.1, f32[6,4,4,128]{3,2,1,0:T(4,128)S(1)} %collective-permute-done.2, f32[6,4,4,128]{3,2,1,0:T(4,128)S(1)} %fusion.5, f32[6,4,4,128]{3,2,1,0:T(4,128)S(1)} %collective-permute-done.3, f32[6,4,4,128]{3,2,1,0:T(4,128)S(1)} %collective-permute-done.4), dimensions={2} | concatenate | bytes 491520 | tf_op jit(solution)/shard_map/concatenate | solution.py:233
  22.9 9.8 %shard_map.76 = (f32[3,4,4,128]{3,2,1,0:T(4,128)}, f32[16,3,4,4,128]{4,3,2,1,0:T(4,128)}, f32[4,16,4,128]{3,2,1,0:T(4,128)}) custom-call(f32[6,4,20,128]{3,2,1,0:T(8,128)} %concatenate.14.win_ref, f32[16,3,4,12,128]{4,3,2,1,0:T(8,128)} %broadcast_multiply_fusion.start_ref), custom_call_target="tpu_custom_call" | custom-call | flops 53329920 | bytes 2015232 | tf_op jit(solution)/shard_map/pallas_call | solution.py:194
  32.7 1.1 %reduce_sum.26 = f32[4,16]{1,0:T(4,128)S(1)} reduce(f32[4,16,4,128]{3,2,1,0:T(4,128)} %get-tuple-element.8, f32[]{:T(128)} %constant.97.clone.1), dimensions={2,3}, to_apply=%region_1.2 | reduce | flops 32704 | bytes 131332 | tf_op jit(solution)/shard_map/reduce_sum | solution.py:249
  33.9 0.1 copy.14
  34.0 1.2 %collective-permute-done.5 = f32[8,4]{1,0:T(8,128)S(1)} collective-permute-done((f32[8,4]{1,0:T(8,128)S(1)}, f32[8,4]{1,0:T(8,128)S(1)}, u32[]{:S(2)}, u32[]{:S(2)}) %collective-permute-start.5) | collective-permute-done | bytes 160 | tf_op jit(solution)/shard_map/ppermute | solution.py:99
  35.2 3.6 %collective-permute-done.6 = f32[8,4]{1,0:T(8,128)S(1)} collective-permute-done((f32[8,4]{1,0:T(8,128)S(1)}, f32[8,4]{1,0:T(8,128)S(1)}, u32[]{:S(2)}, u32[]{:S(2)}) %collective-permute-start.6) | collective-permute-done | bytes 160 | tf_op jit(solution)/shard_map/ppermute | solution.py:99
  38.8 1.4 %constant_dynamic-slice_fusion = f32[3,4,4,64]{3,2,1,0:T(4,128)} fusion(f32[3,4,4,128]{3,2,1,0:T(4,128)} %get-tuple-element.6, s32[]{:T(128)S(6)} %select_n.82), kind=kLoop, calls=%fused_computation.58 | loop fusion | bytes 24580 | tf_op jit(solution)/shard_map/dynamic_slice | solution.py:247
  40.2 2.2 %collective-permute-done.7 = f32[8,4]{1,0:T(8,128)S(1)} collective-permute-done((f32[8,4]{1,0:T(8,128)S(1)}, f32[8,4]{1,0:T(8,128)S(1)}, u32[]{:S(2)}, u32[]{:S(2)}) %collective-permute-start.7) | collective-permute-done | bytes 160 | tf_op jit(solution)/shard_map/ppermute | solution.py:99
  42.4 1.7 %convert_element_type.49 = bf16[16,3,4,4,128]{4,3,2,1,0:T(4,128)(2,1)} convert(f32[16,3,4,4,128]{4,3,2,1,0:T(4,128)} %get-tuple-element.7) | non-fusion elementwise | flops 98304 | bytes 589824 | tf_op jit(solution)/shard_map/convert_element_type | solution.py:248
  44.2 2.8 %collective-permute-done.8 = f32[8,4]{1,0:T(8,128)S(1)} collective-permute-done((f32[8,4]{1,0:T(8,128)S(1)}, f32[8,4]{1,0:T(8,128)S(1)}, u32[]{:S(2)}, u32[]{:S(2)}) %collective-permute-start.8) | collective-permute-done | bytes 160 | tf_op jit(solution)/shard_map/ppermute | solution.py:99
  46.9 0.7 %copy.15 = f32[8,4]{0,1:T(4,128)} copy(f32[8,4]{1,0:T(8,128)S(1)} %add_multiply_fusion.1) | data formatting | bytes 256
  (26 shorter events, 0.7 us)
Async XLA Ops:
  0.6 7.9 %copy-start = (f32[4,4,64]{2,1,0:T(4,128)S(1)}, f32[4,4,64]{2,1,0:T(4,128)}, u32[]{:S(2)}) copy-start(f32[4,4,64]{2,1,0:T(4,128)} %param.5) | copy-start | bytes 12292
  3.1 5.5 %collective-permute-start = (f32[6,4,4,64]{3,2,1,0:T(4,128)S(1)}, f32[6,4,4,64]{3,2,1,0:T(4,128)S(1)}, u32[]{:S(2)}, u32[]{:S(2)}) collective-permute-start(f32[6,4,4,64]{3,2,1,0:T(4,128)S(1)} %pad_maximum_fusion.1), channel_id=1, source_target_pairs={{0,16},{16,0},{1,17},{17,1},{2,18},{18,2},{3,19},{19,3},{4,20},{20... | collective-permute-start | bytes 73736 | tf_op jit(solution)/shard_map/ppermute | solution.py:24
  8.8 6.9 %collective-permute-start.4 = (f32[6,4,4,128]{3,2,1,0:T(4,128)S(1)}, f32[6,4,4,128]{3,2,1,0:T(4,128)S(1)}, u32[]{:S(2)}, u32[]{:S(2)}) collective-permute-start(f32[6,4,4,128]{3,2,1,0:T(4,128)S(1)} %fusion.5), channel_id=1, source_target_pairs={{0,14},{1,15},{2,0},{3,1},{4,2},{5,3},{6,4},{7,5},{8,6},{9,7},{10,... | collective-permute-start | bytes 147464 | tf_op jit(solution)/shard_map/ppermute | solution.py:24
  13.6 2.2 %collective-permute-start.3 = (f32[6,4,4,128]{3,2,1,0:T(4,128)S(1)}, f32[6,4,4,128]{3,2,1,0:T(4,128)S(1)}, u32[]{:S(2)}, u32[]{:S(2)}) collective-permute-start(f32[6,4,4,128]{3,2,1,0:T(4,128)S(1)} %fusion.5), channel_id=1, source_target_pairs={{0,15},{1,0},{2,1},{3,2},{4,3},{5,4},{6,5},{7,6},{8,7},{9,8},{10,9... | collective-permute-start | bytes 147464 | tf_op jit(solution)/shard_map/ppermute | solution.py:24
  13.6 6.2 %collective-permute-start.2 = (f32[6,4,4,128]{3,2,1,0:T(4,128)S(1)}, f32[6,4,4,128]{3,2,1,0:T(4,128)S(1)}, u32[]{:S(2)}, u32[]{:S(2)}) collective-permute-start(f32[6,4,4,128]{3,2,1,0:T(4,128)S(1)} %fusion.5), channel_id=1, source_target_pairs={{0,1},{1,2},{2,3},{3,4},{4,5},{5,6},{6,7},{7,8},{8,9},{9,10},{10,1... | collective-permute-start | bytes 147464 | tf_op jit(solution)/shard_map/ppermute | solution.py:24
  14.1 6.8 %collective-permute-start.1 = (f32[6,4,4,128]{3,2,1,0:T(4,128)S(1)}, f32[6,4,4,128]{3,2,1,0:T(4,128)S(1)}, u32[]{:S(2)}, u32[]{:S(2)}) collective-permute-start(f32[6,4,4,128]{3,2,1,0:T(4,128)S(1)} %fusion.5), channel_id=1, source_target_pairs={{0,2},{1,3},{2,4},{3,5},{4,6},{5,7},{6,8},{7,9},{8,10},{9,11},{10,... | collective-permute-start | bytes 147464 | tf_op jit(solution)/shard_map/ppermute | solution.py:24
  34.0 1.2 %collective-permute-start.5 = (f32[8,4]{1,0:T(8,128)S(1)}, f32[8,4]{1,0:T(8,128)S(1)}, u32[]{:S(2)}, u32[]{:S(2)}) collective-permute-start(f32[8,4]{1,0:T(8,128)S(1)} %bitcast.23), channel_id=1, source_target_pairs={{0,1},{1,0},{2,3},{3,2},{4,5},{5,4},{6,7},{7,6},{8,9},{9,8},{10,11... | collective-permute-start | bytes 392 | tf_op jit(solution)/shard_map/ppermute | solution.py:99
  35.2 3.6 %collective-permute-start.6 = (f32[8,4]{1,0:T(8,128)S(1)}, f32[8,4]{1,0:T(8,128)S(1)}, u32[]{:S(2)}, u32[]{:S(2)}) collective-permute-start(f32[8,4]{1,0:T(8,128)S(1)} %bitcast_add_fusion), channel_id=1, source_target_pairs={{0,2},{1,3},{2,0},{3,1},{4,6},{5,7},{6,4},{7,5},{8,10},{9,11},{10,... | collective-permute-start | bytes 392 | tf_op jit(solution)/shard_map/ppermute | solution.py:99
  38.8 3.6 %collective-permute-start.7 = (f32[8,4]{1,0:T(8,128)S(1)}, f32[8,4]{1,0:T(8,128)S(1)}, u32[]{:S(2)}, u32[]{:S(2)}) collective-permute-start(f32[8,4]{1,0:T(8,128)S(1)} %add.173), channel_id=1, source_target_pairs={{0,4},{1,5},{2,6},{3,7},{4,0},{5,1},{6,2},{7,3},{8,12},{9,13},{10,... | collective-permute-start | bytes 392 | tf_op jit(solution)/shard_map/ppermute | solution.py:99
  42.4 4.5 %collective-permute-start.8 = (f32[8,4]{1,0:T(8,128)S(1)}, f32[8,4]{1,0:T(8,128)S(1)}, u32[]{:S(2)}, u32[]{:S(2)}) collective-permute-start(f32[8,4]{1,0:T(8,128)S(1)} %add.174), channel_id=1, source_target_pairs={{0,8},{1,9},{2,10},{3,11},{4,12},{5,13},{6,14},{7,15},{8,0},{9,1},... | collective-permute-start | bytes 392 | tf_op jit(solution)/shard_map/ppermute | solution.py:99

commit v4 on v3

--- a/solution.py
+++ b/solution.py
@@ -128,86 +128,113 @@
     return total
 
 
-def local_kernel(halo, slab_rows, win_ref, start_ref, relaxed_ref, last_ref, sq_ref, sweep_a, sweep_b, t_refs):
-    width = win_ref.shape[2]
+def local_kernel(halo, slab_rows, *refs):
+    slab_refs = refs[:2 * HALO_SLABS + 1]
+    start_ref, relaxed_ref, last_ref, sums_ref, win, sweep_a, sweep_b, bonds_b, bonds_yr, bonds_zr, spins_b, t1, t2, t3 = refs[2 * HALO_SLABS + 1:]
+    for k, slab_ref in enumerate(slab_refs):
+        win[:, :, k * slab_rows:(k + 1) * slab_rows, :] = slab_ref[...]
+    width = len(slab_refs) * slab_rows
 
     def bond(d, a, b):
-        return win_ref[3 + d, :, a:b, :]
+        return win[3 + d, :, a:b, :]
 
     def from_window(a, b):
-        return win_ref[0:3, :, a:b, :]
+        return win[0:3, :, a:b, :]
 
     def from_a(a, b):
         return sweep_a[:, :, a - 1:b - 1, :]
 
     rows_a = width - 2
-    sweep_a[:, :, 0:rows_a, :] = relax_update(win_ref[0:3, :, 1:width - 1, :], field_rows(from_window, bond, 0, width))
+    sweep_a[:, :, 0:rows_a, :] = relax_update(win[0:3, :, 1:width - 1, :], field_rows(from_window, bond, 0, width))
     rows_b = width - 4
     sweep_b[:, :, 0:rows_b, :] = relax_update(sweep_a[:, :, 1:rows_a - 1, :], field_rows(from_a, bond, 1, width - 2))
     relaxed_ref[...] = sweep_b[:, :, halo - SWEEPS:halo - SWEEPS + slab_rows, :]
 
     first = halo - CHEB
     n_start = slab_rows + 2 * CHEB
-
-    def one_vector(q, carry):
-        def from_start(a, b):
-            return start_ref[q, :, :, a - first:b - first, :]
-
-        loaders = [from_start]
-        for order in range(CHEB):
-            lo = first + order
-            n = n_start - 2 * order
-            spin_rows = sweep_b[:, :, lo + 1 - SWEEPS:lo + n - 1 - SWEEPS, :]
-            advanced = cross_product(spin_rows, field_rows(loaders[-1], bond, lo, n)) * -precess_scale
+    lanes = win.shape[3]
+    depth = win.shape[1]
+    probes = start_ref.shape[4]
+    for xr in range(n_start):
+        w = first + xr
+        site = jnp.broadcast_to(win[3:6, :, w:w + 1, :], (3, depth, probes, lanes))
+        bonds_b[xr] = site
+        bonds_yr[xr] = y_roll(site[1], 1)
+        bonds_zr[xr] = z_roll(site[2], 1)
+    for xr in range(n_start - 2):
+        w = first + 1 + xr
+        spins_b[xr] = jnp.broadcast_to(sweep_b[:, :, w - SWEEPS:w - SWEEPS + 1, :], (3, depth, probes, lanes))
+
+    t_refs = (start_ref, t1, t2, t3, last_ref)
+    sums = []
+    for order in range(CHEB):
+        lo = first + order
+        n = n_start - 2 * order
+        source = t_refs[order]
+        target = t_refs[order + 1]
+        acc = None
+        for i in range(n - 2):
+            w = lo + 1 + i
+            b = w - first
+            up = source[i + 2]
+            down = source[i]
+            centre = source[i + 1]
+            total = bonds_b[b, 0] * up + bonds_b[b - 1, 0] * down
+            total = total + bonds_b[b, 1] * y_roll(centre, -1) + bonds_yr[b] * y_roll(centre, 1)
+            total = total + bonds_b[b, 2] * z_roll(centre, -1) + bonds_zr[b] * z_roll(centre, 1)
+            advanced = cross_product(spins_b[b - 1], total) * -precess_scale
             if order > 0:
-                advanced = 2.0 * advanced - loaders[-2](lo + 1, lo + n - 1)
-            mine = advanced[:, :, halo - lo - 1:halo - lo - 1 + slab_rows, :]
-            squares = mine * mine
-            total = squares[0] + squares[1] + squares[2]
-            sq_ref[order, q] = total[0] + total[1] + total[2] + total[3]
-            if order == CHEB - 1:
-                last_ref[q] = advanced
-            else:
-                t_ref = t_refs[order]
-                t_ref[:, :, 0:n - 2, :] = advanced
-
-                def from_t(a, b, t_ref=t_ref, base=lo + 1):
-                    return t_ref[:, :, a - base:b - base, :]
-
-                loaders.append(from_t)
-        return carry
-
-    lax.fori_loop(0, start_ref.shape[0], one_vector, 0)
-
-
-def run_local(window, start, halo, slab_rows):
-    width = window.shape[2]
-    vectors = start.shape[0]
-    depth, lanes = window.shape[1], window.shape[3]
-    spin_shape = (3, depth, width, lanes)
-    vector_rows = start.shape[3]
-
-    def body(win_ref, start_ref, relaxed_ref, last_ref, sq_ref, sweep_a, sweep_b, t1, t2, t3):
-        local_kernel(halo, slab_rows, win_ref, start_ref, relaxed_ref, last_ref, sq_ref, sweep_a, sweep_b, (t1, t2, t3))
-
-    sites = vectors * 3 * depth * vector_rows * lanes
+                advanced = 2.0 * advanced - t_refs[order - 1][i + 2]
+            target[i] = advanced
+            if halo <= w < halo + slab_rows:
+                squares = advanced * advanced
+                part = squares[0] + squares[1]
+                part = part[0] + part[1] + part[2]
+                part = part[0] + part[1] + part[2] + part[3]
+                acc = part if acc is None else acc + part
+        sums.append(jnp.sum(acc, axis=-1, keepdims=True))
+    lane = lax.broadcasted_iota(jnp.int32, sums_ref.shape, 1)
+    out = jnp.zeros(sums_ref.shape, jnp.float32)
+    for order in range(CHEB):
+        out = jnp.where(lane == order, sums[order], out)
+    sums_ref[...] = out
+
+
+def run_local(slab_blocks, start, halo, slab_rows):
+    depth, lanes = slab_blocks[0].shape[1], slab_blocks[0].shape[3]
+    width = len(slab_blocks) * slab_rows
+    n_start, probes = start.shape[0], start.shape[4]
+    vec_shape = start.shape[1:]
+
+    def body(*refs):
+        local_kernel(halo, slab_rows, *refs)
+
+    sites = n_start * start[0].size
     return pl.pallas_call(
         body,
         out_shape=(
             jax.ShapeDtypeStruct((3, depth, slab_rows, lanes), jnp.float32),
-            jax.ShapeDtypeStruct((vectors, 3, depth, slab_rows, lanes), jnp.float32),
-            jax.ShapeDtypeStruct((CHEB, vectors, slab_rows, lanes), jnp.float32),
-        ),
-        in_specs=[pl.BlockSpec(memory_space=pltpu.VMEM)] * 2,
+            jax.ShapeDtypeStruct((slab_rows,) + vec_shape, jnp.float32),
+            jax.ShapeDtypeStruct((probes, 128), jnp.float32),
+        ),
+        in_specs=[pl.BlockSpec(memory_space=pltpu.VMEM)] * (len(slab_blocks) + 1),
         out_specs=[pl.BlockSpec(memory_space=pltpu.VMEM)] * 3,
-        scratch_shapes=[pltpu.VMEM(spin_shape, jnp.float32)] * 2
-        + [pltpu.VMEM((3, depth, vector_rows, lanes), jnp.float32)] * (CHEB - 1),
+        scratch_shapes=[
+            pltpu.VMEM((6, depth, width, lanes), jnp.float32),
+            pltpu.VMEM((3, depth, width, lanes), jnp.float32),
+            pltpu.VMEM((3, depth, width, lanes), jnp.float32),
+            pltpu.VMEM((n_start, 3, depth, probes, lanes), jnp.float32),
+            pltpu.VMEM((n_start, depth, probes, lanes), jnp.float32),
+            pltpu.VMEM((n_start, depth, probes, lanes), jnp.float32),
+            pltpu.VMEM((n_start, 3, depth, probes, lanes), jnp.float32),
+        ]
+        + [pltpu.VMEM((n_start - 2 * k,) + vec_shape, jnp.float32) for k in range(1, CHEB)],
         cost_estimate=pl.CostEstimate(
-            flops=40 * CHEB * sites + 200 * 3 * depth * width * lanes,
+            flops=30 * sites + 200 * 3 * depth * width * lanes,
             transcendentals=0,
-            bytes_accessed=4 * (window.size + start.size + sites // 2),
-        ),
-    )(window, start)
+            bytes_accessed=4 * (6 * depth * width * lanes + start.size + start.size // 3),
+        ),
+    )(*slab_blocks, start)
 
 
 def shards(cos_polar, azimuth, bond_class, exchange, probe_wave):
@@ -230,9 +257,7 @@
     rotated = jnp.concatenate(pieces, -1)
     full_y = jnp.roll(rotated, group * block_y, -1) if groups > 1 else rotated
 
-    window = jnp.concatenate(
-        [shifted(full_y, "space", k) for k in range(-HALO_SLABS, HALO_SLABS + 1)], -2
-    )
+    slab_blocks = [shifted(full_y, "space", k) for k in range(-HALO_SLABS, HALO_SLABS + 1)]
     halo = HALO_SLABS * slab_rows
 
     width = slab_rows + 2 * CHEB
@@ -241,13 +266,12 @@
     group_size = probe_wave.shape[0]
     probe_ids = group * group_size + jnp.arange(group_size, dtype=jnp.int32)
     start = make_probes(probe_wave, probe_ids, x_coords, y_coords, total_x, total_y, LZ)
-    start = start.reshape((group_size * 2,) + start.shape[2:])
-
-    relaxed, last, squares = run_local(window, start, halo, slab_rows)
+    start = jnp.transpose(start, (4, 1, 2, 3, 0, 5))
+
+    relaxed, last, sums = run_local(slab_blocks, start, halo, slab_rows)
     relaxed_own = lax.dynamic_slice_in_dim(relaxed, group * block_y, block_y, -1)
-    last = last.reshape((group_size, 2) + last.shape[1:]).astype(jnp.bfloat16)
-    terms = squares.reshape((CHEB, group_size, 2 * slab_rows * total_y)).sum(-1)
-    moment_rows = butterfly_sum(terms.T, "space") / site_count
+    last = jnp.transpose(last, (4, 1, 2, 3, 0, 5)).astype(jnp.bfloat16)
+    moment_rows = butterfly_sum(sums[:, :CHEB], "space") / site_count
     return (relaxed_own, last, moment_rows)
 
 

time: 48 us -> 41.1 us (0.86)
  Pallas kernels: 9.83 us -> 4.67 us
  other arithmetic: 8.42 us -> 6.75 us
  local copies, waits for them, and re-layouts: 5.1 us -> 4.35 us
  waiting for transfers between devices: 14.9 us -> 15.4 us
    pallas_call x1, Pallas kernels: 9.83 us -> 4.67 us  [run_local(): pl.pallas_call(body, out_shape=(jax.ShapeDtypeStruct((3, depth, slab_rows...]
    concatenate x1 -> x0, local copies, waits for them, and re-layouts: 2.05 us -> none  [shards(): jnp.concatenate([shifted(full_y, 'space', k) for k in range(-HALO_SLABS,...]
    unnamed x4 -> x14, local copies, waits for them, and re-layouts: 0.74 us -> 2.12 us
    reduce_sum x2 -> x0, other arithmetic: 1.12 us -> none  [shards(): terms = squares.reshape((CHEB, group_size, 2 * slab_rows * total_y)).sum(-1)]
    convert_element_type x1, other arithmetic: 1.74 us -> 1.02 us  [shards(): last = jnp.transpose(last, (4, 1, 2, 3, 0, 5)).astype(jnp.bfloat16)]
    add x3, other arithmetic: 0.01 us -> 0.7 us  [butterfly_sum(): value + lax.ppermute(value, axis, [(i, i ^ step) for i in range(size)])]
    mul x1 -> x2, other arithmetic: 1.35 us -> 1.27 us  [make_probes(): return waves[:, :, None] * polar[:, None, :, None, None, None]]
  transfers between devices with their start and end apart: 9 -> 9, of which waited for: 7 -> 8; matrix products, arithmetic and copies ran while one was open for 15% -> 16% of each run, Pallas kernels for 0% -> 0%
where the time goes in v4:
time: 41.1 us; the launch traced here: 40.6 us
  waiting for transfers between devices  15.4 us (37%)
  starting transfers between devices  8.67 us (21%)
  other arithmetic  6.75 us (16%)
  Pallas kernels  4.67 us (11%)
  local copies, waits for them, and re-layouts  4.35 us (11%)
  between operations  0.76 us (2%)
    ppermute x4, waiting for transfers between devices, butterfly_sum(): lax.ppermute(value, axis, [(i, i ^ step) for i in range(size)])  9.8 us
    ppermute x5, starting transfers between devices, shifted(): lax.ppermute(array, axis, [(i, (i - shift) % size) for i in range(size)])  8.66 us
    ppermute x5, waiting for transfers between devices, shifted(): lax.ppermute(array, axis, [(i, (i - shift) % size) for i in range(size)])  5.65 us
    pallas_call x1, Pallas kernels, run_local(): pl.pallas_call(body, out_shape=(jax.ShapeDtypeStruct((3, depth, slab_rows...  4.67 us
    unnamed x14, local copies, waits for them, and re-layouts  2.12 us
    dynamic_slice x1, local copies, waits for them, and re-layouts, shards(): lax.dynamic_slice_in_dim(relaxed, group * block_y, block_y, -1)  1.43 us
    mul x2, other arithmetic, make_probes(): return waves[:, :, None] * polar[:, None, :, None, None, None]  1.27 us
    convert_element_type x1, other arithmetic, shards(): last = jnp.transpose(last, (4, 1, 2, 3, 0, 5)).astype(jnp.bfloat16)  1.02 us
  transfers between devices with their start and end apart: 9, of which 8 were waited for; matrix products, arithmetic and copies ran while one was open for 16% of the time, Pallas kernels for 0%

profile of v4, /device:TPU:0, one launch (start us, length us, event | category | flops | bytes accessed | tf_op | source)
XLA Modules:
  0.0 40.6 jit_solution(5290916691109230346)
XLA Ops:
  0.6 0.8 %multiply_bitcast_fusion = (f32[1,4,4,64]{3,2,1,0:T(4,128)S(1)}, f32[1,4,4,64]{3,2,1,0:T(4,128)S(1)}) fusion(f32[4,4,64]{2,1,0:T(4,128)} %param.6, f32[4,4,64]{2,1,0:T(4,128)} %param.5), kind=kLoop, calls=%fused_computation.37 | loop fusion | flops 4096 | bytes 16384 | tf_op jit(solution)/shard_map/stack | solution.py:253
  1.5 0.9 %select_reduce_fusion = f32[3,4,4,64]{3,2,1,0:T(4,128)S(1)} fusion(f32[8]{0:T(128)} %param.8, s32[3,4,4,64]{3,2,1,0:T(4,128)} %param.7), kind=kLoop, calls=%fused_computation.6 | loop fusion | flops 70656 | bytes 24608 | tf_op jit(solution)/shard_map/reduce_sum | solution.py:30
  2.4 0.7 %pad_maximum_fusion = f32[6,4,4,64]{3,2,1,0:T(4,128)S(1)} fusion(f32[3,4,4,64]{3,2,1,0:T(4,128)S(1)} %select_reduce_fusion, f32[1,4,4,64]{3,2,1,0:T(4,128)} %bitcast.16, f32[1,4,4,64]{3,2,1,0:T(4,128)S(1)} %get-tuple-element.17, f32[1,4,4,64]{3,2,1,0:T(4,128)S(1)} %get-tuple-element.18), kind=kLoop, calls=%fused_computation.27 | loop fusion | flops 18432 | bytes 49152 | tf_op jit(solution)/shard_map/concatenate | solution.py:254
  3.1 3.0 %collective-permute-start = (f32[6,4,4,64]{3,2,1,0:T(4,128)S(1)}, f32[6,4,4,64]{3,2,1,0:T(4,128)S(1)}, u32[]{:S(2)}, u32[]{:S(2)}) collective-permute-start(f32[6,4,4,64]{3,2,1,0:T(4,128)S(1)} %pad_maximum_fusion), channel_id=1, source_target_pairs={{0,16},{16,0},{1,17},{17,1},{2,18},{18,2},{3,19},{19,3},{4,20},{20... | collective-permute-start | bytes 73736 | tf_op jit(solution)/shard_map/ppermute | solution.py:24
  6.2 0.8 %slice_bitcast_fusion.2 = (s32[8]{0:T(128)S(1)}, s32[8]{0:T(128)S(1)}, s32[8]{0:T(128)S(1)}) fusion(s32[8,3]{0,1:T(4,128)} %param.9), kind=kLoop, calls=%fused_computation.67 | loop fusion | bytes 192 | tf_op jit(solution)/shard_map/slice | solution.py:75
  7.2 0.8 %cosine_multiply_fusion = (f32[8,1,4,12,128]{4,0,2,1,3:T(8,128)S(1)}, f32[8,1,4,12,128]{4,0,2,1,3:T(8,128)S(1)}) fusion(f32[12]{0:T(128)S(1)} %add_sqrt_fusion, f32[8,128]{1,0:T(8,128)S(1)} %fusion.14, f32[8,4,12]{0,1,2:T(4,128)S(1)} %broadcast_add_fusion), kind=kLoop, calls=%fused_computation.4 | loop fusion | flops 196608 | bytes 398896 | tf_op jit(solution)/shard_map/mul | solution.py:86
  8.2 0.2 fusion.5.refs_2_
  8.4 5.1 %collective-permute-start.4 = (f32[6,4,4,128]{3,2,1,0:T(4,128)S(1)}, f32[6,4,4,128]{3,2,1,0:T(4,128)S(1)}, u32[]{:S(2)}, u32[]{:S(2)}) collective-permute-start(f32[6,4,4,128]{3,2,1,0:T(4,128)S(1)} %fusion.5.refs_2_), channel_id=1, source_target_pairs={{0,14},{1,15},{2,0},{3,1},{4,2},{5,3},{6,4},{7,5},{8,6},{9,7},{10,... | collective-permute-start | bytes 147464 | tf_op jit(solution)/shard_map/ppermute | solution.py:24
  13.6 0.5 %collective-permute-start.2 = (f32[6,4,4,128]{3,2,1,0:T(4,128)S(1)}, f32[6,4,4,128]{3,2,1,0:T(4,128)S(1)}, u32[]{:S(2)}, u32[]{:S(2)}) collective-permute-start(f32[6,4,4,128]{3,2,1,0:T(4,128)S(1)} %fusion.5.refs_2_), channel_id=1, source_target_pairs={{0,1},{1,2},{2,3},{3,4},{4,5},{5,6},{6,7},{7,8},{8,9},{9,10},{10,1... | collective-permute-start | bytes 147464 | tf_op jit(solution)/shard_map/ppermute | solution.py:24
  14.1 1.2 %broadcast_multiply_fusion.refs_5_ = f32[12,2,3,4,8,128]{5,4,3,2,1,0:T(8,128)} fusion(f32[3,8]{1,0:T(4,128)S(1)} %fusion.21, f32[12,2,4,8,128]{4,3,2,1,0:T(8,128)S(1)} %maximum_bitcast_fusion), kind=kLoop, calls=%fused_computation | loop fusion | flops 294912 | bytes 1572960 | tf_op jit(solution)/shard_map/mul | solution.py:90
  15.3 0.5 %collective-permute-done.3.refs_3_ = f32[6,4,4,128]{3,2,1,0:T(4,128)S(1)} collective-permute-done((f32[6,4,4,128]{3,2,1,0:T(4,128)S(1)}, f32[6,4,4,128]{3,2,1,0:T(4,128)S(1)}, u32[]{:S(2)}, u32[]{:S(2)}) %collective-permute-start.3) | collective-permute-done | bytes 49184 | tf_op jit(solution)/shard_map/ppermute | solution.py:24
  15.8 4.0 %collective-permute-done.2.refs_1_ = f32[6,4,4,128]{3,2,1,0:T(4,128)S(1)} collective-permute-done((f32[6,4,4,128]{3,2,1,0:T(4,128)S(1)}, f32[6,4,4,128]{3,2,1,0:T(4,128)S(1)}, u32[]{:S(2)}, u32[]{:S(2)}) %collective-permute-start.2) | collective-permute-done | bytes 49184 | tf_op jit(solution)/shard_map/ppermute | solution.py:24
  19.8 1.1 %collective-permute-done.1.refs_0_ = f32[6,4,4,128]{3,2,1,0:T(4,128)S(1)} collective-permute-done((f32[6,4,4,128]{3,2,1,0:T(4,128)S(1)}, f32[6,4,4,128]{3,2,1,0:T(4,128)S(1)}, u32[]{:S(2)}, u32[]{:S(2)}) %collective-permute-start.1) | collective-permute-done | bytes 49184 | tf_op jit(solution)/shard_map/ppermute | solution.py:24
  20.9 0.6 %copy-done.5 = f32[6,4,4,128]{3,2,1,0:T(4,128)} copy-done((f32[6,4,4,128]{3,2,1,0:T(4,128)}, f32[6,4,4,128]{3,2,1,0:T(4,128)S(1)}, u32[]{:S(2)}) %copy-start.5) | copy-done | bytes 49176
  21.5 4.7 %shard_map.76 = (f32[3,4,4,128]{3,2,1,0:T(4,128)}, f32[4,2,3,4,8,128]{5,4,3,2,1,0:T(8,128)}, f32[8,128]{1,0:T(8,128)}) custom-call(f32[6,4,4,128]{3,2,1,0:T(4,128)} %copy-done.5, f32[6,4,4,128]{3,2,1,0:T(4,128)} %copy-done.4, f32[6,4,4,128]{3,2,1,0:T(4,128)} %copy-done, f32[6,4,4,128]{3,2,1,0:T(4,128)} %copy-done.3, f32[6,4,4,128]{3,2,1,0:T(4,128)} %copy-done.2, ...), custom_call_target="tpu_custom_call" | custom-call | flops 14991360 | bytes 1818624 | tf_op jit(solution)/shard_map/pallas_call | solution.py:213
  26.2 1.4 %collective-permute-done.5 = f32[8,4]{1,0:T(8,128)S(1)} collective-permute-done((f32[8,4]{1,0:T(8,128)}, f32[8,4]{1,0:T(8,128)S(1)}, u32[]{:S(2)}, u32[]{:S(2)}) %collective-permute-start.5) | collective-permute-done | bytes 160 | tf_op jit(solution)/shard_map/ppermute | solution.py:99
  27.6 0.7 %slice_add_fusion = f32[8,4]{1,0:T(8,128)S(1)} fusion(f32[8,4]{1,0:T(8,128)S(1)} %collective-permute-done.5, f32[8,128]{1,0:T(8,128)} %get-tuple-element.8), kind=kLoop, calls=%fused_computation.68 | loop fusion | flops 32 | bytes 384 | tf_op jit(solution)/shard_map/add | solution.py:99
  28.3 3.6 %collective-permute-done.6 = f32[8,4]{1,0:T(8,128)S(1)} collective-permute-done((f32[8,4]{1,0:T(8,128)S(1)}, f32[8,4]{1,0:T(8,128)S(1)}, u32[]{:S(2)}, u32[]{:S(2)}) %collective-permute-start.6) | collective-permute-done | bytes 160 | tf_op jit(solution)/shard_map/ppermute | solution.py:99
  31.9 1.0 %convert_bitcast_fusion = bf16[8,2,3,4,4,128]{5,0,3,2,1,4:T(8,128)(2,1)S(1)} fusion(f32[4,2,3,4,8,128]{5,4,3,2,1,0:T(8,128)} %get-tuple-element.7), kind=kLoop, calls=%fused_computation.2 | loop fusion | flops 98304 | bytes 589824 | tf_op jit(solution)/shard_map/convert_element_type | solution.py:273
  32.9 2.6 %collective-permute-done.7 = f32[8,4]{1,0:T(8,128)S(1)} collective-permute-done((f32[8,4]{1,0:T(8,128)S(1)}, f32[8,4]{1,0:T(8,128)S(1)}, u32[]{:S(2)}, u32[]{:S(2)}) %collective-permute-start.7) | collective-permute-done | bytes 160 | tf_op jit(solution)/shard_map/ppermute | solution.py:99
  35.5 1.4 %constant_dynamic-slice_fusion = f32[3,4,4,64]{3,2,1,0:T(4,128)} fusion(f32[3,4,4,128]{3,2,1,0:T(4,128)} %get-tuple-element.6, s32[]{:T(128)S(6)} %select_n.82), kind=kLoop, calls=%fused_computation.53 | loop fusion | bytes 24580 | tf_op jit(solution)/shard_map/dynamic_slice | solution.py:272
  36.9 0.8 %copy.10 = bf16[8,2,3,4,4,128]{5,4,3,2,1,0:T(4,128)(2,1)} copy(bf16[8,2,3,4,4,128]{5,0,3,2,1,4:T(8,128)(2,1)S(1)} %convert_bitcast_fusion) | data formatting | bytes 393216
  37.7 2.2 %collective-permute-done.8 = f32[8,4]{1,0:T(8,128)S(1)} collective-permute-done((f32[8,4]{1,0:T(8,128)S(1)}, f32[8,4]{1,0:T(8,128)S(1)}, u32[]{:S(2)}, u32[]{:S(2)}) %collective-permute-start.8) | collective-permute-done | bytes 160 | tf_op jit(solution)/shard_map/ppermute | solution.py:99
  40.0 0.7 %copy.11 = f32[8,4]{0,1:T(4,128)} copy(f32[8,4]{1,0:T(8,128)S(1)} %add_multiply_fusion.1) | data formatting | bytes 256
  (31 shorter events, 0.4 us)
Async XLA Ops:
  0.6 7.5 %copy-start.1 = (f32[4,4,64]{2,1,0:T(4,128)S(1)}, f32[4,4,64]{2,1,0:T(4,128)}, u32[]{:S(2)}) copy-start(f32[4,4,64]{2,1,0:T(4,128)} %param.5) | copy-start | bytes 12292
  3.1 5.1 %collective-permute-start = (f32[6,4,4,64]{3,2,1,0:T(4,128)S(1)}, f32[6,4,4,64]{3,2,1,0:T(4,128)S(1)}, u32[]{:S(2)}, u32[]{:S(2)}) collective-permute-start(f32[6,4,4,64]{3,2,1,0:T(4,128)S(1)} %pad_maximum_fusion), channel_id=1, source_target_pairs={{0,16},{16,0},{1,17},{17,1},{2,18},{18,2},{3,19},{19,3},{4,20},{20... | collective-permute-start | bytes 73736 | tf_op jit(solution)/shard_map/ppermute | solution.py:24
  8.4 12.4 %copy-start = (f32[6,4,4,128]{3,2,1,0:T(4,128)}, f32[6,4,4,128]{3,2,1,0:T(4,128)S(1)}, u32[]{:S(2)}) copy-start(f32[6,4,4,128]{3,2,1,0:T(4,128)S(1)} %fusion.5.refs_2_) | copy-start | bytes 147460
  8.4 6.9 %collective-permute-start.4 = (f32[6,4,4,128]{3,2,1,0:T(4,128)S(1)}, f32[6,4,4,128]{3,2,1,0:T(4,128)S(1)}, u32[]{:S(2)}, u32[]{:S(2)}) collective-permute-start(f32[6,4,4,128]{3,2,1,0:T(4,128)S(1)} %fusion.5.refs_2_), channel_id=1, source_target_pairs={{0,14},{1,15},{2,0},{3,1},{4,2},{5,3},{6,4},{7,5},{8,6},{9,7},{10,... | collective-permute-start | bytes 147464 | tf_op jit(solution)/shard_map/ppermute | solution.py:24
  13.6 2.2 %collective-permute-start.3 = (f32[6,4,4,128]{3,2,1,0:T(4,128)S(1)}, f32[6,4,4,128]{3,2,1,0:T(4,128)S(1)}, u32[]{:S(2)}, u32[]{:S(2)}) collective-permute-start(f32[6,4,4,128]{3,2,1,0:T(4,128)S(1)} %fusion.5.refs_2_), channel_id=1, source_target_pairs={{0,15},{1,0},{2,1},{3,2},{4,3},{5,4},{6,5},{7,6},{8,7},{9,8},{10,9... | collective-permute-start | bytes 147464 | tf_op jit(solution)/shard_map/ppermute | solution.py:24
  13.6 6.2 %collective-permute-start.2 = (f32[6,4,4,128]{3,2,1,0:T(4,128)S(1)}, f32[6,4,4,128]{3,2,1,0:T(4,128)S(1)}, u32[]{:S(2)}, u32[]{:S(2)}) collective-permute-start(f32[6,4,4,128]{3,2,1,0:T(4,128)S(1)} %fusion.5.refs_2_), channel_id=1, source_target_pairs={{0,1},{1,2},{2,3},{3,4},{4,5},{5,6},{6,7},{7,8},{8,9},{9,10},{10,1... | collective-permute-start | bytes 147464 | tf_op jit(solution)/shard_map/ppermute | solution.py:24
  14.1 6.8 %collective-permute-start.1 = (f32[6,4,4,128]{3,2,1,0:T(4,128)S(1)}, f32[6,4,4,128]{3,2,1,0:T(4,128)S(1)}, u32[]{:S(2)}, u32[]{:S(2)}) collective-permute-start(f32[6,4,4,128]{3,2,1,0:T(4,128)S(1)} %fusion.5.refs_2_), channel_id=1, source_target_pairs={{0,2},{1,3},{2,4},{3,5},{4,6},{5,7},{6,8},{7,9},{8,10},{9,11},{10,... | collective-permute-start | bytes 147464 | tf_op jit(solution)/shard_map/ppermute | solution.py:24
  15.3 5.5 %copy-start.2 = (f32[6,4,4,128]{3,2,1,0:T(4,128)}, f32[6,4,4,128]{3,2,1,0:T(4,128)S(1)}, u32[]{:S(2)}) copy-start(f32[6,4,4,128]{3,2,1,0:T(4,128)S(1)} %collective-permute-done.4.refs_4_) | copy-start | bytes 147460
  15.8 5.1 %copy-start.3 = (f32[6,4,4,128]{3,2,1,0:T(4,128)}, f32[6,4,4,128]{3,2,1,0:T(4,128)S(1)}, u32[]{:S(2)}) copy-start(f32[6,4,4,128]{3,2,1,0:T(4,128)S(1)} %collective-permute-done.3.refs_3_) | copy-start | bytes 147460
  19.8 1.1 %copy-start.4 = (f32[6,4,4,128]{3,2,1,0:T(4,128)}, f32[6,4,4,128]{3,2,1,0:T(4,128)S(1)}, u32[]{:S(2)}) copy-start(f32[6,4,4,128]{3,2,1,0:T(4,128)S(1)} %collective-permute-done.2.refs_1_) | copy-start | bytes 147460
  20.9 0.6 %copy-start.5 = (f32[6,4,4,128]{3,2,1,0:T(4,128)}, f32[6,4,4,128]{3,2,1,0:T(4,128)S(1)}, u32[]{:S(2)}) copy-start(f32[6,4,4,128]{3,2,1,0:T(4,128)S(1)} %collective-permute-done.1.refs_0_) | copy-start | bytes 147460
  26.2 1.4 %collective-permute-start.5 = (f32[8,4]{1,0:T(8,128)}, f32[8,4]{1,0:T(8,128)S(1)}, u32[]{:S(2)}, u32[]{:S(2)}) collective-permute-start(f32[8,4]{1,0:T(8,128)} %bitcast.18), channel_id=1, source_target_pairs={{0,1},{1,0},{2,3},{3,2},{4,5},{5,4},{6,7},{7,6},{8,9},{9,8},{10,11... | collective-permute-start | bytes 392 | tf_op jit(solution)/shard_map/ppermute | solution.py:99
  28.3 3.6 %collective-permute-start.6 = (f32[8,4]{1,0:T(8,128)S(1)}, f32[8,4]{1,0:T(8,128)S(1)}, u32[]{:S(2)}, u32[]{:S(2)}) collective-permute-start(f32[8,4]{1,0:T(8,128)S(1)} %slice_add_fusion), channel_id=1, source_target_pairs={{0,2},{1,3},{2,0},{3,1},{4,6},{5,7},{6,4},{7,5},{8,10},{9,11},{10,... | collective-permute-start | bytes 392 | tf_op jit(solution)/shard_map/ppermute | solution.py:99
  31.9 3.6 %collective-permute-start.7 = (f32[8,4]{1,0:T(8,128)S(1)}, f32[8,4]{1,0:T(8,128)S(1)}, u32[]{:S(2)}, u32[]{:S(2)}) collective-permute-start(f32[8,4]{1,0:T(8,128)S(1)} %add.173), channel_id=1, source_target_pairs={{0,4},{1,5},{2,6},{3,7},{4,0},{5,1},{6,2},{7,3},{8,12},{9,13},{10,... | collective-permute-start | bytes 392 | tf_op jit(solution)/shard_map/ppermute | solution.py:99
  35.5 4.5 %collective-permute-start.8 = (f32[8,4]{1,0:T(8,128)S(1)}, f32[8,4]{1,0:T(8,128)S(1)}, u32[]{:S(2)}, u32[]{:S(2)}) collective-permute-start(f32[8,4]{1,0:T(8,128)S(1)} %add.174), channel_id=1, source_target_pairs={{0,8},{1,9},{2,10},{3,11},{4,12},{5,13},{6,14},{7,15},{8,0},{9,1},... | collective-permute-start | bytes 392 | tf_op jit(solution)/shard_map/ppermute | solution.py:99

commit v5 on v4

--- a/solution.py
+++ b/solution.py
@@ -11,6 +11,7 @@
 SWEEPS = 2
 CHEB = 4
 HALO_SLABS = 2
+NCLASS = 8
 
 
 relax_rate = 0.15
@@ -22,12 +23,6 @@
     if shift % size == 0:
         return array
     return lax.ppermute(array, axis, [(i, (i - shift) % size) for i in range(size)])
-
-
-def bond_strengths(bond_class, exchange):
-    classes = jnp.arange(exchange.shape[0], dtype=bond_class.dtype)
-    picked = jnp.where(bond_class[..., None] == classes, exchange, 0.0)
-    return jnp.sum(picked, axis=-1)
 
 
 def cross_product(spin_core, vector):
@@ -130,9 +125,16 @@
 
 def local_kernel(halo, slab_rows, *refs):
     slab_refs = refs[:2 * HALO_SLABS + 1]
-    start_ref, relaxed_ref, last_ref, sums_ref, win, sweep_a, sweep_b, bonds_b, bonds_yr, bonds_zr, spins_b, t1, t2, t3 = refs[2 * HALO_SLABS + 1:]
+    start_ref, exchange_ref, relaxed_ref, last_ref, sums_ref, win, sweep_a, sweep_b, bonds_b, bonds_yr, bonds_zr, spins_b, t1, t2, t3 = refs[2 * HALO_SLABS + 1:]
     for k, slab_ref in enumerate(slab_refs):
-        win[:, :, k * slab_rows:(k + 1) * slab_rows, :] = slab_ref[...]
+        block = slab_ref[...]
+        cos_polar, azimuth, bond_class = block[0], block[1], block[2:5]
+        radial = jnp.sqrt(1.0 - cos_polar * cos_polar)
+        strengths = jnp.zeros(bond_class.shape, jnp.float32)
+        for class_index in range(NCLASS):
+            strengths = jnp.where(bond_class == class_index, exchange_ref[class_index], strengths)
+        site = jnp.stack([radial * jnp.cos(azimuth), radial * jnp.sin(azimuth), cos_polar], 0)
+        win[:, :, k * slab_rows:(k + 1) * slab_rows, :] = jnp.concatenate([site, strengths], 0)
     width = len(slab_refs) * slab_rows
 
     def bond(d, a, b):
@@ -166,7 +168,6 @@
         spins_b[xr] = jnp.broadcast_to(sweep_b[:, :, w - SWEEPS:w - SWEEPS + 1, :], (3, depth, probes, lanes))
 
     t_refs = (start_ref, t1, t2, t3, last_ref)
-    sums = []
     for order in range(CHEB):
         lo = first + order
         n = n_start - 2 * order
@@ -192,15 +193,10 @@
                 part = part[0] + part[1] + part[2]
                 part = part[0] + part[1] + part[2] + part[3]
                 acc = part if acc is None else acc + part
-        sums.append(jnp.sum(acc, axis=-1, keepdims=True))
-    lane = lax.broadcasted_iota(jnp.int32, sums_ref.shape, 1)
-    out = jnp.zeros(sums_ref.shape, jnp.float32)
-    for order in range(CHEB):
-        out = jnp.where(lane == order, sums[order], out)
-    sums_ref[...] = out
-
-
-def run_local(slab_blocks, start, halo, slab_rows):
+        sums_ref[order:order + 1, :] = jnp.sum(acc.T, axis=0, keepdims=True)
+
+
+def run_local(slab_blocks, start, exchange, halo, slab_rows):
     depth, lanes = slab_blocks[0].shape[1], slab_blocks[0].shape[3]
     width = len(slab_blocks) * slab_rows
     n_start, probes = start.shape[0], start.shape[4]
@@ -215,9 +211,10 @@
         out_shape=(
             jax.ShapeDtypeStruct((3, depth, slab_rows, lanes), jnp.float32),
             jax.ShapeDtypeStruct((slab_rows,) + vec_shape, jnp.float32),
-            jax.ShapeDtypeStruct((probes, 128), jnp.float32),
-        ),
-        in_specs=[pl.BlockSpec(memory_space=pltpu.VMEM)] * (len(slab_blocks) + 1),
+            jax.ShapeDtypeStruct((CHEB, probes), jnp.float32),
+        ),
+        in_specs=[pl.BlockSpec(memory_space=pltpu.VMEM)] * (len(slab_blocks) + 1)
+        + [pl.BlockSpec(memory_space=pltpu.SMEM)],
         out_specs=[pl.BlockSpec(memory_space=pltpu.VMEM)] * 3,
         scratch_shapes=[
             pltpu.VMEM((6, depth, width, lanes), jnp.float32),
@@ -234,7 +231,7 @@
             transcendentals=0,
             bytes_accessed=4 * (6 * depth * width * lanes + start.size + start.size // 3),
         ),
-    )(*slab_blocks, start)
+    )(*slab_blocks, start, exchange)
 
 
 def shards(cos_polar, azimuth, bond_class, exchange, probe_wave):
@@ -248,10 +245,7 @@
     total_y = block_y * groups
     site_count = total_x * total_y * LZ
 
-    bonds = bond_strengths(bond_class, exchange)
-    radial = jnp.sqrt(1.0 - cos_polar * cos_polar)
-    spins0 = jnp.stack([radial * jnp.cos(azimuth), radial * jnp.sin(azimuth), cos_polar], 0)
-    local = jnp.concatenate([spins0, bonds], 0)
+    local = jnp.concatenate([cos_polar[None], azimuth[None], bond_class.astype(jnp.float32)], 0)
 
     pieces = [shifted(local, "probe", k) for k in range(groups)]
     rotated = jnp.concatenate(pieces, -1)
@@ -268,11 +262,11 @@
     start = make_probes(probe_wave, probe_ids, x_coords, y_coords, total_x, total_y, LZ)
     start = jnp.transpose(start, (4, 1, 2, 3, 0, 5))
 
-    relaxed, last, sums = run_local(slab_blocks, start, halo, slab_rows)
+    relaxed, last, sums = run_local(slab_blocks, start, exchange, halo, slab_rows)
     relaxed_own = lax.dynamic_slice_in_dim(relaxed, group * block_y, block_y, -1)
     last = jnp.transpose(last, (4, 1, 2, 3, 0, 5)).astype(jnp.bfloat16)
-    moment_rows = butterfly_sum(sums[:, :CHEB], "space") / site_count
-    return (relaxed_own, last, moment_rows)
+    moment_rows = butterfly_sum(sums, "space") / site_count
+    return (relaxed_own, last, moment_rows.T)
 
 
 def solution(mesh):

time: 41.1 us -> 40.1 us (0.976)
  local copies, waits for them, and re-layouts: 4.35 us -> 3.69 us
    reduce_sum x1 -> x0, other arithmetic: 0.9 us -> none  [bond_strengths(): return jnp.sum(picked, axis=-1)]
    another operation x1 -> x0, other arithmetic: 0.84 us -> none  [shards(): jnp.stack([radial * jnp.cos(azimuth), radial * jnp.sin(azimuth), cos_pola...]
    convert_element_type x0 -> x1, other arithmetic: none -> 0.75 us  [shards(): bond_class.astype(jnp.float32)]
    unnamed x14 -> x15, local copies, waits for them, and re-layouts: 2.12 us -> 1.47 us
    transpose x0 -> x1, other arithmetic: none -> 0.58 us  [shards(): return (relaxed_own, last, moment_rows.T)]
  transfers between devices with their start and end apart: 9 -> 9, of which waited for: 8 -> 7; matrix products, arithmetic and copies ran while one was open for 16% -> 16% of each run, Pallas kernels for 0% -> 0%
where the time goes in v5:
time: 40.1 us; the launch traced here: 39.7 us
  waiting for transfers between devices  15.2 us (38%)
  starting transfers between devices  8.66 us (22%)
  other arithmetic  6.34 us (16%)
  Pallas kernels  5.04 us (13%)
  local copies, waits for them, and re-layouts  3.69 us (9%)
  between operations  0.75 us (2%)
    ppermute x4, waiting for transfers between devices, butterfly_sum(): lax.ppermute(value, axis, [(i, i ^ step) for i in range(size)])  9.72 us
    ppermute x5, starting transfers between devices, shifted(): lax.ppermute(array, axis, [(i, (i - shift) % size) for i in range(size)])  8.65 us
    ppermute x5, waiting for transfers between devices, shifted(): lax.ppermute(array, axis, [(i, (i - shift) % size) for i in range(size)])  5.44 us
    pallas_call x1, Pallas kernels, run_local(): pl.pallas_call(body, out_shape=(jax.ShapeDtypeStruct((3, depth, slab_rows...  5.04 us
    unnamed x15, local copies, waits for them, and re-layouts  1.47 us
    dynamic_slice x1, local copies, waits for them, and re-layouts, shards(): lax.dynamic_slice_in_dim(relaxed, group * block_y, block_y, -1)  1.43 us
    mul x2, other arithmetic, make_probes(): return waves[:, :, None] * polar[:, None, :, None, None, None]  1.3 us
    convert_element_type x1, other arithmetic, shards(): last = jnp.transpose(last, (4, 1, 2, 3, 0, 5)).astype(jnp.bfloat16)  1.02 us
  transfers between devices with their start and end apart: 9, of which 7 were waited for; matrix products, arithmetic and copies ran while one was open for 16% of the time, Pallas kernels for 0%

profile of v5, /device:TPU:0, one launch (start us, length us, event | category | flops | bytes accessed | tf_op | source)
XLA Modules:
  0.0 39.7 jit_solution(7715690099819587630)
XLA Ops:
  0.7 0.8 %convert_element_type.48 = f32[3,4,4,64]{3,2,1,0:T(4,128)S(1)} convert(s32[3,4,4,64]{3,2,1,0:T(4,128)} %param.7) | non-fusion elementwise | flops 3072 | bytes 24576 | tf_op jit(solution)/shard_map/convert_element_type | solution.py:248
  1.4 0.7 %pad_maximum_fusion = f32[5,4,4,64]{3,2,1,0:T(4,128)S(1)} fusion(f32[3,4,4,64]{3,2,1,0:T(4,128)S(1)} %convert_element_type.48, f32[1,4,4,64]{3,2,1,0:T(4,128)} %bitcast.16, f32[1,4,4,64]{3,2,1,0:T(4,128)} %bitcast.14), kind=kLoop, calls=%fused_computation.21 | loop fusion | flops 10240 | bytes 40960 | tf_op jit(solution)/shard_map/concatenate | solution.py:248
  2.1 3.0 %collective-permute-start = (f32[5,4,4,64]{3,2,1,0:T(4,128)S(1)}, f32[5,4,4,64]{3,2,1,0:T(4,128)S(1)}, u32[]{:S(2)}, u32[]{:S(2)}) collective-permute-start(f32[5,4,4,64]{3,2,1,0:T(4,128)S(1)} %pad_maximum_fusion), channel_id=1, source_target_pairs={{0,16},{16,0},{1,17},{17,1},{2,18},{18,2},{3,19},{19,3},{4,20},{20... | collective-permute-start | bytes 61448 | tf_op jit(solution)/shard_map/ppermute | solution.py:25
  5.2 0.8 %slice_bitcast_fusion.2 = (s32[8]{0:T(128)S(1)}, s32[8]{0:T(128)S(1)}, s32[8]{0:T(128)S(1)}) fusion(s32[8,3]{0,1:T(4,128)} %param.9), kind=kLoop, calls=%fused_computation.58 | loop fusion | bytes 192 | tf_op jit(solution)/shard_map/slice | solution.py:70
  6.0 0.1 fusion.12
  6.2 0.8 %cosine_multiply_fusion = (f32[8,1,4,12,128]{4,0,2,1,3:T(8,128)S(1)}, f32[8,1,4,12,128]{4,0,2,1,3:T(8,128)S(1)}) fusion(f32[12]{0:T(128)S(1)} %add_sqrt_fusion, f32[8,128]{1,0:T(8,128)S(1)} %fusion.12, f32[8,4,12]{0,1,2:T(4,128)S(1)} %broadcast_add_fusion), kind=kLoop, calls=%fused_computation.4 | loop fusion | flops 196608 | bytes 398896 | tf_op jit(solution)/shard_map/mul | solution.py:81
  7.1 0.2 fusion.4.refs_2_
  7.3 5.1 %collective-permute-start.4 = (f32[5,4,4,128]{3,2,1,0:T(4,128)S(1)}, f32[5,4,4,128]{3,2,1,0:T(4,128)S(1)}, u32[]{:S(2)}, u32[]{:S(2)}) collective-permute-start(f32[5,4,4,128]{3,2,1,0:T(4,128)S(1)} %fusion.4.refs_2_), channel_id=1, source_target_pairs={{0,14},{1,15},{2,0},{3,1},{4,2},{5,3},{6,4},{7,5},{8,6},{9,7},{10,... | collective-permute-start | bytes 122888 | tf_op jit(solution)/shard_map/ppermute | solution.py:25
  12.5 0.5 %collective-permute-start.2 = (f32[5,4,4,128]{3,2,1,0:T(4,128)S(1)}, f32[5,4,4,128]{3,2,1,0:T(4,128)S(1)}, u32[]{:S(2)}, u32[]{:S(2)}) collective-permute-start(f32[5,4,4,128]{3,2,1,0:T(4,128)S(1)} %fusion.4.refs_2_), channel_id=1, source_target_pairs={{0,1},{1,2},{2,3},{3,4},{4,5},{5,6},{6,7},{7,8},{8,9},{9,10},{10,1... | collective-permute-start | bytes 122888 | tf_op jit(solution)/shard_map/ppermute | solution.py:25
  13.0 1.3 %broadcast_multiply_fusion.refs_5_ = f32[12,2,3,4,8,128]{5,4,3,2,1,0:T(8,128)} fusion(f32[3,8]{1,0:T(4,128)S(1)} %fusion.19, f32[12,2,4,8,128]{4,3,2,1,0:T(8,128)S(1)} %maximum_bitcast_fusion), kind=kLoop, calls=%fused_computation | loop fusion | flops 294912 | bytes 1572960 | tf_op jit(solution)/shard_map/mul | solution.py:85
  14.3 0.3 collective-permute-done.3.refs_3_
  14.5 4.1 %collective-permute-done.2.refs_1_ = f32[5,4,4,128]{3,2,1,0:T(4,128)S(1)} collective-permute-done((f32[5,4,4,128]{3,2,1,0:T(4,128)S(1)}, f32[5,4,4,128]{3,2,1,0:T(4,128)S(1)}, u32[]{:S(2)}, u32[]{:S(2)}) %collective-permute-start.2) | collective-permute-done | bytes 40992 | tf_op jit(solution)/shard_map/ppermute | solution.py:25
  18.6 1.1 %collective-permute-done.1.refs_0_ = f32[5,4,4,128]{3,2,1,0:T(4,128)S(1)} collective-permute-done((f32[5,4,4,128]{3,2,1,0:T(4,128)S(1)}, f32[5,4,4,128]{3,2,1,0:T(4,128)S(1)}, u32[]{:S(2)}, u32[]{:S(2)}) %collective-permute-start.1) | collective-permute-done | bytes 40992 | tf_op jit(solution)/shard_map/ppermute | solution.py:25
  19.7 0.6 %copy-done.4 = f32[5,4,4,128]{3,2,1,0:T(4,128)} copy-done((f32[5,4,4,128]{3,2,1,0:T(4,128)}, f32[5,4,4,128]{3,2,1,0:T(4,128)S(1)}, u32[]{:S(2)}) %copy-start.4) | copy-done | bytes 40984
  20.3 5.0 %shard_map.76 = (f32[3,4,4,128]{3,2,1,0:T(4,128)}, f32[4,2,3,4,8,128]{5,4,3,2,1,0:T(8,128)}, f32[4,8]{1,0:T(4,128)}) custom-call(f32[5,4,4,128]{3,2,1,0:T(4,128)} %copy-done.4, f32[5,4,4,128]{3,2,1,0:T(4,128)} %copy-done.3, f32[5,4,4,128]{3,2,1,0:T(4,128)} %copy-done, f32[5,4,4,128]{3,2,1,0:T(4,128)} %copy-done.2, f32[5,4,4,128]{3,2,1,0:T(4,128)} %copy-done.1, ...), custom_call_target="tpu_custom_call" | custom-call | flops 14991360 | bytes 1818624 | tf_op jit(solution)/shard_map/pallas_call | solution.py:209
  25.4 1.4 %collective-permute-done.5 = f32[4,8]{1,0:T(4,128)S(1)} collective-permute-done((f32[4,8]{1,0:T(4,128)}, f32[4,8]{1,0:T(4,128)S(1)}, u32[]{:S(2)}, u32[]{:S(2)}) %collective-permute-start.5) | collective-permute-done | bytes 160 | tf_op jit(solution)/shard_map/ppermute | solution.py:94
  26.7 0.7 %add.172 = f32[4,8]{1,0:T(4,128)S(1)} add(f32[4,8]{1,0:T(4,128)} %get-tuple-element.8, f32[4,8]{1,0:T(4,128)S(1)} %collective-permute-done.5) | non-fusion elementwise | flops 32 | bytes 384 | tf_op jit(solution)/shard_map/add | solution.py:94
  27.4 3.6 %collective-permute-done.6 = f32[4,8]{1,0:T(4,128)S(1)} collective-permute-done((f32[4,8]{1,0:T(4,128)S(1)}, f32[4,8]{1,0:T(4,128)S(1)}, u32[]{:S(2)}, u32[]{:S(2)}) %collective-permute-start.6) | collective-permute-done | bytes 160 | tf_op jit(solution)/shard_map/ppermute | solution.py:94
  31.0 1.0 %convert_bitcast_fusion = bf16[8,2,3,4,4,128]{5,0,3,2,1,4:T(8,128)(2,1)S(1)} fusion(f32[4,2,3,4,8,128]{5,4,3,2,1,0:T(8,128)} %get-tuple-element.7), kind=kLoop, calls=%fused_computation.2 | loop fusion | flops 98304 | bytes 589824 | tf_op jit(solution)/shard_map/convert_element_type | solution.py:267
  32.0 2.6 %collective-permute-done.7 = f32[4,8]{1,0:T(4,128)S(1)} collective-permute-done((f32[4,8]{1,0:T(4,128)S(1)}, f32[4,8]{1,0:T(4,128)S(1)}, u32[]{:S(2)}, u32[]{:S(2)}) %collective-permute-start.7) | collective-permute-done | bytes 160 | tf_op jit(solution)/shard_map/ppermute | solution.py:94
  34.6 1.4 %constant_dynamic-slice_fusion = f32[3,4,4,64]{3,2,1,0:T(4,128)} fusion(f32[3,4,4,128]{3,2,1,0:T(4,128)} %get-tuple-element.6, s32[]{:T(128)S(6)} %select_n.77), kind=kLoop, calls=%fused_computation.43 | loop fusion | bytes 24580 | tf_op jit(solution)/shard_map/dynamic_slice | solution.py:266
  36.0 0.8 %copy.8 = bf16[8,2,3,4,4,128]{5,4,3,2,1,0:T(4,128)(2,1)} copy(bf16[8,2,3,4,4,128]{5,0,3,2,1,4:T(8,128)(2,1)S(1)} %convert_bitcast_fusion) | data formatting | bytes 393216
  36.8 2.2 %collective-permute-done.8 = f32[4,8]{1,0:T(4,128)S(1)} collective-permute-done((f32[4,8]{1,0:T(4,128)S(1)}, f32[4,8]{1,0:T(4,128)S(1)}, u32[]{:S(2)}, u32[]{:S(2)}) %collective-permute-start.8) | collective-permute-done | bytes 160 | tf_op jit(solution)/shard_map/ppermute | solution.py:94
  39.1 0.6 %multiply_bitcast_fusion = f32[8,4]{0,1:T(4,128)} fusion(f32[4,8]{1,0:T(4,128)S(1)} %add.174, f32[4,8]{1,0:T(4,128)S(1)} %collective-permute-done.8), kind=kLoop, calls=%fused_computation.49 | loop fusion | flops 64 | bytes 384 | tf_op jit(solution)/shard_map/transpose | solution.py:269
  (31 shorter events, 0.3 us)
Async XLA Ops:
  0.6 6.5 %copy-start.6 = (f32[4,4,64]{2,1,0:T(4,128)S(1)}, f32[4,4,64]{2,1,0:T(4,128)}, u32[]{:S(2)}) copy-start(f32[4,4,64]{2,1,0:T(4,128)} %param.6) | copy-start | bytes 12292
  0.6 6.5 %copy-start.5 = (f32[4,4,64]{2,1,0:T(4,128)S(1)}, f32[4,4,64]{2,1,0:T(4,128)}, u32[]{:S(2)}) copy-start(f32[4,4,64]{2,1,0:T(4,128)} %param.5) | copy-start | bytes 12292
  2.1 5.0 %collective-permute-start = (f32[5,4,4,64]{3,2,1,0:T(4,128)S(1)}, f32[5,4,4,64]{3,2,1,0:T(4,128)S(1)}, u32[]{:S(2)}, u32[]{:S(2)}) collective-permute-start(f32[5,4,4,64]{3,2,1,0:T(4,128)S(1)} %pad_maximum_fusion), channel_id=1, source_target_pairs={{0,16},{16,0},{1,17},{17,1},{2,18},{18,2},{3,19},{19,3},{4,20},{20... | collective-permute-start | bytes 61448 | tf_op jit(solution)/shard_map/ppermute | solution.py:25
  7.3 12.4 %copy-start = (f32[5,4,4,128]{3,2,1,0:T(4,128)}, f32[5,4,4,128]{3,2,1,0:T(4,128)S(1)}, u32[]{:S(2)}) copy-start(f32[5,4,4,128]{3,2,1,0:T(4,128)S(1)} %fusion.4.refs_2_) | copy-start | bytes 122884
  7.3 6.9 %collective-permute-start.4 = (f32[5,4,4,128]{3,2,1,0:T(4,128)S(1)}, f32[5,4,4,128]{3,2,1,0:T(4,128)S(1)}, u32[]{:S(2)}, u32[]{:S(2)}) collective-permute-start(f32[5,4,4,128]{3,2,1,0:T(4,128)S(1)} %fusion.4.refs_2_), channel_id=1, source_target_pairs={{0,14},{1,15},{2,0},{3,1},{4,2},{5,3},{6,4},{7,5},{8,6},{9,7},{10,... | collective-permute-start | bytes 122888 | tf_op jit(solution)/shard_map/ppermute | solution.py:25
  12.5 2.1 %collective-permute-start.3 = (f32[5,4,4,128]{3,2,1,0:T(4,128)S(1)}, f32[5,4,4,128]{3,2,1,0:T(4,128)S(1)}, u32[]{:S(2)}, u32[]{:S(2)}) collective-permute-start(f32[5,4,4,128]{3,2,1,0:T(4,128)S(1)} %fusion.4.refs_2_), channel_id=1, source_target_pairs={{0,15},{1,0},{2,1},{3,2},{4,3},{5,4},{6,5},{7,6},{8,7},{9,8},{10,9... | collective-permute-start | bytes 122888 | tf_op jit(solution)/shard_map/ppermute | solution.py:25
  12.5 6.1 %collective-permute-start.2 = (f32[5,4,4,128]{3,2,1,0:T(4,128)S(1)}, f32[5,4,4,128]{3,2,1,0:T(4,128)S(1)}, u32[]{:S(2)}, u32[]{:S(2)}) collective-permute-start(f32[5,4,4,128]{3,2,1,0:T(4,128)S(1)} %fusion.4.refs_2_), channel_id=1, source_target_pairs={{0,1},{1,2},{2,3},{3,4},{4,5},{5,6},{6,7},{7,8},{8,9},{9,10},{10,1... | collective-permute-start | bytes 122888 | tf_op jit(solution)/shard_map/ppermute | solution.py:25
  13.0 6.7 %collective-permute-start.1 = (f32[5,4,4,128]{3,2,1,0:T(4,128)S(1)}, f32[5,4,4,128]{3,2,1,0:T(4,128)S(1)}, u32[]{:S(2)}, u32[]{:S(2)}) collective-permute-start(f32[5,4,4,128]{3,2,1,0:T(4,128)S(1)} %fusion.4.refs_2_), channel_id=1, source_target_pairs={{0,2},{1,3},{2,4},{3,5},{4,6},{5,7},{6,8},{7,9},{8,10},{9,11},{10,... | collective-permute-start | bytes 122888 | tf_op jit(solution)/shard_map/ppermute | solution.py:25
  14.3 5.4 %copy-start.1 = (f32[5,4,4,128]{3,2,1,0:T(4,128)}, f32[5,4,4,128]{3,2,1,0:T(4,128)S(1)}, u32[]{:S(2)}) copy-start(f32[5,4,4,128]{3,2,1,0:T(4,128)S(1)} %collective-permute-done.4.refs_4_) | copy-start | bytes 122884
  14.5 5.2 %copy-start.2 = (f32[5,4,4,128]{3,2,1,0:T(4,128)}, f32[5,4,4,128]{3,2,1,0:T(4,128)S(1)}, u32[]{:S(2)}) copy-start(f32[5,4,4,128]{3,2,1,0:T(4,128)S(1)} %collective-permute-done.3.refs_3_) | copy-start | bytes 122884
  18.6 1.1 %copy-start.3 = (f32[5,4,4,128]{3,2,1,0:T(4,128)}, f32[5,4,4,128]{3,2,1,0:T(4,128)S(1)}, u32[]{:S(2)}) copy-start(f32[5,4,4,128]{3,2,1,0:T(4,128)S(1)} %collective-permute-done.2.refs_1_) | copy-start | bytes 122884
  19.7 0.6 %copy-start.4 = (f32[5,4,4,128]{3,2,1,0:T(4,128)}, f32[5,4,4,128]{3,2,1,0:T(4,128)S(1)}, u32[]{:S(2)}) copy-start(f32[5,4,4,128]{3,2,1,0:T(4,128)S(1)} %collective-permute-done.1.refs_0_) | copy-start | bytes 122884
  25.4 1.4 %collective-permute-start.5 = (f32[4,8]{1,0:T(4,128)}, f32[4,8]{1,0:T(4,128)S(1)}, u32[]{:S(2)}, u32[]{:S(2)}) collective-permute-start(f32[4,8]{1,0:T(4,128)} %get-tuple-element.8), channel_id=1, source_target_pairs={{0,1},{1,0},{2,3},{3,2},{4,5},{5,4},{6,7},{7,6},{8,9},{9,8},{10,11... | collective-permute-start | bytes 392 | tf_op jit(solution)/shard_map/ppermute | solution.py:94
  27.4 3.6 %collective-permute-start.6 = (f32[4,8]{1,0:T(4,128)S(1)}, f32[4,8]{1,0:T(4,128)S(1)}, u32[]{:S(2)}, u32[]{:S(2)}) collective-permute-start(f32[4,8]{1,0:T(4,128)S(1)} %add.172), channel_id=1, source_target_pairs={{0,2},{1,3},{2,0},{3,1},{4,6},{5,7},{6,4},{7,5},{8,10},{9,11},{10,... | collective-permute-start | bytes 392 | tf_op jit(solution)/shard_map/ppermute | solution.py:94
  31.0 3.6 %collective-permute-start.7 = (f32[4,8]{1,0:T(4,128)S(1)}, f32[4,8]{1,0:T(4,128)S(1)}, u32[]{:S(2)}, u32[]{:S(2)}) collective-permute-start(f32[4,8]{1,0:T(4,128)S(1)} %add.173), channel_id=1, source_target_pairs={{0,4},{1,5},{2,6},{3,7},{4,0},{5,1},{6,2},{7,3},{8,12},{9,13},{10,... | collective-permute-start | bytes 392 | tf_op jit(solution)/shard_map/ppermute | solution.py:94
  34.6 4.5 %collective-permute-start.8 = (f32[4,8]{1,0:T(4,128)S(1)}, f32[4,8]{1,0:T(4,128)S(1)}, u32[]{:S(2)}, u32[]{:S(2)}) collective-permute-start(f32[4,8]{1,0:T(4,128)S(1)} %add.174), channel_id=1, source_target_pairs={{0,8},{1,9},{2,10},{3,11},{4,12},{5,13},{6,14},{7,15},{8,0},{9,1},... | collective-permute-start | bytes 392 | tf_op jit(solution)/shard_map/ppermute | solution.py:94

commit v6 on v5

--- a/solution.py
+++ b/solution.py
@@ -10,7 +10,6 @@
 LZ = 4
 SWEEPS = 2
 CHEB = 4
-HALO_SLABS = 2
 NCLASS = 8
 
 
@@ -123,10 +122,12 @@
     return total
 
 
-def local_kernel(halo, slab_rows, *refs):
-    slab_refs = refs[:2 * HALO_SLABS + 1]
-    start_ref, exchange_ref, relaxed_ref, last_ref, sums_ref, win, sweep_a, sweep_b, bonds_b, bonds_yr, bonds_zr, spins_b, t1, t2, t3 = refs[2 * HALO_SLABS + 1:]
-    for k, slab_ref in enumerate(slab_refs):
+def local_kernel(halo, slab_rows, scale, n_blocks, *refs):
+    slab_refs = refs[:n_blocks]
+    start_ref, exchange_ref, relaxed_ref, last_ref, sums_ref, win, sweep_a, sweep_b, bonds_b, bonds_yr, bonds_zr, spins_b, t1, t2, t3 = refs[n_blocks:]
+    offset = 0
+    for slab_ref in slab_refs:
+        count = slab_ref.shape[2]
         block = slab_ref[...]
         cos_polar, azimuth, bond_class = block[0], block[1], block[2:5]
         radial = jnp.sqrt(1.0 - cos_polar * cos_polar)
@@ -134,8 +135,9 @@
         for class_index in range(NCLASS):
             strengths = jnp.where(bond_class == class_index, exchange_ref[class_index], strengths)
         site = jnp.stack([radial * jnp.cos(azimuth), radial * jnp.sin(azimuth), cos_polar], 0)
-        win[:, :, k * slab_rows:(k + 1) * slab_rows, :] = jnp.concatenate([site, strengths], 0)
-    width = len(slab_refs) * slab_rows
+        win[:, :, offset:offset + count, :] = jnp.concatenate([site, strengths], 0)
+        offset += count
+    width = offset
 
     def bond(d, a, b):
         return win[3 + d, :, a:b, :]
@@ -193,17 +195,17 @@
                 part = part[0] + part[1] + part[2]
                 part = part[0] + part[1] + part[2] + part[3]
                 acc = part if acc is None else acc + part
-        sums_ref[order:order + 1, :] = jnp.sum(acc.T, axis=0, keepdims=True)
-
-
-def run_local(slab_blocks, start, exchange, halo, slab_rows):
+        sums_ref[order:order + 1, :] = jnp.sum(acc.T, axis=0, keepdims=True) * scale
+
+
+def run_local(slab_blocks, start, exchange, halo, slab_rows, site_count):
     depth, lanes = slab_blocks[0].shape[1], slab_blocks[0].shape[3]
-    width = len(slab_blocks) * slab_rows
+    width = sum(block.shape[2] for block in slab_blocks)
     n_start, probes = start.shape[0], start.shape[4]
     vec_shape = start.shape[1:]
 
     def body(*refs):
-        local_kernel(halo, slab_rows, *refs)
+        local_kernel(halo, slab_rows, 1.0 / site_count, len(slab_blocks), *refs)
 
     sites = n_start * start[0].size
     return pl.pallas_call(
@@ -251,8 +253,13 @@
     rotated = jnp.concatenate(pieces, -1)
     full_y = jnp.roll(rotated, group * block_y, -1) if groups > 1 else rotated
 
-    slab_blocks = [shifted(full_y, "space", k) for k in range(-HALO_SLABS, HALO_SLABS + 1)]
-    halo = HALO_SLABS * slab_rows
+    halo = SWEEPS + CHEB - 1
+    reach = -(-halo // slab_rows)
+    slab_blocks = []
+    for k in range(-reach, reach + 1):
+        low = max(k * slab_rows, -halo) - k * slab_rows
+        high = min((k + 1) * slab_rows, slab_rows + halo) - k * slab_rows
+        slab_blocks.append(shifted(full_y[:, :, low:high, :], "space", k))
 
     width = slab_rows + 2 * CHEB
     x_coords = (slab * slab_rows - CHEB + jnp.arange(width, dtype=jnp.int32)) % total_x
@@ -262,10 +269,10 @@
     start = make_probes(probe_wave, probe_ids, x_coords, y_coords, total_x, total_y, LZ)
     start = jnp.transpose(start, (4, 1, 2, 3, 0, 5))
 
-    relaxed, last, sums = run_local(slab_blocks, start, exchange, halo, slab_rows)
+    relaxed, last, sums = run_local(slab_blocks, start, exchange, halo, slab_rows, site_count)
     relaxed_own = lax.dynamic_slice_in_dim(relaxed, group * block_y, block_y, -1)
     last = jnp.transpose(last, (4, 1, 2, 3, 0, 5)).astype(jnp.bfloat16)
-    moment_rows = butterfly_sum(sums, "space") / site_count
+    moment_rows = butterfly_sum(sums, "space")
     return (relaxed_own, last, moment_rows.T)
 
 

time: 40.1 us -> 41.3 us (1.030)
  starting transfers between devices: 8.66 us -> 10.3 us
  waiting for transfers between devices: 15.2 us -> 14.4 us
  local copies, waits for them, and re-layouts: 3.69 us -> 4.3 us
    ppermute x4, starting transfers between devices: 0.01 us -> 1.54 us  [butterfly_sum(): lax.ppermute(value, axis, [(i, i ^ step) for i in range(size)])]
    unnamed x15, local copies, waits for them, and re-layouts: 1.47 us -> 2.05 us
    ppermute x5, waiting for transfers between devices: 5.44 us -> 4.98 us  [shifted(): lax.ppermute(array, axis, [(i, (i - shift) % size) for i in range(size)])]
  transfers between devices with their start and end apart: 9 -> 9, of which waited for: 7 -> 6; matrix products, arithmetic and copies ran while one was open for 16% -> 16% of each run, Pallas kernels for 0% -> 0%
where the time goes in v6:
time: 41.3 us; the launch traced here: 40.9 us
  waiting for transfers between devices  14.4 us (35%)
  starting transfers between devices  10.3 us (25%)
  other arithmetic  6.33 us (15%)
  Pallas kernels  4.84 us (12%)
  local copies, waits for them, and re-layouts  4.3 us (10%)
  between operations  0.76 us (2%)
    ppermute x4, waiting for transfers between devices, butterfly_sum(): lax.ppermute(value, axis, [(i, i ^ step) for i in range(size)])  9.39 us
    ppermute x5, starting transfers between devices, shifted(): lax.ppermute(array, axis, [(i, (i - shift) % size) for i in range(size)])  8.8 us
    ppermute x5, waiting for transfers between devices, shifted(): lax.ppermute(array, axis, [(i, (i - shift) % size) for i in range(size)])  4.98 us
    pallas_call x1, Pallas kernels, run_local(): pl.pallas_call(body, out_shape=(jax.ShapeDtypeStruct((3, depth, slab_rows...  4.84 us
    unnamed x15, local copies, waits for them, and re-layouts  2.05 us
    ppermute x4, starting transfers between devices, butterfly_sum(): lax.ppermute(value, axis, [(i, i ^ step) for i in range(size)])  1.54 us
    dynamic_slice x1, local copies, waits for them, and re-layouts, shards(): lax.dynamic_slice_in_dim(relaxed, group * block_y, block_y, -1)  1.43 us
    mul x2, other arithmetic, make_probes(): return waves[:, :, None] * polar[:, None, :, None, None, None]  1.29 us
  transfers between devices with their start and end apart: 9, of which 6 were waited for; matrix products, arithmetic and copies ran while one was open for 16% of the time, Pallas kernels for 0%

profile of v6, /device:TPU:0, one launch (start us, length us, event | category | flops | bytes accessed | tf_op | source)
XLA Modules:
  0.0 40.9 jit_solution(16077385406587569016)
XLA Ops:
  0.7 0.8 %convert_element_type.48 = f32[3,4,4,64]{3,2,1,0:T(4,128)S(1)} convert(s32[3,4,4,64]{3,2,1,0:T(4,128)} %param.7) | non-fusion elementwise | flops 3072 | bytes 24576 | tf_op jit(solution)/shard_map/convert_element_type | solution.py:250
  1.4 0.7 %pad_maximum_fusion = f32[5,4,4,64]{3,2,1,0:T(4,128)S(1)} fusion(f32[3,4,4,64]{3,2,1,0:T(4,128)S(1)} %convert_element_type.48, f32[1,4,4,64]{3,2,1,0:T(4,128)} %bitcast.16, f32[1,4,4,64]{3,2,1,0:T(4,128)} %bitcast.14), kind=kLoop, calls=%fused_computation.21 | loop fusion | flops 10240 | bytes 40960 | tf_op jit(solution)/shard_map/concatenate | solution.py:250
  2.1 3.0 %collective-permute-start = (f32[5,4,4,64]{3,2,1,0:T(4,128)S(1)}, f32[5,4,4,64]{3,2,1,0:T(4,128)S(1)}, u32[]{:S(2)}, u32[]{:S(2)}) collective-permute-start(f32[5,4,4,64]{3,2,1,0:T(4,128)S(1)} %pad_maximum_fusion), channel_id=1, source_target_pairs={{0,16},{16,0},{1,17},{17,1},{2,18},{18,2},{3,19},{19,3},{4,20},{20... | collective-permute-start | bytes 61448 | tf_op jit(solution)/shard_map/ppermute | solution.py:24
  5.2 0.8 %slice_bitcast_fusion.2 = (s32[8]{0:T(128)S(1)}, s32[8]{0:T(128)S(1)}, s32[8]{0:T(128)S(1)}) fusion(s32[8,3]{0,1:T(4,128)} %param.9), kind=kLoop, calls=%fused_computation.58 | loop fusion | bytes 192 | tf_op jit(solution)/shard_map/slice | solution.py:69
  6.2 0.8 %cosine_multiply_fusion = (f32[8,1,4,12,128]{4,0,2,1,3:T(8,128)S(1)}, f32[8,1,4,12,128]{4,0,2,1,3:T(8,128)S(1)}) fusion(f32[12]{0:T(128)S(1)} %add_sqrt_fusion, f32[8,128]{1,0:T(8,128)S(1)} %fusion.12, f32[8,4,12]{0,1,2:T(4,128)S(1)} %broadcast_add_fusion), kind=kLoop, calls=%fused_computation.4 | loop fusion | flops 196608 | bytes 398896 | tf_op jit(solution)/shard_map/mul | solution.py:80
  7.1 0.2 fusion.4.refs_2_
  7.4 3.8 %collective-permute-start.3 = (f32[5,4,4,128]{3,2,1,0:T(4,128)S(1)}, f32[5,4,4,128]{3,2,1,0:T(4,128)S(1)}, u32[]{:S(2)}, u32[]{:S(2)}) collective-permute-start(f32[5,4,4,128]{3,2,1,0:T(4,128)S(1)} %fusion.4.refs_2_), channel_id=1, source_target_pairs={{0,15},{1,0},{2,1},{3,2},{4,3},{5,4},{6,5},{7,6},{8,7},{9,8},{10,9... | collective-permute-start | bytes 122888 | tf_op jit(solution)/shard_map/ppermute | solution.py:24
  11.1 1.9 %collective-permute-start.4 = (f32[5,4,1,128]{3,2,1,0:T(1,128)S(1)}, f32[5,4,1,128]{3,2,1,0:T(1,128)S(1)}, u32[]{:S(2)}, u32[]{:S(2)}) collective-permute-start(f32[5,4,1,128]{3,2,1,0:T(1,128)S(1)} %get-tuple-element.12), channel_id=1, source_target_pairs={{0,14},{1,15},{2,0},{3,1},{4,2},{5,3},{6,4},{7,5},{8,6},{9,7},{10,... | collective-permute-start | bytes 30728 | tf_op jit(solution)/shard_map/ppermute | solution.py:24
  13.2 1.3 %broadcast_multiply_fusion.refs_5_ = f32[12,2,3,4,8,128]{5,4,3,2,1,0:T(8,128)} fusion(f32[3,8]{1,0:T(4,128)S(1)} %fusion.19, f32[12,2,4,8,128]{4,3,2,1,0:T(8,128)S(1)} %maximum_bitcast_fusion), kind=kLoop, calls=%fused_computation | loop fusion | flops 294912 | bytes 1572960 | tf_op jit(solution)/shard_map/mul | solution.py:84
  14.4 0.4 collective-permute-done.4.refs_4_
  14.8 4.6 %collective-permute-done.1.refs_0_ = f32[5,4,1,128]{3,2,1,0:T(1,128)S(1)} collective-permute-done((f32[5,4,1,128]{3,2,1,0:T(1,128)S(1)}, f32[5,4,1,128]{3,2,1,0:T(1,128)S(1)}, u32[]{:S(2)}, u32[]{:S(2)}) %collective-permute-start.1) | collective-permute-done | bytes 10272 | tf_op jit(solution)/shard_map/ppermute | solution.py:24
  19.4 0.6 %copy-done.6 = f32[5,4,1,128]{3,2,1,0:T(1,128)} copy-done((f32[5,4,1,128]{3,2,1,0:T(1,128)}, f32[5,4,1,128]{3,2,1,0:T(1,128)S(1)}, u32[]{:S(2)}) %copy-start.6) | copy-done | bytes 10264
  20.0 0.6 %copy-done.2 = f32[5,4,4,128]{3,2,1,0:T(4,128)} copy-done((f32[5,4,4,128]{3,2,1,0:T(4,128)}, f32[5,4,4,128]{3,2,1,0:T(4,128)S(1)}, u32[]{:S(2)}) %copy-start.2) | copy-done | bytes 40984
  20.6 4.8 %shard_map.76 = (f32[3,4,4,128]{3,2,1,0:T(4,128)}, f32[4,2,3,4,8,128]{5,4,3,2,1,0:T(8,128)}, f32[4,8]{1,0:T(4,128)}) custom-call(f32[5,4,1,128]{3,2,1,0:T(1,128)} %copy-done.6, f32[5,4,4,128]{3,2,1,0:T(4,128)} %copy-done.2, f32[5,4,4,128]{3,2,1,0:T(4,128)} %copy-done, f32[5,4,4,128]{3,2,1,0:T(4,128)} %copy-done.1, f32[5,4,1,128]{3,2,1,0:T(1,128)} %copy-done.5, ...), custom_call_target="tpu_custom_call" | custom-call | flops 13148160 | bytes 1744896 | tf_op jit(solution)/shard_map/pallas_call | solution.py:211
  25.5 1.5 %collective-permute-start.5 = (f32[4,8]{1,0:T(4,128)}, f32[4,8]{1,0:T(4,128)S(1)}, u32[]{:S(2)}, u32[]{:S(2)}) collective-permute-start(f32[4,8]{1,0:T(4,128)} %get-tuple-element.8), channel_id=1, source_target_pairs={{0,1},{1,0},{2,3},{3,2},{4,5},{5,4},{6,7},{7,6},{8,9},{9,8},{10,11... | collective-permute-start | bytes 392 | tf_op jit(solution)/shard_map/ppermute | solution.py:93
  27.0 1.0 %collective-permute-done.5 = f32[4,8]{1,0:T(4,128)S(1)} collective-permute-done((f32[4,8]{1,0:T(4,128)}, f32[4,8]{1,0:T(4,128)S(1)}, u32[]{:S(2)}, u32[]{:S(2)}) %collective-permute-start.5) | collective-permute-done | bytes 160 | tf_op jit(solution)/shard_map/ppermute | solution.py:93
  28.0 0.7 %add.172 = f32[4,8]{1,0:T(4,128)S(1)} add(f32[4,8]{1,0:T(4,128)} %get-tuple-element.8, f32[4,8]{1,0:T(4,128)S(1)} %collective-permute-done.5) | non-fusion elementwise | flops 32 | bytes 384 | tf_op jit(solution)/shard_map/add | solution.py:93
  28.7 3.6 %collective-permute-done.6 = f32[4,8]{1,0:T(4,128)S(1)} collective-permute-done((f32[4,8]{1,0:T(4,128)S(1)}, f32[4,8]{1,0:T(4,128)S(1)}, u32[]{:S(2)}, u32[]{:S(2)}) %collective-permute-start.6) | collective-permute-done | bytes 160 | tf_op jit(solution)/shard_map/ppermute | solution.py:93
  32.3 1.0 %convert_bitcast_fusion = bf16[8,2,3,4,4,128]{5,0,3,2,1,4:T(8,128)(2,1)S(1)} fusion(f32[4,2,3,4,8,128]{5,4,3,2,1,0:T(8,128)} %get-tuple-element.7), kind=kLoop, calls=%fused_computation.2 | loop fusion | flops 98304 | bytes 589824 | tf_op jit(solution)/shard_map/convert_element_type | solution.py:274
  33.3 2.6 %collective-permute-done.7 = f32[4,8]{1,0:T(4,128)S(1)} collective-permute-done((f32[4,8]{1,0:T(4,128)S(1)}, f32[4,8]{1,0:T(4,128)S(1)}, u32[]{:S(2)}, u32[]{:S(2)}) %collective-permute-start.7) | collective-permute-done | bytes 160 | tf_op jit(solution)/shard_map/ppermute | solution.py:93
  35.9 1.4 %constant_dynamic-slice_fusion = f32[3,4,4,64]{3,2,1,0:T(4,128)} fusion(f32[3,4,4,128]{3,2,1,0:T(4,128)} %get-tuple-element.6, s32[]{:T(128)S(6)} %select_n.77), kind=kLoop, calls=%fused_computation.43 | loop fusion | bytes 24580 | tf_op jit(solution)/shard_map/dynamic_slice | solution.py:273
  37.3 0.8 %copy.8 = bf16[8,2,3,4,4,128]{5,4,3,2,1,0:T(4,128)(2,1)} copy(bf16[8,2,3,4,4,128]{5,0,3,2,1,4:T(8,128)(2,1)S(1)} %convert_bitcast_fusion) | data formatting | bytes 393216
  38.1 2.2 %collective-permute-done.8 = f32[4,8]{1,0:T(4,128)S(1)} collective-permute-done((f32[4,8]{1,0:T(4,128)S(1)}, f32[4,8]{1,0:T(4,128)S(1)}, u32[]{:S(2)}, u32[]{:S(2)}) %collective-permute-start.8) | collective-permute-done | bytes 160 | tf_op jit(solution)/shard_map/ppermute | solution.py:93
  40.4 0.6 %add_bitcast_fusion = f32[8,4]{0,1:T(4,128)} fusion(f32[4,8]{1,0:T(4,128)S(1)} %add.174, f32[4,8]{1,0:T(4,128)S(1)} %collective-permute-done.8), kind=kLoop, calls=%fused_computation.49 | loop fusion | flops 32 | bytes 384 | tf_op jit(solution)/shard_map/transpose | solution.py:276
  (32 shorter events, 0.5 us)
Async XLA Ops:
  0.6 6.5 %copy-start.4 = (f32[4,4,64]{2,1,0:T(4,128)S(1)}, f32[4,4,64]{2,1,0:T(4,128)}, u32[]{:S(2)}) copy-start(f32[4,4,64]{2,1,0:T(4,128)} %param.6) | copy-start | bytes 12292
  0.6 6.5 %copy-start.3 = (f32[4,4,64]{2,1,0:T(4,128)S(1)}, f32[4,4,64]{2,1,0:T(4,128)}, u32[]{:S(2)}) copy-start(f32[4,4,64]{2,1,0:T(4,128)} %param.5) | copy-start | bytes 12292
  2.1 5.0 %collective-permute-start = (f32[5,4,4,64]{3,2,1,0:T(4,128)S(1)}, f32[5,4,4,64]{3,2,1,0:T(4,128)S(1)}, u32[]{:S(2)}, u32[]{:S(2)}) collective-permute-start(f32[5,4,4,64]{3,2,1,0:T(4,128)S(1)} %pad_maximum_fusion), channel_id=1, source_target_pairs={{0,16},{16,0},{1,17},{17,1},{2,18},{18,2},{3,19},{19,3},{4,20},{20... | collective-permute-start | bytes 61448 | tf_op jit(solution)/shard_map/ppermute | solution.py:24
  7.3 12.1 %copy-start = (f32[5,4,4,128]{3,2,1,0:T(4,128)}, f32[5,4,4,128]{3,2,1,0:T(4,128)S(1)}, u32[]{:S(2)}) copy-start(f32[5,4,4,128]{3,2,1,0:T(4,128)S(1)} %fusion.4.refs_2_) | copy-start | bytes 122884
  7.4 12.0 %collective-permute-start.3 = (f32[5,4,4,128]{3,2,1,0:T(4,128)S(1)}, f32[5,4,4,128]{3,2,1,0:T(4,128)S(1)}, u32[]{:S(2)}, u32[]{:S(2)}) collective-permute-start(f32[5,4,4,128]{3,2,1,0:T(4,128)S(1)} %fusion.4.refs_2_), channel_id=1, source_target_pairs={{0,15},{1,0},{2,1},{3,2},{4,3},{5,4},{6,5},{7,6},{8,7},{9,8},{10,9... | collective-permute-start | bytes 122888 | tf_op jit(solution)/shard_map/ppermute | solution.py:24
  11.1 8.3 %collective-permute-start.2 = (f32[5,4,4,128]{3,2,1,0:T(4,128)S(1)}, f32[5,4,4,128]{3,2,1,0:T(4,128)S(1)}, u32[]{:S(2)}, u32[]{:S(2)}) collective-permute-start(f32[5,4,4,128]{3,2,1,0:T(4,128)S(1)} %fusion.4.refs_2_), channel_id=1, source_target_pairs={{0,1},{1,2},{2,3},{3,4},{4,5},{5,6},{6,7},{7,8},{8,9},{9,10},{10,1... | collective-permute-start | bytes 122888 | tf_op jit(solution)/shard_map/ppermute | solution.py:24
  11.1 3.7 %collective-permute-start.4 = (f32[5,4,1,128]{3,2,1,0:T(1,128)S(1)}, f32[5,4,1,128]{3,2,1,0:T(1,128)S(1)}, u32[]{:S(2)}, u32[]{:S(2)}) collective-permute-start(f32[5,4,1,128]{3,2,1,0:T(1,128)S(1)} %get-tuple-element.12), channel_id=1, source_target_pairs={{0,14},{1,15},{2,0},{3,1},{4,2},{5,3},{6,4},{7,5},{8,6},{9,7},{10,... | collective-permute-start | bytes 30728 | tf_op jit(solution)/shard_map/ppermute | solution.py:24
  13.0 6.4 %collective-permute-start.1 = (f32[5,4,1,128]{3,2,1,0:T(1,128)S(1)}, f32[5,4,1,128]{3,2,1,0:T(1,128)S(1)}, u32[]{:S(2)}, u32[]{:S(2)}) collective-permute-start(f32[5,4,1,128]{3,2,1,0:T(1,128)S(1)} %get-tuple-element.13), channel_id=1, source_target_pairs={{0,2},{1,3},{2,4},{3,5},{4,6},{5,7},{6,8},{7,9},{8,10},{9,11},{10,... | collective-permute-start | bytes 30728 | tf_op jit(solution)/shard_map/ppermute | solution.py:24
  14.8 4.6 %copy-start.5 = (f32[5,4,1,128]{3,2,1,0:T(1,128)}, f32[5,4,1,128]{3,2,1,0:T(1,128)S(1)}, u32[]{:S(2)}) copy-start(f32[5,4,1,128]{3,2,1,0:T(1,128)S(1)} %collective-permute-done.4.refs_4_) | copy-start | bytes 30724
  19.4 0.6 %copy-start.6 = (f32[5,4,1,128]{3,2,1,0:T(1,128)}, f32[5,4,1,128]{3,2,1,0:T(1,128)S(1)}, u32[]{:S(2)}) copy-start(f32[5,4,1,128]{3,2,1,0:T(1,128)S(1)} %collective-permute-done.1.refs_0_) | copy-start | bytes 30724
  19.4 0.6 %copy-start.1 = (f32[5,4,4,128]{3,2,1,0:T(4,128)}, f32[5,4,4,128]{3,2,1,0:T(4,128)S(1)}, u32[]{:S(2)}) copy-start(f32[5,4,4,128]{3,2,1,0:T(4,128)S(1)} %collective-permute-done.3.refs_3_) | copy-start | bytes 122884
  20.0 0.6 %copy-start.2 = (f32[5,4,4,128]{3,2,1,0:T(4,128)}, f32[5,4,4,128]{3,2,1,0:T(4,128)S(1)}, u32[]{:S(2)}) copy-start(f32[5,4,4,128]{3,2,1,0:T(4,128)S(1)} %collective-permute-done.2.refs_1_) | copy-start | bytes 122884
  25.5 2.6 %collective-permute-start.5 = (f32[4,8]{1,0:T(4,128)}, f32[4,8]{1,0:T(4,128)S(1)}, u32[]{:S(2)}, u32[]{:S(2)}) collective-permute-start(f32[4,8]{1,0:T(4,128)} %get-tuple-element.8), channel_id=1, source_target_pairs={{0,1},{1,0},{2,3},{3,2},{4,5},{5,4},{6,7},{7,6},{8,9},{9,8},{10,11... | collective-permute-start | bytes 392 | tf_op jit(solution)/shard_map/ppermute | solution.py:93
  28.7 3.6 %collective-permute-start.6 = (f32[4,8]{1,0:T(4,128)S(1)}, f32[4,8]{1,0:T(4,128)S(1)}, u32[]{:S(2)}, u32[]{:S(2)}) collective-permute-start(f32[4,8]{1,0:T(4,128)S(1)} %add.172), channel_id=1, source_target_pairs={{0,2},{1,3},{2,0},{3,1},{4,6},{5,7},{6,4},{7,5},{8,10},{9,11},{10,... | collective-permute-start | bytes 392 | tf_op jit(solution)/shard_map/ppermute | solution.py:93
  32.3 3.6 %collective-permute-start.7 = (f32[4,8]{1,0:T(4,128)S(1)}, f32[4,8]{1,0:T(4,128)S(1)}, u32[]{:S(2)}, u32[]{:S(2)}) collective-permute-start(f32[4,8]{1,0:T(4,128)S(1)} %add.173), channel_id=1, source_target_pairs={{0,4},{1,5},{2,6},{3,7},{4,0},{5,1},{6,2},{7,3},{8,12},{9,13},{10,... | collective-permute-start | bytes 392 | tf_op jit(solution)/shard_map/ppermute | solution.py:93
  35.9 4.5 %collective-permute-start.8 = (f32[4,8]{1,0:T(4,128)S(1)}, f32[4,8]{1,0:T(4,128)S(1)}, u32[]{:S(2)}, u32[]{:S(2)}) collective-permute-start(f32[4,8]{1,0:T(4,128)S(1)} %add.174), channel_id=1, source_target_pairs={{0,8},{1,9},{2,10},{3,11},{4,12},{5,13},{6,14},{7,15},{8,0},{9,1},... | collective-permute-start | bytes 392 | tf_op jit(solution)/shard_map/ppermute | solution.py:93

commit v7 on v5

--- a/solution.py
+++ b/solution.py
@@ -123,11 +123,9 @@
     return total
 
 
-def local_kernel(halo, slab_rows, *refs):
-    slab_refs = refs[:2 * HALO_SLABS + 1]
-    start_ref, exchange_ref, relaxed_ref, last_ref, sums_ref, win, sweep_a, sweep_b, bonds_b, bonds_yr, bonds_zr, spins_b, t1, t2, t3 = refs[2 * HALO_SLABS + 1:]
-    for k, slab_ref in enumerate(slab_refs):
-        block = slab_ref[...]
+def local_kernel(halo, slab_rows, raw_ref, start_ref, exchange_ref, relaxed_ref, last_ref, sums_ref, win, sweep_a, sweep_b, bonds_b, bonds_yr, bonds_zr, spins_b, t1, t2, t3):
+    for k in range(2 * HALO_SLABS + 1):
+        block = raw_ref[:, :, k * slab_rows:(k + 1) * slab_rows, :]
         cos_polar, azimuth, bond_class = block[0], block[1], block[2:5]
         radial = jnp.sqrt(1.0 - cos_polar * cos_polar)
         strengths = jnp.zeros(bond_class.shape, jnp.float32)
@@ -135,7 +133,7 @@
             strengths = jnp.where(bond_class == class_index, exchange_ref[class_index], strengths)
         site = jnp.stack([radial * jnp.cos(azimuth), radial * jnp.sin(azimuth), cos_polar], 0)
         win[:, :, k * slab_rows:(k + 1) * slab_rows, :] = jnp.concatenate([site, strengths], 0)
-    width = len(slab_refs) * slab_rows
+    width = raw_ref.shape[2]
 
     def bond(d, a, b):
         return win[3 + d, :, a:b, :]
@@ -196,9 +194,8 @@
         sums_ref[order:order + 1, :] = jnp.sum(acc.T, axis=0, keepdims=True)
 
 
-def run_local(slab_blocks, start, exchange, halo, slab_rows):
-    depth, lanes = slab_blocks[0].shape[1], slab_blocks[0].shape[3]
-    width = len(slab_blocks) * slab_rows
+def run_local(raw, start, exchange, halo, slab_rows):
+    depth, width, lanes = raw.shape[1], raw.shape[2], raw.shape[3]
     n_start, probes = start.shape[0], start.shape[4]
     vec_shape = start.shape[1:]
 
@@ -213,7 +210,7 @@
             jax.ShapeDtypeStruct((slab_rows,) + vec_shape, jnp.float32),
             jax.ShapeDtypeStruct((CHEB, probes), jnp.float32),
         ),
-        in_specs=[pl.BlockSpec(memory_space=pltpu.VMEM)] * (len(slab_blocks) + 1)
+        in_specs=[pl.BlockSpec(memory_space=pltpu.VMEM)] * 2
         + [pl.BlockSpec(memory_space=pltpu.SMEM)],
         out_specs=[pl.BlockSpec(memory_space=pltpu.VMEM)] * 3,
         scratch_shapes=[
@@ -231,7 +228,7 @@
             transcendentals=0,
             bytes_accessed=4 * (6 * depth * width * lanes + start.size + start.size // 3),
         ),
-    )(*slab_blocks, start, exchange)
+    )(raw, start, exchange)
 
 
 def shards(cos_polar, azimuth, bond_class, exchange, probe_wave):
@@ -247,24 +244,25 @@
 
     local = jnp.concatenate([cos_polar[None], azimuth[None], bond_class.astype(jnp.float32)], 0)
 
-    pieces = [shifted(local, "probe", k) for k in range(groups)]
-    rotated = jnp.concatenate(pieces, -1)
-    full_y = jnp.roll(rotated, group * block_y, -1) if groups > 1 else rotated
-
-    slab_blocks = [shifted(full_y, "space", k) for k in range(-HALO_SLABS, HALO_SLABS + 1)]
+    half = jnp.concatenate(
+        [shifted(local, "space", k) for k in range(-HALO_SLABS, HALO_SLABS + 1)], 2
+    )
     halo = HALO_SLABS * slab_rows
+    raw = jnp.concatenate([shifted(half, "probe", k) for k in range(groups)], -1)
 
     width = slab_rows + 2 * CHEB
     x_coords = (slab * slab_rows - CHEB + jnp.arange(width, dtype=jnp.int32)) % total_x
-    y_coords = jnp.arange(total_y, dtype=jnp.int32)
+    y_coords = (group * block_y + jnp.arange(total_y, dtype=jnp.int32)) % total_y
     group_size = probe_wave.shape[0]
     probe_ids = group * group_size + jnp.arange(group_size, dtype=jnp.int32)
     start = make_probes(probe_wave, probe_ids, x_coords, y_coords, total_x, total_y, LZ)
     start = jnp.transpose(start, (4, 1, 2, 3, 0, 5))
 
-    relaxed, last, sums = run_local(slab_blocks, start, exchange, halo, slab_rows)
-    relaxed_own = lax.dynamic_slice_in_dim(relaxed, group * block_y, block_y, -1)
+    relaxed, last, sums = run_local(raw, start, exchange, halo, slab_rows)
+    relaxed_own = relaxed[..., :block_y]
     last = jnp.transpose(last, (4, 1, 2, 3, 0, 5)).astype(jnp.bfloat16)
+    if groups > 1:
+        last = jnp.roll(last, group * block_y, -1)
     moment_rows = butterfly_sum(sums, "space") / site_count
     return (relaxed_own, last, moment_rows.T)
 

time: 40.1 us -> 44.1 us (1.100)
  waiting for transfers between devices: 15.2 us -> 20.3 us
  local copies, waits for them, and re-layouts: 3.69 us -> 1.73 us
  other arithmetic: 6.34 us -> 7.15 us
    ppermute x5, waiting for transfers between devices: 5.44 us -> 9.35 us  [shifted(): lax.ppermute(array, axis, [(i, (i - shift) % size) for i in range(size)])]
    dynamic_slice x1 -> x0, local copies, waits for them, and re-layouts: 1.43 us -> none  [shards(): lax.dynamic_slice_in_dim(relaxed, group * block_y, block_y, -1)]
    ppermute x4, waiting for transfers between devices: 9.72 us -> 11 us  [butterfly_sum(): lax.ppermute(value, axis, [(i, i ^ step) for i in range(size)])]
    concatenate x1 -> x2, other arithmetic: 0.19 us -> 1.03 us  [the longest x1 0.84 us: shards(): jnp.concatenate([shifted(half, 'probe', k) for k in range(groups)], -1)]
    unnamed x15 -> x1, local copies, waits for them, and re-layouts: 1.47 us -> 0.83 us
  transfers between devices with their start and end apart: 9 -> 9, of which waited for: 7 -> 7; matrix products, arithmetic and copies ran while one was open for 16% -> 12% of each run, Pallas kernels for 0% -> 0%
where the time goes in v7:
time: 44.1 us; the launch traced here: 43.8 us
  waiting for transfers between devices  20.3 us (46%)
  starting transfers between devices  8.84 us (20%)
  other arithmetic  7.15 us (16%)
  Pallas kernels  5.07 us (11%)
  local copies, waits for them, and re-layouts  1.73 us (4%)
  between operations  0.71 us (2%)
    ppermute x4, waiting for transfers between devices, butterfly_sum(): lax.ppermute(value, axis, [(i, i ^ step) for i in range(size)])  11 us
    ppermute x5, waiting for transfers between devices, shifted(): lax.ppermute(array, axis, [(i, (i - shift) % size) for i in range(size)])  9.35 us
    ppermute x5, starting transfers between devices, shifted(): lax.ppermute(array, axis, [(i, (i - shift) % size) for i in range(size)])  8.83 us
    pallas_call x1, Pallas kernels, run_local(): pl.pallas_call(body, out_shape=(jax.ShapeDtypeStruct((3, depth, slab_rows...  5.07 us
    mul x2, other arithmetic, make_probes(): return waves[:, :, None] * polar[:, None, :, None, None, None]  1.26 us
    convert_element_type x1, other arithmetic, shards(): last = jnp.transpose(last, (4, 1, 2, 3, 0, 5)).astype(jnp.bfloat16)  1.02 us
  transfers between devices with their start and end apart: 9, of which 7 were waited for; matrix products, arithmetic and copies ran while one was open for 12% of the time, Pallas kernels for 0%

profile of v7, /device:TPU:0, one launch (start us, length us, event | category | flops | bytes accessed | tf_op | source)
XLA Modules:
  0.0 43.8 jit_solution(14610790225598688150)
XLA Ops:
  0.6 0.7 %convert_element_type.48 = f32[3,4,4,64]{3,2,1,0:T(4,128)S(1)} convert(s32[3,4,4,64]{3,2,1,0:T(4,128)} %param.7) | non-fusion elementwise | flops 3072 | bytes 24576 | tf_op jit(solution)/shard_map/convert_element_type | solution.py:245
  1.4 0.7 %pad_maximum_fusion.1 = f32[5,4,4,64]{3,2,1,0:T(4,128)S(1)} fusion(f32[3,4,4,64]{3,2,1,0:T(4,128)S(1)} %convert_element_type.48, f32[1,4,4,64]{3,2,1,0:T(4,128)} %bitcast.15, f32[1,4,4,64]{3,2,1,0:T(4,128)} %bitcast.16), kind=kLoop, calls=%fused_computation.10 | loop fusion | flops 10240 | bytes 40960 | tf_op jit(solution)/shard_map/concatenate | solution.py:245
  2.1 6.1 %collective-permute-start.3 = (f32[5,4,4,64]{3,2,1,0:T(4,128)S(1)}, f32[5,4,4,64]{3,2,1,0:T(4,128)S(1)}, u32[]{:S(2)}, u32[]{:S(2)}) collective-permute-start(f32[5,4,4,64]{3,2,1,0:T(4,128)S(1)} %pad_maximum_fusion.1), channel_id=1, source_target_pairs={{0,14},{1,15},{2,0},{3,1},{4,2},{5,3},{6,4},{7,5},{8,6},{9,7},{10,... | collective-permute-start | bytes 61448 | tf_op jit(solution)/shard_map/ppermute | solution.py:25
  8.2 0.5 %collective-permute-start.1 = (f32[5,4,4,64]{3,2,1,0:T(4,128)S(1)}, f32[5,4,4,64]{3,2,1,0:T(4,128)S(1)}, u32[]{:S(2)}, u32[]{:S(2)}) collective-permute-start(f32[5,4,4,64]{3,2,1,0:T(4,128)S(1)} %pad_maximum_fusion.1), channel_id=1, source_target_pairs={{0,1},{1,2},{2,3},{3,4},{4,5},{5,6},{6,7},{7,8},{8,9},{9,10},{10,1... | collective-permute-start | bytes 61448 | tf_op jit(solution)/shard_map/ppermute | solution.py:25
  8.7 0.7 %collective-permute-start = (f32[5,4,4,64]{3,2,1,0:T(4,128)S(1)}, f32[5,4,4,64]{3,2,1,0:T(4,128)S(1)}, u32[]{:S(2)}, u32[]{:S(2)}) collective-permute-start(f32[5,4,4,64]{3,2,1,0:T(4,128)S(1)} %pad_maximum_fusion.1), channel_id=1, source_target_pairs={{0,2},{1,3},{2,4},{3,5},{4,6},{5,7},{6,8},{7,9},{8,10},{9,11},{10,... | collective-permute-start | bytes 61448 | tf_op jit(solution)/shard_map/ppermute | solution.py:25
  9.5 0.8 %slice_bitcast_fusion.2 = (s32[8]{0:T(128)S(1)}, s32[8]{0:T(128)S(1)}, s32[8]{0:T(128)S(1)}) fusion(s32[8,3]{0,1:T(4,128)} %param.9), kind=kLoop, calls=%fused_computation.49 | loop fusion | bytes 192 | tf_op jit(solution)/shard_map/slice | solution.py:70
  10.4 0.8 %cosine_multiply_fusion = (f32[8,1,4,12,128]{4,0,2,1,3:T(8,128)S(1)}, f32[8,1,4,12,128]{4,0,2,1,3:T(8,128)S(1)}) fusion(f32[12]{0:T(128)S(1)} %add_sqrt_fusion, f32[8,128]{1,0:T(8,128)S(1)} %fusion.5, f32[8,4,12]{0,1,2:T(4,128)S(1)} %broadcast_add_fusion), kind=kLoop, calls=%fused_computation.8 | loop fusion | flops 196608 | bytes 398896 | tf_op jit(solution)/shard_map/mul | solution.py:81
  11.4 2.9 %collective-permute-done.1 = f32[5,4,4,64]{3,2,1,0:T(4,128)S(1)} collective-permute-done((f32[5,4,4,64]{3,2,1,0:T(4,128)S(1)}, f32[5,4,4,64]{3,2,1,0:T(4,128)S(1)}, u32[]{:S(2)}, u32[]{:S(2)}) %collective-permute-start.1) | collective-permute-done | bytes 20512 | tf_op jit(solution)/shard_map/ppermute | solution.py:25
  14.3 1.3 %collective-permute-done = f32[5,4,4,64]{3,2,1,0:T(4,128)S(1)} collective-permute-done((f32[5,4,4,64]{3,2,1,0:T(4,128)S(1)}, f32[5,4,4,64]{3,2,1,0:T(4,128)S(1)}, u32[]{:S(2)}, u32[]{:S(2)}) %collective-permute-start) | collective-permute-done | bytes 20512 | tf_op jit(solution)/shard_map/ppermute | solution.py:25
  15.6 0.1 concatenate.14
  15.7 1.6 %collective-permute-start.4 = (f32[5,4,20,64]{3,2,1,0:T(8,128)S(1)}, f32[5,4,20,64]{3,2,1,0:T(8,128)S(1)}, u32[]{:S(2)}, u32[]{:S(2)}) collective-permute-start(f32[5,4,20,64]{3,2,1,0:T(8,128)S(1)} %concatenate.14), channel_id=1, source_target_pairs={{0,16},{16,0},{1,17},{17,1},{2,18},{18,2},{3,19},{19,3},{4,20},{20... | collective-permute-start | bytes 307208 | tf_op jit(solution)/shard_map/ppermute | solution.py:25
  17.3 1.2 %broadcast_multiply_fusion.refs_1_ = f32[12,2,3,4,8,128]{5,4,3,2,1,0:T(8,128)} fusion(f32[3,8]{1,0:T(4,128)S(1)} %fusion.10, f32[12,2,4,8,128]{4,3,2,1,0:T(8,128)S(1)} %maximum_bitcast_fusion), kind=kLoop, calls=%fused_computation | loop fusion | flops 294912 | bytes 1572960 | tf_op jit(solution)/shard_map/mul | solution.py:85
  18.5 5.1 %collective-permute-done.4 = f32[5,4,20,64]{3,2,1,0:T(8,128)S(1)} collective-permute-done((f32[5,4,20,64]{3,2,1,0:T(8,128)S(1)}, f32[5,4,20,64]{3,2,1,0:T(8,128)S(1)}, u32[]{:S(2)}, u32[]{:S(2)}) %collective-permute-start.4) | collective-permute-done | bytes 102432 | tf_op jit(solution)/shard_map/ppermute | solution.py:25
  23.6 0.8 %pad_maximum_fusion.refs_0_ = f32[5,4,20,128]{3,2,1,0:T(8,128)} fusion(f32[5,4,20,64]{3,2,1,0:T(8,128)S(1)} %collective-permute-done.4, f32[5,4,20,64]{3,2,1,0:T(8,128)S(1)} %concatenate.14), kind=kLoop, calls=%fused_computation.4 | loop fusion | flops 51200 | bytes 409600 | tf_op jit(solution)/shard_map/concatenate | solution.py:251
  24.4 5.1 %shard_map.76 = (f32[3,4,4,128]{3,2,1,0:T(4,128)}, f32[4,2,3,4,8,128]{5,4,3,2,1,0:T(8,128)}, f32[4,8]{1,0:T(4,128)}) custom-call(f32[5,4,20,128]{3,2,1,0:T(8,128)} %pad_maximum_fusion.refs_0_, f32[12,2,3,4,8,128]{5,4,3,2,1,0:T(8,128)} %broadcast_multiply_fusion.refs_1_, f32[8]{0:T(128)} %refs_2_.1), custom_call_target="tpu_custom_call" | custom-call | flops 14991360 | bytes 1818624 | tf_op jit(solution)/shard_map/pallas_call | solution.py:206
  29.5 1.4 %collective-permute-done.5 = f32[4,8]{1,0:T(4,128)S(1)} collective-permute-done((f32[4,8]{1,0:T(4,128)}, f32[4,8]{1,0:T(4,128)S(1)}, u32[]{:S(2)}, u32[]{:S(2)}) %collective-permute-start.5) | collective-permute-done | bytes 160 | tf_op jit(solution)/shard_map/ppermute | solution.py:94
  30.9 0.7 %add.191 = f32[4,8]{1,0:T(4,128)S(1)} add(f32[4,8]{1,0:T(4,128)} %get-tuple-element.8, f32[4,8]{1,0:T(4,128)S(1)} %collective-permute-done.5) | non-fusion elementwise | flops 32 | bytes 384 | tf_op jit(solution)/shard_map/add | solution.py:94
  31.6 3.6 %collective-permute-done.6 = f32[4,8]{1,0:T(4,128)S(1)} collective-permute-done((f32[4,8]{1,0:T(4,128)S(1)}, f32[4,8]{1,0:T(4,128)S(1)}, u32[]{:S(2)}, u32[]{:S(2)}) %collective-permute-start.6) | collective-permute-done | bytes 160 | tf_op jit(solution)/shard_map/ppermute | solution.py:94
  35.1 1.0 %convert_bitcast_fusion = bf16[8,2,3,4,4,128]{5,0,3,2,1,4:T(8,128)(2,1)S(1)} fusion(f32[4,2,3,4,8,128]{5,4,3,2,1,0:T(8,128)} %get-tuple-element.7), kind=kLoop, calls=%fused_computation.6 | loop fusion | flops 98304 | bytes 589824 | tf_op jit(solution)/shard_map/convert_element_type | solution.py:263
  36.2 2.6 %collective-permute-done.7 = f32[4,8]{1,0:T(4,128)S(1)} collective-permute-done((f32[4,8]{1,0:T(4,128)S(1)}, f32[4,8]{1,0:T(4,128)S(1)}, u32[]{:S(2)}, u32[]{:S(2)}) %collective-permute-start.7) | collective-permute-done | bytes 160 | tf_op jit(solution)/shard_map/ppermute | solution.py:94
  38.7 0.2 fusion
  38.9 0.8 %copy.8 = bf16[8,2,3,4,4,128]{5,4,3,2,1,0:T(4,128)(2,1)} copy(bf16[8,2,3,4,4,128]{5,0,3,2,1,4:T(8,128)(2,1)S(1)} %fusion) | data formatting | bytes 393216
  39.8 3.4 %collective-permute-done.8 = f32[4,8]{1,0:T(4,128)S(1)} collective-permute-done((f32[4,8]{1,0:T(4,128)S(1)}, f32[4,8]{1,0:T(4,128)S(1)}, u32[]{:S(2)}, u32[]{:S(2)}) %collective-permute-start.8) | collective-permute-done | bytes 160 | tf_op jit(solution)/shard_map/ppermute | solution.py:94
  43.2 0.6 %multiply_bitcast_fusion = f32[8,4]{0,1:T(4,128)} fusion(f32[4,8]{1,0:T(4,128)S(1)} %add.193, f32[4,8]{1,0:T(4,128)S(1)} %collective-permute-done.8), kind=kLoop, calls=%fused_computation.38 | loop fusion | flops 64 | bytes 384 | tf_op jit(solution)/shard_map/transpose | solution.py:267
  (19 shorter events, 0.3 us)
Async XLA Ops:
  2.1 9.2 %collective-permute-start.3 = (f32[5,4,4,64]{3,2,1,0:T(4,128)S(1)}, f32[5,4,4,64]{3,2,1,0:T(4,128)S(1)}, u32[]{:S(2)}, u32[]{:S(2)}) collective-permute-start(f32[5,4,4,64]{3,2,1,0:T(4,128)S(1)} %pad_maximum_fusion.1), channel_id=1, source_target_pairs={{0,14},{1,15},{2,0},{3,1},{4,2},{5,3},{6,4},{7,5},{8,6},{9,7},{10,... | collective-permute-start | bytes 61448 | tf_op jit(solution)/shard_map/ppermute | solution.py:25
  8.2 3.2 %collective-permute-start.2 = (f32[5,4,4,64]{3,2,1,0:T(4,128)S(1)}, f32[5,4,4,64]{3,2,1,0:T(4,128)S(1)}, u32[]{:S(2)}, u32[]{:S(2)}) collective-permute-start(f32[5,4,4,64]{3,2,1,0:T(4,128)S(1)} %pad_maximum_fusion.1), channel_id=1, source_target_pairs={{0,15},{1,0},{2,1},{3,2},{4,3},{5,4},{6,5},{7,6},{8,7},{9,8},{10,9... | collective-permute-start | bytes 61448 | tf_op jit(solution)/shard_map/ppermute | solution.py:25
  8.2 6.1 %collective-permute-start.1 = (f32[5,4,4,64]{3,2,1,0:T(4,128)S(1)}, f32[5,4,4,64]{3,2,1,0:T(4,128)S(1)}, u32[]{:S(2)}, u32[]{:S(2)}) collective-permute-start(f32[5,4,4,64]{3,2,1,0:T(4,128)S(1)} %pad_maximum_fusion.1), channel_id=1, source_target_pairs={{0,1},{1,2},{2,3},{3,4},{4,5},{5,6},{6,7},{7,8},{8,9},{9,10},{10,1... | collective-permute-start | bytes 61448 | tf_op jit(solution)/shard_map/ppermute | solution.py:25
  8.7 7.0 %collective-permute-start = (f32[5,4,4,64]{3,2,1,0:T(4,128)S(1)}, f32[5,4,4,64]{3,2,1,0:T(4,128)S(1)}, u32[]{:S(2)}, u32[]{:S(2)}) collective-permute-start(f32[5,4,4,64]{3,2,1,0:T(4,128)S(1)} %pad_maximum_fusion.1), channel_id=1, source_target_pairs={{0,2},{1,3},{2,4},{3,5},{4,6},{5,7},{6,8},{7,9},{8,10},{9,11},{10,... | collective-permute-start | bytes 61448 | tf_op jit(solution)/shard_map/ppermute | solution.py:25
  15.7 7.9 %collective-permute-start.4 = (f32[5,4,20,64]{3,2,1,0:T(8,128)S(1)}, f32[5,4,20,64]{3,2,1,0:T(8,128)S(1)}, u32[]{:S(2)}, u32[]{:S(2)}) collective-permute-start(f32[5,4,20,64]{3,2,1,0:T(8,128)S(1)} %concatenate.14), channel_id=1, source_target_pairs={{0,16},{16,0},{1,17},{17,1},{2,18},{18,2},{3,19},{19,3},{4,20},{20... | collective-permute-start | bytes 307208 | tf_op jit(solution)/shard_map/ppermute | solution.py:25
  29.5 1.4 %collective-permute-start.5 = (f32[4,8]{1,0:T(4,128)}, f32[4,8]{1,0:T(4,128)S(1)}, u32[]{:S(2)}, u32[]{:S(2)}) collective-permute-start(f32[4,8]{1,0:T(4,128)} %get-tuple-element.8), channel_id=1, source_target_pairs={{0,1},{1,0},{2,3},{3,2},{4,5},{5,4},{6,7},{7,6},{8,9},{9,8},{10,11... | collective-permute-start | bytes 392 | tf_op jit(solution)/shard_map/ppermute | solution.py:94
  31.6 3.6 %collective-permute-start.6 = (f32[4,8]{1,0:T(4,128)S(1)}, f32[4,8]{1,0:T(4,128)S(1)}, u32[]{:S(2)}, u32[]{:S(2)}) collective-permute-start(f32[4,8]{1,0:T(4,128)S(1)} %add.191), channel_id=1, source_target_pairs={{0,2},{1,3},{2,0},{3,1},{4,6},{5,7},{6,4},{7,5},{8,10},{9,11},{10,... | collective-permute-start | bytes 392 | tf_op jit(solution)/shard_map/ppermute | solution.py:94
  35.1 3.6 %collective-permute-start.7 = (f32[4,8]{1,0:T(4,128)S(1)}, f32[4,8]{1,0:T(4,128)S(1)}, u32[]{:S(2)}, u32[]{:S(2)}) collective-permute-start(f32[4,8]{1,0:T(4,128)S(1)} %add.192), channel_id=1, source_target_pairs={{0,4},{1,5},{2,6},{3,7},{4,0},{5,1},{6,2},{7,3},{8,12},{9,13},{10,... | collective-permute-start | bytes 392 | tf_op jit(solution)/shard_map/ppermute | solution.py:94
  38.7 4.5 %collective-permute-start.8 = (f32[4,8]{1,0:T(4,128)S(1)}, f32[4,8]{1,0:T(4,128)S(1)}, u32[]{:S(2)}, u32[]{:S(2)}) collective-permute-start(f32[4,8]{1,0:T(4,128)S(1)} %add.193), channel_id=1, source_target_pairs={{0,8},{1,9},{2,10},{3,11},{4,12},{5,13},{6,14},{7,15},{8,0},{9,1},... | collective-permute-start | bytes 392 | tf_op jit(solution)/shard_map/ppermute | solution.py:94

commit v8 on v7

--- a/solution.py
+++ b/solution.py
@@ -10,7 +10,6 @@
 LZ = 4
 SWEEPS = 2
 CHEB = 4
-HALO_SLABS = 2
 NCLASS = 8
 
 
@@ -124,15 +123,14 @@
 
 
 def local_kernel(halo, slab_rows, raw_ref, start_ref, exchange_ref, relaxed_ref, last_ref, sums_ref, win, sweep_a, sweep_b, bonds_b, bonds_yr, bonds_zr, spins_b, t1, t2, t3):
-    for k in range(2 * HALO_SLABS + 1):
-        block = raw_ref[:, :, k * slab_rows:(k + 1) * slab_rows, :]
-        cos_polar, azimuth, bond_class = block[0], block[1], block[2:5]
-        radial = jnp.sqrt(1.0 - cos_polar * cos_polar)
-        strengths = jnp.zeros(bond_class.shape, jnp.float32)
-        for class_index in range(NCLASS):
-            strengths = jnp.where(bond_class == class_index, exchange_ref[class_index], strengths)
-        site = jnp.stack([radial * jnp.cos(azimuth), radial * jnp.sin(azimuth), cos_polar], 0)
-        win[:, :, k * slab_rows:(k + 1) * slab_rows, :] = jnp.concatenate([site, strengths], 0)
+    block = raw_ref[...]
+    cos_polar, azimuth, bond_class = block[0], block[1], block[2:5]
+    radial = jnp.sqrt(1.0 - cos_polar * cos_polar)
+    strengths = jnp.zeros(bond_class.shape, jnp.float32)
+    for class_index in range(NCLASS):
+        strengths = jnp.where(bond_class == class_index, exchange_ref[class_index], strengths)
+    site = jnp.stack([radial * jnp.cos(azimuth), radial * jnp.sin(azimuth), cos_polar], 0)
+    win[...] = jnp.concatenate([site, strengths], 0)
     width = raw_ref.shape[2]
 
     def bond(d, a, b):
@@ -244,11 +242,25 @@
 
     local = jnp.concatenate([cos_polar[None], azimuth[None], bond_class.astype(jnp.float32)], 0)
 
-    half = jnp.concatenate(
-        [shifted(local, "space", k) for k in range(-HALO_SLABS, HALO_SLABS + 1)], 2
-    )
-    halo = HALO_SLABS * slab_rows
-    raw = jnp.concatenate([shifted(half, "probe", k) for k in range(groups)], -1)
+    def pair_block(array, group_shift):
+        pairs = []
+        for g in range(groups):
+            for i in range(slabs):
+                pairs.append((((g + group_shift) % groups) * slabs + (i ^ 1), g * slabs + i))
+        return lax.ppermute(array, ("probe", "space"), pairs)
+
+    mine = jnp.concatenate([shifted(local, "probe", k) for k in range(groups)], -1)
+    beside = jnp.concatenate([pair_block(local, k) for k in range(groups)], -1)
+    odd = slab % 2 == 1
+    chip = jnp.where(odd, jnp.concatenate([beside, mine], 2), jnp.concatenate([mine, beside], 2))
+    halo = SWEEPS + CHEB - 1
+    pair_rows = 2 * slab_rows
+    edge = halo
+    before = shifted(chip[:, :, pair_rows - edge:, :], "space", -2)
+    after = shifted(chip[:, :, :edge, :], "space", 2)
+    rows_all = jnp.concatenate([before, chip, after], 2)
+    window_rows = slab_rows + 2 * halo
+    raw = lax.dynamic_slice_in_dim(rows_all, odd.astype(jnp.int32) * slab_rows, window_rows, 2)
 
     width = slab_rows + 2 * CHEB
     x_coords = (slab * slab_rows - CHEB + jnp.arange(width, dtype=jnp.int32)) % total_x

time: 44.1 us -> 40.7 us (0.923)
  waiting for transfers between devices: 20.3 us -> 18.3 us
  starting transfers between devices: 8.84 us -> 7.82 us
    ppermute x5 -> x3, waiting for transfers between devices: 9.35 us -> 5.89 us  [shifted(): lax.ppermute(array, axis, [(i, (i - shift) % size) for i in range(size)])]
    ppermute x0 -> x2, waiting for transfers between devices: none -> 1.43 us  [pair_block(): return lax.ppermute(array, ('probe', 'space'), pairs)]
    ppermute x5 -> x3, starting transfers between devices: 8.83 us -> 7.62 us  [shifted(): lax.ppermute(array, axis, [(i, (i - shift) % size) for i in range(size)])]
    pallas_call x1, Pallas kernels: 5.07 us -> 4.63 us  [run_local(): pl.pallas_call(body, out_shape=(jax.ShapeDtypeStruct((3, depth, slab_rows...]
  transfers between devices with their start and end apart: 9 -> 9, of which waited for: 7 -> 7; matrix products, arithmetic and copies ran while one was open for 12% -> 13% of each run, Pallas kernels for 0% -> 0%
where the time goes in v8:
time: 40.7 us; the launch traced here: 40.4 us
  waiting for transfers between devices  18.3 us (45%)
  starting transfers between devices  7.82 us (19%)
  other arithmetic  7.24 us (18%)
  Pallas kernels  4.63 us (11%)
  local copies, waits for them, and re-layouts  1.66 us (4%)
  between operations  0.75 us (2%)
    ppermute x4, waiting for transfers between devices, butterfly_sum(): lax.ppermute(value, axis, [(i, i ^ step) for i in range(size)])  11 us
    ppermute x3, starting transfers between devices, shifted(): lax.ppermute(array, axis, [(i, (i - shift) % size) for i in range(size)])  7.62 us
    ppermute x3, waiting for transfers between devices, shifted(): lax.ppermute(array, axis, [(i, (i - shift) % size) for i in range(size)])  5.89 us
    pallas_call x1, Pallas kernels, run_local(): pl.pallas_call(body, out_shape=(jax.ShapeDtypeStruct((3, depth, slab_rows...  4.63 us
    ppermute x2, waiting for transfers between devices, pair_block(): return lax.ppermute(array, ('probe', 'space'), pairs)  1.43 us
    mul x2, other arithmetic, make_probes(): return waves[:, :, None] * polar[:, None, :, None, None, None]  1.28 us
    convert_element_type x1, other arithmetic, shards(): last = jnp.transpose(last, (4, 1, 2, 3, 0, 5)).astype(jnp.bfloat16)  1.02 us
    mul x1, other arithmetic, make_probes(): waves = jnp.stack([jnp.cos(angle) * ramp, jnp.sin(angle) * ramp], 1)  0.85 us
  transfers between devices with their start and end apart: 9, of which 7 were waited for; matrix products, arithmetic and copies ran while one was open for 13% of the time, Pallas kernels for 0%

profile of v8, /device:TPU:0, one launch (start us, length us, event | category | flops | bytes accessed | tf_op | source)
XLA Modules:
  0.0 40.4 jit_solution(6111230751099869079)
XLA Ops:
  0.7 0.8 %convert_element_type.49 = f32[3,4,4,64]{3,2,1,0:T(4,128)S(1)} convert(s32[3,4,4,64]{3,2,1,0:T(4,128)} %param.7) | non-fusion elementwise | flops 3072 | bytes 24576 | tf_op jit(solution)/shard_map/convert_element_type | solution.py:243
  1.4 0.7 %pad_maximum_fusion = f32[5,4,4,64]{3,2,1,0:T(4,128)S(1)} fusion(f32[3,4,4,64]{3,2,1,0:T(4,128)S(1)} %convert_element_type.49, f32[1,4,4,64]{3,2,1,0:T(4,128)} %bitcast.15, f32[1,4,4,64]{3,2,1,0:T(4,128)} %bitcast.17), kind=kLoop, calls=%fused_computation.15 | loop fusion | flops 10240 | bytes 40960 | tf_op jit(solution)/shard_map/concatenate | solution.py:243
  2.1 3.0 %collective-permute-start.2 = (f32[5,4,4,64]{3,2,1,0:T(4,128)S(1)}, f32[5,4,4,64]{3,2,1,0:T(4,128)S(1)}, u32[]{:S(2)}, u32[]{:S(2)}) collective-permute-start(f32[5,4,4,64]{3,2,1,0:T(4,128)S(1)} %pad_maximum_fusion), channel_id=1, source_target_pairs={{0,16},{16,0},{1,17},{17,1},{2,18},{18,2},{3,19},{19,3},{4,20},{20... | collective-permute-start | bytes 61448 | tf_op jit(solution)/shard_map/ppermute | solution.py:24
  5.1 0.2 collective-permute-start
  5.4 0.8 %slice_bitcast_fusion.2 = (s32[8]{0:T(128)S(1)}, s32[8]{0:T(128)S(1)}, s32[8]{0:T(128)S(1)}) fusion(s32[8,3]{0,1:T(4,128)} %param.9), kind=kLoop, calls=%fused_computation.54 | loop fusion | bytes 192 | tf_op jit(solution)/shard_map/slice | solution.py:69
  6.3 0.1 fusion.4
  6.4 0.8 %cosine_multiply_fusion = (f32[8,1,4,12,128]{4,0,2,1,3:T(8,128)S(1)}, f32[8,1,4,12,128]{4,0,2,1,3:T(8,128)S(1)}) fusion(f32[12]{0:T(128)S(1)} %add_sqrt_fusion, f32[8,128]{1,0:T(8,128)S(1)} %fusion.7, f32[8,4,12]{0,1,2:T(4,128)S(1)} %broadcast_add_fusion), kind=kLoop, calls=%fused_computation.10 | loop fusion | flops 196608 | bytes 398896 | tf_op jit(solution)/shard_map/mul | solution.py:80
  7.3 1.4 %collective-permute-done.1 = f32[5,4,4,64]{3,2,1,0:T(4,128)S(1)} collective-permute-done((f32[5,4,4,64]{3,2,1,0:T(4,128)S(1)}, f32[5,4,4,64]{3,2,1,0:T(4,128)S(1)}, u32[]{:S(2)}, u32[]{:S(2)}) %collective-permute-start.1) | collective-permute-done | bytes 20512 | tf_op jit(solution)/shard_map/ppermute | solution.py:250
  8.8 0.2 maximum_select_fusion
  8.9 4.6 %collective-permute-start.4 = (f32[5,4,5,128]{3,2,1,0:T(8,128)S(1)}, f32[5,4,5,128]{3,2,1,0:T(8,128)S(1)}, u32[]{:S(2)}, u32[]{:S(2)}) collective-permute-start(f32[5,4,5,128]{3,2,1,0:T(8,128)S(1)} %get-tuple-element.12), channel_id=1, source_target_pairs={{0,14},{1,15},{2,0},{3,1},{4,2},{5,3},{6,4},{7,5},{8,6},{9,7},{10,... | collective-permute-start | bytes 153608 | tf_op jit(solution)/shard_map/ppermute | solution.py:24
  13.5 1.3 %broadcast_multiply_fusion.refs_1_ = f32[12,2,3,4,8,128]{5,4,3,2,1,0:T(8,128)} fusion(f32[3,8]{1,0:T(4,128)S(1)} %fusion.12, f32[12,2,4,8,128]{4,3,2,1,0:T(8,128)S(1)} %maximum_bitcast_fusion), kind=kLoop, calls=%fused_computation | loop fusion | flops 294912 | bytes 1572960 | tf_op jit(solution)/shard_map/mul | solution.py:84
  14.8 0.8 %collective-permute-done.4 = f32[5,4,5,128]{3,2,1,0:T(8,128)S(1)} collective-permute-done((f32[5,4,5,128]{3,2,1,0:T(8,128)S(1)}, f32[5,4,5,128]{3,2,1,0:T(8,128)S(1)}, u32[]{:S(2)}, u32[]{:S(2)}) %collective-permute-start.4) | collective-permute-done | bytes 51232 | tf_op jit(solution)/shard_map/ppermute | solution.py:24
  15.6 5.1 %collective-permute-done.3 = f32[5,4,5,128]{3,2,1,0:T(8,128)S(1)} collective-permute-done((f32[5,4,5,128]{3,2,1,0:T(8,128)S(1)}, f32[5,4,5,128]{3,2,1,0:T(8,128)S(1)}, u32[]{:S(2)}, u32[]{:S(2)}) %collective-permute-start.3) | collective-permute-done | bytes 51232 | tf_op jit(solution)/shard_map/ppermute | solution.py:24
  20.7 0.7 %fusion.2.refs_0_ = f32[5,4,14,128]{3,2,1,0:T(8,128)} fusion(s32[]{:T(128)S(6)} %mul.131, f32[5,4,5,128]{3,2,1,0:T(8,128)S(1)} %collective-permute-done.3, f32[5,4,8,128]{3,2,1,0:T(8,128)S(1)} %maximum_select_fusion, f32[5,4,5,128]{3,2,1,0:T(8,128)S(1)} %collective-permute-done.4), kind=kLoop, calls=%fused_computation.13 | loop fusion | flops 71680 | bytes 327684 | tf_op jit(solution)/shard_map/concatenate | solution.py:261
  21.4 4.6 %shard_map.76 = (f32[3,4,4,128]{3,2,1,0:T(4,128)}, f32[4,2,3,4,8,128]{5,4,3,2,1,0:T(8,128)}, f32[4,8]{1,0:T(4,128)}) custom-call(f32[5,4,14,128]{3,2,1,0:T(8,128)} %fusion.2.refs_0_, f32[12,2,3,4,8,128]{5,4,3,2,1,0:T(8,128)} %broadcast_multiply_fusion.refs_1_, f32[8]{0:T(128)} %refs_2_.1), custom_call_target="tpu_custom_call" | custom-call | flops 13148160 | bytes 1744896 | tf_op jit(solution)/shard_map/pallas_call | solution.py:204
  26.1 1.4 %collective-permute-done.5 = f32[4,8]{1,0:T(4,128)S(1)} collective-permute-done((f32[4,8]{1,0:T(4,128)}, f32[4,8]{1,0:T(4,128)S(1)}, u32[]{:S(2)}, u32[]{:S(2)}) %collective-permute-start.5) | collective-permute-done | bytes 160 | tf_op jit(solution)/shard_map/ppermute | solution.py:93
  27.4 0.7 %add.197 = f32[4,8]{1,0:T(4,128)S(1)} add(f32[4,8]{1,0:T(4,128)} %get-tuple-element.8, f32[4,8]{1,0:T(4,128)S(1)} %collective-permute-done.5) | non-fusion elementwise | flops 32 | bytes 384 | tf_op jit(solution)/shard_map/add | solution.py:93
  28.1 3.6 %collective-permute-done.6 = f32[4,8]{1,0:T(4,128)S(1)} collective-permute-done((f32[4,8]{1,0:T(4,128)S(1)}, f32[4,8]{1,0:T(4,128)S(1)}, u32[]{:S(2)}, u32[]{:S(2)}) %collective-permute-start.6) | collective-permute-done | bytes 160 | tf_op jit(solution)/shard_map/ppermute | solution.py:93
  31.7 1.0 %convert_bitcast_fusion = bf16[8,2,3,4,4,128]{5,0,3,2,1,4:T(8,128)(2,1)S(1)} fusion(f32[4,2,3,4,8,128]{5,4,3,2,1,0:T(8,128)} %get-tuple-element.7), kind=kLoop, calls=%fused_computation.8 | loop fusion | flops 98304 | bytes 589824 | tf_op jit(solution)/shard_map/convert_element_type | solution.py:275
  32.7 2.6 %collective-permute-done.7 = f32[4,8]{1,0:T(4,128)S(1)} collective-permute-done((f32[4,8]{1,0:T(4,128)S(1)}, f32[4,8]{1,0:T(4,128)S(1)}, u32[]{:S(2)}, u32[]{:S(2)}) %collective-permute-start.7) | collective-permute-done | bytes 160 | tf_op jit(solution)/shard_map/ppermute | solution.py:93
  35.3 0.2 fusion
  35.5 0.8 %copy.8 = bf16[8,2,3,4,4,128]{5,4,3,2,1,0:T(4,128)(2,1)} copy(bf16[8,2,3,4,4,128]{5,0,3,2,1,4:T(8,128)(2,1)S(1)} %fusion) | data formatting | bytes 393216
  36.3 3.4 %collective-permute-done.8 = f32[4,8]{1,0:T(4,128)S(1)} collective-permute-done((f32[4,8]{1,0:T(4,128)S(1)}, f32[4,8]{1,0:T(4,128)S(1)}, u32[]{:S(2)}, u32[]{:S(2)}) %collective-permute-start.8) | collective-permute-done | bytes 160 | tf_op jit(solution)/shard_map/ppermute | solution.py:93
  39.8 0.6 %multiply_bitcast_fusion = f32[8,4]{0,1:T(4,128)} fusion(f32[4,8]{1,0:T(4,128)S(1)} %add.199, f32[4,8]{1,0:T(4,128)S(1)} %collective-permute-done.8), kind=kLoop, calls=%fused_computation.43 | loop fusion | flops 64 | bytes 384 | tf_op jit(solution)/shard_map/transpose | solution.py:279
  (24 shorter events, 0.2 us)
Async XLA Ops:
  0.6 8.1 %copy-start = (f32[4,4,64]{2,1,0:T(4,128)S(1)}, f32[4,4,64]{2,1,0:T(4,128)}, u32[]{:S(2)}) copy-start(f32[4,4,64]{2,1,0:T(4,128)} %param.6) | copy-start | bytes 12292
  0.6 8.1 %copy-start.1 = (f32[4,4,64]{2,1,0:T(4,128)S(1)}, f32[4,4,64]{2,1,0:T(4,128)}, u32[]{:S(2)}) copy-start(f32[4,4,64]{2,1,0:T(4,128)} %param.5) | copy-start | bytes 12292
  2.1 5.2 %collective-permute-start.2 = (f32[5,4,4,64]{3,2,1,0:T(4,128)S(1)}, f32[5,4,4,64]{3,2,1,0:T(4,128)S(1)}, u32[]{:S(2)}, u32[]{:S(2)}) collective-permute-start(f32[5,4,4,64]{3,2,1,0:T(4,128)S(1)} %pad_maximum_fusion), channel_id=1, source_target_pairs={{0,16},{16,0},{1,17},{17,1},{2,18},{18,2},{3,19},{19,3},{4,20},{20... | collective-permute-start | bytes 61448 | tf_op jit(solution)/shard_map/ppermute | solution.py:24
  5.1 3.6 %collective-permute-start.1 = (f32[5,4,4,64]{3,2,1,0:T(4,128)S(1)}, f32[5,4,4,64]{3,2,1,0:T(4,128)S(1)}, u32[]{:S(2)}, u32[]{:S(2)}) collective-permute-start(f32[5,4,4,64]{3,2,1,0:T(4,128)S(1)} %pad_maximum_fusion), channel_id=1, source_target_pairs={{17,0},{16,1},{19,2},{18,3},{21,4},{20,5},{23,6},{22,7},{25,8},{24... | collective-permute-start | bytes 61448 | tf_op jit(solution)/shard_map/ppermute | solution.py:250
  5.1 3.6 %collective-permute-start = (f32[5,4,4,64]{3,2,1,0:T(4,128)S(1)}, f32[5,4,4,64]{3,2,1,0:T(4,128)S(1)}, u32[]{:S(2)}, u32[]{:S(2)}) collective-permute-start(f32[5,4,4,64]{3,2,1,0:T(4,128)S(1)} %pad_maximum_fusion), channel_id=1, source_target_pairs={{1,0},{0,1},{3,2},{2,3},{5,4},{4,5},{7,6},{6,7},{9,8},{8,9},{11,10... | collective-permute-start | bytes 61448 | tf_op jit(solution)/shard_map/ppermute | solution.py:250
  8.9 6.7 %collective-permute-start.4 = (f32[5,4,5,128]{3,2,1,0:T(8,128)S(1)}, f32[5,4,5,128]{3,2,1,0:T(8,128)S(1)}, u32[]{:S(2)}, u32[]{:S(2)}) collective-permute-start(f32[5,4,5,128]{3,2,1,0:T(8,128)S(1)} %get-tuple-element.12), channel_id=1, source_target_pairs={{0,14},{1,15},{2,0},{3,1},{4,2},{5,3},{6,4},{7,5},{8,6},{9,7},{10,... | collective-permute-start | bytes 153608 | tf_op jit(solution)/shard_map/ppermute | solution.py:24
  13.5 7.1 %collective-permute-start.3 = (f32[5,4,5,128]{3,2,1,0:T(8,128)S(1)}, f32[5,4,5,128]{3,2,1,0:T(8,128)S(1)}, u32[]{:S(2)}, u32[]{:S(2)}) collective-permute-start(f32[5,4,5,128]{3,2,1,0:T(8,128)S(1)} %get-tuple-element.13), channel_id=1, source_target_pairs={{0,2},{1,3},{2,4},{3,5},{4,6},{5,7},{6,8},{7,9},{8,10},{9,11},{10,... | collective-permute-start | bytes 153608 | tf_op jit(solution)/shard_map/ppermute | solution.py:24
  26.1 1.4 %collective-permute-start.5 = (f32[4,8]{1,0:T(4,128)}, f32[4,8]{1,0:T(4,128)S(1)}, u32[]{:S(2)}, u32[]{:S(2)}) collective-permute-start(f32[4,8]{1,0:T(4,128)} %get-tuple-element.8), channel_id=1, source_target_pairs={{0,1},{1,0},{2,3},{3,2},{4,5},{5,4},{6,7},{7,6},{8,9},{9,8},{10,11... | collective-permute-start | bytes 392 | tf_op jit(solution)/shard_map/ppermute | solution.py:93
  28.1 3.6 %collective-permute-start.6 = (f32[4,8]{1,0:T(4,128)S(1)}, f32[4,8]{1,0:T(4,128)S(1)}, u32[]{:S(2)}, u32[]{:S(2)}) collective-permute-start(f32[4,8]{1,0:T(4,128)S(1)} %add.197), channel_id=1, source_target_pairs={{0,2},{1,3},{2,0},{3,1},{4,6},{5,7},{6,4},{7,5},{8,10},{9,11},{10,... | collective-permute-start | bytes 392 | tf_op jit(solution)/shard_map/ppermute | solution.py:93
  31.7 3.6 %collective-permute-start.7 = (f32[4,8]{1,0:T(4,128)S(1)}, f32[4,8]{1,0:T(4,128)S(1)}, u32[]{:S(2)}, u32[]{:S(2)}) collective-permute-start(f32[4,8]{1,0:T(4,128)S(1)} %add.198), channel_id=1, source_target_pairs={{0,4},{1,5},{2,6},{3,7},{4,0},{5,1},{6,2},{7,3},{8,12},{9,13},{10,... | collective-permute-start | bytes 392 | tf_op jit(solution)/shard_map/ppermute | solution.py:93
  35.3 4.5 %collective-permute-start.8 = (f32[4,8]{1,0:T(4,128)S(1)}, f32[4,8]{1,0:T(4,128)S(1)}, u32[]{:S(2)}, u32[]{:S(2)}) collective-permute-start(f32[4,8]{1,0:T(4,128)S(1)} %add.199), channel_id=1, source_target_pairs={{0,8},{1,9},{2,10},{3,11},{4,12},{5,13},{6,14},{7,15},{8,0},{9,1},... | collective-permute-start | bytes 392 | tf_op jit(solution)/shard_map/ppermute | solution.py:93

commit v9 on v5

--- a/solution.py
+++ b/solution.py
@@ -251,7 +251,32 @@
     rotated = jnp.concatenate(pieces, -1)
     full_y = jnp.roll(rotated, group * block_y, -1) if groups > 1 else rotated
 
-    slab_blocks = [shifted(full_y, "space", k) for k in range(-HALO_SLABS, HALO_SLABS + 1)]
+    def wraps(i, k):
+        return not 0 <= i + k < slabs
+
+    def far_block(k):
+        blocks = []
+        for j in range(groups):
+            pairs = [
+                (((g + j) % groups) * slabs + (i + k) % slabs, g * slabs + i)
+                for g in range(groups)
+                for i in range(slabs)
+                if wraps(i, k)
+            ]
+            blocks.append(lax.ppermute(local, ("probe", "space"), pairs))
+        joined = jnp.concatenate(blocks, -1)
+        return jnp.roll(joined, group * block_y, -1) if groups > 1 else joined
+
+    shifts = [k for k in range(-HALO_SLABS, HALO_SLABS + 1) if k != 0]
+    far = {k: far_block(k) for k in shifts}
+    slab_blocks = []
+    for k in range(-HALO_SLABS, HALO_SLABS + 1):
+        if k == 0:
+            slab_blocks.append(full_y)
+            continue
+        near = lax.ppermute(full_y, "space", [(i + k, i) for i in range(slabs) if not wraps(i, k)])
+        wrapped = (slab + k < 0) | (slab + k >= slabs)
+        slab_blocks.append(jnp.where(wrapped, far[k], near))
     halo = HALO_SLABS * slab_rows
 
     width = slab_rows + 2 * CHEB

time: 40.1 us -> 60.8 us (1.52)
  starting transfers between devices: 8.66 us -> 33.3 us
  waiting for transfers between devices: 15.2 us -> 8.45 us
  other arithmetic: 6.34 us -> 9.48 us
  local copies, waits for them, and re-layouts: 3.69 us -> 3.07 us
    ppermute x0 -> x12, starting transfers between devices: none -> 24.5 us  [the longest x8 17.3 us: far_block(): blocks.append(lax.ppermute(local, ('probe', 'space'), pairs))]
    ppermute x4, starting transfers between devices: 0.01 us -> 7.6 us  [butterfly_sum(): lax.ppermute(value, axis, [(i, i ^ step) for i in range(size)])]
    ppermute x5 -> x1, starting transfers between devices: 8.65 us -> 1.19 us  [shifted(): lax.ppermute(array, axis, [(i, (i - shift) % size) for i in range(size)])]
    ppermute x4, waiting for transfers between devices: 9.72 us -> 4.92 us  [butterfly_sum(): lax.ppermute(value, axis, [(i, i ^ step) for i in range(size)])]
    ppermute x5 -> x1, waiting for transfers between devices: 5.44 us -> 0.92 us  [shifted(): lax.ppermute(array, axis, [(i, (i - shift) % size) for i in range(size)])]
    select_n x0 -> x4, other arithmetic: none -> 3.17 us  [shards(): slab_blocks.append(jnp.where(wrapped, far[k], near))]
    ppermute x0 -> x12, waiting for transfers between devices: none -> 2.61 us  [the longest x8 1.86 us: far_block(): blocks.append(lax.ppermute(local, ('probe', 'space'), pairs))]
    unnamed x15 -> x7, local copies, waits for them, and re-layouts: 1.47 us -> 0.85 us
  transfers between devices with their start and end apart: 9 -> 17, of which waited for: 7 -> 7; matrix products, arithmetic and copies ran while one was open for 16% -> 15% of each run, Pallas kernels for 0% -> 0%
where the time goes in v9:
time: 60.8 us; the launch traced here: 60.2 us
  starting transfers between devices  33.3 us (55%)
  other arithmetic  9.48 us (16%)
  waiting for transfers between devices  8.45 us (14%)
  Pallas kernels  5.03 us (8%)
  local copies, waits for them, and re-layouts  3.07 us (5%)
  between operations  0.87 us (1%)
    ppermute x8, starting transfers between devices, far_block(): blocks.append(lax.ppermute(local, ('probe', 'space'), pairs))  17.3 us
    ppermute x4, starting transfers between devices, butterfly_sum(): lax.ppermute(value, axis, [(i, i ^ step) for i in range(size)])  7.6 us
    ppermute x4, starting transfers between devices, shards(): lax.ppermute(full_y, 'space', [(i + k, i) for i in range(slabs) if not wr...  7.23 us
    pallas_call x1, Pallas kernels, run_local(): pl.pallas_call(body, out_shape=(jax.ShapeDtypeStruct((3, depth, slab_rows...  5.03 us
    ppermute x4, waiting for transfers between devices, butterfly_sum(): lax.ppermute(value, axis, [(i, i ^ step) for i in range(size)])  4.92 us
    select_n x4, other arithmetic, shards(): slab_blocks.append(jnp.where(wrapped, far[k], near))  3.17 us
    ppermute x8, waiting for transfers between devices, far_block(): blocks.append(lax.ppermute(local, ('probe', 'space'), pairs))  1.86 us
    dynamic_slice x1, local copies, waits for them, and re-layouts, shards(): lax.dynamic_slice_in_dim(relaxed, group * block_y, block_y, -1)  1.43 us
  transfers between devices with their start and end apart: 17, of which 7 were waited for; matrix products, arithmetic and copies ran while one was open for 15% of the time, Pallas kernels for 0%

profile of v9, /device:TPU:0, one launch (start us, length us, event | category | flops | bytes accessed | tf_op | source)
XLA Modules:
  0.0 60.2 jit_solution(14783427194809666779)
XLA Ops:
  2.1 7.9 %collective-permute-start.10 = (f32[5,4,4,64]{3,2,1,0:T(4,128)S(1)}, f32[5,4,4,64]{3,2,1,0:T(4,128)S(1)}, u32[]{:S(2)}, u32[]{:S(2)}) collective-permute-start(f32[5,4,4,64]{3,2,1,0:T(4,128)S(1)} %pad_maximum_fusion), channel_id=1, source_target_pairs={{0,14},{1,15},{16,30},{17,31}} | collective-permute-start | bytes 61448 | tf_op jit(solution)/shard_map/ppermute | solution.py:266
  10.1 1.7 %collective-permute-start.8 = (f32[5,4,4,64]{3,2,1,0:T(4,128)S(1)}, f32[5,4,4,64]{3,2,1,0:T(4,128)S(1)}, u32[]{:S(2)}, u32[]{:S(2)}) collective-permute-start(f32[5,4,4,64]{3,2,1,0:T(4,128)S(1)} %pad_maximum_fusion), channel_id=1, source_target_pairs={{16,15},{0,31}} | collective-permute-start | bytes 61448 | tf_op jit(solution)/shard_map/ppermute | solution.py:266
  11.7 1.3 %collective-permute-start.7 = (f32[5,4,4,64]{3,2,1,0:T(4,128)S(1)}, f32[5,4,4,64]{3,2,1,0:T(4,128)S(1)}, u32[]{:S(2)}, u32[]{:S(2)}) collective-permute-start(f32[5,4,4,64]{3,2,1,0:T(4,128)S(1)} %pad_maximum_fusion), channel_id=1, source_target_pairs={{0,15},{16,31}} | collective-permute-start | bytes 61448 | tf_op jit(solution)/shard_map/ppermute | solution.py:266
  13.0 1.3 %collective-permute-start.11 = (f32[5,4,4,64]{3,2,1,0:T(4,128)S(1)}, f32[5,4,4,64]{3,2,1,0:T(4,128)S(1)}, u32[]{:S(2)}, u32[]{:S(2)}) collective-permute-start(f32[5,4,4,64]{3,2,1,0:T(4,128)S(1)} %pad_maximum_fusion), channel_id=1, source_target_pairs={{16,14},{17,15},{0,30},{1,31}} | collective-permute-start | bytes 61448 | tf_op jit(solution)/shard_map/ppermute | solution.py:266
  14.3 1.2 %collective-permute-start.2 = (f32[5,4,4,64]{3,2,1,0:T(4,128)S(1)}, f32[5,4,4,64]{3,2,1,0:T(4,128)S(1)}, u32[]{:S(2)}, u32[]{:S(2)}) collective-permute-start(f32[5,4,4,64]{3,2,1,0:T(4,128)S(1)} %pad_maximum_fusion), channel_id=1, source_target_pairs={{0,16},{16,0},{1,17},{17,1},{2,18},{18,2},{3,19},{19,3},{4,20},{20... | collective-permute-start | bytes 61448 | tf_op jit(solution)/shard_map/ppermute | solution.py:25
  18.6 1.3 %collective-permute-start.12 = (f32[5,4,4,128]{3,2,1,0:T(4,128)S(1)}, f32[5,4,4,128]{3,2,1,0:T(4,128)S(1)}, u32[]{:S(2)}, u32[]{:S(2)}) collective-permute-start(f32[5,4,4,128]{3,2,1,0:T(4,128)S(1)} %fusion.15.refs_2_), channel_id=1, source_target_pairs={{2,0},{3,1},{4,2},{5,3},{6,4},{7,5},{8,6},{9,7},{10,8},{11,9},{12,... | collective-permute-start | bytes 122888 | tf_op jit(solution)/shard_map/ppermute | solution.py:277
  19.9 1.2 %broadcast_multiply_fusion.refs_5_ = f32[12,2,3,4,8,128]{5,4,3,2,1,0:T(8,128)} fusion(f32[3,8]{1,0:T(4,128)S(1)} %fusion.35, f32[12,2,4,8,128]{4,3,2,1,0:T(8,128)S(1)} %maximum_bitcast_fusion), kind=kLoop, calls=%fused_computation | loop fusion | flops 294912 | bytes 1572960 | tf_op jit(solution)/shard_map/mul | solution.py:85
  21.1 1.3 %collective-permute-start.5 = (f32[5,4,4,64]{3,2,1,0:T(4,128)S(1)}, f32[5,4,4,64]{3,2,1,0:T(4,128)S(1)}, u32[]{:S(2)}, u32[]{:S(2)}) collective-permute-start(f32[5,4,4,64]{3,2,1,0:T(4,128)S(1)} %pad_maximum_fusion), channel_id=1, source_target_pairs={{31,0},{15,16}} | collective-permute-start | bytes 61448 | tf_op jit(solution)/shard_map/ppermute | solution.py:266
  22.4 1.3 %collective-permute-start.4 = (f32[5,4,4,64]{3,2,1,0:T(4,128)S(1)}, f32[5,4,4,64]{3,2,1,0:T(4,128)S(1)}, u32[]{:S(2)}, u32[]{:S(2)}) collective-permute-start(f32[5,4,4,64]{3,2,1,0:T(4,128)S(1)} %pad_maximum_fusion), channel_id=1, source_target_pairs={{15,0},{31,16}} | collective-permute-start | bytes 61448 | tf_op jit(solution)/shard_map/ppermute | solution.py:266
  24.5 1.3 %collective-permute-start.9 = (f32[5,4,4,128]{3,2,1,0:T(4,128)S(1)}, f32[5,4,4,128]{3,2,1,0:T(4,128)S(1)}, u32[]{:S(2)}, u32[]{:S(2)}) collective-permute-start(f32[5,4,4,128]{3,2,1,0:T(4,128)S(1)} %fusion.15.refs_2_), channel_id=1, source_target_pairs={{1,0},{2,1},{3,2},{4,3},{5,4},{6,5},{7,6},{8,7},{9,8},{10,9},{11,1... | collective-permute-start | bytes 122888 | tf_op jit(solution)/shard_map/ppermute | solution.py:277
  26.6 1.3 %collective-permute-start.1 = (f32[5,4,4,64]{3,2,1,0:T(4,128)S(1)}, f32[5,4,4,64]{3,2,1,0:T(4,128)S(1)}, u32[]{:S(2)}, u32[]{:S(2)}) collective-permute-start(f32[5,4,4,64]{3,2,1,0:T(4,128)S(1)} %pad_maximum_fusion), channel_id=1, source_target_pairs={{30,0},{31,1},{14,16},{15,17}} | collective-permute-start | bytes 61448 | tf_op jit(solution)/shard_map/ppermute | solution.py:266
  27.9 1.3 %collective-permute-start = (f32[5,4,4,64]{3,2,1,0:T(4,128)S(1)}, f32[5,4,4,64]{3,2,1,0:T(4,128)S(1)}, u32[]{:S(2)}, u32[]{:S(2)}) collective-permute-start(f32[5,4,4,64]{3,2,1,0:T(4,128)S(1)} %pad_maximum_fusion), channel_id=1, source_target_pairs={{14,0},{15,1},{30,16},{31,17}} | collective-permute-start | bytes 61448 | tf_op jit(solution)/shard_map/ppermute | solution.py:266
  29.2 3.0 %collective-permute-start.6 = (f32[5,4,4,128]{3,2,1,0:T(4,128)S(1)}, f32[5,4,4,128]{3,2,1,0:T(4,128)S(1)}, u32[]{:S(2)}, u32[]{:S(2)}) collective-permute-start(f32[5,4,4,128]{3,2,1,0:T(4,128)S(1)} %fusion.15.refs_2_), channel_id=1, source_target_pairs={{0,1},{1,2},{2,3},{3,4},{4,5},{5,6},{6,7},{7,8},{8,9},{9,10},{10,1... | collective-permute-start | bytes 122888 | tf_op jit(solution)/shard_map/ppermute | solution.py:277
  33.0 1.6 %collective-permute-start.3 = (f32[5,4,4,128]{3,2,1,0:T(4,128)S(1)}, f32[5,4,4,128]{3,2,1,0:T(4,128)S(1)}, u32[]{:S(2)}, u32[]{:S(2)}) collective-permute-start(f32[5,4,4,128]{3,2,1,0:T(4,128)S(1)} %fusion.15.refs_2_), channel_id=1, source_target_pairs={{0,2},{1,3},{2,4},{3,5},{4,6},{5,7},{6,8},{7,9},{8,10},{9,11},{10,... | collective-permute-start | bytes 122888 | tf_op jit(solution)/shard_map/ppermute | solution.py:277
  36.3 1.0 %collective-permute-done = f32[5,4,4,64]{3,2,1,0:T(4,128)S(1)} collective-permute-done((f32[5,4,4,64]{3,2,1,0:T(4,128)S(1)}, f32[5,4,4,64]{3,2,1,0:T(4,128)S(1)}, u32[]{:S(2)}, u32[]{:S(2)}) %collective-permute-start) | collective-permute-done | bytes 20512 | tf_op jit(solution)/shard_map/ppermute | solution.py:266
  38.1 5.0 %shard_map.76 = (f32[3,4,4,128]{3,2,1,0:T(4,128)}, f32[4,2,3,4,8,128]{5,4,3,2,1,0:T(8,128)}, f32[4,8]{1,0:T(4,128)}) custom-call(f32[5,4,4,128]{3,2,1,0:T(4,128)} %fusion.21.refs_0_, f32[5,4,4,128]{3,2,1,0:T(4,128)} %fusion.10.refs_1_, f32[5,4,4,128]{3,2,1,0:T(4,128)} %copy-done, f32[5,4,4,128]{3,2,1,0:T(4,128)} %fusion.6.refs_3_, ...), custom_call_target="tpu_custom_call" | custom-call | flops 14991360 | bytes 1818624 | tf_op jit(solution)/shard_map/pallas_call | solution.py:209
  43.3 1.3 %collective-permute-done.13 = f32[4,8]{1,0:T(4,128)S(1)} collective-permute-done((f32[4,8]{1,0:T(4,128)}, f32[4,8]{1,0:T(4,128)S(1)}, u32[]{:S(2)}, u32[]{:S(2)}) %collective-permute-start.13) | collective-permute-done | bytes 160 | tf_op jit(solution)/shard_map/ppermute | solution.py:94
  45.2 1.3 %collective-permute-start.14 = (f32[4,8]{1,0:T(4,128)S(1)}, f32[4,8]{1,0:T(4,128)S(1)}, u32[]{:S(2)}, u32[]{:S(2)}) collective-permute-start(f32[4,8]{1,0:T(4,128)S(1)} %add.188), channel_id=1, source_target_pairs={{0,2},{1,3},{2,0},{3,1},{4,6},{5,7},{6,4},{7,5},{8,10},{9,11},{10,... | collective-permute-start | bytes 392 | tf_op jit(solution)/shard_map/ppermute | solution.py:94
  46.5 2.3 %collective-permute-done.14 = f32[4,8]{1,0:T(4,128)S(1)} collective-permute-done((f32[4,8]{1,0:T(4,128)S(1)}, f32[4,8]{1,0:T(4,128)S(1)}, u32[]{:S(2)}, u32[]{:S(2)}) %collective-permute-start.14) | collective-permute-done | bytes 160 | tf_op jit(solution)/shard_map/ppermute | solution.py:94
  48.8 1.2 %collective-permute-start.15 = (f32[4,8]{1,0:T(4,128)S(1)}, f32[4,8]{1,0:T(4,128)S(1)}, u32[]{:S(2)}, u32[]{:S(2)}) collective-permute-start(f32[4,8]{1,0:T(4,128)S(1)} %add.189), channel_id=1, source_target_pairs={{0,4},{1,5},{2,6},{3,7},{4,0},{5,1},{6,2},{7,3},{8,12},{9,13},{10,... | collective-permute-start | bytes 392 | tf_op jit(solution)/shard_map/ppermute | solution.py:94
  49.9 1.0 %convert_bitcast_fusion = bf16[8,2,3,4,4,128]{5,0,3,2,1,4:T(8,128)(2,1)S(1)} fusion(f32[4,2,3,4,8,128]{5,4,3,2,1,0:T(8,128)} %get-tuple-element.8), kind=kLoop, calls=%fused_computation.2 | loop fusion | flops 98304 | bytes 589824 | tf_op jit(solution)/shard_map/convert_element_type | solution.py:292
  51.0 1.4 %collective-permute-done.15 = f32[4,8]{1,0:T(4,128)S(1)} collective-permute-done((f32[4,8]{1,0:T(4,128)S(1)}, f32[4,8]{1,0:T(4,128)S(1)}, u32[]{:S(2)}, u32[]{:S(2)}) %collective-permute-start.15) | collective-permute-done | bytes 160 | tf_op jit(solution)/shard_map/ppermute | solution.py:94
  52.4 5.0 %collective-permute-start.16 = (f32[4,8]{1,0:T(4,128)S(1)}, f32[4,8]{1,0:T(4,128)S(1)}, u32[]{:S(2)}, u32[]{:S(2)}) collective-permute-start(f32[4,8]{1,0:T(4,128)S(1)} %add.190), channel_id=1, source_target_pairs={{0,8},{1,9},{2,10},{3,11},{4,12},{5,13},{6,14},{7,15},{8,0},{9,1},... | collective-permute-start | bytes 392 | tf_op jit(solution)/shard_map/ppermute | solution.py:94
  57.4 1.4 %constant_dynamic-slice_fusion = f32[3,4,4,64]{3,2,1,0:T(4,128)} fusion(f32[3,4,4,128]{3,2,1,0:T(4,128)} %get-tuple-element.7, s32[]{:T(128)S(6)} %select_n.106), kind=kLoop, calls=%fused_computation.63 | loop fusion | bytes 24580 | tf_op jit(solution)/shard_map/dynamic_slice | solution.py:291
  (43 shorter events, 11.5 us)
Async XLA Ops:
  0.6 17.8 %copy-start.2 = (f32[4,4,64]{2,1,0:T(4,128)S(1)}, f32[4,4,64]{2,1,0:T(4,128)}, u32[]{:S(2)}) copy-start(f32[4,4,64]{2,1,0:T(4,128)} %param.8) | copy-start | bytes 12292
  0.6 17.8 %copy-start.1 = (f32[4,4,64]{2,1,0:T(4,128)S(1)}, f32[4,4,64]{2,1,0:T(4,128)}, u32[]{:S(2)}) copy-start(f32[4,4,64]{2,1,0:T(4,128)} %param.7) | copy-start | bytes 12292
  2.1 19.0 %collective-permute-start.10 = (f32[5,4,4,64]{3,2,1,0:T(4,128)S(1)}, f32[5,4,4,64]{3,2,1,0:T(4,128)S(1)}, u32[]{:S(2)}, u32[]{:S(2)}) collective-permute-start(f32[5,4,4,64]{3,2,1,0:T(4,128)S(1)} %pad_maximum_fusion), channel_id=1, source_target_pairs={{0,14},{1,15},{16,30},{17,31}} | collective-permute-start | bytes 61448 | tf_op jit(solution)/shard_map/ppermute | solution.py:266
  10.1 16.5 %collective-permute-start.8 = (f32[5,4,4,64]{3,2,1,0:T(4,128)S(1)}, f32[5,4,4,64]{3,2,1,0:T(4,128)S(1)}, u32[]{:S(2)}, u32[]{:S(2)}) collective-permute-start(f32[5,4,4,64]{3,2,1,0:T(4,128)S(1)} %pad_maximum_fusion), channel_id=1, source_target_pairs={{16,15},{0,31}} | collective-permute-start | bytes 61448 | tf_op jit(solution)/shard_map/ppermute | solution.py:266
  11.7 16.1 %collective-permute-start.7 = (f32[5,4,4,64]{3,2,1,0:T(4,128)S(1)}, f32[5,4,4,64]{3,2,1,0:T(4,128)S(1)}, u32[]{:S(2)}, u32[]{:S(2)}) collective-permute-start(f32[5,4,4,64]{3,2,1,0:T(4,128)S(1)} %pad_maximum_fusion), channel_id=1, source_target_pairs={{0,15},{16,31}} | collective-permute-start | bytes 61448 | tf_op jit(solution)/shard_map/ppermute | solution.py:266
  13.0 9.4 %collective-permute-start.11 = (f32[5,4,4,64]{3,2,1,0:T(4,128)S(1)}, f32[5,4,4,64]{3,2,1,0:T(4,128)S(1)}, u32[]{:S(2)}, u32[]{:S(2)}) collective-permute-start(f32[5,4,4,64]{3,2,1,0:T(4,128)S(1)} %pad_maximum_fusion), channel_id=1, source_target_pairs={{16,14},{17,15},{0,30},{1,31}} | collective-permute-start | bytes 61448 | tf_op jit(solution)/shard_map/ppermute | solution.py:266
  14.3 4.1 %collective-permute-start.2 = (f32[5,4,4,64]{3,2,1,0:T(4,128)S(1)}, f32[5,4,4,64]{3,2,1,0:T(4,128)S(1)}, u32[]{:S(2)}, u32[]{:S(2)}) collective-permute-start(f32[5,4,4,64]{3,2,1,0:T(4,128)S(1)} %pad_maximum_fusion), channel_id=1, source_target_pairs={{0,16},{16,0},{1,17},{17,1},{2,18},{18,2},{3,19},{19,3},{4,20},{20... | collective-permute-start | bytes 61448 | tf_op jit(solution)/shard_map/ppermute | solution.py:25
  18.6 19.5 %copy-start = (f32[5,4,4,128]{3,2,1,0:T(4,128)}, f32[5,4,4,128]{3,2,1,0:T(4,128)S(1)}, u32[]{:S(2)}) copy-start(f32[5,4,4,128]{3,2,1,0:T(4,128)S(1)} %fusion.15.refs_2_) | copy-start | bytes 122884
  18.6 5.9 %collective-permute-start.12 = (f32[5,4,4,128]{3,2,1,0:T(4,128)S(1)}, f32[5,4,4,128]{3,2,1,0:T(4,128)S(1)}, u32[]{:S(2)}, u32[]{:S(2)}) collective-permute-start(f32[5,4,4,128]{3,2,1,0:T(4,128)S(1)} %fusion.15.refs_2_), channel_id=1, source_target_pairs={{2,0},{3,1},{4,2},{5,3},{6,4},{7,5},{8,6},{9,7},{10,8},{11,9},{12,... | collective-permute-start | bytes 122888 | tf_op jit(solution)/shard_map/ppermute | solution.py:277
  21.1 11.9 %collective-permute-start.5 = (f32[5,4,4,64]{3,2,1,0:T(4,128)S(1)}, f32[5,4,4,64]{3,2,1,0:T(4,128)S(1)}, u32[]{:S(2)}, u32[]{:S(2)}) collective-permute-start(f32[5,4,4,64]{3,2,1,0:T(4,128)S(1)} %pad_maximum_fusion), channel_id=1, source_target_pairs={{31,0},{15,16}} | collective-permute-start | bytes 61448 | tf_op jit(solution)/shard_map/ppermute | solution.py:266
  22.4 12.2 %collective-permute-start.4 = (f32[5,4,4,64]{3,2,1,0:T(4,128)S(1)}, f32[5,4,4,64]{3,2,1,0:T(4,128)S(1)}, u32[]{:S(2)}, u32[]{:S(2)}) collective-permute-start(f32[5,4,4,64]{3,2,1,0:T(4,128)S(1)} %pad_maximum_fusion), channel_id=1, source_target_pairs={{15,0},{31,16}} | collective-permute-start | bytes 61448 | tf_op jit(solution)/shard_map/ppermute | solution.py:266
  24.5 4.7 %collective-permute-start.9 = (f32[5,4,4,128]{3,2,1,0:T(4,128)S(1)}, f32[5,4,4,128]{3,2,1,0:T(4,128)S(1)}, u32[]{:S(2)}, u32[]{:S(2)}) collective-permute-start(f32[5,4,4,128]{3,2,1,0:T(4,128)S(1)} %fusion.15.refs_2_), channel_id=1, source_target_pairs={{1,0},{2,1},{3,2},{4,3},{5,4},{6,5},{7,6},{8,7},{9,8},{10,9},{11,1... | collective-permute-start | bytes 122888 | tf_op jit(solution)/shard_map/ppermute | solution.py:277
  26.6 9.8 %collective-permute-start.1 = (f32[5,4,4,64]{3,2,1,0:T(4,128)S(1)}, f32[5,4,4,64]{3,2,1,0:T(4,128)S(1)}, u32[]{:S(2)}, u32[]{:S(2)}) collective-permute-start(f32[5,4,4,64]{3,2,1,0:T(4,128)S(1)} %pad_maximum_fusion), channel_id=1, source_target_pairs={{30,0},{31,1},{14,16},{15,17}} | collective-permute-start | bytes 61448 | tf_op jit(solution)/shard_map/ppermute | solution.py:266
  27.9 9.4 %collective-permute-start = (f32[5,4,4,64]{3,2,1,0:T(4,128)S(1)}, f32[5,4,4,64]{3,2,1,0:T(4,128)S(1)}, u32[]{:S(2)}, u32[]{:S(2)}) collective-permute-start(f32[5,4,4,64]{3,2,1,0:T(4,128)S(1)} %pad_maximum_fusion), channel_id=1, source_target_pairs={{14,0},{15,1},{30,16},{31,17}} | collective-permute-start | bytes 61448 | tf_op jit(solution)/shard_map/ppermute | solution.py:266
  29.2 5.5 %collective-permute-start.6 = (f32[5,4,4,128]{3,2,1,0:T(4,128)S(1)}, f32[5,4,4,128]{3,2,1,0:T(4,128)S(1)}, u32[]{:S(2)}, u32[]{:S(2)}) collective-permute-start(f32[5,4,4,128]{3,2,1,0:T(4,128)S(1)} %fusion.15.refs_2_), channel_id=1, source_target_pairs={{0,1},{1,2},{2,3},{3,4},{4,5},{5,6},{6,7},{7,8},{8,9},{9,10},{10,1... | collective-permute-start | bytes 122888 | tf_op jit(solution)/shard_map/ppermute | solution.py:277
  33.0 4.3 %collective-permute-start.3 = (f32[5,4,4,128]{3,2,1,0:T(4,128)S(1)}, f32[5,4,4,128]{3,2,1,0:T(4,128)S(1)}, u32[]{:S(2)}, u32[]{:S(2)}) collective-permute-start(f32[5,4,4,128]{3,2,1,0:T(4,128)S(1)} %fusion.15.refs_2_), channel_id=1, source_target_pairs={{0,2},{1,3},{2,4},{3,5},{4,6},{5,7},{6,8},{7,9},{8,10},{9,11},{10,... | collective-permute-start | bytes 122888 | tf_op jit(solution)/shard_map/ppermute | solution.py:277
  43.1 1.4 %collective-permute-start.13 = (f32[4,8]{1,0:T(4,128)}, f32[4,8]{1,0:T(4,128)S(1)}, u32[]{:S(2)}, u32[]{:S(2)}) collective-permute-start(f32[4,8]{1,0:T(4,128)} %get-tuple-element.9), channel_id=1, source_target_pairs={{0,1},{1,0},{2,3},{3,2},{4,5},{5,4},{6,7},{7,6},{8,9},{9,8},{10,11... | collective-permute-start | bytes 392 | tf_op jit(solution)/shard_map/ppermute | solution.py:94
  45.2 3.6 %collective-permute-start.14 = (f32[4,8]{1,0:T(4,128)S(1)}, f32[4,8]{1,0:T(4,128)S(1)}, u32[]{:S(2)}, u32[]{:S(2)}) collective-permute-start(f32[4,8]{1,0:T(4,128)S(1)} %add.188), channel_id=1, source_target_pairs={{0,2},{1,3},{2,0},{3,1},{4,6},{5,7},{6,4},{7,5},{8,10},{9,11},{10,... | collective-permute-start | bytes 392 | tf_op jit(solution)/shard_map/ppermute | solution.py:94
  48.8 3.6 %collective-permute-start.15 = (f32[4,8]{1,0:T(4,128)S(1)}, f32[4,8]{1,0:T(4,128)S(1)}, u32[]{:S(2)}, u32[]{:S(2)}) collective-permute-start(f32[4,8]{1,0:T(4,128)S(1)} %add.189), channel_id=1, source_target_pairs={{0,4},{1,5},{2,6},{3,7},{4,0},{5,1},{6,2},{7,3},{8,12},{9,13},{10,... | collective-permute-start | bytes 392 | tf_op jit(solution)/shard_map/ppermute | solution.py:94
  52.4 7.3 %collective-permute-start.16 = (f32[4,8]{1,0:T(4,128)S(1)}, f32[4,8]{1,0:T(4,128)S(1)}, u32[]{:S(2)}, u32[]{:S(2)}) collective-permute-start(f32[4,8]{1,0:T(4,128)S(1)} %add.190), channel_id=1, source_target_pairs={{0,8},{1,9},{2,10},{3,11},{4,12},{5,13},{6,14},{7,15},{8,0},{9,1},... | collective-permute-start | bytes 392 | tf_op jit(solution)/shard_map/ppermute | solution.py:94

commit v10 on v5

--- a/solution.py
+++ b/solution.py
@@ -82,7 +82,7 @@
     polar = ((probe_ids % 3)[:, None] == jnp.arange(3, dtype=jnp.int32)[None, :]).astype(
         jnp.float32
     )
-    return waves[:, :, None] * polar[:, None, :, None, None, None]
+    return waves, polar
 
 
 def butterfly_sum(value, axis):
@@ -125,7 +125,7 @@
 
 def local_kernel(halo, slab_rows, *refs):
     slab_refs = refs[:2 * HALO_SLABS + 1]
-    start_ref, exchange_ref, relaxed_ref, last_ref, sums_ref, win, sweep_a, sweep_b, bonds_b, bonds_yr, bonds_zr, spins_b, t1, t2, t3 = refs[2 * HALO_SLABS + 1:]
+    start_ref, polar_ref, exchange_ref, relaxed_ref, last_ref, sums_ref, win, sweep_a, sweep_b, bonds_b, bonds_yr, bonds_zr, spins_b, t1, t2, t3 = refs[2 * HALO_SLABS + 1:]
     for k, slab_ref in enumerate(slab_refs):
         block = slab_ref[...]
         cos_polar, azimuth, bond_class = block[0], block[1], block[2:5]
@@ -156,7 +156,7 @@
     n_start = slab_rows + 2 * CHEB
     lanes = win.shape[3]
     depth = win.shape[1]
-    probes = start_ref.shape[4]
+    probes = start_ref.shape[3]
     for xr in range(n_start):
         w = first + xr
         site = jnp.broadcast_to(win[3:6, :, w:w + 1, :], (3, depth, probes, lanes))
@@ -166,6 +166,12 @@
     for xr in range(n_start - 2):
         w = first + 1 + xr
         spins_b[xr] = jnp.broadcast_to(sweep_b[:, :, w - SWEEPS:w - SWEEPS + 1, :], (3, depth, probes, lanes))
+
+    polar = [polar_ref[j] for j in range(3)]
+
+    def start_row(i):
+        wave = start_ref[i]
+        return jnp.stack([wave * polar[j] for j in range(3)], 1)
 
     t_refs = (start_ref, t1, t2, t3, last_ref)
     for order in range(CHEB):
@@ -183,9 +189,12 @@
             total = bonds_b[b, 0] * up + bonds_b[b - 1, 0] * down
             total = total + bonds_b[b, 1] * y_roll(centre, -1) + bonds_yr[b] * y_roll(centre, 1)
             total = total + bonds_b[b, 2] * z_roll(centre, -1) + bonds_zr[b] * z_roll(centre, 1)
-            advanced = cross_product(spins_b[b - 1], total) * -precess_scale
-            if order > 0:
-                advanced = 2.0 * advanced - t_refs[order - 1][i + 2]
+            if order == 0:
+                total = jnp.stack([total * polar[j] for j in range(3)], 1)
+                advanced = cross_product(spins_b[b - 1], total) * -precess_scale
+            else:
+                previous = start_row(i + 2) if order == 1 else t_refs[order - 1][i + 2]
+                advanced = cross_product(spins_b[b - 1], total) * (-2.0 * precess_scale) - previous
             target[i] = advanced
             if halo <= w < halo + slab_rows:
                 squares = advanced * advanced
@@ -196,16 +205,16 @@
         sums_ref[order:order + 1, :] = jnp.sum(acc.T, axis=0, keepdims=True)
 
 
-def run_local(slab_blocks, start, exchange, halo, slab_rows):
+def run_local(slab_blocks, start, polar, exchange, halo, slab_rows):
     depth, lanes = slab_blocks[0].shape[1], slab_blocks[0].shape[3]
     width = len(slab_blocks) * slab_rows
-    n_start, probes = start.shape[0], start.shape[4]
-    vec_shape = start.shape[1:]
+    n_start, probes = start.shape[0], start.shape[3]
+    vec_shape = (start.shape[1], 3) + start.shape[2:]
 
     def body(*refs):
         local_kernel(halo, slab_rows, *refs)
 
-    sites = n_start * start[0].size
+    sites = n_start * 3 * start[0].size
     return pl.pallas_call(
         body,
         out_shape=(
@@ -213,7 +222,7 @@
             jax.ShapeDtypeStruct((slab_rows,) + vec_shape, jnp.float32),
             jax.ShapeDtypeStruct((CHEB, probes), jnp.float32),
         ),
-        in_specs=[pl.BlockSpec(memory_space=pltpu.VMEM)] * (len(slab_blocks) + 1)
+        in_specs=[pl.BlockSpec(memory_space=pltpu.VMEM)] * (len(slab_blocks) + 2)
         + [pl.BlockSpec(memory_space=pltpu.SMEM)],
         out_specs=[pl.BlockSpec(memory_space=pltpu.VMEM)] * 3,
         scratch_shapes=[
@@ -229,9 +238,9 @@
         cost_estimate=pl.CostEstimate(
             flops=30 * sites + 200 * 3 * depth * width * lanes,
             transcendentals=0,
-            bytes_accessed=4 * (6 * depth * width * lanes + start.size + start.size // 3),
-        ),
-    )(*slab_blocks, start, exchange)
+            bytes_accessed=4 * (6 * depth * width * lanes + 2 * start.size),
+        ),
+    )(*slab_blocks, start, polar, exchange)
 
 
 def shards(cos_polar, azimuth, bond_class, exchange, probe_wave):
@@ -259,10 +268,11 @@
     y_coords = jnp.arange(total_y, dtype=jnp.int32)
     group_size = probe_wave.shape[0]
     probe_ids = group * group_size + jnp.arange(group_size, dtype=jnp.int32)
-    start = make_probes(probe_wave, probe_ids, x_coords, y_coords, total_x, total_y, LZ)
-    start = jnp.transpose(start, (4, 1, 2, 3, 0, 5))
-
-    relaxed, last, sums = run_local(slab_blocks, start, exchange, halo, slab_rows)
+    waves, polar = make_probes(probe_wave, probe_ids, x_coords, y_coords, total_x, total_y, LZ)
+    waves = jnp.transpose(waves, (3, 1, 2, 0, 4))
+    polar = jnp.broadcast_to(polar.T[:, :, None], (3, group_size, total_y))
+
+    relaxed, last, sums = run_local(slab_blocks, waves, polar, exchange, halo, slab_rows)
     relaxed_own = lax.dynamic_slice_in_dim(relaxed, group * block_y, block_y, -1)
     last = jnp.transpose(last, (4, 1, 2, 3, 0, 5)).astype(jnp.bfloat16)
     moment_rows = butterfly_sum(sums, "space") / site_count

time: 40.1 us -> 38.3 us (0.955)
  waiting for transfers between devices: 15.2 us -> 16.5 us
  other arithmetic: 6.34 us -> 5.12 us
  Pallas kernels: 5.04 us -> 4.07 us
  local copies, waits for them, and re-layouts: 3.69 us -> 2.89 us
    mul x2 -> x0, other arithmetic: 1.3 us -> none  [make_probes(): return waves[:, :, None] * polar[:, None, :, None, None, None]]
    pallas_call x1, Pallas kernels: 5.04 us -> 4.07 us  [run_local(): pl.pallas_call(body, out_shape=(jax.ShapeDtypeStruct((3, depth, slab_rows...]
    slice x1, local copies, waits for them, and re-layouts: 0.8 us -> 0.01 us  [make_probes(): wave_z = probe_wave[:, 2][:, None]]
    transpose x0 -> x1, other arithmetic: none -> 0.78 us  [shards(): waves = jnp.transpose(waves, (3, 1, 2, 0, 4))]
    dynamic_slice x1, local copies, waits for them, and re-layouts: 1.43 us -> 0.7 us  [shards(): lax.dynamic_slice_in_dim(relaxed, group * block_y, block_y, -1)]
    concatenate x1, other arithmetic: 0.73 us -> 0.01 us  [shards(): jnp.concatenate([cos_polar[None], azimuth[None], bond_class.astype(jnp.fl...]
    ppermute x4, waiting for transfers between devices: 9.72 us -> 10.4 us  [butterfly_sum(): lax.ppermute(value, axis, [(i, i ^ step) for i in range(size)])]
    broadcast_in_dim x0 -> x1, local copies, waits for them, and re-layouts: none -> 0.67 us  [shards(): polar = jnp.broadcast_to(polar.T[:, :, None], (3, group_size, total_y))]
  transfers between devices with their start and end apart: 9 -> 9, of which waited for: 7 -> 9; matrix products, arithmetic and copies ran while one was open for 16% -> 12% of each run, Pallas kernels for 0% -> 0%
where the time goes in v10:
time: 38.3 us; the launch traced here: 38 us
  waiting for transfers between devices  16.5 us (43%)
  starting transfers between devices  8.67 us (23%)
  other arithmetic  5.12 us (13%)
  Pallas kernels  4.07 us (11%)
  local copies, waits for them, and re-layouts  2.89 us (8%)
  between operations  0.75 us (2%)
    ppermute x4, waiting for transfers between devices, butterfly_sum(): lax.ppermute(value, axis, [(i, i ^ step) for i in range(size)])  10.4 us
    ppermute x5, starting transfers between devices, shifted(): lax.ppermute(array, axis, [(i, (i - shift) % size) for i in range(size)])  8.66 us
    ppermute x5, waiting for transfers between devices, shifted(): lax.ppermute(array, axis, [(i, (i - shift) % size) for i in range(size)])  6.09 us
    pallas_call x1, Pallas kernels, run_local(): pl.pallas_call(body, out_shape=(jax.ShapeDtypeStruct((3, depth, slab_rows...  4.07 us
    unnamed x19, local copies, waits for them, and re-layouts  1.52 us
    convert_element_type x1, other arithmetic, shards(): last = jnp.transpose(last, (4, 1, 2, 3, 0, 5)).astype(jnp.bfloat16)  1.04 us
    mul x1, other arithmetic, make_probes(): waves = jnp.stack([jnp.cos(angle) * ramp, jnp.sin(angle) * ramp], 1)  0.85 us
    transpose x1, other arithmetic, shards(): waves = jnp.transpose(waves, (3, 1, 2, 0, 4))  0.78 us
  transfers between devices with their start and end apart: 9, of which 9 were waited for; matrix products, arithmetic and copies ran while one was open for 12% of the time, Pallas kernels for 0%

profile of v10, /device:TPU:0, one launch (start us, length us, event | category | flops | bytes accessed | tf_op | source)
XLA Modules:
  0.0 38.0 jit_solution(14949491625193380427)
XLA Ops:
  0.7 0.8 %convert_element_type.48 = f32[3,4,4,64]{3,2,1,0:T(4,128)S(1)} convert(s32[3,4,4,64]{3,2,1,0:T(4,128)} %param.7) | non-fusion elementwise | flops 3072 | bytes 24576 | tf_op jit(solution)/shard_map/convert_element_type | solution.py:257
  1.4 3.0 %collective-permute-start = (f32[5,4,4,64]{3,2,1,0:T(4,128)S(1)}, f32[5,4,4,64]{3,2,1,0:T(4,128)S(1)}, u32[]{:S(2)}, u32[]{:S(2)}) collective-permute-start(f32[5,4,4,64]{3,2,1,0:T(4,128)S(1)} %pad_maximum_fusion), channel_id=1, source_target_pairs={{0,16},{16,0},{1,17},{17,1},{2,18},{18,2},{3,19},{19,3},{4,20},{20... | collective-permute-start | bytes 61448 | tf_op jit(solution)/shard_map/ppermute | solution.py:25
  4.5 0.7 %copy-done.8 = s32[8,3]{0,1:T(4,128)S(1)} copy-done((s32[8,3]{0,1:T(4,128)S(1)}, s32[8,3]{0,1:T(4,128)}, u32[]{:S(2)}) %copy-start.8) | copy-done | bytes 120
  5.4 0.8 %cosine_multiply_fusion = (f32[8,1,4,12,128]{4,0,2,1,3:T(8,128)S(1)}, f32[8,1,4,12,128]{4,0,2,1,3:T(8,128)S(1)}) fusion(f32[12]{0:T(128)S(1)} %add_sqrt_fusion, f32[8,128]{1,0:T(8,128)S(1)} %fusion.12, f32[8,4,12]{0,1,2:T(4,128)S(1)} %broadcast_add_fusion), kind=kLoop, calls=%fused_computation.3 | loop fusion | flops 196608 | bytes 398896 | tf_op jit(solution)/shard_map/mul | solution.py:81
  6.2 0.2 collective-permute-done
  6.4 0.2 fusion.4.refs_2_
  6.6 5.1 %collective-permute-start.4 = (f32[5,4,4,128]{3,2,1,0:T(4,128)S(1)}, f32[5,4,4,128]{3,2,1,0:T(4,128)S(1)}, u32[]{:S(2)}, u32[]{:S(2)}) collective-permute-start(f32[5,4,4,128]{3,2,1,0:T(4,128)S(1)} %fusion.4.refs_2_), channel_id=1, source_target_pairs={{0,14},{1,15},{2,0},{3,1},{4,2},{5,3},{6,4},{7,5},{8,6},{9,7},{10,... | collective-permute-start | bytes 122888 | tf_op jit(solution)/shard_map/ppermute | solution.py:25
  11.8 0.5 %collective-permute-start.2 = (f32[5,4,4,128]{3,2,1,0:T(4,128)S(1)}, f32[5,4,4,128]{3,2,1,0:T(4,128)S(1)}, u32[]{:S(2)}, u32[]{:S(2)}) collective-permute-start(f32[5,4,4,128]{3,2,1,0:T(4,128)S(1)} %fusion.4.refs_2_), channel_id=1, source_target_pairs={{0,1},{1,2},{2,3},{3,4},{4,5},{5,6},{6,7},{7,8},{8,9},{9,10},{10,1... | collective-permute-start | bytes 122888 | tf_op jit(solution)/shard_map/ppermute | solution.py:25
  12.3 0.8 %maximum_bitcast_fusion.refs_5_ = f32[12,2,4,8,128]{4,3,2,1,0:T(8,128)} fusion(f32[8,1,4,12,128]{4,0,2,1,3:T(8,128)S(1)} %get-tuple-element.13, f32[8,1,4,12,128]{4,0,2,1,3:T(8,128)S(1)} %get-tuple-element.12), kind=kLoop, calls=%fused_computation | loop fusion | flops 98304 | bytes 786432 | tf_op jit(solution)/shard_map/transpose | solution.py:272
  13.1 0.4 collective-permute-done.4.refs_4_
  13.4 0.4 %collective-permute-done.3.refs_3_ = f32[5,4,4,128]{3,2,1,0:T(4,128)S(1)} collective-permute-done((f32[5,4,4,128]{3,2,1,0:T(4,128)S(1)}, f32[5,4,4,128]{3,2,1,0:T(4,128)S(1)}, u32[]{:S(2)}, u32[]{:S(2)}) %collective-permute-start.3) | collective-permute-done | bytes 40992 | tf_op jit(solution)/shard_map/ppermute | solution.py:25
  13.8 4.1 %collective-permute-done.2.refs_1_ = f32[5,4,4,128]{3,2,1,0:T(4,128)S(1)} collective-permute-done((f32[5,4,4,128]{3,2,1,0:T(4,128)S(1)}, f32[5,4,4,128]{3,2,1,0:T(4,128)S(1)}, u32[]{:S(2)}, u32[]{:S(2)}) %collective-permute-start.2) | collective-permute-done | bytes 40992 | tf_op jit(solution)/shard_map/ppermute | solution.py:25
  17.9 1.1 %collective-permute-done.1.refs_0_ = f32[5,4,4,128]{3,2,1,0:T(4,128)S(1)} collective-permute-done((f32[5,4,4,128]{3,2,1,0:T(4,128)S(1)}, f32[5,4,4,128]{3,2,1,0:T(4,128)S(1)}, u32[]{:S(2)}, u32[]{:S(2)}) %collective-permute-start.1) | collective-permute-done | bytes 40992 | tf_op jit(solution)/shard_map/ppermute | solution.py:25
  19.0 0.7 %broadcast_in_dim.8.refs_6_ = f32[3,8,128]{2,1,0:T(8,128)} broadcast(f32[3,8]{1,0:T(4,128)S(1)} %fusion.19), dimensions={0,1} | broadcast | bytes 12384 | tf_op jit(solution)/shard_map/broadcast_in_dim | solution.py:273
  19.7 4.1 %shard_map.76 = (f32[3,4,4,128]{3,2,1,0:T(4,128)}, f32[4,2,3,4,8,128]{5,4,3,2,1,0:T(8,128)}, f32[4,8]{1,0:T(4,128)}) custom-call(f32[5,4,4,128]{3,2,1,0:T(4,128)} %copy-done.4, f32[5,4,4,128]{3,2,1,0:T(4,128)} %copy-done.3, f32[5,4,4,128]{3,2,1,0:T(4,128)} %copy-done, f32[5,4,4,128]{3,2,1,0:T(4,128)} %copy-done.2, f32[5,4,4,128]{3,2,1,0:T(4,128)} %copy-done.1, ...), custom_call_target="tpu_custom_call" | custom-call | flops 14991360 | bytes 1032192 | tf_op jit(solution)/shard_map/pallas_call | solution.py:218
  23.7 1.4 %collective-permute-done.5 = f32[4,8]{1,0:T(4,128)S(1)} collective-permute-done((f32[4,8]{1,0:T(4,128)}, f32[4,8]{1,0:T(4,128)S(1)}, u32[]{:S(2)}, u32[]{:S(2)}) %collective-permute-start.5) | collective-permute-done | bytes 160 | tf_op jit(solution)/shard_map/ppermute | solution.py:94
  25.1 0.7 %add.172 = f32[4,8]{1,0:T(4,128)S(1)} add(f32[4,8]{1,0:T(4,128)} %get-tuple-element.8, f32[4,8]{1,0:T(4,128)S(1)} %collective-permute-done.5) | non-fusion elementwise | flops 32 | bytes 384 | tf_op jit(solution)/shard_map/add | solution.py:94
  25.8 3.6 %collective-permute-done.6 = f32[4,8]{1,0:T(4,128)S(1)} collective-permute-done((f32[4,8]{1,0:T(4,128)S(1)}, f32[4,8]{1,0:T(4,128)S(1)}, u32[]{:S(2)}, u32[]{:S(2)}) %collective-permute-start.6) | collective-permute-done | bytes 160 | tf_op jit(solution)/shard_map/ppermute | solution.py:94
  29.4 1.0 %convert_bitcast_fusion = bf16[8,2,3,4,4,128]{5,0,3,2,1,4:T(8,128)(2,1)S(1)} fusion(f32[4,2,3,4,8,128]{5,4,3,2,1,0:T(8,128)} %get-tuple-element.7), kind=kLoop, calls=%fused_computation.1 | loop fusion | flops 98304 | bytes 589824 | tf_op jit(solution)/shard_map/convert_element_type | solution.py:277
  30.4 2.5 %collective-permute-done.7 = f32[4,8]{1,0:T(4,128)S(1)} collective-permute-done((f32[4,8]{1,0:T(4,128)S(1)}, f32[4,8]{1,0:T(4,128)S(1)}, u32[]{:S(2)}, u32[]{:S(2)}) %collective-permute-start.7) | collective-permute-done | bytes 160 | tf_op jit(solution)/shard_map/ppermute | solution.py:94
  33.0 0.7 %constant_dynamic-slice_fusion = f32[3,4,4,64]{3,2,1,0:T(4,128)} fusion(f32[3,4,4,128]{3,2,1,0:T(4,128)S(1)} %copy-done.7, s32[]{:T(128)S(6)} %select_n.77), kind=kLoop, calls=%fused_computation.42 | loop fusion | bytes 24580 | tf_op jit(solution)/shard_map/dynamic_slice | solution.py:276
  33.7 0.8 %copy.8 = bf16[8,2,3,4,4,128]{5,4,3,2,1,0:T(4,128)(2,1)} copy(bf16[8,2,3,4,4,128]{5,0,3,2,1,4:T(8,128)(2,1)S(1)} %convert_bitcast_fusion) | data formatting | bytes 393216
  34.5 2.9 %collective-permute-done.8 = f32[4,8]{1,0:T(4,128)S(1)} collective-permute-done((f32[4,8]{1,0:T(4,128)S(1)}, f32[4,8]{1,0:T(4,128)S(1)}, u32[]{:S(2)}, u32[]{:S(2)}) %collective-permute-start.8) | collective-permute-done | bytes 160 | tf_op jit(solution)/shard_map/ppermute | solution.py:94
  37.4 0.6 %multiply_bitcast_fusion = f32[8,4]{0,1:T(4,128)} fusion(f32[4,8]{1,0:T(4,128)S(1)} %add.174, f32[4,8]{1,0:T(4,128)S(1)} %collective-permute-done.8), kind=kLoop, calls=%fused_computation.48 | loop fusion | flops 64 | bytes 384 | tf_op jit(solution)/shard_map/transpose | solution.py:279
  (35 shorter events, 0.3 us)
Async XLA Ops:
  0.6 0.8 %copy-start.5 = (f32[4,4,64]{2,1,0:T(4,128)S(1)}, f32[4,4,64]{2,1,0:T(4,128)}, u32[]{:S(2)}) copy-start(f32[4,4,64]{2,1,0:T(4,128)} %param.5) | copy-start | bytes 12292
  0.6 0.8 %copy-start.6 = (f32[4,4,64]{2,1,0:T(4,128)S(1)}, f32[4,4,64]{2,1,0:T(4,128)}, u32[]{:S(2)}) copy-start(f32[4,4,64]{2,1,0:T(4,128)} %param.6) | copy-start | bytes 12292
  1.4 5.0 %collective-permute-start = (f32[5,4,4,64]{3,2,1,0:T(4,128)S(1)}, f32[5,4,4,64]{3,2,1,0:T(4,128)S(1)}, u32[]{:S(2)}, u32[]{:S(2)}) collective-permute-start(f32[5,4,4,64]{3,2,1,0:T(4,128)S(1)} %pad_maximum_fusion), channel_id=1, source_target_pairs={{0,16},{16,0},{1,17},{17,1},{2,18},{18,2},{3,19},{19,3},{4,20},{20... | collective-permute-start | bytes 61448 | tf_op jit(solution)/shard_map/ppermute | solution.py:25
  4.5 0.7 %copy-start.8 = (s32[8,3]{0,1:T(4,128)S(1)}, s32[8,3]{0,1:T(4,128)}, u32[]{:S(2)}) copy-start(s32[8,3]{0,1:T(4,128)} %param.9) | copy-start | bytes 292
  6.6 6.4 %copy-start = (f32[5,4,4,128]{3,2,1,0:T(4,128)}, f32[5,4,4,128]{3,2,1,0:T(4,128)S(1)}, u32[]{:S(2)}) copy-start(f32[5,4,4,128]{3,2,1,0:T(4,128)S(1)} %fusion.4.refs_2_) | copy-start | bytes 122884
  6.6 6.8 %collective-permute-start.4 = (f32[5,4,4,128]{3,2,1,0:T(4,128)S(1)}, f32[5,4,4,128]{3,2,1,0:T(4,128)S(1)}, u32[]{:S(2)}, u32[]{:S(2)}) collective-permute-start(f32[5,4,4,128]{3,2,1,0:T(4,128)S(1)} %fusion.4.refs_2_), channel_id=1, source_target_pairs={{0,14},{1,15},{2,0},{3,1},{4,2},{5,3},{6,4},{7,5},{8,6},{9,7},{10,... | collective-permute-start | bytes 122888 | tf_op jit(solution)/shard_map/ppermute | solution.py:25
  11.8 2.1 %collective-permute-start.3 = (f32[5,4,4,128]{3,2,1,0:T(4,128)S(1)}, f32[5,4,4,128]{3,2,1,0:T(4,128)S(1)}, u32[]{:S(2)}, u32[]{:S(2)}) collective-permute-start(f32[5,4,4,128]{3,2,1,0:T(4,128)S(1)} %fusion.4.refs_2_), channel_id=1, source_target_pairs={{0,15},{1,0},{2,1},{3,2},{4,3},{5,4},{6,5},{7,6},{8,7},{9,8},{10,9... | collective-permute-start | bytes 122888 | tf_op jit(solution)/shard_map/ppermute | solution.py:25
  11.8 6.1 %collective-permute-start.2 = (f32[5,4,4,128]{3,2,1,0:T(4,128)S(1)}, f32[5,4,4,128]{3,2,1,0:T(4,128)S(1)}, u32[]{:S(2)}, u32[]{:S(2)}) collective-permute-start(f32[5,4,4,128]{3,2,1,0:T(4,128)S(1)} %fusion.4.refs_2_), channel_id=1, source_target_pairs={{0,1},{1,2},{2,3},{3,4},{4,5},{5,6},{6,7},{7,8},{8,9},{9,10},{10,1... | collective-permute-start | bytes 122888 | tf_op jit(solution)/shard_map/ppermute | solution.py:25
  12.3 6.7 %collective-permute-start.1 = (f32[5,4,4,128]{3,2,1,0:T(4,128)S(1)}, f32[5,4,4,128]{3,2,1,0:T(4,128)S(1)}, u32[]{:S(2)}, u32[]{:S(2)}) collective-permute-start(f32[5,4,4,128]{3,2,1,0:T(4,128)S(1)} %fusion.4.refs_2_), channel_id=1, source_target_pairs={{0,2},{1,3},{2,4},{3,5},{4,6},{5,7},{6,8},{7,9},{8,10},{9,11},{10,... | collective-permute-start | bytes 122888 | tf_op jit(solution)/shard_map/ppermute | solution.py:25
  13.4 6.2 %copy-start.1 = (f32[5,4,4,128]{3,2,1,0:T(4,128)}, f32[5,4,4,128]{3,2,1,0:T(4,128)S(1)}, u32[]{:S(2)}) copy-start(f32[5,4,4,128]{3,2,1,0:T(4,128)S(1)} %collective-permute-done.4.refs_4_) | copy-start | bytes 122884
  13.8 5.8 %copy-start.2 = (f32[5,4,4,128]{3,2,1,0:T(4,128)}, f32[5,4,4,128]{3,2,1,0:T(4,128)S(1)}, u32[]{:S(2)}) copy-start(f32[5,4,4,128]{3,2,1,0:T(4,128)S(1)} %collective-permute-done.3.refs_3_) | copy-start | bytes 122884
  17.9 1.8 %copy-start.3 = (f32[5,4,4,128]{3,2,1,0:T(4,128)}, f32[5,4,4,128]{3,2,1,0:T(4,128)S(1)}, u32[]{:S(2)}) copy-start(f32[5,4,4,128]{3,2,1,0:T(4,128)S(1)} %collective-permute-done.2.refs_1_) | copy-start | bytes 122884
  19.0 0.7 %copy-start.4 = (f32[5,4,4,128]{3,2,1,0:T(4,128)}, f32[5,4,4,128]{3,2,1,0:T(4,128)S(1)}, u32[]{:S(2)}) copy-start(f32[5,4,4,128]{3,2,1,0:T(4,128)S(1)} %collective-permute-done.1.refs_0_) | copy-start | bytes 122884
  23.7 1.4 %collective-permute-start.5 = (f32[4,8]{1,0:T(4,128)}, f32[4,8]{1,0:T(4,128)S(1)}, u32[]{:S(2)}, u32[]{:S(2)}) collective-permute-start(f32[4,8]{1,0:T(4,128)} %get-tuple-element.8), channel_id=1, source_target_pairs={{0,1},{1,0},{2,3},{3,2},{4,5},{5,4},{6,7},{7,6},{8,9},{9,8},{10,11... | collective-permute-start | bytes 392 | tf_op jit(solution)/shard_map/ppermute | solution.py:94
  25.8 3.6 %collective-permute-start.6 = (f32[4,8]{1,0:T(4,128)S(1)}, f32[4,8]{1,0:T(4,128)S(1)}, u32[]{:S(2)}, u32[]{:S(2)}) collective-permute-start(f32[4,8]{1,0:T(4,128)S(1)} %add.172), channel_id=1, source_target_pairs={{0,2},{1,3},{2,0},{3,1},{4,6},{5,7},{6,4},{7,5},{8,10},{9,11},{10,... | collective-permute-start | bytes 392 | tf_op jit(solution)/shard_map/ppermute | solution.py:94
  29.4 3.6 %collective-permute-start.7 = (f32[4,8]{1,0:T(4,128)S(1)}, f32[4,8]{1,0:T(4,128)S(1)}, u32[]{:S(2)}, u32[]{:S(2)}) collective-permute-start(f32[4,8]{1,0:T(4,128)S(1)} %add.173), channel_id=1, source_target_pairs={{0,4},{1,5},{2,6},{3,7},{4,0},{5,1},{6,2},{7,3},{8,12},{9,13},{10,... | collective-permute-start | bytes 392 | tf_op jit(solution)/shard_map/ppermute | solution.py:94
  29.4 3.6 %copy-start.7 = (f32[3,4,4,128]{3,2,1,0:T(4,128)S(1)}, f32[3,4,4,128]{3,2,1,0:T(4,128)}, u32[]{:S(2)}) copy-start(f32[3,4,4,128]{3,2,1,0:T(4,128)} %get-tuple-element.6) | copy-start | bytes 73732
  33.0 4.5 %collective-permute-start.8 = (f32[4,8]{1,0:T(4,128)S(1)}, f32[4,8]{1,0:T(4,128)S(1)}, u32[]{:S(2)}, u32[]{:S(2)}) collective-permute-start(f32[4,8]{1,0:T(4,128)S(1)} %add.174), channel_id=1, source_target_pairs={{0,8},{1,9},{2,10},{3,11},{4,12},{5,13},{6,14},{7,15},{8,0},{9,1},... | collective-permute-start | bytes 392 | tf_op jit(solution)/shard_map/ppermute | solution.py:94

commit v11 on v10

--- a/solution.py
+++ b/solution.py
@@ -167,7 +167,13 @@
         w = first + 1 + xr
         spins_b[xr] = jnp.broadcast_to(sweep_b[:, :, w - SWEEPS:w - SWEEPS + 1, :], (3, depth, probes, lanes))
 
-    polar = [polar_ref[j] for j in range(3)]
+    sublane = lax.broadcasted_iota(jnp.int32, (probes, lanes), 0)
+    local_comp = jnp.zeros((probes, lanes), jnp.int32)
+    for p in range(probes):
+        local_comp = jnp.where(sublane == p, p % 3, local_comp)
+    comp = local_comp + polar_ref[0] % 3
+    comp = jnp.where(comp >= 3, comp - 3, comp)
+    polar = [jnp.where(comp == j, 1.0, 0.0).astype(jnp.float32) for j in range(3)]
 
     def start_row(i):
         wave = start_ref[i]
@@ -222,8 +228,8 @@
             jax.ShapeDtypeStruct((slab_rows,) + vec_shape, jnp.float32),
             jax.ShapeDtypeStruct((CHEB, probes), jnp.float32),
         ),
-        in_specs=[pl.BlockSpec(memory_space=pltpu.VMEM)] * (len(slab_blocks) + 2)
-        + [pl.BlockSpec(memory_space=pltpu.SMEM)],
+        in_specs=[pl.BlockSpec(memory_space=pltpu.VMEM)] * (len(slab_blocks) + 1)
+        + [pl.BlockSpec(memory_space=pltpu.SMEM)] * 2,
         out_specs=[pl.BlockSpec(memory_space=pltpu.VMEM)] * 3,
         scratch_shapes=[
             pltpu.VMEM((6, depth, width, lanes), jnp.float32),
@@ -270,9 +276,9 @@
     probe_ids = group * group_size + jnp.arange(group_size, dtype=jnp.int32)
     waves, polar = make_probes(probe_wave, probe_ids, x_coords, y_coords, total_x, total_y, LZ)
     waves = jnp.transpose(waves, (3, 1, 2, 0, 4))
-    polar = jnp.broadcast_to(polar.T[:, :, None], (3, group_size, total_y))
-
-    relaxed, last, sums = run_local(slab_blocks, waves, polar, exchange, halo, slab_rows)
+    first_id = (group * group_size).astype(jnp.int32).reshape(1)
+
+    relaxed, last, sums = run_local(slab_blocks, waves, first_id, exchange, halo, slab_rows)
     relaxed_own = lax.dynamic_slice_in_dim(relaxed, group * block_y, block_y, -1)
     last = jnp.transpose(last, (4, 1, 2, 3, 0, 5)).astype(jnp.bfloat16)
     moment_rows = butterfly_sum(sums, "space") / site_count

time: 38.3 us -> 38.3 us (level)
    broadcast_in_dim x1 -> x0, local copies, waits for them, and re-layouts: 0.67 us -> none  [shards(): polar = jnp.broadcast_to(polar.T[:, :, None], (3, group_size, total_y))]
    unnamed x19, local copies, waits for them, and re-layouts: 1.52 us -> 2.11 us
where the time goes in v11:
time: 38.3 us; the launch traced here: 38 us
  waiting for transfers between devices  16.6 us (43%)
  starting transfers between devices  8.67 us (23%)
  other arithmetic  5.1 us (13%)
  Pallas kernels  4.14 us (11%)
  local copies, waits for them, and re-layouts  2.81 us (7%)
  between operations  0.73 us (2%)
    ppermute x4, waiting for transfers between devices, butterfly_sum(): lax.ppermute(value, axis, [(i, i ^ step) for i in range(size)])  10.4 us
    ppermute x5, starting transfers between devices, shifted(): lax.ppermute(array, axis, [(i, (i - shift) % size) for i in range(size)])  8.66 us
    ppermute x5, waiting for transfers between devices, shifted(): lax.ppermute(array, axis, [(i, (i - shift) % size) for i in range(size)])  6.14 us
    pallas_call x1, Pallas kernels, run_local(): pl.pallas_call(body, out_shape=(jax.ShapeDtypeStruct((3, depth, slab_rows...  4.14 us
    unnamed x19, local copies, waits for them, and re-layouts  2.11 us
    convert_element_type x1, other arithmetic, shards(): last = jnp.transpose(last, (4, 1, 2, 3, 0, 5)).astype(jnp.bfloat16)  1.04 us
    mul x1, other arithmetic, make_probes(): waves = jnp.stack([jnp.cos(angle) * ramp, jnp.sin(angle) * ramp], 1)  0.85 us
    transpose x1, other arithmetic, shards(): waves = jnp.transpose(waves, (3, 1, 2, 0, 4))  0.78 us
  transfers between devices with their start and end apart: 9, of which 9 were waited for; matrix products, arithmetic and copies ran while one was open for 12% of the time, Pallas kernels for 0%

profile of v11, /device:TPU:0, one launch (start us, length us, event | category | flops | bytes accessed | tf_op | source)
XLA Modules:
  0.0 38.0 jit_solution(8391141882725596857)
XLA Ops:
  0.7 0.8 %convert_element_type.40 = f32[3,4,4,64]{3,2,1,0:T(4,128)S(1)} convert(s32[3,4,4,64]{3,2,1,0:T(4,128)} %param.7) | non-fusion elementwise | flops 3072 | bytes 24576 | tf_op jit(solution)/shard_map/convert_element_type | solution.py:263
  1.4 3.0 %collective-permute-start = (f32[5,4,4,64]{3,2,1,0:T(4,128)S(1)}, f32[5,4,4,64]{3,2,1,0:T(4,128)S(1)}, u32[]{:S(2)}, u32[]{:S(2)}) collective-permute-start(f32[5,4,4,64]{3,2,1,0:T(4,128)S(1)} %pad_maximum_fusion), channel_id=1, source_target_pairs={{0,16},{16,0},{1,17},{17,1},{2,18},{18,2},{3,19},{19,3},{4,20},{20... | collective-permute-start | bytes 61448 | tf_op jit(solution)/shard_map/ppermute | solution.py:25
  4.5 0.6 %copy-done.8 = s32[8,3]{0,1:T(4,128)S(1)} copy-done((s32[8,3]{0,1:T(4,128)S(1)}, s32[8,3]{0,1:T(4,128)}, u32[]{:S(2)}) %copy-start.8) | copy-done | bytes 120
  5.3 0.8 %cosine_multiply_fusion = (f32[8,1,4,12,128]{4,0,2,1,3:T(8,128)S(1)}, f32[8,1,4,12,128]{4,0,2,1,3:T(8,128)S(1)}) fusion(f32[12]{0:T(128)S(1)} %add_sqrt_fusion, f32[8,128]{1,0:T(8,128)S(1)} %fusion.12, f32[8,4,12]{0,1,2:T(4,128)S(1)} %broadcast_add_fusion), kind=kLoop, calls=%fused_computation.3 | loop fusion | flops 196608 | bytes 398896 | tf_op jit(solution)/shard_map/mul | solution.py:81
  6.2 0.2 collective-permute-done
  6.4 0.2 fusion.4.refs_2_
  6.6 5.1 %collective-permute-start.4 = (f32[5,4,4,128]{3,2,1,0:T(4,128)S(1)}, f32[5,4,4,128]{3,2,1,0:T(4,128)S(1)}, u32[]{:S(2)}, u32[]{:S(2)}) collective-permute-start(f32[5,4,4,128]{3,2,1,0:T(4,128)S(1)} %fusion.4.refs_2_), channel_id=1, source_target_pairs={{0,14},{1,15},{2,0},{3,1},{4,2},{5,3},{6,4},{7,5},{8,6},{9,7},{10,... | collective-permute-start | bytes 122888 | tf_op jit(solution)/shard_map/ppermute | solution.py:25
  11.8 0.5 %collective-permute-start.2 = (f32[5,4,4,128]{3,2,1,0:T(4,128)S(1)}, f32[5,4,4,128]{3,2,1,0:T(4,128)S(1)}, u32[]{:S(2)}, u32[]{:S(2)}) collective-permute-start(f32[5,4,4,128]{3,2,1,0:T(4,128)S(1)} %fusion.4.refs_2_), channel_id=1, source_target_pairs={{0,1},{1,2},{2,3},{3,4},{4,5},{5,6},{6,7},{7,8},{8,9},{9,10},{10,1... | collective-permute-start | bytes 122888 | tf_op jit(solution)/shard_map/ppermute | solution.py:25
  12.3 0.8 %maximum_bitcast_fusion.refs_5_ = f32[12,2,4,8,128]{4,3,2,1,0:T(8,128)} fusion(f32[8,1,4,12,128]{4,0,2,1,3:T(8,128)S(1)} %get-tuple-element.13, f32[8,1,4,12,128]{4,0,2,1,3:T(8,128)S(1)} %get-tuple-element.12), kind=kLoop, calls=%fused_computation | loop fusion | flops 98304 | bytes 786432 | tf_op jit(solution)/shard_map/transpose | solution.py:278
  13.1 0.4 collective-permute-done.4.refs_4_
  13.4 0.4 %collective-permute-done.3.refs_3_ = f32[5,4,4,128]{3,2,1,0:T(4,128)S(1)} collective-permute-done((f32[5,4,4,128]{3,2,1,0:T(4,128)S(1)}, f32[5,4,4,128]{3,2,1,0:T(4,128)S(1)}, u32[]{:S(2)}, u32[]{:S(2)}) %collective-permute-start.3) | collective-permute-done | bytes 40992 | tf_op jit(solution)/shard_map/ppermute | solution.py:25
  13.8 4.1 %collective-permute-done.2.refs_1_ = f32[5,4,4,128]{3,2,1,0:T(4,128)S(1)} collective-permute-done((f32[5,4,4,128]{3,2,1,0:T(4,128)S(1)}, f32[5,4,4,128]{3,2,1,0:T(4,128)S(1)}, u32[]{:S(2)}, u32[]{:S(2)}) %collective-permute-start.2) | collective-permute-done | bytes 40992 | tf_op jit(solution)/shard_map/ppermute | solution.py:25
  17.9 1.1 %collective-permute-done.1.refs_0_ = f32[5,4,4,128]{3,2,1,0:T(4,128)S(1)} collective-permute-done((f32[5,4,4,128]{3,2,1,0:T(4,128)S(1)}, f32[5,4,4,128]{3,2,1,0:T(4,128)S(1)}, u32[]{:S(2)}, u32[]{:S(2)}) %collective-permute-start.1) | collective-permute-done | bytes 40992 | tf_op jit(solution)/shard_map/ppermute | solution.py:25
  19.0 0.6 %copy-done.4 = f32[5,4,4,128]{3,2,1,0:T(4,128)} copy-done((f32[5,4,4,128]{3,2,1,0:T(4,128)}, f32[5,4,4,128]{3,2,1,0:T(4,128)S(1)}, u32[]{:S(2)}) %copy-start.4) | copy-done | bytes 40984
  19.6 4.1 %shard_map.76 = (f32[3,4,4,128]{3,2,1,0:T(4,128)}, f32[4,2,3,4,8,128]{5,4,3,2,1,0:T(8,128)}, f32[4,8]{1,0:T(4,128)}) custom-call(f32[5,4,4,128]{3,2,1,0:T(4,128)} %copy-done.4, f32[5,4,4,128]{3,2,1,0:T(4,128)} %copy-done.3, f32[5,4,4,128]{3,2,1,0:T(4,128)} %copy-done, f32[5,4,4,128]{3,2,1,0:T(4,128)} %copy-done.2, f32[5,4,4,128]{3,2,1,0:T(4,128)} %copy-done.1, ...), custom_call_target="tpu_custom_call" | custom-call | flops 14991360 | bytes 1032192 | tf_op jit(solution)/shard_map/pallas_call | solution.py:224
  23.7 1.4 %collective-permute-done.5 = f32[4,8]{1,0:T(4,128)S(1)} collective-permute-done((f32[4,8]{1,0:T(4,128)}, f32[4,8]{1,0:T(4,128)S(1)}, u32[]{:S(2)}, u32[]{:S(2)}) %collective-permute-start.5) | collective-permute-done | bytes 160 | tf_op jit(solution)/shard_map/ppermute | solution.py:94
  25.1 0.7 %add.149 = f32[4,8]{1,0:T(4,128)S(1)} add(f32[4,8]{1,0:T(4,128)} %get-tuple-element.8, f32[4,8]{1,0:T(4,128)S(1)} %collective-permute-done.5) | non-fusion elementwise | flops 32 | bytes 384 | tf_op jit(solution)/shard_map/add | solution.py:94
  25.8 3.6 %collective-permute-done.6 = f32[4,8]{1,0:T(4,128)S(1)} collective-permute-done((f32[4,8]{1,0:T(4,128)S(1)}, f32[4,8]{1,0:T(4,128)S(1)}, u32[]{:S(2)}, u32[]{:S(2)}) %collective-permute-start.6) | collective-permute-done | bytes 160 | tf_op jit(solution)/shard_map/ppermute | solution.py:94
  29.4 1.0 %convert_bitcast_fusion = bf16[8,2,3,4,4,128]{5,0,3,2,1,4:T(8,128)(2,1)S(1)} fusion(f32[4,2,3,4,8,128]{5,4,3,2,1,0:T(8,128)} %get-tuple-element.7), kind=kLoop, calls=%fused_computation.1 | loop fusion | flops 98304 | bytes 589824 | tf_op jit(solution)/shard_map/convert_element_type | solution.py:283
  30.4 2.5 %collective-permute-done.7 = f32[4,8]{1,0:T(4,128)S(1)} collective-permute-done((f32[4,8]{1,0:T(4,128)S(1)}, f32[4,8]{1,0:T(4,128)S(1)}, u32[]{:S(2)}, u32[]{:S(2)}) %collective-permute-start.7) | collective-permute-done | bytes 160 | tf_op jit(solution)/shard_map/ppermute | solution.py:94
  33.0 0.7 %constant_dynamic-slice_fusion = f32[3,4,4,64]{3,2,1,0:T(4,128)} fusion(f32[3,4,4,128]{3,2,1,0:T(4,128)S(1)} %copy-done.7, s32[]{:T(128)S(6)} %select_n.66), kind=kLoop, calls=%fused_computation.42 | loop fusion | bytes 24580 | tf_op jit(solution)/shard_map/dynamic_slice | solution.py:282
  33.7 0.8 %copy.8 = bf16[8,2,3,4,4,128]{5,4,3,2,1,0:T(4,128)(2,1)} copy(bf16[8,2,3,4,4,128]{5,0,3,2,1,4:T(8,128)(2,1)S(1)} %convert_bitcast_fusion) | data formatting | bytes 393216
  34.5 2.9 %collective-permute-done.8 = f32[4,8]{1,0:T(4,128)S(1)} collective-permute-done((f32[4,8]{1,0:T(4,128)S(1)}, f32[4,8]{1,0:T(4,128)S(1)}, u32[]{:S(2)}, u32[]{:S(2)}) %collective-permute-start.8) | collective-permute-done | bytes 160 | tf_op jit(solution)/shard_map/ppermute | solution.py:94
  37.4 0.6 %multiply_bitcast_fusion = f32[8,4]{0,1:T(4,128)} fusion(f32[4,8]{1,0:T(4,128)S(1)} %add.151, f32[4,8]{1,0:T(4,128)S(1)} %collective-permute-done.8), kind=kLoop, calls=%fused_computation.48 | loop fusion | flops 64 | bytes 384 | tf_op jit(solution)/shard_map/transpose | solution.py:285
  (32 shorter events, 0.3 us)
Async XLA Ops:
  0.6 0.8 %copy-start.5 = (f32[4,4,64]{2,1,0:T(4,128)S(1)}, f32[4,4,64]{2,1,0:T(4,128)}, u32[]{:S(2)}) copy-start(f32[4,4,64]{2,1,0:T(4,128)} %param.5) | copy-start | bytes 12292
  0.6 0.8 %copy-start.6 = (f32[4,4,64]{2,1,0:T(4,128)S(1)}, f32[4,4,64]{2,1,0:T(4,128)}, u32[]{:S(2)}) copy-start(f32[4,4,64]{2,1,0:T(4,128)} %param.6) | copy-start | bytes 12292
  1.4 5.0 %collective-permute-start = (f32[5,4,4,64]{3,2,1,0:T(4,128)S(1)}, f32[5,4,4,64]{3,2,1,0:T(4,128)S(1)}, u32[]{:S(2)}, u32[]{:S(2)}) collective-permute-start(f32[5,4,4,64]{3,2,1,0:T(4,128)S(1)} %pad_maximum_fusion), channel_id=1, source_target_pairs={{0,16},{16,0},{1,17},{17,1},{2,18},{18,2},{3,19},{19,3},{4,20},{20... | collective-permute-start | bytes 61448 | tf_op jit(solution)/shard_map/ppermute | solution.py:25
  4.4 0.7 %copy-start.8 = (s32[8,3]{0,1:T(4,128)S(1)}, s32[8,3]{0,1:T(4,128)}, u32[]{:S(2)}) copy-start(s32[8,3]{0,1:T(4,128)} %param.9) | copy-start | bytes 292
  6.6 6.4 %copy-start = (f32[5,4,4,128]{3,2,1,0:T(4,128)}, f32[5,4,4,128]{3,2,1,0:T(4,128)S(1)}, u32[]{:S(2)}) copy-start(f32[5,4,4,128]{3,2,1,0:T(4,128)S(1)} %fusion.4.refs_2_) | copy-start | bytes 122884
  6.6 6.8 %collective-permute-start.4 = (f32[5,4,4,128]{3,2,1,0:T(4,128)S(1)}, f32[5,4,4,128]{3,2,1,0:T(4,128)S(1)}, u32[]{:S(2)}, u32[]{:S(2)}) collective-permute-start(f32[5,4,4,128]{3,2,1,0:T(4,128)S(1)} %fusion.4.refs_2_), channel_id=1, source_target_pairs={{0,14},{1,15},{2,0},{3,1},{4,2},{5,3},{6,4},{7,5},{8,6},{9,7},{10,... | collective-permute-start | bytes 122888 | tf_op jit(solution)/shard_map/ppermute | solution.py:25
  11.8 2.1 %collective-permute-start.3 = (f32[5,4,4,128]{3,2,1,0:T(4,128)S(1)}, f32[5,4,4,128]{3,2,1,0:T(4,128)S(1)}, u32[]{:S(2)}, u32[]{:S(2)}) collective-permute-start(f32[5,4,4,128]{3,2,1,0:T(4,128)S(1)} %fusion.4.refs_2_), channel_id=1, source_target_pairs={{0,15},{1,0},{2,1},{3,2},{4,3},{5,4},{6,5},{7,6},{8,7},{9,8},{10,9... | collective-permute-start | bytes 122888 | tf_op jit(solution)/shard_map/ppermute | solution.py:25
  11.8 6.1 %collective-permute-start.2 = (f32[5,4,4,128]{3,2,1,0:T(4,128)S(1)}, f32[5,4,4,128]{3,2,1,0:T(4,128)S(1)}, u32[]{:S(2)}, u32[]{:S(2)}) collective-permute-start(f32[5,4,4,128]{3,2,1,0:T(4,128)S(1)} %fusion.4.refs_2_), channel_id=1, source_target_pairs={{0,1},{1,2},{2,3},{3,4},{4,5},{5,6},{6,7},{7,8},{8,9},{9,10},{10,1... | collective-permute-start | bytes 122888 | tf_op jit(solution)/shard_map/ppermute | solution.py:25
  12.3 6.7 %collective-permute-start.1 = (f32[5,4,4,128]{3,2,1,0:T(4,128)S(1)}, f32[5,4,4,128]{3,2,1,0:T(4,128)S(1)}, u32[]{:S(2)}, u32[]{:S(2)}) collective-permute-start(f32[5,4,4,128]{3,2,1,0:T(4,128)S(1)} %fusion.4.refs_2_), channel_id=1, source_target_pairs={{0,2},{1,3},{2,4},{3,5},{4,6},{5,7},{6,8},{7,9},{8,10},{9,11},{10,... | collective-permute-start | bytes 122888 | tf_op jit(solution)/shard_map/ppermute | solution.py:25
  13.4 5.5 %copy-start.1 = (f32[5,4,4,128]{3,2,1,0:T(4,128)}, f32[5,4,4,128]{3,2,1,0:T(4,128)S(1)}, u32[]{:S(2)}) copy-start(f32[5,4,4,128]{3,2,1,0:T(4,128)S(1)} %collective-permute-done.4.refs_4_) | copy-start | bytes 122884
  13.8 5.2 %copy-start.2 = (f32[5,4,4,128]{3,2,1,0:T(4,128)}, f32[5,4,4,128]{3,2,1,0:T(4,128)S(1)}, u32[]{:S(2)}) copy-start(f32[5,4,4,128]{3,2,1,0:T(4,128)S(1)} %collective-permute-done.3.refs_3_) | copy-start | bytes 122884
  17.9 1.1 %copy-start.3 = (f32[5,4,4,128]{3,2,1,0:T(4,128)}, f32[5,4,4,128]{3,2,1,0:T(4,128)S(1)}, u32[]{:S(2)}) copy-start(f32[5,4,4,128]{3,2,1,0:T(4,128)S(1)} %collective-permute-done.2.refs_1_) | copy-start | bytes 122884
  19.0 0.6 %copy-start.4 = (f32[5,4,4,128]{3,2,1,0:T(4,128)}, f32[5,4,4,128]{3,2,1,0:T(4,128)S(1)}, u32[]{:S(2)}) copy-start(f32[5,4,4,128]{3,2,1,0:T(4,128)S(1)} %collective-permute-done.1.refs_0_) | copy-start | bytes 122884
  23.7 1.4 %collective-permute-start.5 = (f32[4,8]{1,0:T(4,128)}, f32[4,8]{1,0:T(4,128)S(1)}, u32[]{:S(2)}, u32[]{:S(2)}) collective-permute-start(f32[4,8]{1,0:T(4,128)} %get-tuple-element.8), channel_id=1, source_target_pairs={{0,1},{1,0},{2,3},{3,2},{4,5},{5,4},{6,7},{7,6},{8,9},{9,8},{10,11... | collective-permute-start | bytes 392 | tf_op jit(solution)/shard_map/ppermute | solution.py:94
  25.8 3.6 %collective-permute-start.6 = (f32[4,8]{1,0:T(4,128)S(1)}, f32[4,8]{1,0:T(4,128)S(1)}, u32[]{:S(2)}, u32[]{:S(2)}) collective-permute-start(f32[4,8]{1,0:T(4,128)S(1)} %add.149), channel_id=1, source_target_pairs={{0,2},{1,3},{2,0},{3,1},{4,6},{5,7},{6,4},{7,5},{8,10},{9,11},{10,... | collective-permute-start | bytes 392 | tf_op jit(solution)/shard_map/ppermute | solution.py:94
  29.4 3.6 %collective-permute-start.7 = (f32[4,8]{1,0:T(4,128)S(1)}, f32[4,8]{1,0:T(4,128)S(1)}, u32[]{:S(2)}, u32[]{:S(2)}) collective-permute-start(f32[4,8]{1,0:T(4,128)S(1)} %add.150), channel_id=1, source_target_pairs={{0,4},{1,5},{2,6},{3,7},{4,0},{5,1},{6,2},{7,3},{8,12},{9,13},{10,... | collective-permute-start | bytes 392 | tf_op jit(solution)/shard_map/ppermute | solution.py:94
  29.4 3.6 %copy-start.7 = (f32[3,4,4,128]{3,2,1,0:T(4,128)S(1)}, f32[3,4,4,128]{3,2,1,0:T(4,128)}, u32[]{:S(2)}) copy-start(f32[3,4,4,128]{3,2,1,0:T(4,128)} %get-tuple-element.6) | copy-start | bytes 73732
  33.0 4.5 %collective-permute-start.8 = (f32[4,8]{1,0:T(4,128)S(1)}, f32[4,8]{1,0:T(4,128)S(1)}, u32[]{:S(2)}, u32[]{:S(2)}) collective-permute-start(f32[4,8]{1,0:T(4,128)S(1)} %add.151), channel_id=1, source_target_pairs={{0,8},{1,9},{2,10},{3,11},{4,12},{5,13},{6,14},{7,15},{8,0},{9,1},... | collective-permute-start | bytes 392 | tf_op jit(solution)/shard_map/ppermute | solution.py:94

commit v12 on v11

--- a/solution.py
+++ b/solution.py
@@ -262,7 +262,9 @@
 
     local = jnp.concatenate([cos_polar[None], azimuth[None], bond_class.astype(jnp.float32)], 0)
 
-    pieces = [shifted(local, "probe", k) for k in range(groups)]
+    dense = (slab_rows * block_y) % 128 == 0 and block_y < 128
+    packed = local.reshape(local.shape[:2] + (slab_rows * block_y // 128, 128)) if dense else local
+    pieces = [shifted(packed, "probe", k).reshape(local.shape) for k in range(groups)]
     rotated = jnp.concatenate(pieces, -1)
     full_y = jnp.roll(rotated, group * block_y, -1) if groups > 1 else rotated
 

time: 38.3 us -> 39.8 us (1.039)
  local copies, waits for them, and re-layouts: 2.81 us -> 4.46 us
    concatenate x0 -> x3, local copies, waits for them, and re-layouts: none -> 0.96 us  [shards(): jnp.concatenate([cos_polar[None], azimuth[None], bond_class.astype(jnp.fl...]
    unnamed x19, local copies, waits for them, and re-layouts: 2.11 us -> 2.7 us
  transfers between devices with their start and end apart: 9 -> 9, of which waited for: 9 -> 8; matrix products, arithmetic and copies ran while one was open for 12% -> 11% of each run, Pallas kernels for 0% -> 0%
where the time goes in v12:
time: 39.8 us; the launch traced here: 39.4 us
  waiting for transfers between devices  16.4 us (41%)
  starting transfers between devices  8.67 us (22%)
  other arithmetic  5.09 us (13%)
  local copies, waits for them, and re-layouts  4.46 us (11%)
  Pallas kernels  4.14 us (10%)
  between operations  0.72 us (2%)
    ppermute x4, waiting for transfers between devices, butterfly_sum(): lax.ppermute(value, axis, [(i, i ^ step) for i in range(size)])  10.4 us
    ppermute x5, starting transfers between devices, shifted(): lax.ppermute(array, axis, [(i, (i - shift) % size) for i in range(size)])  8.66 us
    ppermute x5, waiting for transfers between devices, shifted(): lax.ppermute(array, axis, [(i, (i - shift) % size) for i in range(size)])  5.92 us
    pallas_call x1, Pallas kernels, run_local(): pl.pallas_call(body, out_shape=(jax.ShapeDtypeStruct((3, depth, slab_rows...  4.14 us
    unnamed x19, local copies, waits for them, and re-layouts  2.7 us
    convert_element_type x1, other arithmetic, shards(): last = jnp.transpose(last, (4, 1, 2, 3, 0, 5)).astype(jnp.bfloat16)  1.04 us
    concatenate x3, local copies, waits for them, and re-layouts, shards(): jnp.concatenate([cos_polar[None], azimuth[None], bond_class.astype(jnp.fl...  0.96 us
    mul x1, other arithmetic, make_probes(): waves = jnp.stack([jnp.cos(angle) * ramp, jnp.sin(angle) * ramp], 1)  0.85 us
  transfers between devices with their start and end apart: 9, of which 8 were waited for; matrix products, arithmetic and copies ran while one was open for 11% of the time, Pallas kernels for 0%

profile of v12, /device:TPU:0, one launch (start us, length us, event | category | flops | bytes accessed | tf_op | source)
XLA Modules:
  0.0 39.4 jit_solution(14763798051091280493)
XLA Ops:
  0.6 0.8 %concatenate.19 = f32[1,4,2,128]{3,2,1,0:T(2,128)S(1)} reshape(f32[4,4,64]{2,1,0:T(4,128)} %param.5) | data formatting | bytes 8192 | tf_op jit(solution)/shard_map/concatenate | solution.py:263
  1.5 0.7 %convert_element_type.40 = f32[3,4,4,64]{3,2,1,0:T(4,128)S(1)} convert(s32[3,4,4,64]{3,2,1,0:T(4,128)} %param.7) | non-fusion elementwise | flops 3072 | bytes 24576 | tf_op jit(solution)/shard_map/convert_element_type | solution.py:263
  2.4 3.0 %collective-permute-start = (f32[5,4,2,128]{3,2,1,0:T(2,128)S(1)}, f32[5,4,2,128]{3,2,1,0:T(2,128)S(1)}, u32[]{:S(2)}, u32[]{:S(2)}) collective-permute-start(f32[5,4,2,128]{3,2,1,0:T(2,128)S(1)} %pad_maximum_fusion), channel_id=1, source_target_pairs={{0,16},{16,0},{1,17},{17,1},{2,18},{18,2},{3,19},{19,3},{4,20},{20... | collective-permute-start | bytes 61448 | tf_op jit(solution)/shard_map/ppermute | solution.py:25
  5.4 0.6 %copy-done.8 = s32[8,3]{0,1:T(4,128)S(1)} copy-done((s32[8,3]{0,1:T(4,128)S(1)}, s32[8,3]{0,1:T(4,128)}, u32[]{:S(2)}) %copy-start.8) | copy-done | bytes 120
  6.2 0.8 %cosine_multiply_fusion = (f32[8,1,4,12,128]{4,0,2,1,3:T(8,128)S(1)}, f32[8,1,4,12,128]{4,0,2,1,3:T(8,128)S(1)}) fusion(f32[12]{0:T(128)S(1)} %add_sqrt_fusion, f32[8,128]{1,0:T(8,128)S(1)} %fusion.12, f32[8,4,12]{0,1,2:T(4,128)S(1)} %broadcast_add_fusion), kind=kLoop, calls=%fused_computation.3 | loop fusion | flops 196608 | bytes 398896 | tf_op jit(solution)/shard_map/mul | solution.py:81
  7.2 0.6 %copy-done.5 = f32[4,4,64]{2,1,0:T(4,128)S(1)} copy-done((f32[4,4,64]{2,1,0:T(4,128)S(1)}, f32[4,4,64]{2,1,0:T(4,128)}, u32[]{:S(2)}) %copy-start.5) | copy-done | bytes 4120
  8.0 5.1 %collective-permute-start.4 = (f32[5,4,4,128]{3,2,1,0:T(4,128)S(1)}, f32[5,4,4,128]{3,2,1,0:T(4,128)S(1)}, u32[]{:S(2)}, u32[]{:S(2)}) collective-permute-start(f32[5,4,4,128]{3,2,1,0:T(4,128)S(1)} %fusion.4.refs_2_), channel_id=1, source_target_pairs={{0,14},{1,15},{2,0},{3,1},{4,2},{5,3},{6,4},{7,5},{8,6},{9,7},{10,... | collective-permute-start | bytes 122888 | tf_op jit(solution)/shard_map/ppermute | solution.py:25
  13.2 0.5 %collective-permute-start.2 = (f32[5,4,4,128]{3,2,1,0:T(4,128)S(1)}, f32[5,4,4,128]{3,2,1,0:T(4,128)S(1)}, u32[]{:S(2)}, u32[]{:S(2)}) collective-permute-start(f32[5,4,4,128]{3,2,1,0:T(4,128)S(1)} %fusion.4.refs_2_), channel_id=1, source_target_pairs={{0,1},{1,2},{2,3},{3,4},{4,5},{5,6},{6,7},{7,8},{8,9},{9,10},{10,1... | collective-permute-start | bytes 122888 | tf_op jit(solution)/shard_map/ppermute | solution.py:25
  13.7 0.8 %maximum_bitcast_fusion.refs_5_ = f32[12,2,4,8,128]{4,3,2,1,0:T(8,128)} fusion(f32[8,1,4,12,128]{4,0,2,1,3:T(8,128)S(1)} %get-tuple-element.13, f32[8,1,4,12,128]{4,0,2,1,3:T(8,128)S(1)} %get-tuple-element.12), kind=kLoop, calls=%fused_computation | loop fusion | flops 98304 | bytes 786432 | tf_op jit(solution)/shard_map/transpose | solution.py:280
  14.5 0.4 collective-permute-done.4.refs_4_
  14.8 0.4 collective-permute-done.3.refs_3_
  15.2 4.1 %collective-permute-done.2.refs_1_ = f32[5,4,4,128]{3,2,1,0:T(4,128)S(1)} collective-permute-done((f32[5,4,4,128]{3,2,1,0:T(4,128)S(1)}, f32[5,4,4,128]{3,2,1,0:T(4,128)S(1)}, u32[]{:S(2)}, u32[]{:S(2)}) %collective-permute-start.2) | collective-permute-done | bytes 40992 | tf_op jit(solution)/shard_map/ppermute | solution.py:25
  19.3 1.1 %collective-permute-done.1.refs_0_ = f32[5,4,4,128]{3,2,1,0:T(4,128)S(1)} collective-permute-done((f32[5,4,4,128]{3,2,1,0:T(4,128)S(1)}, f32[5,4,4,128]{3,2,1,0:T(4,128)S(1)}, u32[]{:S(2)}, u32[]{:S(2)}) %collective-permute-start.1) | collective-permute-done | bytes 40992 | tf_op jit(solution)/shard_map/ppermute | solution.py:25
  20.4 0.6 %copy-done.4 = f32[5,4,4,128]{3,2,1,0:T(4,128)} copy-done((f32[5,4,4,128]{3,2,1,0:T(4,128)}, f32[5,4,4,128]{3,2,1,0:T(4,128)S(1)}, u32[]{:S(2)}) %copy-start.4) | copy-done | bytes 40984
  21.0 4.1 %shard_map.76 = (f32[3,4,4,128]{3,2,1,0:T(4,128)}, f32[4,2,3,4,8,128]{5,4,3,2,1,0:T(8,128)}, f32[4,8]{1,0:T(4,128)}) custom-call(f32[5,4,4,128]{3,2,1,0:T(4,128)} %copy-done.4, f32[5,4,4,128]{3,2,1,0:T(4,128)} %copy-done.3, f32[5,4,4,128]{3,2,1,0:T(4,128)} %copy-done, f32[5,4,4,128]{3,2,1,0:T(4,128)} %copy-done.2, f32[5,4,4,128]{3,2,1,0:T(4,128)} %copy-done.1, ...), custom_call_target="tpu_custom_call" | custom-call | flops 14991360 | bytes 1032192 | tf_op jit(solution)/shard_map/pallas_call | solution.py:224
  25.1 1.4 %collective-permute-done.5 = f32[4,8]{1,0:T(4,128)S(1)} collective-permute-done((f32[4,8]{1,0:T(4,128)}, f32[4,8]{1,0:T(4,128)S(1)}, u32[]{:S(2)}, u32[]{:S(2)}) %collective-permute-start.5) | collective-permute-done | bytes 160 | tf_op jit(solution)/shard_map/ppermute | solution.py:94
  26.5 0.7 %add.149 = f32[4,8]{1,0:T(4,128)S(1)} add(f32[4,8]{1,0:T(4,128)} %get-tuple-element.8, f32[4,8]{1,0:T(4,128)S(1)} %collective-permute-done.5) | non-fusion elementwise | flops 32 | bytes 384 | tf_op jit(solution)/shard_map/add | solution.py:94
  27.2 3.6 %collective-permute-done.6 = f32[4,8]{1,0:T(4,128)S(1)} collective-permute-done((f32[4,8]{1,0:T(4,128)S(1)}, f32[4,8]{1,0:T(4,128)S(1)}, u32[]{:S(2)}, u32[]{:S(2)}) %collective-permute-start.6) | collective-permute-done | bytes 160 | tf_op jit(solution)/shard_map/ppermute | solution.py:94
  30.8 1.0 %convert_bitcast_fusion = bf16[8,2,3,4,4,128]{5,0,3,2,1,4:T(8,128)(2,1)S(1)} fusion(f32[4,2,3,4,8,128]{5,4,3,2,1,0:T(8,128)} %get-tuple-element.7), kind=kLoop, calls=%fused_computation.1 | loop fusion | flops 98304 | bytes 589824 | tf_op jit(solution)/shard_map/convert_element_type | solution.py:285
  31.8 2.5 %collective-permute-done.7 = f32[4,8]{1,0:T(4,128)S(1)} collective-permute-done((f32[4,8]{1,0:T(4,128)S(1)}, f32[4,8]{1,0:T(4,128)S(1)}, u32[]{:S(2)}, u32[]{:S(2)}) %collective-permute-start.7) | collective-permute-done | bytes 160 | tf_op jit(solution)/shard_map/ppermute | solution.py:94
  34.4 0.7 %constant_dynamic-slice_fusion = f32[3,4,4,64]{3,2,1,0:T(4,128)} fusion(f32[3,4,4,128]{3,2,1,0:T(4,128)S(1)} %copy-done.7, s32[]{:T(128)S(6)} %select_n.66), kind=kLoop, calls=%fused_computation.42 | loop fusion | bytes 24580 | tf_op jit(solution)/shard_map/dynamic_slice | solution.py:284
  35.1 0.8 %copy.8 = bf16[8,2,3,4,4,128]{5,4,3,2,1,0:T(4,128)(2,1)} copy(bf16[8,2,3,4,4,128]{5,0,3,2,1,4:T(8,128)(2,1)S(1)} %convert_bitcast_fusion) | data formatting | bytes 393216
  35.9 2.9 %collective-permute-done.8 = f32[4,8]{1,0:T(4,128)S(1)} collective-permute-done((f32[4,8]{1,0:T(4,128)S(1)}, f32[4,8]{1,0:T(4,128)S(1)}, u32[]{:S(2)}, u32[]{:S(2)}) %collective-permute-start.8) | collective-permute-done | bytes 160 | tf_op jit(solution)/shard_map/ppermute | solution.py:94
  38.8 0.6 %multiply_bitcast_fusion = f32[8,4]{0,1:T(4,128)} fusion(f32[4,8]{1,0:T(4,128)S(1)} %add.151, f32[4,8]{1,0:T(4,128)S(1)} %collective-permute-done.8), kind=kLoop, calls=%fused_computation.48 | loop fusion | flops 64 | bytes 384 | tf_op jit(solution)/shard_map/transpose | solution.py:287
  (36 shorter events, 0.8 us)
Async XLA Ops:
  0.6 0.8 %copy-start.6 = (f32[4,4,64]{2,1,0:T(4,128)S(1)}, f32[4,4,64]{2,1,0:T(4,128)}, u32[]{:S(2)}) copy-start(f32[4,4,64]{2,1,0:T(4,128)} %param.6) | copy-start | bytes 12292
  2.4 4.8 %collective-permute-start = (f32[5,4,2,128]{3,2,1,0:T(2,128)S(1)}, f32[5,4,2,128]{3,2,1,0:T(2,128)S(1)}, u32[]{:S(2)}, u32[]{:S(2)}) collective-permute-start(f32[5,4,2,128]{3,2,1,0:T(2,128)S(1)} %pad_maximum_fusion), channel_id=1, source_target_pairs={{0,16},{16,0},{1,17},{17,1},{2,18},{18,2},{3,19},{19,3},{4,20},{20... | collective-permute-start | bytes 61448 | tf_op jit(solution)/shard_map/ppermute | solution.py:25
  5.4 0.7 %copy-start.8 = (s32[8,3]{0,1:T(4,128)S(1)}, s32[8,3]{0,1:T(4,128)}, u32[]{:S(2)}) copy-start(s32[8,3]{0,1:T(4,128)} %param.9) | copy-start | bytes 292
  7.1 0.7 %copy-start.5 = (f32[4,4,64]{2,1,0:T(4,128)S(1)}, f32[4,4,64]{2,1,0:T(4,128)}, u32[]{:S(2)}) copy-start(f32[4,4,64]{2,1,0:T(4,128)} %param.5) | copy-start | bytes 12292
  8.0 6.4 %copy-start = (f32[5,4,4,128]{3,2,1,0:T(4,128)}, f32[5,4,4,128]{3,2,1,0:T(4,128)S(1)}, u32[]{:S(2)}) copy-start(f32[5,4,4,128]{3,2,1,0:T(4,128)S(1)} %fusion.4.refs_2_) | copy-start | bytes 122884
  8.0 6.8 %collective-permute-start.4 = (f32[5,4,4,128]{3,2,1,0:T(4,128)S(1)}, f32[5,4,4,128]{3,2,1,0:T(4,128)S(1)}, u32[]{:S(2)}, u32[]{:S(2)}) collective-permute-start(f32[5,4,4,128]{3,2,1,0:T(4,128)S(1)} %fusion.4.refs_2_), channel_id=1, source_target_pairs={{0,14},{1,15},{2,0},{3,1},{4,2},{5,3},{6,4},{7,5},{8,6},{9,7},{10,... | collective-permute-start | bytes 122888 | tf_op jit(solution)/shard_map/ppermute | solution.py:25
  13.2 2.1 %collective-permute-start.3 = (f32[5,4,4,128]{3,2,1,0:T(4,128)S(1)}, f32[5,4,4,128]{3,2,1,0:T(4,128)S(1)}, u32[]{:S(2)}, u32[]{:S(2)}) collective-permute-start(f32[5,4,4,128]{3,2,1,0:T(4,128)S(1)} %fusion.4.refs_2_), channel_id=1, source_target_pairs={{0,15},{1,0},{2,1},{3,2},{4,3},{5,4},{6,5},{7,6},{8,7},{9,8},{10,9... | collective-permute-start | bytes 122888 | tf_op jit(solution)/shard_map/ppermute | solution.py:25
  13.2 6.1 %collective-permute-start.2 = (f32[5,4,4,128]{3,2,1,0:T(4,128)S(1)}, f32[5,4,4,128]{3,2,1,0:T(4,128)S(1)}, u32[]{:S(2)}, u32[]{:S(2)}) collective-permute-start(f32[5,4,4,128]{3,2,1,0:T(4,128)S(1)} %fusion.4.refs_2_), channel_id=1, source_target_pairs={{0,1},{1,2},{2,3},{3,4},{4,5},{5,6},{6,7},{7,8},{8,9},{9,10},{10,1... | collective-permute-start | bytes 122888 | tf_op jit(solution)/shard_map/ppermute | solution.py:25
  13.7 6.7 %collective-permute-start.1 = (f32[5,4,4,128]{3,2,1,0:T(4,128)S(1)}, f32[5,4,4,128]{3,2,1,0:T(4,128)S(1)}, u32[]{:S(2)}, u32[]{:S(2)}) collective-permute-start(f32[5,4,4,128]{3,2,1,0:T(4,128)S(1)} %fusion.4.refs_2_), channel_id=1, source_target_pairs={{0,2},{1,3},{2,4},{3,5},{4,6},{5,7},{6,8},{7,9},{8,10},{9,11},{10,... | collective-permute-start | bytes 122888 | tf_op jit(solution)/shard_map/ppermute | solution.py:25
  14.8 5.5 %copy-start.1 = (f32[5,4,4,128]{3,2,1,0:T(4,128)}, f32[5,4,4,128]{3,2,1,0:T(4,128)S(1)}, u32[]{:S(2)}) copy-start(f32[5,4,4,128]{3,2,1,0:T(4,128)S(1)} %collective-permute-done.4.refs_4_) | copy-start | bytes 122884
  15.2 5.2 %copy-start.2 = (f32[5,4,4,128]{3,2,1,0:T(4,128)}, f32[5,4,4,128]{3,2,1,0:T(4,128)S(1)}, u32[]{:S(2)}) copy-start(f32[5,4,4,128]{3,2,1,0:T(4,128)S(1)} %collective-permute-done.3.refs_3_) | copy-start | bytes 122884
  19.3 1.1 %copy-start.3 = (f32[5,4,4,128]{3,2,1,0:T(4,128)}, f32[5,4,4,128]{3,2,1,0:T(4,128)S(1)}, u32[]{:S(2)}) copy-start(f32[5,4,4,128]{3,2,1,0:T(4,128)S(1)} %collective-permute-done.2.refs_1_) | copy-start | bytes 122884
  20.4 0.6 %copy-start.4 = (f32[5,4,4,128]{3,2,1,0:T(4,128)}, f32[5,4,4,128]{3,2,1,0:T(4,128)S(1)}, u32[]{:S(2)}) copy-start(f32[5,4,4,128]{3,2,1,0:T(4,128)S(1)} %collective-permute-done.1.refs_0_) | copy-start | bytes 122884
  25.1 1.4 %collective-permute-start.5 = (f32[4,8]{1,0:T(4,128)}, f32[4,8]{1,0:T(4,128)S(1)}, u32[]{:S(2)}, u32[]{:S(2)}) collective-permute-start(f32[4,8]{1,0:T(4,128)} %get-tuple-element.8), channel_id=1, source_target_pairs={{0,1},{1,0},{2,3},{3,2},{4,5},{5,4},{6,7},{7,6},{8,9},{9,8},{10,11... | collective-permute-start | bytes 392 | tf_op jit(solution)/shard_map/ppermute | solution.py:94
  27.2 3.6 %collective-permute-start.6 = (f32[4,8]{1,0:T(4,128)S(1)}, f32[4,8]{1,0:T(4,128)S(1)}, u32[]{:S(2)}, u32[]{:S(2)}) collective-permute-start(f32[4,8]{1,0:T(4,128)S(1)} %add.149), channel_id=1, source_target_pairs={{0,2},{1,3},{2,0},{3,1},{4,6},{5,7},{6,4},{7,5},{8,10},{9,11},{10,... | collective-permute-start | bytes 392 | tf_op jit(solution)/shard_map/ppermute | solution.py:94
  30.8 3.6 %collective-permute-start.7 = (f32[4,8]{1,0:T(4,128)S(1)}, f32[4,8]{1,0:T(4,128)S(1)}, u32[]{:S(2)}, u32[]{:S(2)}) collective-permute-start(f32[4,8]{1,0:T(4,128)S(1)} %add.150), channel_id=1, source_target_pairs={{0,4},{1,5},{2,6},{3,7},{4,0},{5,1},{6,2},{7,3},{8,12},{9,13},{10,... | collective-permute-start | bytes 392 | tf_op jit(solution)/shard_map/ppermute | solution.py:94
  30.8 3.6 %copy-start.7 = (f32[3,4,4,128]{3,2,1,0:T(4,128)S(1)}, f32[3,4,4,128]{3,2,1,0:T(4,128)}, u32[]{:S(2)}) copy-start(f32[3,4,4,128]{3,2,1,0:T(4,128)} %get-tuple-element.6) | copy-start | bytes 73732
  34.4 4.5 %collective-permute-start.8 = (f32[4,8]{1,0:T(4,128)S(1)}, f32[4,8]{1,0:T(4,128)S(1)}, u32[]{:S(2)}, u32[]{:S(2)}) collective-permute-start(f32[4,8]{1,0:T(4,128)S(1)} %add.151), channel_id=1, source_target_pairs={{0,8},{1,9},{2,10},{3,11},{4,12},{5,13},{6,14},{7,15},{8,0},{9,1},... | collective-permute-start | bytes 392 | tf_op jit(solution)/shard_map/ppermute | solution.py:94

commit v13 on v10

--- a/solution.py
+++ b/solution.py
@@ -143,17 +143,21 @@
     def from_window(a, b):
         return win[0:3, :, a:b, :]
 
-    def from_a(a, b):
-        return sweep_a[:, :, a - 1:b - 1, :]
-
-    rows_a = width - 2
-    sweep_a[:, :, 0:rows_a, :] = relax_update(win[0:3, :, 1:width - 1, :], field_rows(from_window, bond, 0, width))
-    rows_b = width - 4
-    sweep_b[:, :, 0:rows_b, :] = relax_update(sweep_a[:, :, 1:rows_a - 1, :], field_rows(from_a, bond, 1, width - 2))
-    relaxed_ref[...] = sweep_b[:, :, halo - SWEEPS:halo - SWEEPS + slab_rows, :]
-
     first = halo - CHEB
     n_start = slab_rows + 2 * CHEB
+    base_a = first
+
+    def from_a(a, b):
+        return sweep_a[:, :, a - base_a:b - base_a, :]
+
+    sweep_a[:, :, 0:n_start, :] = relax_update(
+        win[0:3, :, first:first + n_start, :], field_rows(from_window, bond, first - 1, n_start + 2)
+    )
+    sweep_b[:, :, 0:n_start - 2, :] = relax_update(
+        sweep_a[:, :, 1:n_start - 1, :], field_rows(from_a, bond, first, n_start)
+    )
+    base_b = first + 1
+    relaxed_ref[...] = sweep_b[:, :, halo - base_b:halo - base_b + slab_rows, :]
     lanes = win.shape[3]
     depth = win.shape[1]
     probes = start_ref.shape[3]
@@ -165,7 +169,7 @@
         bonds_zr[xr] = z_roll(site[2], 1)
     for xr in range(n_start - 2):
         w = first + 1 + xr
-        spins_b[xr] = jnp.broadcast_to(sweep_b[:, :, w - SWEEPS:w - SWEEPS + 1, :], (3, depth, probes, lanes))
+        spins_b[xr] = jnp.broadcast_to(sweep_b[:, :, w - base_b:w - base_b + 1, :], (3, depth, probes, lanes))
 
     polar = [polar_ref[j] for j in range(3)]
 

time: 38.3 us -> 38.2 us (level)
  no operation moved by 1% of the time
where the time goes in v13:
time: 38.2 us; the launch traced here: 37.9 us
  waiting for transfers between devices  16.5 us (43%)
  starting transfers between devices  8.67 us (23%)
  other arithmetic  5.12 us (13%)
  Pallas kernels  3.97 us (10%)
  local copies, waits for them, and re-layouts  2.89 us (8%)
  between operations  0.75 us (2%)
    ppermute x4, waiting for transfers between devices, butterfly_sum(): lax.ppermute(value, axis, [(i, i ^ step) for i in range(size)])  10.4 us
    ppermute x5, starting transfers between devices, shifted(): lax.ppermute(array, axis, [(i, (i - shift) % size) for i in range(size)])  8.66 us
    ppermute x5, waiting for transfers between devices, shifted(): lax.ppermute(array, axis, [(i, (i - shift) % size) for i in range(size)])  6.09 us
    pallas_call x1, Pallas kernels, run_local(): pl.pallas_call(body, out_shape=(jax.ShapeDtypeStruct((3, depth, slab_rows...  3.97 us
    unnamed x19, local copies, waits for them, and re-layouts  1.52 us
    convert_element_type x1, other arithmetic, shards(): last = jnp.transpose(last, (4, 1, 2, 3, 0, 5)).astype(jnp.bfloat16)  1.04 us
    mul x1, other arithmetic, make_probes(): waves = jnp.stack([jnp.cos(angle) * ramp, jnp.sin(angle) * ramp], 1)  0.85 us
    transpose x1, other arithmetic, shards(): waves = jnp.transpose(waves, (3, 1, 2, 0, 4))  0.78 us
  transfers between devices with their start and end apart: 9, of which 9 were waited for; matrix products, arithmetic and copies ran while one was open for 12% of the time, Pallas kernels for 0%

profile of v13, /device:TPU:0, one launch (start us, length us, event | category | flops | bytes accessed | tf_op | source)
XLA Modules:
  0.0 37.9 jit_solution(15956209442657878613)
XLA Ops:
  0.7 0.8 %convert_element_type.48 = f32[3,4,4,64]{3,2,1,0:T(4,128)S(1)} convert(s32[3,4,4,64]{3,2,1,0:T(4,128)} %param.7) | non-fusion elementwise | flops 3072 | bytes 24576 | tf_op jit(solution)/shard_map/convert_element_type | solution.py:261
  1.4 3.0 %collective-permute-start = (f32[5,4,4,64]{3,2,1,0:T(4,128)S(1)}, f32[5,4,4,64]{3,2,1,0:T(4,128)S(1)}, u32[]{:S(2)}, u32[]{:S(2)}) collective-permute-start(f32[5,4,4,64]{3,2,1,0:T(4,128)S(1)} %pad_maximum_fusion), channel_id=1, source_target_pairs={{0,16},{16,0},{1,17},{17,1},{2,18},{18,2},{3,19},{19,3},{4,20},{20... | collective-permute-start | bytes 61448 | tf_op jit(solution)/shard_map/ppermute | solution.py:25
  4.5 0.7 %copy-done.8 = s32[8,3]{0,1:T(4,128)S(1)} copy-done((s32[8,3]{0,1:T(4,128)S(1)}, s32[8,3]{0,1:T(4,128)}, u32[]{:S(2)}) %copy-start.8) | copy-done | bytes 120
  5.4 0.8 %cosine_multiply_fusion = (f32[8,1,4,12,128]{4,0,2,1,3:T(8,128)S(1)}, f32[8,1,4,12,128]{4,0,2,1,3:T(8,128)S(1)}) fusion(f32[12]{0:T(128)S(1)} %add_sqrt_fusion, f32[8,128]{1,0:T(8,128)S(1)} %fusion.12, f32[8,4,12]{0,1,2:T(4,128)S(1)} %broadcast_add_fusion), kind=kLoop, calls=%fused_computation.3 | loop fusion | flops 196608 | bytes 398896 | tf_op jit(solution)/shard_map/mul | solution.py:81
  6.2 0.2 collective-permute-done
  6.4 0.2 fusion.4.refs_2_
  6.6 5.1 %collective-permute-start.4 = (f32[5,4,4,128]{3,2,1,0:T(4,128)S(1)}, f32[5,4,4,128]{3,2,1,0:T(4,128)S(1)}, u32[]{:S(2)}, u32[]{:S(2)}) collective-permute-start(f32[5,4,4,128]{3,2,1,0:T(4,128)S(1)} %fusion.4.refs_2_), channel_id=1, source_target_pairs={{0,14},{1,15},{2,0},{3,1},{4,2},{5,3},{6,4},{7,5},{8,6},{9,7},{10,... | collective-permute-start | bytes 122888 | tf_op jit(solution)/shard_map/ppermute | solution.py:25
  11.8 0.5 %collective-permute-start.2 = (f32[5,4,4,128]{3,2,1,0:T(4,128)S(1)}, f32[5,4,4,128]{3,2,1,0:T(4,128)S(1)}, u32[]{:S(2)}, u32[]{:S(2)}) collective-permute-start(f32[5,4,4,128]{3,2,1,0:T(4,128)S(1)} %fusion.4.refs_2_), channel_id=1, source_target_pairs={{0,1},{1,2},{2,3},{3,4},{4,5},{5,6},{6,7},{7,8},{8,9},{9,10},{10,1... | collective-permute-start | bytes 122888 | tf_op jit(solution)/shard_map/ppermute | solution.py:25
  12.3 0.8 %maximum_bitcast_fusion.refs_5_ = f32[12,2,4,8,128]{4,3,2,1,0:T(8,128)} fusion(f32[8,1,4,12,128]{4,0,2,1,3:T(8,128)S(1)} %get-tuple-element.13, f32[8,1,4,12,128]{4,0,2,1,3:T(8,128)S(1)} %get-tuple-element.12), kind=kLoop, calls=%fused_computation | loop fusion | flops 98304 | bytes 786432 | tf_op jit(solution)/shard_map/transpose | solution.py:276
  13.1 0.4 collective-permute-done.4.refs_4_
  13.4 0.4 %collective-permute-done.3.refs_3_ = f32[5,4,4,128]{3,2,1,0:T(4,128)S(1)} collective-permute-done((f32[5,4,4,128]{3,2,1,0:T(4,128)S(1)}, f32[5,4,4,128]{3,2,1,0:T(4,128)S(1)}, u32[]{:S(2)}, u32[]{:S(2)}) %collective-permute-start.3) | collective-permute-done | bytes 40992 | tf_op jit(solution)/shard_map/ppermute | solution.py:25
  13.8 4.1 %collective-permute-done.2.refs_1_ = f32[5,4,4,128]{3,2,1,0:T(4,128)S(1)} collective-permute-done((f32[5,4,4,128]{3,2,1,0:T(4,128)S(1)}, f32[5,4,4,128]{3,2,1,0:T(4,128)S(1)}, u32[]{:S(2)}, u32[]{:S(2)}) %collective-permute-start.2) | collective-permute-done | bytes 40992 | tf_op jit(solution)/shard_map/ppermute | solution.py:25
  17.9 1.1 %collective-permute-done.1.refs_0_ = f32[5,4,4,128]{3,2,1,0:T(4,128)S(1)} collective-permute-done((f32[5,4,4,128]{3,2,1,0:T(4,128)S(1)}, f32[5,4,4,128]{3,2,1,0:T(4,128)S(1)}, u32[]{:S(2)}, u32[]{:S(2)}) %collective-permute-start.1) | collective-permute-done | bytes 40992 | tf_op jit(solution)/shard_map/ppermute | solution.py:25
  19.0 0.7 %broadcast_in_dim.8.refs_6_ = f32[3,8,128]{2,1,0:T(8,128)} broadcast(f32[3,8]{1,0:T(4,128)S(1)} %fusion.19), dimensions={0,1} | broadcast | bytes 12384 | tf_op jit(solution)/shard_map/broadcast_in_dim | solution.py:277
  19.7 4.0 %shard_map.76 = (f32[3,4,4,128]{3,2,1,0:T(4,128)}, f32[4,2,3,4,8,128]{5,4,3,2,1,0:T(8,128)}, f32[4,8]{1,0:T(4,128)}) custom-call(f32[5,4,4,128]{3,2,1,0:T(4,128)} %copy-done.4, f32[5,4,4,128]{3,2,1,0:T(4,128)} %copy-done.3, f32[5,4,4,128]{3,2,1,0:T(4,128)} %copy-done, f32[5,4,4,128]{3,2,1,0:T(4,128)} %copy-done.2, f32[5,4,4,128]{3,2,1,0:T(4,128)} %copy-done.1, ...), custom_call_target="tpu_custom_call" | custom-call | flops 14991360 | bytes 1032192 | tf_op jit(solution)/shard_map/pallas_call | solution.py:222
  23.6 1.4 %collective-permute-done.5 = f32[4,8]{1,0:T(4,128)S(1)} collective-permute-done((f32[4,8]{1,0:T(4,128)}, f32[4,8]{1,0:T(4,128)S(1)}, u32[]{:S(2)}, u32[]{:S(2)}) %collective-permute-start.5) | collective-permute-done | bytes 160 | tf_op jit(solution)/shard_map/ppermute | solution.py:94
  25.0 0.7 %add.172 = f32[4,8]{1,0:T(4,128)S(1)} add(f32[4,8]{1,0:T(4,128)} %get-tuple-element.8, f32[4,8]{1,0:T(4,128)S(1)} %collective-permute-done.5) | non-fusion elementwise | flops 32 | bytes 384 | tf_op jit(solution)/shard_map/add | solution.py:94
  25.7 3.6 %collective-permute-done.6 = f32[4,8]{1,0:T(4,128)S(1)} collective-permute-done((f32[4,8]{1,0:T(4,128)S(1)}, f32[4,8]{1,0:T(4,128)S(1)}, u32[]{:S(2)}, u32[]{:S(2)}) %collective-permute-start.6) | collective-permute-done | bytes 160 | tf_op jit(solution)/shard_map/ppermute | solution.py:94
  29.3 1.0 %convert_bitcast_fusion = bf16[8,2,3,4,4,128]{5,0,3,2,1,4:T(8,128)(2,1)S(1)} fusion(f32[4,2,3,4,8,128]{5,4,3,2,1,0:T(8,128)} %get-tuple-element.7), kind=kLoop, calls=%fused_computation.1 | loop fusion | flops 98304 | bytes 589824 | tf_op jit(solution)/shard_map/convert_element_type | solution.py:281
  30.3 2.5 %collective-permute-done.7 = f32[4,8]{1,0:T(4,128)S(1)} collective-permute-done((f32[4,8]{1,0:T(4,128)S(1)}, f32[4,8]{1,0:T(4,128)S(1)}, u32[]{:S(2)}, u32[]{:S(2)}) %collective-permute-start.7) | collective-permute-done | bytes 160 | tf_op jit(solution)/shard_map/ppermute | solution.py:94
  32.9 0.7 %constant_dynamic-slice_fusion = f32[3,4,4,64]{3,2,1,0:T(4,128)} fusion(f32[3,4,4,128]{3,2,1,0:T(4,128)S(1)} %copy-done.7, s32[]{:T(128)S(6)} %select_n.77), kind=kLoop, calls=%fused_computation.42 | loop fusion | bytes 24580 | tf_op jit(solution)/shard_map/dynamic_slice | solution.py:280
  33.6 0.8 %copy.8 = bf16[8,2,3,4,4,128]{5,4,3,2,1,0:T(4,128)(2,1)} copy(bf16[8,2,3,4,4,128]{5,0,3,2,1,4:T(8,128)(2,1)S(1)} %convert_bitcast_fusion) | data formatting | bytes 393216
  34.4 2.9 %collective-permute-done.8 = f32[4,8]{1,0:T(4,128)S(1)} collective-permute-done((f32[4,8]{1,0:T(4,128)S(1)}, f32[4,8]{1,0:T(4,128)S(1)}, u32[]{:S(2)}, u32[]{:S(2)}) %collective-permute-start.8) | collective-permute-done | bytes 160 | tf_op jit(solution)/shard_map/ppermute | solution.py:94
  37.3 0.6 %multiply_bitcast_fusion = f32[8,4]{0,1:T(4,128)} fusion(f32[4,8]{1,0:T(4,128)S(1)} %add.174, f32[4,8]{1,0:T(4,128)S(1)} %collective-permute-done.8), kind=kLoop, calls=%fused_computation.48 | loop fusion | flops 64 | bytes 384 | tf_op jit(solution)/shard_map/transpose | solution.py:283
  (35 shorter events, 0.3 us)
Async XLA Ops:
  0.6 0.8 %copy-start.5 = (f32[4,4,64]{2,1,0:T(4,128)S(1)}, f32[4,4,64]{2,1,0:T(4,128)}, u32[]{:S(2)}) copy-start(f32[4,4,64]{2,1,0:T(4,128)} %param.5) | copy-start | bytes 12292
  0.6 0.8 %copy-start.6 = (f32[4,4,64]{2,1,0:T(4,128)S(1)}, f32[4,4,64]{2,1,0:T(4,128)}, u32[]{:S(2)}) copy-start(f32[4,4,64]{2,1,0:T(4,128)} %param.6) | copy-start | bytes 12292
  1.4 5.0 %collective-permute-start = (f32[5,4,4,64]{3,2,1,0:T(4,128)S(1)}, f32[5,4,4,64]{3,2,1,0:T(4,128)S(1)}, u32[]{:S(2)}, u32[]{:S(2)}) collective-permute-start(f32[5,4,4,64]{3,2,1,0:T(4,128)S(1)} %pad_maximum_fusion), channel_id=1, source_target_pairs={{0,16},{16,0},{1,17},{17,1},{2,18},{18,2},{3,19},{19,3},{4,20},{20... | collective-permute-start | bytes 61448 | tf_op jit(solution)/shard_map/ppermute | solution.py:25
  4.5 0.7 %copy-start.8 = (s32[8,3]{0,1:T(4,128)S(1)}, s32[8,3]{0,1:T(4,128)}, u32[]{:S(2)}) copy-start(s32[8,3]{0,1:T(4,128)} %param.9) | copy-start | bytes 292
  6.6 6.4 %copy-start = (f32[5,4,4,128]{3,2,1,0:T(4,128)}, f32[5,4,4,128]{3,2,1,0:T(4,128)S(1)}, u32[]{:S(2)}) copy-start(f32[5,4,4,128]{3,2,1,0:T(4,128)S(1)} %fusion.4.refs_2_) | copy-start | bytes 122884
  6.6 6.8 %collective-permute-start.4 = (f32[5,4,4,128]{3,2,1,0:T(4,128)S(1)}, f32[5,4,4,128]{3,2,1,0:T(4,128)S(1)}, u32[]{:S(2)}, u32[]{:S(2)}) collective-permute-start(f32[5,4,4,128]{3,2,1,0:T(4,128)S(1)} %fusion.4.refs_2_), channel_id=1, source_target_pairs={{0,14},{1,15},{2,0},{3,1},{4,2},{5,3},{6,4},{7,5},{8,6},{9,7},{10,... | collective-permute-start | bytes 122888 | tf_op jit(solution)/shard_map/ppermute | solution.py:25
  11.8 2.1 %collective-permute-start.3 = (f32[5,4,4,128]{3,2,1,0:T(4,128)S(1)}, f32[5,4,4,128]{3,2,1,0:T(4,128)S(1)}, u32[]{:S(2)}, u32[]{:S(2)}) collective-permute-start(f32[5,4,4,128]{3,2,1,0:T(4,128)S(1)} %fusion.4.refs_2_), channel_id=1, source_target_pairs={{0,15},{1,0},{2,1},{3,2},{4,3},{5,4},{6,5},{7,6},{8,7},{9,8},{10,9... | collective-permute-start | bytes 122888 | tf_op jit(solution)/shard_map/ppermute | solution.py:25
  11.8 6.1 %collective-permute-start.2 = (f32[5,4,4,128]{3,2,1,0:T(4,128)S(1)}, f32[5,4,4,128]{3,2,1,0:T(4,128)S(1)}, u32[]{:S(2)}, u32[]{:S(2)}) collective-permute-start(f32[5,4,4,128]{3,2,1,0:T(4,128)S(1)} %fusion.4.refs_2_), channel_id=1, source_target_pairs={{0,1},{1,2},{2,3},{3,4},{4,5},{5,6},{6,7},{7,8},{8,9},{9,10},{10,1... | collective-permute-start | bytes 122888 | tf_op jit(solution)/shard_map/ppermute | solution.py:25
  12.3 6.7 %collective-permute-start.1 = (f32[5,4,4,128]{3,2,1,0:T(4,128)S(1)}, f32[5,4,4,128]{3,2,1,0:T(4,128)S(1)}, u32[]{:S(2)}, u32[]{:S(2)}) collective-permute-start(f32[5,4,4,128]{3,2,1,0:T(4,128)S(1)} %fusion.4.refs_2_), channel_id=1, source_target_pairs={{0,2},{1,3},{2,4},{3,5},{4,6},{5,7},{6,8},{7,9},{8,10},{9,11},{10,... | collective-permute-start | bytes 122888 | tf_op jit(solution)/shard_map/ppermute | solution.py:25
  13.4 6.2 %copy-start.1 = (f32[5,4,4,128]{3,2,1,0:T(4,128)}, f32[5,4,4,128]{3,2,1,0:T(4,128)S(1)}, u32[]{:S(2)}) copy-start(f32[5,4,4,128]{3,2,1,0:T(4,128)S(1)} %collective-permute-done.4.refs_4_) | copy-start | bytes 122884
  13.8 5.8 %copy-start.2 = (f32[5,4,4,128]{3,2,1,0:T(4,128)}, f32[5,4,4,128]{3,2,1,0:T(4,128)S(1)}, u32[]{:S(2)}) copy-start(f32[5,4,4,128]{3,2,1,0:T(4,128)S(1)} %collective-permute-done.3.refs_3_) | copy-start | bytes 122884
  17.9 1.8 %copy-start.3 = (f32[5,4,4,128]{3,2,1,0:T(4,128)}, f32[5,4,4,128]{3,2,1,0:T(4,128)S(1)}, u32[]{:S(2)}) copy-start(f32[5,4,4,128]{3,2,1,0:T(4,128)S(1)} %collective-permute-done.2.refs_1_) | copy-start | bytes 122884
  19.0 0.7 %copy-start.4 = (f32[5,4,4,128]{3,2,1,0:T(4,128)}, f32[5,4,4,128]{3,2,1,0:T(4,128)S(1)}, u32[]{:S(2)}) copy-start(f32[5,4,4,128]{3,2,1,0:T(4,128)S(1)} %collective-permute-done.1.refs_0_) | copy-start | bytes 122884
  23.6 1.4 %collective-permute-start.5 = (f32[4,8]{1,0:T(4,128)}, f32[4,8]{1,0:T(4,128)S(1)}, u32[]{:S(2)}, u32[]{:S(2)}) collective-permute-start(f32[4,8]{1,0:T(4,128)} %get-tuple-element.8), channel_id=1, source_target_pairs={{0,1},{1,0},{2,3},{3,2},{4,5},{5,4},{6,7},{7,6},{8,9},{9,8},{10,11... | collective-permute-start | bytes 392 | tf_op jit(solution)/shard_map/ppermute | solution.py:94
  25.7 3.6 %collective-permute-start.6 = (f32[4,8]{1,0:T(4,128)S(1)}, f32[4,8]{1,0:T(4,128)S(1)}, u32[]{:S(2)}, u32[]{:S(2)}) collective-permute-start(f32[4,8]{1,0:T(4,128)S(1)} %add.172), channel_id=1, source_target_pairs={{0,2},{1,3},{2,0},{3,1},{4,6},{5,7},{6,4},{7,5},{8,10},{9,11},{10,... | collective-permute-start | bytes 392 | tf_op jit(solution)/shard_map/ppermute | solution.py:94
  29.3 3.6 %collective-permute-start.7 = (f32[4,8]{1,0:T(4,128)S(1)}, f32[4,8]{1,0:T(4,128)S(1)}, u32[]{:S(2)}, u32[]{:S(2)}) collective-permute-start(f32[4,8]{1,0:T(4,128)S(1)} %add.173), channel_id=1, source_target_pairs={{0,4},{1,5},{2,6},{3,7},{4,0},{5,1},{6,2},{7,3},{8,12},{9,13},{10,... | collective-permute-start | bytes 392 | tf_op jit(solution)/shard_map/ppermute | solution.py:94
  29.3 3.6 %copy-start.7 = (f32[3,4,4,128]{3,2,1,0:T(4,128)S(1)}, f32[3,4,4,128]{3,2,1,0:T(4,128)}, u32[]{:S(2)}) copy-start(f32[3,4,4,128]{3,2,1,0:T(4,128)} %get-tuple-element.6) | copy-start | bytes 73732
  32.9 4.5 %collective-permute-start.8 = (f32[4,8]{1,0:T(4,128)S(1)}, f32[4,8]{1,0:T(4,128)S(1)}, u32[]{:S(2)}, u32[]{:S(2)}) collective-permute-start(f32[4,8]{1,0:T(4,128)S(1)} %add.174), channel_id=1, source_target_pairs={{0,8},{1,9},{2,10},{3,11},{4,12},{5,13},{6,14},{7,15},{8,0},{9,1},... | collective-permute-start | bytes 392 | tf_op jit(solution)/shard_map/ppermute | solution.py:94

commit v14 on v13

--- a/solution.py
+++ b/solution.py
@@ -194,12 +194,17 @@
             total = total + bonds_b[b, 1] * y_roll(centre, -1) + bonds_yr[b] * y_roll(centre, 1)
             total = total + bonds_b[b, 2] * z_roll(centre, -1) + bonds_zr[b] * z_roll(centre, 1)
             if order == 0:
-                total = jnp.stack([total * polar[j] for j in range(3)], 1)
-                advanced = cross_product(spins_b[b - 1], total) * -precess_scale
+                spin = spins_b[b - 1]
+                turn = (
+                    spin[1] * polar[2] - spin[2] * polar[1],
+                    spin[2] * polar[0] - spin[0] * polar[2],
+                    spin[0] * polar[1] - spin[1] * polar[0],
+                )
+                advanced = jnp.stack([total * turn[j] for j in range(3)], 1) * -precess_scale
             else:
                 previous = start_row(i + 2) if order == 1 else t_refs[order - 1][i + 2]
                 advanced = cross_product(spins_b[b - 1], total) * (-2.0 * precess_scale) - previous
-            target[i] = advanced
+            target[i] = advanced.astype(target.dtype)
             if halo <= w < halo + slab_rows:
                 squares = advanced * advanced
                 part = squares[0] + squares[1]
@@ -223,7 +228,7 @@
         body,
         out_shape=(
             jax.ShapeDtypeStruct((3, depth, slab_rows, lanes), jnp.float32),
-            jax.ShapeDtypeStruct((slab_rows,) + vec_shape, jnp.float32),
+            jax.ShapeDtypeStruct((slab_rows,) + vec_shape, jnp.bfloat16),
             jax.ShapeDtypeStruct((CHEB, probes), jnp.float32),
         ),
         in_specs=[pl.BlockSpec(memory_space=pltpu.VMEM)] * (len(slab_blocks) + 2)
@@ -278,7 +283,7 @@
 
     relaxed, last, sums = run_local(slab_blocks, waves, polar, exchange, halo, slab_rows)
     relaxed_own = lax.dynamic_slice_in_dim(relaxed, group * block_y, block_y, -1)
-    last = jnp.transpose(last, (4, 1, 2, 3, 0, 5)).astype(jnp.bfloat16)
+    last = jnp.transpose(last, (4, 1, 2, 3, 0, 5))
     moment_rows = butterfly_sum(sums, "space") / site_count
     return (relaxed_own, last, moment_rows.T)
 

time: 38.2 us -> 36.6 us (0.958)
  waiting for transfers between devices: 16.5 us -> 12 us
  starting transfers between devices: 8.67 us -> 10.8 us
  local copies, waits for them, and re-layouts: 2.89 us -> 4.56 us
  other arithmetic: 5.12 us -> 4.08 us
    ppermute x5, waiting for transfers between devices: 6.09 us -> 2.99 us  [shifted(): lax.ppermute(array, axis, [(i, (i - shift) % size) for i in range(size)])]
    ppermute x4, waiting for transfers between devices: 10.4 us -> 9.04 us  [butterfly_sum(): lax.ppermute(value, axis, [(i, i ^ step) for i in range(size)])]
    ppermute x5, starting transfers between devices: 8.66 us -> 9.95 us  [shifted(): lax.ppermute(array, axis, [(i, (i - shift) % size) for i in range(size)])]
    convert_element_type x1 -> x0, other arithmetic: 1.04 us -> none  [shards(): last = jnp.transpose(last, (4, 1, 2, 3, 0, 5)).astype(jnp.bfloat16)]
    unnamed x19 -> x17, local copies, waits for them, and re-layouts: 1.52 us -> 2.46 us
    ppermute x4, starting transfers between devices: 0.01 us -> 0.8 us  [butterfly_sum(): lax.ppermute(value, axis, [(i, i ^ step) for i in range(size)])]
    dynamic_slice x1, local copies, waits for them, and re-layouts: 0.7 us -> 1.43 us  [shards(): lax.dynamic_slice_in_dim(relaxed, group * block_y, block_y, -1)]
  transfers between devices with their start and end apart: 9 -> 9, of which waited for: 9 -> 7; matrix products, arithmetic and copies ran while one was open for 12% -> 14% of each run, Pallas kernels for 0% -> 0%
where the time goes in v14:
time: 36.6 us; the launch traced here: 36.2 us
  waiting for transfers between devices  12 us (33%)
  starting transfers between devices  10.8 us (30%)
  local copies, waits for them, and re-layouts  4.56 us (12%)
  Pallas kernels  4.09 us (11%)
  other arithmetic  4.08 us (11%)
  between operations  0.73 us (2%)
    ppermute x5, starting transfers between devices, shifted(): lax.ppermute(array, axis, [(i, (i - shift) % size) for i in range(size)])  9.95 us
    ppermute x4, waiting for transfers between devices, butterfly_sum(): lax.ppermute(value, axis, [(i, i ^ step) for i in range(size)])  9.04 us
    pallas_call x1, Pallas kernels, run_local(): pl.pallas_call(body, out_shape=(jax.ShapeDtypeStruct((3, depth, slab_rows...  4.09 us
    ppermute x5, waiting for transfers between devices, shifted(): lax.ppermute(array, axis, [(i, (i - shift) % size) for i in range(size)])  2.99 us
    unnamed x17, local copies, waits for them, and re-layouts  2.46 us
    dynamic_slice x1, local copies, waits for them, and re-layouts, shards(): lax.dynamic_slice_in_dim(relaxed, group * block_y, block_y, -1)  1.43 us
    mul x1, other arithmetic, make_probes(): waves = jnp.stack([jnp.cos(angle) * ramp, jnp.sin(angle) * ramp], 1)  0.85 us
    ppermute x4, starting transfers between devices, butterfly_sum(): lax.ppermute(value, axis, [(i, i ^ step) for i in range(size)])  0.8 us
  transfers between devices with their start and end apart: 9, of which 7 were waited for; matrix products, arithmetic and copies ran while one was open for 14% of the time, Pallas kernels for 0%

profile of v14, /device:TPU:0, one launch (start us, length us, event | category | flops | bytes accessed | tf_op | source)
XLA Modules:
  0.0 36.2 jit_solution(9304675834492895554)
XLA Ops:
  0.7 0.8 %convert_element_type.42 = f32[3,4,4,64]{3,2,1,0:T(4,128)S(1)} convert(s32[3,4,4,64]{3,2,1,0:T(4,128)} %param.7) | non-fusion elementwise | flops 3072 | bytes 24576 | tf_op jit(solution)/shard_map/convert_element_type | solution.py:266
  1.4 3.0 %collective-permute-start = (f32[5,4,4,64]{3,2,1,0:T(4,128)S(1)}, f32[5,4,4,64]{3,2,1,0:T(4,128)S(1)}, u32[]{:S(2)}, u32[]{:S(2)}) collective-permute-start(f32[5,4,4,64]{3,2,1,0:T(4,128)S(1)} %pad_maximum_fusion), channel_id=1, source_target_pairs={{0,16},{16,0},{1,17},{17,1},{2,18},{18,2},{3,19},{19,3},{4,20},{20... | collective-permute-start | bytes 61448 | tf_op jit(solution)/shard_map/ppermute | solution.py:25
  4.5 0.7 %copy-done.7 = s32[8,3]{0,1:T(4,128)S(1)} copy-done((s32[8,3]{0,1:T(4,128)S(1)}, s32[8,3]{0,1:T(4,128)}, u32[]{:S(2)}) %copy-start.7) | copy-done | bytes 120
  5.3 0.1 fusion.8
  5.4 0.8 %cosine_multiply_fusion = (f32[8,1,4,12,128]{4,0,2,1,3:T(8,128)S(1)}, f32[8,1,4,12,128]{4,0,2,1,3:T(8,128)S(1)}) fusion(f32[12]{0:T(128)S(1)} %add_sqrt_fusion, f32[8,128]{1,0:T(8,128)S(1)} %fusion.12, f32[8,4,12]{0,1,2:T(4,128)S(1)} %broadcast_add_fusion), kind=kLoop, calls=%fused_computation.2 | loop fusion | flops 196608 | bytes 398896 | tf_op jit(solution)/shard_map/mul | solution.py:81
  6.2 0.2 collective-permute-done
  6.4 0.2 fusion.4.refs_2_
  6.6 2.1 %collective-permute-start.1 = (f32[5,4,4,128]{3,2,1,0:T(4,128)S(1)}, f32[5,4,4,128]{3,2,1,0:T(4,128)S(1)}, u32[]{:S(2)}, u32[]{:S(2)}) collective-permute-start(f32[5,4,4,128]{3,2,1,0:T(4,128)S(1)} %fusion.4.refs_2_), channel_id=1, source_target_pairs={{0,2},{1,3},{2,4},{3,5},{4,6},{5,7},{6,8},{7,9},{8,10},{9,11},{10,... | collective-permute-start | bytes 122888 | tf_op jit(solution)/shard_map/ppermute | solution.py:25
  8.7 4.4 %collective-permute-start.3 = (f32[5,4,4,128]{3,2,1,0:T(4,128)S(1)}, f32[5,4,4,128]{3,2,1,0:T(4,128)S(1)}, u32[]{:S(2)}, u32[]{:S(2)}) collective-permute-start(f32[5,4,4,128]{3,2,1,0:T(4,128)S(1)} %fusion.4.refs_2_), channel_id=1, source_target_pairs={{0,15},{1,0},{2,1},{3,2},{4,3},{5,4},{6,5},{7,6},{8,7},{9,8},{10,9... | collective-permute-start | bytes 122888 | tf_op jit(solution)/shard_map/ppermute | solution.py:25
  13.2 0.4 %collective-permute-start.4 = (f32[5,4,4,128]{3,2,1,0:T(4,128)S(1)}, f32[5,4,4,128]{3,2,1,0:T(4,128)S(1)}, u32[]{:S(2)}, u32[]{:S(2)}) collective-permute-start(f32[5,4,4,128]{3,2,1,0:T(4,128)S(1)} %fusion.4.refs_2_), channel_id=1, source_target_pairs={{0,14},{1,15},{2,0},{3,1},{4,2},{5,3},{6,4},{7,5},{8,6},{9,7},{10,... | collective-permute-start | bytes 122888 | tf_op jit(solution)/shard_map/ppermute | solution.py:25
  13.6 0.8 %maximum_bitcast_fusion.refs_5_ = f32[12,2,4,8,128]{4,3,2,1,0:T(8,128)} fusion(f32[8,1,4,12,128]{4,0,2,1,3:T(8,128)S(1)} %get-tuple-element.13, f32[8,1,4,12,128]{4,0,2,1,3:T(8,128)S(1)} %get-tuple-element.12), kind=kLoop, calls=%fused_computation | loop fusion | flops 98304 | bytes 786432 | tf_op jit(solution)/shard_map/transpose | solution.py:281
  14.4 0.5 %collective-permute-done.2.refs_1_ = f32[5,4,4,128]{3,2,1,0:T(4,128)S(1)} collective-permute-done((f32[5,4,4,128]{3,2,1,0:T(4,128)S(1)}, f32[5,4,4,128]{3,2,1,0:T(4,128)S(1)}, u32[]{:S(2)}, u32[]{:S(2)}) %collective-permute-start.2) | collective-permute-done | bytes 40992 | tf_op jit(solution)/shard_map/ppermute | solution.py:25
  14.9 2.3 %collective-permute-done.4.refs_4_ = f32[5,4,4,128]{3,2,1,0:T(4,128)S(1)} collective-permute-done((f32[5,4,4,128]{3,2,1,0:T(4,128)S(1)}, f32[5,4,4,128]{3,2,1,0:T(4,128)S(1)}, u32[]{:S(2)}, u32[]{:S(2)}) %collective-permute-start.4) | collective-permute-done | bytes 40992 | tf_op jit(solution)/shard_map/ppermute | solution.py:25
  17.2 0.7 %broadcast_in_dim.8.refs_6_ = f32[3,8,128]{2,1,0:T(8,128)} broadcast(f32[3,8]{1,0:T(4,128)S(1)} %fusion.19), dimensions={0,1} | broadcast | bytes 12384 | tf_op jit(solution)/shard_map/broadcast_in_dim | solution.py:282
  17.9 4.1 %shard_map.76 = (f32[3,4,4,128]{3,2,1,0:T(4,128)}, bf16[4,2,3,4,8,128]{5,4,3,2,1,0:T(8,128)(2,1)}, f32[4,8]{1,0:T(4,128)}) custom-call(f32[5,4,4,128]{3,2,1,0:T(4,128)} %copy-done.1, f32[5,4,4,128]{3,2,1,0:T(4,128)} %copy-done.2, f32[5,4,4,128]{3,2,1,0:T(4,128)} %copy-done, f32[5,4,4,128]{3,2,1,0:T(4,128)} %copy-done.3, f32[5,4,4,128]{3,2,1,0:T(4,128)} %copy-done.4, ...), custom_call_target="tpu_custom_call" | custom-call | flops 14991360 | bytes 1032192 | tf_op jit(solution)/shard_map/pallas_call | solution.py:227
  21.9 1.4 %collective-permute-done.5 = f32[4,8]{1,0:T(4,128)S(1)} collective-permute-done((f32[4,8]{1,0:T(4,128)}, f32[4,8]{1,0:T(4,128)S(1)}, u32[]{:S(2)}, u32[]{:S(2)}) %collective-permute-start.5) | collective-permute-done | bytes 160 | tf_op jit(solution)/shard_map/ppermute | solution.py:94
  23.3 0.7 %add.172 = f32[4,8]{1,0:T(4,128)S(1)} add(f32[4,8]{1,0:T(4,128)} %get-tuple-element.8, f32[4,8]{1,0:T(4,128)S(1)} %collective-permute-done.5) | non-fusion elementwise | flops 32 | bytes 384 | tf_op jit(solution)/shard_map/add | solution.py:94
  24.0 3.6 %collective-permute-done.6 = f32[4,8]{1,0:T(4,128)S(1)} collective-permute-done((f32[4,8]{1,0:T(4,128)S(1)}, f32[4,8]{1,0:T(4,128)S(1)}, u32[]{:S(2)}, u32[]{:S(2)}) %collective-permute-start.6) | collective-permute-done | bytes 160 | tf_op jit(solution)/shard_map/ppermute | solution.py:94
  27.6 1.4 %constant_dynamic-slice_fusion = f32[3,4,4,64]{3,2,1,0:T(4,128)} fusion(f32[3,4,4,128]{3,2,1,0:T(4,128)} %get-tuple-element.6, s32[]{:T(128)S(6)} %select_n.77), kind=kLoop, calls=%fused_computation.41 | loop fusion | bytes 24580 | tf_op jit(solution)/shard_map/dynamic_slice | solution.py:285
  29.0 2.2 %collective-permute-done.7 = f32[4,8]{1,0:T(4,128)S(1)} collective-permute-done((f32[4,8]{1,0:T(4,128)S(1)}, f32[4,8]{1,0:T(4,128)S(1)}, u32[]{:S(2)}, u32[]{:S(2)}) %collective-permute-start.7) | collective-permute-done | bytes 160 | tf_op jit(solution)/shard_map/ppermute | solution.py:94
  31.2 0.8 %collective-permute-start.8 = (f32[4,8]{1,0:T(4,128)S(1)}, f32[4,8]{1,0:T(4,128)S(1)}, u32[]{:S(2)}, u32[]{:S(2)}) collective-permute-start(f32[4,8]{1,0:T(4,128)S(1)} %add.174), channel_id=1, source_target_pairs={{0,8},{1,9},{2,10},{3,11},{4,12},{5,13},{6,14},{7,15},{8,0},{9,1},... | collective-permute-start | bytes 392 | tf_op jit(solution)/shard_map/ppermute | solution.py:94
  32.0 1.8 %copy.8 = bf16[8,2,3,4,4,128]{5,4,3,2,1,0:T(4,128)(2,1)} copy(bf16[8,2,3,4,4,128]{5,0,3,2,1,4:T(8,128)(2,1)} %bitcast.13) | data formatting | bytes 393216
  33.7 1.9 %collective-permute-done.8 = f32[4,8]{1,0:T(4,128)S(1)} collective-permute-done((f32[4,8]{1,0:T(4,128)S(1)}, f32[4,8]{1,0:T(4,128)S(1)}, u32[]{:S(2)}, u32[]{:S(2)}) %collective-permute-start.8) | collective-permute-done | bytes 160 | tf_op jit(solution)/shard_map/ppermute | solution.py:94
  35.7 0.6 %multiply_bitcast_fusion = f32[8,4]{0,1:T(4,128)} fusion(f32[4,8]{1,0:T(4,128)S(1)} %add.174, f32[4,8]{1,0:T(4,128)S(1)} %collective-permute-done.8), kind=kLoop, calls=%fused_computation.47 | loop fusion | flops 64 | bytes 384 | tf_op jit(solution)/shard_map/transpose | solution.py:288
  (32 shorter events, 0.2 us)
Async XLA Ops:
  0.6 0.8 %copy-start.5 = (f32[4,4,64]{2,1,0:T(4,128)S(1)}, f32[4,4,64]{2,1,0:T(4,128)}, u32[]{:S(2)}) copy-start(f32[4,4,64]{2,1,0:T(4,128)} %param.5) | copy-start | bytes 12292
  0.6 0.8 %copy-start.6 = (f32[4,4,64]{2,1,0:T(4,128)S(1)}, f32[4,4,64]{2,1,0:T(4,128)}, u32[]{:S(2)}) copy-start(f32[4,4,64]{2,1,0:T(4,128)} %param.6) | copy-start | bytes 12292
  1.4 5.0 %collective-permute-start = (f32[5,4,4,64]{3,2,1,0:T(4,128)S(1)}, f32[5,4,4,64]{3,2,1,0:T(4,128)S(1)}, u32[]{:S(2)}, u32[]{:S(2)}) collective-permute-start(f32[5,4,4,64]{3,2,1,0:T(4,128)S(1)} %pad_maximum_fusion), channel_id=1, source_target_pairs={{0,16},{16,0},{1,17},{17,1},{2,18},{18,2},{3,19},{19,3},{4,20},{20... | collective-permute-start | bytes 61448 | tf_op jit(solution)/shard_map/ppermute | solution.py:25
  4.5 0.7 %copy-start.7 = (s32[8,3]{0,1:T(4,128)S(1)}, s32[8,3]{0,1:T(4,128)}, u32[]{:S(2)}) copy-start(s32[8,3]{0,1:T(4,128)} %param.9) | copy-start | bytes 292
  6.6 7.7 %copy-start = (f32[5,4,4,128]{3,2,1,0:T(4,128)}, f32[5,4,4,128]{3,2,1,0:T(4,128)S(1)}, u32[]{:S(2)}) copy-start(f32[5,4,4,128]{3,2,1,0:T(4,128)S(1)} %fusion.4.refs_2_) | copy-start | bytes 122884
  6.6 7.7 %collective-permute-start.1 = (f32[5,4,4,128]{3,2,1,0:T(4,128)S(1)}, f32[5,4,4,128]{3,2,1,0:T(4,128)S(1)}, u32[]{:S(2)}, u32[]{:S(2)}) collective-permute-start(f32[5,4,4,128]{3,2,1,0:T(4,128)S(1)} %fusion.4.refs_2_), channel_id=1, source_target_pairs={{0,2},{1,3},{2,4},{3,5},{4,6},{5,7},{6,8},{7,9},{8,10},{9,11},{10,... | collective-permute-start | bytes 122888 | tf_op jit(solution)/shard_map/ppermute | solution.py:25
  8.7 6.1 %collective-permute-start.2 = (f32[5,4,4,128]{3,2,1,0:T(4,128)S(1)}, f32[5,4,4,128]{3,2,1,0:T(4,128)S(1)}, u32[]{:S(2)}, u32[]{:S(2)}) collective-permute-start(f32[5,4,4,128]{3,2,1,0:T(4,128)S(1)} %fusion.4.refs_2_), channel_id=1, source_target_pairs={{0,1},{1,2},{2,3},{3,4},{4,5},{5,6},{6,7},{7,8},{8,9},{9,10},{10,1... | collective-permute-start | bytes 122888 | tf_op jit(solution)/shard_map/ppermute | solution.py:25
  8.7 6.1 %collective-permute-start.3 = (f32[5,4,4,128]{3,2,1,0:T(4,128)S(1)}, f32[5,4,4,128]{3,2,1,0:T(4,128)S(1)}, u32[]{:S(2)}, u32[]{:S(2)}) collective-permute-start(f32[5,4,4,128]{3,2,1,0:T(4,128)S(1)} %fusion.4.refs_2_), channel_id=1, source_target_pairs={{0,15},{1,0},{2,1},{3,2},{4,3},{5,4},{6,5},{7,6},{8,7},{9,8},{10,9... | collective-permute-start | bytes 122888 | tf_op jit(solution)/shard_map/ppermute | solution.py:25
  13.2 4.0 %collective-permute-start.4 = (f32[5,4,4,128]{3,2,1,0:T(4,128)S(1)}, f32[5,4,4,128]{3,2,1,0:T(4,128)S(1)}, u32[]{:S(2)}, u32[]{:S(2)}) collective-permute-start(f32[5,4,4,128]{3,2,1,0:T(4,128)S(1)} %fusion.4.refs_2_), channel_id=1, source_target_pairs={{0,14},{1,15},{2,0},{3,1},{4,2},{5,3},{6,4},{7,5},{8,6},{9,7},{10,... | collective-permute-start | bytes 122888 | tf_op jit(solution)/shard_map/ppermute | solution.py:25
  14.4 3.5 %copy-start.1 = (f32[5,4,4,128]{3,2,1,0:T(4,128)}, f32[5,4,4,128]{3,2,1,0:T(4,128)S(1)}, u32[]{:S(2)}) copy-start(f32[5,4,4,128]{3,2,1,0:T(4,128)S(1)} %collective-permute-done.1.refs_0_) | copy-start | bytes 122884
  14.8 3.0 %copy-start.2 = (f32[5,4,4,128]{3,2,1,0:T(4,128)}, f32[5,4,4,128]{3,2,1,0:T(4,128)S(1)}, u32[]{:S(2)}) copy-start(f32[5,4,4,128]{3,2,1,0:T(4,128)S(1)} %collective-permute-done.2.refs_1_) | copy-start | bytes 122884
  14.9 3.0 %copy-start.3 = (f32[5,4,4,128]{3,2,1,0:T(4,128)}, f32[5,4,4,128]{3,2,1,0:T(4,128)S(1)}, u32[]{:S(2)}) copy-start(f32[5,4,4,128]{3,2,1,0:T(4,128)S(1)} %collective-permute-done.3.refs_3_) | copy-start | bytes 122884
  17.2 0.7 %copy-start.4 = (f32[5,4,4,128]{3,2,1,0:T(4,128)}, f32[5,4,4,128]{3,2,1,0:T(4,128)S(1)}, u32[]{:S(2)}) copy-start(f32[5,4,4,128]{3,2,1,0:T(4,128)S(1)} %collective-permute-done.4.refs_4_) | copy-start | bytes 122884
  21.9 1.4 %collective-permute-start.5 = (f32[4,8]{1,0:T(4,128)}, f32[4,8]{1,0:T(4,128)S(1)}, u32[]{:S(2)}, u32[]{:S(2)}) collective-permute-start(f32[4,8]{1,0:T(4,128)} %get-tuple-element.8), channel_id=1, source_target_pairs={{0,1},{1,0},{2,3},{3,2},{4,5},{5,4},{6,7},{7,6},{8,9},{9,8},{10,11... | collective-permute-start | bytes 392 | tf_op jit(solution)/shard_map/ppermute | solution.py:94
  24.0 3.6 %collective-permute-start.6 = (f32[4,8]{1,0:T(4,128)S(1)}, f32[4,8]{1,0:T(4,128)S(1)}, u32[]{:S(2)}, u32[]{:S(2)}) collective-permute-start(f32[4,8]{1,0:T(4,128)S(1)} %add.172), channel_id=1, source_target_pairs={{0,2},{1,3},{2,0},{3,1},{4,6},{5,7},{6,4},{7,5},{8,10},{9,11},{10,... | collective-permute-start | bytes 392 | tf_op jit(solution)/shard_map/ppermute | solution.py:94
  27.6 3.6 %collective-permute-start.7 = (f32[4,8]{1,0:T(4,128)S(1)}, f32[4,8]{1,0:T(4,128)S(1)}, u32[]{:S(2)}, u32[]{:S(2)}) collective-permute-start(f32[4,8]{1,0:T(4,128)S(1)} %add.173), channel_id=1, source_target_pairs={{0,4},{1,5},{2,6},{3,7},{4,0},{5,1},{6,2},{7,3},{8,12},{9,13},{10,... | collective-permute-start | bytes 392 | tf_op jit(solution)/shard_map/ppermute | solution.py:94
  31.2 4.5 %collective-permute-start.8 = (f32[4,8]{1,0:T(4,128)S(1)}, f32[4,8]{1,0:T(4,128)S(1)}, u32[]{:S(2)}, u32[]{:S(2)}) collective-permute-start(f32[4,8]{1,0:T(4,128)S(1)} %add.174), channel_id=1, source_target_pairs={{0,8},{1,9},{2,10},{3,11},{4,12},{5,13},{6,14},{7,15},{8,0},{9,1},... | collective-permute-start | bytes 392 | tf_op jit(solution)/shard_map/ppermute | solution.py:94

commit v15 on v14

--- a/solution.py
+++ b/solution.py
@@ -171,7 +171,13 @@
         w = first + 1 + xr
         spins_b[xr] = jnp.broadcast_to(sweep_b[:, :, w - base_b:w - base_b + 1, :], (3, depth, probes, lanes))
 
-    polar = [polar_ref[j] for j in range(3)]
+    sublane = lax.broadcasted_iota(jnp.int32, (probes, lanes), 0)
+    local_comp = jnp.zeros((probes, lanes), jnp.int32)
+    for p in range(probes):
+        local_comp = jnp.where(sublane == p, p % 3, local_comp)
+    comp = local_comp + polar_ref[0] % 3
+    comp = jnp.where(comp >= 3, comp - 3, comp)
+    polar = [jnp.where(comp == j, 1.0, 0.0).astype(jnp.float32) for j in range(3)]
 
     def start_row(i):
         wave = start_ref[i]
@@ -231,8 +237,8 @@
             jax.ShapeDtypeStruct((slab_rows,) + vec_shape, jnp.bfloat16),
             jax.ShapeDtypeStruct((CHEB, probes), jnp.float32),
         ),
-        in_specs=[pl.BlockSpec(memory_space=pltpu.VMEM)] * (len(slab_blocks) + 2)
-        + [pl.BlockSpec(memory_space=pltpu.SMEM)],
+        in_specs=[pl.BlockSpec(memory_space=pltpu.VMEM)] * (len(slab_blocks) + 1)
+        + [pl.BlockSpec(memory_space=pltpu.SMEM)] * 2,
         out_specs=[pl.BlockSpec(memory_space=pltpu.VMEM)] * 3,
         scratch_shapes=[
             pltpu.VMEM((6, depth, width, lanes), jnp.float32),
@@ -279,9 +285,9 @@
     probe_ids = group * group_size + jnp.arange(group_size, dtype=jnp.int32)
     waves, polar = make_probes(probe_wave, probe_ids, x_coords, y_coords, total_x, total_y, LZ)
     waves = jnp.transpose(waves, (3, 1, 2, 0, 4))
-    polar = jnp.broadcast_to(polar.T[:, :, None], (3, group_size, total_y))
-
-    relaxed, last, sums = run_local(slab_blocks, waves, polar, exchange, halo, slab_rows)
+    first_id = (group * group_size).astype(jnp.int32).reshape(1)
+
+    relaxed, last, sums = run_local(slab_blocks, waves, first_id, exchange, halo, slab_rows)
     relaxed_own = lax.dynamic_slice_in_dim(relaxed, group * block_y, block_y, -1)
     last = jnp.transpose(last, (4, 1, 2, 3, 0, 5))
     moment_rows = butterfly_sum(sums, "space") / site_count

time: 36.6 us -> 38.4 us (1.049)
  waiting for transfers between devices: 12 us -> 16 us
  starting transfers between devices: 10.8 us -> 8.67 us
    ppermute x5, waiting for transfers between devices: 2.99 us -> 6.15 us  [shifted(): lax.ppermute(array, axis, [(i, (i - shift) % size) for i in range(size)])]
    ppermute x5, starting transfers between devices: 9.95 us -> 8.66 us  [shifted(): lax.ppermute(array, axis, [(i, (i - shift) % size) for i in range(size)])]
    ppermute x4, starting transfers between devices: 0.8 us -> 0.01 us  [butterfly_sum(): lax.ppermute(value, axis, [(i, i ^ step) for i in range(size)])]
    ppermute x4, waiting for transfers between devices: 9.04 us -> 9.82 us  [butterfly_sum(): lax.ppermute(value, axis, [(i, i ^ step) for i in range(size)])]
    broadcast_in_dim x1 -> x0, local copies, waits for them, and re-layouts: 0.67 us -> none  [shards(): polar = jnp.broadcast_to(polar.T[:, :, None], (3, group_size, total_y))]
    unnamed x17, local copies, waits for them, and re-layouts: 2.46 us -> 3.03 us
  transfers between devices with their start and end apart: 9 -> 9, of which waited for: 7 -> 9; matrix products, arithmetic and copies ran while one was open for 14% -> 13% of each run, Pallas kernels for 0% -> 0%
where the time goes in v15:
time: 38.4 us; the launch traced here: 38.1 us
  waiting for transfers between devices  16 us (42%)
  starting transfers between devices  8.67 us (23%)
  local copies, waits for them, and re-layouts  4.46 us (12%)
  Pallas kernels  4.17 us (11%)
  other arithmetic  4.06 us (11%)
  between operations  0.72 us (2%)
    ppermute x4, waiting for transfers between devices, butterfly_sum(): lax.ppermute(value, axis, [(i, i ^ step) for i in range(size)])  9.82 us
    ppermute x5, starting transfers between devices, shifted(): lax.ppermute(array, axis, [(i, (i - shift) % size) for i in range(size)])  8.66 us
    ppermute x5, waiting for transfers between devices, shifted(): lax.ppermute(array, axis, [(i, (i - shift) % size) for i in range(size)])  6.15 us
    pallas_call x1, Pallas kernels, run_local(): pl.pallas_call(body, out_shape=(jax.ShapeDtypeStruct((3, depth, slab_rows...  4.17 us
    unnamed x17, local copies, waits for them, and re-layouts  3.03 us
    dynamic_slice x1, local copies, waits for them, and re-layouts, shards(): lax.dynamic_slice_in_dim(relaxed, group * block_y, block_y, -1)  1.43 us
    mul x1, other arithmetic, make_probes(): waves = jnp.stack([jnp.cos(angle) * ramp, jnp.sin(angle) * ramp], 1)  0.85 us
    transpose x1, other arithmetic, shards(): waves = jnp.transpose(waves, (3, 1, 2, 0, 4))  0.77 us
  transfers between devices with their start and end apart: 9, of which 9 were waited for; matrix products, arithmetic and copies ran while one was open for 13% of the time, Pallas kernels for 0%

profile of v15, /device:TPU:0, one launch (start us, length us, event | category | flops | bytes accessed | tf_op | source)
XLA Modules:
  0.0 38.1 jit_solution(10958433144017415358)
XLA Ops:
  0.7 0.8 %convert_element_type.34 = f32[3,4,4,64]{3,2,1,0:T(4,128)S(1)} convert(s32[3,4,4,64]{3,2,1,0:T(4,128)} %param.7) | non-fusion elementwise | flops 3072 | bytes 24576 | tf_op jit(solution)/shard_map/convert_element_type | solution.py:272
  1.4 3.0 %collective-permute-start = (f32[5,4,4,64]{3,2,1,0:T(4,128)S(1)}, f32[5,4,4,64]{3,2,1,0:T(4,128)S(1)}, u32[]{:S(2)}, u32[]{:S(2)}) collective-permute-start(f32[5,4,4,64]{3,2,1,0:T(4,128)S(1)} %pad_maximum_fusion), channel_id=1, source_target_pairs={{0,16},{16,0},{1,17},{17,1},{2,18},{18,2},{3,19},{19,3},{4,20},{20... | collective-permute-start | bytes 61448 | tf_op jit(solution)/shard_map/ppermute | solution.py:25
  4.5 0.6 %copy-done.7 = s32[8,3]{0,1:T(4,128)S(1)} copy-done((s32[8,3]{0,1:T(4,128)S(1)}, s32[8,3]{0,1:T(4,128)}, u32[]{:S(2)}) %copy-start.7) | copy-done | bytes 120
  5.1 0.1 fusion.12
  5.3 0.8 %cosine_multiply_fusion = (f32[8,1,4,12,128]{4,0,2,1,3:T(8,128)S(1)}, f32[8,1,4,12,128]{4,0,2,1,3:T(8,128)S(1)}) fusion(f32[12]{0:T(128)S(1)} %add_sqrt_fusion, f32[8,128]{1,0:T(8,128)S(1)} %fusion.12, f32[8,4,12]{0,1,2:T(4,128)S(1)} %broadcast_add_fusion), kind=kLoop, calls=%fused_computation.2 | loop fusion | flops 196608 | bytes 398896 | tf_op jit(solution)/shard_map/mul | solution.py:81
  6.2 0.2 collective-permute-done
  6.4 0.2 fusion.4.refs_2_
  6.6 5.1 %collective-permute-start.4 = (f32[5,4,4,128]{3,2,1,0:T(4,128)S(1)}, f32[5,4,4,128]{3,2,1,0:T(4,128)S(1)}, u32[]{:S(2)}, u32[]{:S(2)}) collective-permute-start(f32[5,4,4,128]{3,2,1,0:T(4,128)S(1)} %fusion.4.refs_2_), channel_id=1, source_target_pairs={{0,14},{1,15},{2,0},{3,1},{4,2},{5,3},{6,4},{7,5},{8,6},{9,7},{10,... | collective-permute-start | bytes 122888 | tf_op jit(solution)/shard_map/ppermute | solution.py:25
  11.8 0.5 %collective-permute-start.2 = (f32[5,4,4,128]{3,2,1,0:T(4,128)S(1)}, f32[5,4,4,128]{3,2,1,0:T(4,128)S(1)}, u32[]{:S(2)}, u32[]{:S(2)}) collective-permute-start(f32[5,4,4,128]{3,2,1,0:T(4,128)S(1)} %fusion.4.refs_2_), channel_id=1, source_target_pairs={{0,1},{1,2},{2,3},{3,4},{4,5},{5,6},{6,7},{7,8},{8,9},{9,10},{10,1... | collective-permute-start | bytes 122888 | tf_op jit(solution)/shard_map/ppermute | solution.py:25
  12.3 0.8 %maximum_bitcast_fusion.refs_5_ = f32[12,2,4,8,128]{4,3,2,1,0:T(8,128)} fusion(f32[8,1,4,12,128]{4,0,2,1,3:T(8,128)S(1)} %get-tuple-element.13, f32[8,1,4,12,128]{4,0,2,1,3:T(8,128)S(1)} %get-tuple-element.12), kind=kLoop, calls=%fused_computation | loop fusion | flops 98304 | bytes 786432 | tf_op jit(solution)/shard_map/transpose | solution.py:287
  13.0 0.4 %collective-permute-done.4.refs_4_ = f32[5,4,4,128]{3,2,1,0:T(4,128)S(1)} collective-permute-done((f32[5,4,4,128]{3,2,1,0:T(4,128)S(1)}, f32[5,4,4,128]{3,2,1,0:T(4,128)S(1)}, u32[]{:S(2)}, u32[]{:S(2)}) %collective-permute-start.4) | collective-permute-done | bytes 40992 | tf_op jit(solution)/shard_map/ppermute | solution.py:25
  13.4 0.4 %collective-permute-done.3.refs_3_ = f32[5,4,4,128]{3,2,1,0:T(4,128)S(1)} collective-permute-done((f32[5,4,4,128]{3,2,1,0:T(4,128)S(1)}, f32[5,4,4,128]{3,2,1,0:T(4,128)S(1)}, u32[]{:S(2)}, u32[]{:S(2)}) %collective-permute-start.3) | collective-permute-done | bytes 40992 | tf_op jit(solution)/shard_map/ppermute | solution.py:25
  13.8 4.1 %collective-permute-done.2.refs_1_ = f32[5,4,4,128]{3,2,1,0:T(4,128)S(1)} collective-permute-done((f32[5,4,4,128]{3,2,1,0:T(4,128)S(1)}, f32[5,4,4,128]{3,2,1,0:T(4,128)S(1)}, u32[]{:S(2)}, u32[]{:S(2)}) %collective-permute-start.2) | collective-permute-done | bytes 40992 | tf_op jit(solution)/shard_map/ppermute | solution.py:25
  17.9 1.1 %collective-permute-done.1.refs_0_ = f32[5,4,4,128]{3,2,1,0:T(4,128)S(1)} collective-permute-done((f32[5,4,4,128]{3,2,1,0:T(4,128)S(1)}, f32[5,4,4,128]{3,2,1,0:T(4,128)S(1)}, u32[]{:S(2)}, u32[]{:S(2)}) %collective-permute-start.1) | collective-permute-done | bytes 40992 | tf_op jit(solution)/shard_map/ppermute | solution.py:25
  19.0 0.6 %copy-done.4 = f32[5,4,4,128]{3,2,1,0:T(4,128)} copy-done((f32[5,4,4,128]{3,2,1,0:T(4,128)}, f32[5,4,4,128]{3,2,1,0:T(4,128)S(1)}, u32[]{:S(2)}) %copy-start.4) | copy-done | bytes 40984
  19.6 4.2 %shard_map.76 = (f32[3,4,4,128]{3,2,1,0:T(4,128)}, bf16[4,2,3,4,8,128]{5,4,3,2,1,0:T(8,128)(2,1)}, f32[4,8]{1,0:T(4,128)}) custom-call(f32[5,4,4,128]{3,2,1,0:T(4,128)} %copy-done.4, f32[5,4,4,128]{3,2,1,0:T(4,128)} %copy-done.3, f32[5,4,4,128]{3,2,1,0:T(4,128)} %copy-done, f32[5,4,4,128]{3,2,1,0:T(4,128)} %copy-done.2, f32[5,4,4,128]{3,2,1,0:T(4,128)} %copy-done.1, ...), custom_call_target="tpu_custom_call" | custom-call | flops 14991360 | bytes 1032192 | tf_op jit(solution)/shard_map/pallas_call | solution.py:233
  23.8 1.4 %collective-permute-done.5 = f32[4,8]{1,0:T(4,128)S(1)} collective-permute-done((f32[4,8]{1,0:T(4,128)}, f32[4,8]{1,0:T(4,128)S(1)}, u32[]{:S(2)}, u32[]{:S(2)}) %collective-permute-start.5) | collective-permute-done | bytes 160 | tf_op jit(solution)/shard_map/ppermute | solution.py:94
  25.1 0.7 %add.149 = f32[4,8]{1,0:T(4,128)S(1)} add(f32[4,8]{1,0:T(4,128)} %get-tuple-element.8, f32[4,8]{1,0:T(4,128)S(1)} %collective-permute-done.5) | non-fusion elementwise | flops 32 | bytes 384 | tf_op jit(solution)/shard_map/add | solution.py:94
  25.8 3.6 %collective-permute-done.6 = f32[4,8]{1,0:T(4,128)S(1)} collective-permute-done((f32[4,8]{1,0:T(4,128)S(1)}, f32[4,8]{1,0:T(4,128)S(1)}, u32[]{:S(2)}, u32[]{:S(2)}) %collective-permute-start.6) | collective-permute-done | bytes 160 | tf_op jit(solution)/shard_map/ppermute | solution.py:94
  29.4 1.4 %constant_dynamic-slice_fusion = f32[3,4,4,64]{3,2,1,0:T(4,128)} fusion(f32[3,4,4,128]{3,2,1,0:T(4,128)} %get-tuple-element.6, s32[]{:T(128)S(6)} %select_n.66), kind=kLoop, calls=%fused_computation.41 | loop fusion | bytes 24580 | tf_op jit(solution)/shard_map/dynamic_slice | solution.py:291
  30.8 2.2 %collective-permute-done.7 = f32[4,8]{1,0:T(4,128)S(1)} collective-permute-done((f32[4,8]{1,0:T(4,128)S(1)}, f32[4,8]{1,0:T(4,128)S(1)}, u32[]{:S(2)}, u32[]{:S(2)}) %collective-permute-start.7) | collective-permute-done | bytes 160 | tf_op jit(solution)/shard_map/ppermute | solution.py:94
  33.0 1.8 %copy.8 = bf16[8,2,3,4,4,128]{5,4,3,2,1,0:T(4,128)(2,1)} copy(bf16[8,2,3,4,4,128]{5,0,3,2,1,4:T(8,128)(2,1)} %bitcast.14) | data formatting | bytes 393216
  34.8 2.7 %collective-permute-done.8 = f32[4,8]{1,0:T(4,128)S(1)} collective-permute-done((f32[4,8]{1,0:T(4,128)S(1)}, f32[4,8]{1,0:T(4,128)S(1)}, u32[]{:S(2)}, u32[]{:S(2)}) %collective-permute-start.8) | collective-permute-done | bytes 160 | tf_op jit(solution)/shard_map/ppermute | solution.py:94
  37.5 0.6 %multiply_bitcast_fusion = f32[8,4]{0,1:T(4,128)} fusion(f32[4,8]{1,0:T(4,128)S(1)} %add.151, f32[4,8]{1,0:T(4,128)S(1)} %collective-permute-done.8), kind=kLoop, calls=%fused_computation.47 | loop fusion | flops 64 | bytes 384 | tf_op jit(solution)/shard_map/transpose | solution.py:294
  (29 shorter events, 0.2 us)
Async XLA Ops:
  0.6 0.8 %copy-start.5 = (f32[4,4,64]{2,1,0:T(4,128)S(1)}, f32[4,4,64]{2,1,0:T(4,128)}, u32[]{:S(2)}) copy-start(f32[4,4,64]{2,1,0:T(4,128)} %param.5) | copy-start | bytes 12292
  0.6 0.8 %copy-start.6 = (f32[4,4,64]{2,1,0:T(4,128)S(1)}, f32[4,4,64]{2,1,0:T(4,128)}, u32[]{:S(2)}) copy-start(f32[4,4,64]{2,1,0:T(4,128)} %param.6) | copy-start | bytes 12292
  1.4 5.0 %collective-permute-start = (f32[5,4,4,64]{3,2,1,0:T(4,128)S(1)}, f32[5,4,4,64]{3,2,1,0:T(4,128)S(1)}, u32[]{:S(2)}, u32[]{:S(2)}) collective-permute-start(f32[5,4,4,64]{3,2,1,0:T(4,128)S(1)} %pad_maximum_fusion), channel_id=1, source_target_pairs={{0,16},{16,0},{1,17},{17,1},{2,18},{18,2},{3,19},{19,3},{4,20},{20... | collective-permute-start | bytes 61448 | tf_op jit(solution)/shard_map/ppermute | solution.py:25
  4.4 0.7 %copy-start.7 = (s32[8,3]{0,1:T(4,128)S(1)}, s32[8,3]{0,1:T(4,128)}, u32[]{:S(2)}) copy-start(s32[8,3]{0,1:T(4,128)} %param.9) | copy-start | bytes 292
  6.6 6.4 %copy-start = (f32[5,4,4,128]{3,2,1,0:T(4,128)}, f32[5,4,4,128]{3,2,1,0:T(4,128)S(1)}, u32[]{:S(2)}) copy-start(f32[5,4,4,128]{3,2,1,0:T(4,128)S(1)} %fusion.4.refs_2_) | copy-start | bytes 122884
  6.6 6.8 %collective-permute-start.4 = (f32[5,4,4,128]{3,2,1,0:T(4,128)S(1)}, f32[5,4,4,128]{3,2,1,0:T(4,128)S(1)}, u32[]{:S(2)}, u32[]{:S(2)}) collective-permute-start(f32[5,4,4,128]{3,2,1,0:T(4,128)S(1)} %fusion.4.refs_2_), channel_id=1, source_target_pairs={{0,14},{1,15},{2,0},{3,1},{4,2},{5,3},{6,4},{7,5},{8,6},{9,7},{10,... | collective-permute-start | bytes 122888 | tf_op jit(solution)/shard_map/ppermute | solution.py:25
  11.8 2.1 %collective-permute-start.3 = (f32[5,4,4,128]{3,2,1,0:T(4,128)S(1)}, f32[5,4,4,128]{3,2,1,0:T(4,128)S(1)}, u32[]{:S(2)}, u32[]{:S(2)}) collective-permute-start(f32[5,4,4,128]{3,2,1,0:T(4,128)S(1)} %fusion.4.refs_2_), channel_id=1, source_target_pairs={{0,15},{1,0},{2,1},{3,2},{4,3},{5,4},{6,5},{7,6},{8,7},{9,8},{10,9... | collective-permute-start | bytes 122888 | tf_op jit(solution)/shard_map/ppermute | solution.py:25
  11.8 6.1 %collective-permute-start.2 = (f32[5,4,4,128]{3,2,1,0:T(4,128)S(1)}, f32[5,4,4,128]{3,2,1,0:T(4,128)S(1)}, u32[]{:S(2)}, u32[]{:S(2)}) collective-permute-start(f32[5,4,4,128]{3,2,1,0:T(4,128)S(1)} %fusion.4.refs_2_), channel_id=1, source_target_pairs={{0,1},{1,2},{2,3},{3,4},{4,5},{5,6},{6,7},{7,8},{8,9},{9,10},{10,1... | collective-permute-start | bytes 122888 | tf_op jit(solution)/shard_map/ppermute | solution.py:25
  12.3 6.7 %collective-permute-start.1 = (f32[5,4,4,128]{3,2,1,0:T(4,128)S(1)}, f32[5,4,4,128]{3,2,1,0:T(4,128)S(1)}, u32[]{:S(2)}, u32[]{:S(2)}) collective-permute-start(f32[5,4,4,128]{3,2,1,0:T(4,128)S(1)} %fusion.4.refs_2_), channel_id=1, source_target_pairs={{0,2},{1,3},{2,4},{3,5},{4,6},{5,7},{6,8},{7,9},{8,10},{9,11},{10,... | collective-permute-start | bytes 122888 | tf_op jit(solution)/shard_map/ppermute | solution.py:25
  13.4 5.5 %copy-start.1 = (f32[5,4,4,128]{3,2,1,0:T(4,128)}, f32[5,4,4,128]{3,2,1,0:T(4,128)S(1)}, u32[]{:S(2)}) copy-start(f32[5,4,4,128]{3,2,1,0:T(4,128)S(1)} %collective-permute-done.4.refs_4_) | copy-start | bytes 122884
  13.8 5.2 %copy-start.2 = (f32[5,4,4,128]{3,2,1,0:T(4,128)}, f32[5,4,4,128]{3,2,1,0:T(4,128)S(1)}, u32[]{:S(2)}) copy-start(f32[5,4,4,128]{3,2,1,0:T(4,128)S(1)} %collective-permute-done.3.refs_3_) | copy-start | bytes 122884
  17.9 1.1 %copy-start.3 = (f32[5,4,4,128]{3,2,1,0:T(4,128)}, f32[5,4,4,128]{3,2,1,0:T(4,128)S(1)}, u32[]{:S(2)}) copy-start(f32[5,4,4,128]{3,2,1,0:T(4,128)S(1)} %collective-permute-done.2.refs_1_) | copy-start | bytes 122884
  19.0 0.6 %copy-start.4 = (f32[5,4,4,128]{3,2,1,0:T(4,128)}, f32[5,4,4,128]{3,2,1,0:T(4,128)S(1)}, u32[]{:S(2)}) copy-start(f32[5,4,4,128]{3,2,1,0:T(4,128)S(1)} %collective-permute-done.1.refs_0_) | copy-start | bytes 122884
  23.8 1.4 %collective-permute-start.5 = (f32[4,8]{1,0:T(4,128)}, f32[4,8]{1,0:T(4,128)S(1)}, u32[]{:S(2)}, u32[]{:S(2)}) collective-permute-start(f32[4,8]{1,0:T(4,128)} %get-tuple-element.8), channel_id=1, source_target_pairs={{0,1},{1,0},{2,3},{3,2},{4,5},{5,4},{6,7},{7,6},{8,9},{9,8},{10,11... | collective-permute-start | bytes 392 | tf_op jit(solution)/shard_map/ppermute | solution.py:94
  25.8 3.6 %collective-permute-start.6 = (f32[4,8]{1,0:T(4,128)S(1)}, f32[4,8]{1,0:T(4,128)S(1)}, u32[]{:S(2)}, u32[]{:S(2)}) collective-permute-start(f32[4,8]{1,0:T(4,128)S(1)} %add.149), channel_id=1, source_target_pairs={{0,2},{1,3},{2,0},{3,1},{4,6},{5,7},{6,4},{7,5},{8,10},{9,11},{10,... | collective-permute-start | bytes 392 | tf_op jit(solution)/shard_map/ppermute | solution.py:94
  29.4 3.6 %collective-permute-start.7 = (f32[4,8]{1,0:T(4,128)S(1)}, f32[4,8]{1,0:T(4,128)S(1)}, u32[]{:S(2)}, u32[]{:S(2)}) collective-permute-start(f32[4,8]{1,0:T(4,128)S(1)} %add.150), channel_id=1, source_target_pairs={{0,4},{1,5},{2,6},{3,7},{4,0},{5,1},{6,2},{7,3},{8,12},{9,13},{10,... | collective-permute-start | bytes 392 | tf_op jit(solution)/shard_map/ppermute | solution.py:94
  33.0 4.5 %collective-permute-start.8 = (f32[4,8]{1,0:T(4,128)S(1)}, f32[4,8]{1,0:T(4,128)S(1)}, u32[]{:S(2)}, u32[]{:S(2)}) collective-permute-start(f32[4,8]{1,0:T(4,128)S(1)} %add.151), channel_id=1, source_target_pairs={{0,8},{1,9},{2,10},{3,11},{4,12},{5,13},{6,14},{7,15},{8,0},{9,1},... | collective-permute-start | bytes 392 | tf_op jit(solution)/shard_map/ppermute | solution.py:94

commit v16 on v14

--- a/solution.py
+++ b/solution.py
@@ -171,7 +171,13 @@
         w = first + 1 + xr
         spins_b[xr] = jnp.broadcast_to(sweep_b[:, :, w - base_b:w - base_b + 1, :], (3, depth, probes, lanes))
 
-    polar = [polar_ref[j] for j in range(3)]
+    sublane = lax.broadcasted_iota(jnp.int32, (probes, lanes), 0)
+    polar = []
+    for j in range(3):
+        factor = jnp.zeros((probes, lanes), jnp.float32)
+        for p in range(probes):
+            factor = jnp.where(sublane == p, polar_ref[j, p], factor)
+        polar.append(factor)
 
     def start_row(i):
         wave = start_ref[i]
@@ -231,8 +237,8 @@
             jax.ShapeDtypeStruct((slab_rows,) + vec_shape, jnp.bfloat16),
             jax.ShapeDtypeStruct((CHEB, probes), jnp.float32),
         ),
-        in_specs=[pl.BlockSpec(memory_space=pltpu.VMEM)] * (len(slab_blocks) + 2)
-        + [pl.BlockSpec(memory_space=pltpu.SMEM)],
+        in_specs=[pl.BlockSpec(memory_space=pltpu.VMEM)] * (len(slab_blocks) + 1)
+        + [pl.BlockSpec(memory_space=pltpu.SMEM)] * 2,
         out_specs=[pl.BlockSpec(memory_space=pltpu.VMEM)] * 3,
         scratch_shapes=[
             pltpu.VMEM((6, depth, width, lanes), jnp.float32),
@@ -279,7 +285,7 @@
     probe_ids = group * group_size + jnp.arange(group_size, dtype=jnp.int32)
     waves, polar = make_probes(probe_wave, probe_ids, x_coords, y_coords, total_x, total_y, LZ)
     waves = jnp.transpose(waves, (3, 1, 2, 0, 4))
-    polar = jnp.broadcast_to(polar.T[:, :, None], (3, group_size, total_y))
+    polar = polar.T
 
     relaxed, last, sums = run_local(slab_blocks, waves, polar, exchange, halo, slab_rows)
     relaxed_own = lax.dynamic_slice_in_dim(relaxed, group * block_y, block_y, -1)

time: 36.6 us -> 36.6 us (level)
  other arithmetic: 4.08 us -> 4.65 us
  starting transfers between devices: 10.8 us -> 10.4 us
    broadcast_in_dim x1 -> x0, local copies, waits for them, and re-layouts: 0.67 us -> none  [shards(): polar = jnp.broadcast_to(polar.T[:, :, None], (3, group_size, total_y))]
    unnamed x17, local copies, waits for them, and re-layouts: 2.46 us -> 3.06 us
    convert_element_type x1, other arithmetic: 0.01 us -> 0.58 us  [make_probes(): ((probe_ids % 3)[:, None] == jnp.arange(3, dtype=jnp.int32)[None, :]).ast...]
    ppermute x5, starting transfers between devices: 9.95 us -> 9.58 us  [shifted(): lax.ppermute(array, axis, [(i, (i - shift) % size) for i in range(size)])]
  transfers between devices with their start and end apart: 9 -> 9, of which waited for: 7 -> 6; matrix products, arithmetic and copies ran while one was open for 14% -> 15% of each run, Pallas kernels for 0% -> 0%
where the time goes in v16:
time: 36.6 us; the launch traced here: 36.3 us
  waiting for transfers between devices  11.9 us (33%)
  starting transfers between devices  10.4 us (28%)
  other arithmetic  4.65 us (13%)
  local copies, waits for them, and re-layouts  4.49 us (12%)
  Pallas kernels  4.17 us (11%)
  between operations  0.72 us (2%)
    ppermute x5, starting transfers between devices, shifted(): lax.ppermute(array, axis, [(i, (i - shift) % size) for i in range(size)])  9.58 us
    ppermute x4, waiting for transfers between devices, butterfly_sum(): lax.ppermute(value, axis, [(i, i ^ step) for i in range(size)])  9.04 us
    pallas_call x1, Pallas kernels, run_local(): pl.pallas_call(body, out_shape=(jax.ShapeDtypeStruct((3, depth, slab_rows...  4.17 us
    unnamed x17, local copies, waits for them, and re-layouts  3.06 us
    ppermute x5, waiting for transfers between devices, shifted(): lax.ppermute(array, axis, [(i, (i - shift) % size) for i in range(size)])  2.81 us
    dynamic_slice x1, local copies, waits for them, and re-layouts, shards(): lax.dynamic_slice_in_dim(relaxed, group * block_y, block_y, -1)  1.43 us
    mul x1, other arithmetic, make_probes(): waves = jnp.stack([jnp.cos(angle) * ramp, jnp.sin(angle) * ramp], 1)  0.85 us
    ppermute x4, starting transfers between devices, butterfly_sum(): lax.ppermute(value, axis, [(i, i ^ step) for i in range(size)])  0.8 us
  transfers between devices with their start and end apart: 9, of which 6 were waited for; matrix products, arithmetic and copies ran while one was open for 15% of the time, Pallas kernels for 0%

profile of v16, /device:TPU:0, one launch (start us, length us, event | category | flops | bytes accessed | tf_op | source)
XLA Modules:
  0.0 36.3 jit_solution(3793903617669485540)
XLA Ops:
  0.7 0.8 %convert_element_type.38 = f32[3,4,4,64]{3,2,1,0:T(4,128)S(1)} convert(s32[3,4,4,64]{3,2,1,0:T(4,128)} %param.7) | non-fusion elementwise | flops 3072 | bytes 24576 | tf_op jit(solution)/shard_map/convert_element_type | solution.py:272
  1.4 3.0 %collective-permute-start = (f32[5,4,4,64]{3,2,1,0:T(4,128)S(1)}, f32[5,4,4,64]{3,2,1,0:T(4,128)S(1)}, u32[]{:S(2)}, u32[]{:S(2)}) collective-permute-start(f32[5,4,4,64]{3,2,1,0:T(4,128)S(1)} %pad_maximum_fusion), channel_id=1, source_target_pairs={{0,16},{16,0},{1,17},{17,1},{2,18},{18,2},{3,19},{19,3},{4,20},{20... | collective-permute-start | bytes 61448 | tf_op jit(solution)/shard_map/ppermute | solution.py:25
  4.5 0.7 %copy-done.7 = s32[8,3]{0,1:T(4,128)S(1)} copy-done((s32[8,3]{0,1:T(4,128)S(1)}, s32[8,3]{0,1:T(4,128)}, u32[]{:S(2)}) %copy-start.7) | copy-done | bytes 120
  5.3 0.1 fusion.8
  5.4 0.8 %cosine_multiply_fusion = (f32[8,1,4,12,128]{4,0,2,1,3:T(8,128)S(1)}, f32[8,1,4,12,128]{4,0,2,1,3:T(8,128)S(1)}) fusion(f32[12]{0:T(128)S(1)} %add_sqrt_fusion, f32[8,128]{1,0:T(8,128)S(1)} %fusion.12, f32[8,4,12]{0,1,2:T(4,128)S(1)} %broadcast_add_fusion), kind=kLoop, calls=%fused_computation.2 | loop fusion | flops 196608 | bytes 398896 | tf_op jit(solution)/shard_map/mul | solution.py:81
  6.2 0.6 %fusion.19.refs_6_ = f32[3,8]{1,0:T(4,128)} fusion(s32[8]{0:T(128)S(1)} %and_select_fusion), kind=kLoop, calls=%fused_computation.49 | loop fusion | flops 48 | bytes 128 | tf_op jit(solution)/shard_map/convert_element_type | solution.py:82
  6.8 0.2 fusion.4.refs_2_
  7.0 1.7 %collective-permute-start.1 = (f32[5,4,4,128]{3,2,1,0:T(4,128)S(1)}, f32[5,4,4,128]{3,2,1,0:T(4,128)S(1)}, u32[]{:S(2)}, u32[]{:S(2)}) collective-permute-start(f32[5,4,4,128]{3,2,1,0:T(4,128)S(1)} %fusion.4.refs_2_), channel_id=1, source_target_pairs={{0,2},{1,3},{2,4},{3,5},{4,6},{5,7},{6,8},{7,9},{8,10},{9,11},{10,... | collective-permute-start | bytes 122888 | tf_op jit(solution)/shard_map/ppermute | solution.py:25
  8.7 4.4 %collective-permute-start.3 = (f32[5,4,4,128]{3,2,1,0:T(4,128)S(1)}, f32[5,4,4,128]{3,2,1,0:T(4,128)S(1)}, u32[]{:S(2)}, u32[]{:S(2)}) collective-permute-start(f32[5,4,4,128]{3,2,1,0:T(4,128)S(1)} %fusion.4.refs_2_), channel_id=1, source_target_pairs={{0,15},{1,0},{2,1},{3,2},{4,3},{5,4},{6,5},{7,6},{8,7},{9,8},{10,9... | collective-permute-start | bytes 122888 | tf_op jit(solution)/shard_map/ppermute | solution.py:25
  13.2 0.4 %collective-permute-start.4 = (f32[5,4,4,128]{3,2,1,0:T(4,128)S(1)}, f32[5,4,4,128]{3,2,1,0:T(4,128)S(1)}, u32[]{:S(2)}, u32[]{:S(2)}) collective-permute-start(f32[5,4,4,128]{3,2,1,0:T(4,128)S(1)} %fusion.4.refs_2_), channel_id=1, source_target_pairs={{0,14},{1,15},{2,0},{3,1},{4,2},{5,3},{6,4},{7,5},{8,6},{9,7},{10,... | collective-permute-start | bytes 122888 | tf_op jit(solution)/shard_map/ppermute | solution.py:25
  13.6 0.8 %maximum_bitcast_fusion.refs_5_ = f32[12,2,4,8,128]{4,3,2,1,0:T(8,128)} fusion(f32[8,1,4,12,128]{4,0,2,1,3:T(8,128)S(1)} %get-tuple-element.13, f32[8,1,4,12,128]{4,0,2,1,3:T(8,128)S(1)} %get-tuple-element.12), kind=kLoop, calls=%fused_computation | loop fusion | flops 98304 | bytes 786432 | tf_op jit(solution)/shard_map/transpose | solution.py:287
  14.4 0.5 %collective-permute-done.2.refs_1_ = f32[5,4,4,128]{3,2,1,0:T(4,128)S(1)} collective-permute-done((f32[5,4,4,128]{3,2,1,0:T(4,128)S(1)}, f32[5,4,4,128]{3,2,1,0:T(4,128)S(1)}, u32[]{:S(2)}, u32[]{:S(2)}) %collective-permute-start.2) | collective-permute-done | bytes 40992 | tf_op jit(solution)/shard_map/ppermute | solution.py:25
  14.9 2.3 %collective-permute-done.4.refs_4_ = f32[5,4,4,128]{3,2,1,0:T(4,128)S(1)} collective-permute-done((f32[5,4,4,128]{3,2,1,0:T(4,128)S(1)}, f32[5,4,4,128]{3,2,1,0:T(4,128)S(1)}, u32[]{:S(2)}, u32[]{:S(2)}) %collective-permute-start.4) | collective-permute-done | bytes 40992 | tf_op jit(solution)/shard_map/ppermute | solution.py:25
  17.2 0.6 %copy-done.4 = f32[5,4,4,128]{3,2,1,0:T(4,128)} copy-done((f32[5,4,4,128]{3,2,1,0:T(4,128)}, f32[5,4,4,128]{3,2,1,0:T(4,128)S(1)}, u32[]{:S(2)}) %copy-start.4) | copy-done | bytes 40984
  17.8 4.2 %shard_map.76 = (f32[3,4,4,128]{3,2,1,0:T(4,128)}, bf16[4,2,3,4,8,128]{5,4,3,2,1,0:T(8,128)(2,1)}, f32[4,8]{1,0:T(4,128)}) custom-call(f32[5,4,4,128]{3,2,1,0:T(4,128)} %copy-done.1, f32[5,4,4,128]{3,2,1,0:T(4,128)} %copy-done.2, f32[5,4,4,128]{3,2,1,0:T(4,128)} %copy-done, f32[5,4,4,128]{3,2,1,0:T(4,128)} %copy-done.3, f32[5,4,4,128]{3,2,1,0:T(4,128)} %copy-done.4, ...), custom_call_target="tpu_custom_call" | custom-call | flops 14991360 | bytes 1032192 | tf_op jit(solution)/shard_map/pallas_call | solution.py:233
  22.0 1.4 %collective-permute-done.5 = f32[4,8]{1,0:T(4,128)S(1)} collective-permute-done((f32[4,8]{1,0:T(4,128)}, f32[4,8]{1,0:T(4,128)S(1)}, u32[]{:S(2)}, u32[]{:S(2)}) %collective-permute-start.5) | collective-permute-done | bytes 160 | tf_op jit(solution)/shard_map/ppermute | solution.py:94
  23.3 0.7 %add.172 = f32[4,8]{1,0:T(4,128)S(1)} add(f32[4,8]{1,0:T(4,128)} %get-tuple-element.8, f32[4,8]{1,0:T(4,128)S(1)} %collective-permute-done.5) | non-fusion elementwise | flops 32 | bytes 384 | tf_op jit(solution)/shard_map/add | solution.py:94
  24.0 3.6 %collective-permute-done.6 = f32[4,8]{1,0:T(4,128)S(1)} collective-permute-done((f32[4,8]{1,0:T(4,128)S(1)}, f32[4,8]{1,0:T(4,128)S(1)}, u32[]{:S(2)}, u32[]{:S(2)}) %collective-permute-start.6) | collective-permute-done | bytes 160 | tf_op jit(solution)/shard_map/ppermute | solution.py:94
  27.6 1.4 %constant_dynamic-slice_fusion = f32[3,4,4,64]{3,2,1,0:T(4,128)} fusion(f32[3,4,4,128]{3,2,1,0:T(4,128)} %get-tuple-element.6, s32[]{:T(128)S(6)} %select_n.77), kind=kLoop, calls=%fused_computation.41 | loop fusion | bytes 24580 | tf_op jit(solution)/shard_map/dynamic_slice | solution.py:291
  29.0 2.2 %collective-permute-done.7 = f32[4,8]{1,0:T(4,128)S(1)} collective-permute-done((f32[4,8]{1,0:T(4,128)S(1)}, f32[4,8]{1,0:T(4,128)S(1)}, u32[]{:S(2)}, u32[]{:S(2)}) %collective-permute-start.7) | collective-permute-done | bytes 160 | tf_op jit(solution)/shard_map/ppermute | solution.py:94
  31.2 0.8 %collective-permute-start.8 = (f32[4,8]{1,0:T(4,128)S(1)}, f32[4,8]{1,0:T(4,128)S(1)}, u32[]{:S(2)}, u32[]{:S(2)}) collective-permute-start(f32[4,8]{1,0:T(4,128)S(1)} %add.174), channel_id=1, source_target_pairs={{0,8},{1,9},{2,10},{3,11},{4,12},{5,13},{6,14},{7,15},{8,0},{9,1},... | collective-permute-start | bytes 392 | tf_op jit(solution)/shard_map/ppermute | solution.py:94
  32.0 1.8 %copy.8 = bf16[8,2,3,4,4,128]{5,4,3,2,1,0:T(4,128)(2,1)} copy(bf16[8,2,3,4,4,128]{5,0,3,2,1,4:T(8,128)(2,1)} %bitcast.13) | data formatting | bytes 393216
  33.7 1.9 %collective-permute-done.8 = f32[4,8]{1,0:T(4,128)S(1)} collective-permute-done((f32[4,8]{1,0:T(4,128)S(1)}, f32[4,8]{1,0:T(4,128)S(1)}, u32[]{:S(2)}, u32[]{:S(2)}) %collective-permute-start.8) | collective-permute-done | bytes 160 | tf_op jit(solution)/shard_map/ppermute | solution.py:94
  35.7 0.6 %multiply_bitcast_fusion = f32[8,4]{0,1:T(4,128)} fusion(f32[4,8]{1,0:T(4,128)S(1)} %add.174, f32[4,8]{1,0:T(4,128)S(1)} %collective-permute-done.8), kind=kLoop, calls=%fused_computation.47 | loop fusion | flops 64 | bytes 384 | tf_op jit(solution)/shard_map/transpose | solution.py:294
  (31 shorter events, 0.2 us)
Async XLA Ops:
  0.6 0.8 %copy-start.5 = (f32[4,4,64]{2,1,0:T(4,128)S(1)}, f32[4,4,64]{2,1,0:T(4,128)}, u32[]{:S(2)}) copy-start(f32[4,4,64]{2,1,0:T(4,128)} %param.5) | copy-start | bytes 12292
  0.6 0.8 %copy-start.6 = (f32[4,4,64]{2,1,0:T(4,128)S(1)}, f32[4,4,64]{2,1,0:T(4,128)}, u32[]{:S(2)}) copy-start(f32[4,4,64]{2,1,0:T(4,128)} %param.6) | copy-start | bytes 12292
  1.4 5.4 %collective-permute-start = (f32[5,4,4,64]{3,2,1,0:T(4,128)S(1)}, f32[5,4,4,64]{3,2,1,0:T(4,128)S(1)}, u32[]{:S(2)}, u32[]{:S(2)}) collective-permute-start(f32[5,4,4,64]{3,2,1,0:T(4,128)S(1)} %pad_maximum_fusion), channel_id=1, source_target_pairs={{0,16},{16,0},{1,17},{17,1},{2,18},{18,2},{3,19},{19,3},{4,20},{20... | collective-permute-start | bytes 61448 | tf_op jit(solution)/shard_map/ppermute | solution.py:25
  4.5 0.7 %copy-start.7 = (s32[8,3]{0,1:T(4,128)S(1)}, s32[8,3]{0,1:T(4,128)}, u32[]{:S(2)}) copy-start(s32[8,3]{0,1:T(4,128)} %param.9) | copy-start | bytes 292
  7.0 7.4 %copy-start = (f32[5,4,4,128]{3,2,1,0:T(4,128)}, f32[5,4,4,128]{3,2,1,0:T(4,128)S(1)}, u32[]{:S(2)}) copy-start(f32[5,4,4,128]{3,2,1,0:T(4,128)S(1)} %fusion.4.refs_2_) | copy-start | bytes 122884
  7.0 7.4 %collective-permute-start.1 = (f32[5,4,4,128]{3,2,1,0:T(4,128)S(1)}, f32[5,4,4,128]{3,2,1,0:T(4,128)S(1)}, u32[]{:S(2)}, u32[]{:S(2)}) collective-permute-start(f32[5,4,4,128]{3,2,1,0:T(4,128)S(1)} %fusion.4.refs_2_), channel_id=1, source_target_pairs={{0,2},{1,3},{2,4},{3,5},{4,6},{5,7},{6,8},{7,9},{8,10},{9,11},{10,... | collective-permute-start | bytes 122888 | tf_op jit(solution)/shard_map/ppermute | solution.py:25
  8.7 6.1 %collective-permute-start.2 = (f32[5,4,4,128]{3,2,1,0:T(4,128)S(1)}, f32[5,4,4,128]{3,2,1,0:T(4,128)S(1)}, u32[]{:S(2)}, u32[]{:S(2)}) collective-permute-start(f32[5,4,4,128]{3,2,1,0:T(4,128)S(1)} %fusion.4.refs_2_), channel_id=1, source_target_pairs={{0,1},{1,2},{2,3},{3,4},{4,5},{5,6},{6,7},{7,8},{8,9},{9,10},{10,1... | collective-permute-start | bytes 122888 | tf_op jit(solution)/shard_map/ppermute | solution.py:25
  8.7 6.1 %collective-permute-start.3 = (f32[5,4,4,128]{3,2,1,0:T(4,128)S(1)}, f32[5,4,4,128]{3,2,1,0:T(4,128)S(1)}, u32[]{:S(2)}, u32[]{:S(2)}) collective-permute-start(f32[5,4,4,128]{3,2,1,0:T(4,128)S(1)} %fusion.4.refs_2_), channel_id=1, source_target_pairs={{0,15},{1,0},{2,1},{3,2},{4,3},{5,4},{6,5},{7,6},{8,7},{9,8},{10,9... | collective-permute-start | bytes 122888 | tf_op jit(solution)/shard_map/ppermute | solution.py:25
  13.2 4.0 %collective-permute-start.4 = (f32[5,4,4,128]{3,2,1,0:T(4,128)S(1)}, f32[5,4,4,128]{3,2,1,0:T(4,128)S(1)}, u32[]{:S(2)}, u32[]{:S(2)}) collective-permute-start(f32[5,4,4,128]{3,2,1,0:T(4,128)S(1)} %fusion.4.refs_2_), channel_id=1, source_target_pairs={{0,14},{1,15},{2,0},{3,1},{4,2},{5,3},{6,4},{7,5},{8,6},{9,7},{10,... | collective-permute-start | bytes 122888 | tf_op jit(solution)/shard_map/ppermute | solution.py:25
  14.4 2.8 %copy-start.1 = (f32[5,4,4,128]{3,2,1,0:T(4,128)}, f32[5,4,4,128]{3,2,1,0:T(4,128)S(1)}, u32[]{:S(2)}) copy-start(f32[5,4,4,128]{3,2,1,0:T(4,128)S(1)} %collective-permute-done.1.refs_0_) | copy-start | bytes 122884
  14.8 2.3 %copy-start.2 = (f32[5,4,4,128]{3,2,1,0:T(4,128)}, f32[5,4,4,128]{3,2,1,0:T(4,128)S(1)}, u32[]{:S(2)}) copy-start(f32[5,4,4,128]{3,2,1,0:T(4,128)S(1)} %collective-permute-done.2.refs_1_) | copy-start | bytes 122884
  14.9 2.3 %copy-start.3 = (f32[5,4,4,128]{3,2,1,0:T(4,128)}, f32[5,4,4,128]{3,2,1,0:T(4,128)S(1)}, u32[]{:S(2)}) copy-start(f32[5,4,4,128]{3,2,1,0:T(4,128)S(1)} %collective-permute-done.3.refs_3_) | copy-start | bytes 122884
  17.2 0.6 %copy-start.4 = (f32[5,4,4,128]{3,2,1,0:T(4,128)}, f32[5,4,4,128]{3,2,1,0:T(4,128)S(1)}, u32[]{:S(2)}) copy-start(f32[5,4,4,128]{3,2,1,0:T(4,128)S(1)} %collective-permute-done.4.refs_4_) | copy-start | bytes 122884
  22.0 1.4 %collective-permute-start.5 = (f32[4,8]{1,0:T(4,128)}, f32[4,8]{1,0:T(4,128)S(1)}, u32[]{:S(2)}, u32[]{:S(2)}) collective-permute-start(f32[4,8]{1,0:T(4,128)} %get-tuple-element.8), channel_id=1, source_target_pairs={{0,1},{1,0},{2,3},{3,2},{4,5},{5,4},{6,7},{7,6},{8,9},{9,8},{10,11... | collective-permute-start | bytes 392 | tf_op jit(solution)/shard_map/ppermute | solution.py:94
  24.0 3.6 %collective-permute-start.6 = (f32[4,8]{1,0:T(4,128)S(1)}, f32[4,8]{1,0:T(4,128)S(1)}, u32[]{:S(2)}, u32[]{:S(2)}) collective-permute-start(f32[4,8]{1,0:T(4,128)S(1)} %add.172), channel_id=1, source_target_pairs={{0,2},{1,3},{2,0},{3,1},{4,6},{5,7},{6,4},{7,5},{8,10},{9,11},{10,... | collective-permute-start | bytes 392 | tf_op jit(solution)/shard_map/ppermute | solution.py:94
  27.6 3.6 %collective-permute-start.7 = (f32[4,8]{1,0:T(4,128)S(1)}, f32[4,8]{1,0:T(4,128)S(1)}, u32[]{:S(2)}, u32[]{:S(2)}) collective-permute-start(f32[4,8]{1,0:T(4,128)S(1)} %add.173), channel_id=1, source_target_pairs={{0,4},{1,5},{2,6},{3,7},{4,0},{5,1},{6,2},{7,3},{8,12},{9,13},{10,... | collective-permute-start | bytes 392 | tf_op jit(solution)/shard_map/ppermute | solution.py:94
  31.2 4.5 %collective-permute-start.8 = (f32[4,8]{1,0:T(4,128)S(1)}, f32[4,8]{1,0:T(4,128)S(1)}, u32[]{:S(2)}, u32[]{:S(2)}) collective-permute-start(f32[4,8]{1,0:T(4,128)S(1)} %add.174), channel_id=1, source_target_pairs={{0,8},{1,9},{2,10},{3,11},{4,12},{5,13},{6,14},{7,15},{8,0},{9,1},... | collective-permute-start | bytes 392 | tf_op jit(solution)/shard_map/ppermute | solution.py:94

commit v17 on v16

--- a/solution.py
+++ b/solution.py
@@ -125,9 +125,15 @@
 
 def local_kernel(halo, slab_rows, *refs):
     slab_refs = refs[:2 * HALO_SLABS + 1]
-    start_ref, polar_ref, exchange_ref, relaxed_ref, last_ref, sums_ref, win, sweep_a, sweep_b, bonds_b, bonds_yr, bonds_zr, spins_b, t1, t2, t3 = refs[2 * HALO_SLABS + 1:]
+    start_ref, polar_ref, exchange_ref, relaxed_ref, last_ref, sums_ref, win, sweep_a, sweep_b, bonds_b, bonds_yr, bonds_zr, spins_b, t1, t2, t3, late_buf, late_sem = refs[2 * HALO_SLABS + 1:]
+    late_copy = pltpu.make_async_copy(slab_refs[-1], late_buf, late_sem)
+    late_copy.start()
     for k, slab_ref in enumerate(slab_refs):
-        block = slab_ref[...]
+        if k == len(slab_refs) - 1:
+            late_copy.wait()
+            block = late_buf[...]
+        else:
+            block = slab_ref[...]
         cos_polar, azimuth, bond_class = block[0], block[1], block[2:5]
         radial = jnp.sqrt(1.0 - cos_polar * cos_polar)
         strengths = jnp.zeros(bond_class.shape, jnp.float32)
@@ -237,7 +243,8 @@
             jax.ShapeDtypeStruct((slab_rows,) + vec_shape, jnp.bfloat16),
             jax.ShapeDtypeStruct((CHEB, probes), jnp.float32),
         ),
-        in_specs=[pl.BlockSpec(memory_space=pltpu.VMEM)] * (len(slab_blocks) + 1)
+        in_specs=[pl.BlockSpec(memory_space=pltpu.VMEM)] * (len(slab_blocks) - 1)
+        + [pl.BlockSpec(memory_space=pl.ANY), pl.BlockSpec(memory_space=pltpu.VMEM)]
         + [pl.BlockSpec(memory_space=pltpu.SMEM)] * 2,
         out_specs=[pl.BlockSpec(memory_space=pltpu.VMEM)] * 3,
         scratch_shapes=[
@@ -249,7 +256,8 @@
             pltpu.VMEM((n_start, depth, probes, lanes), jnp.float32),
             pltpu.VMEM((n_start, 3, depth, probes, lanes), jnp.float32),
         ]
-        + [pltpu.VMEM((n_start - 2 * k,) + vec_shape, jnp.float32) for k in range(1, CHEB)],
+        + [pltpu.VMEM((n_start - 2 * k,) + vec_shape, jnp.float32) for k in range(1, CHEB)]
+        + [pltpu.VMEM(slab_blocks[-1].shape, jnp.float32), pltpu.SemaphoreType.DMA(())],
         cost_estimate=pl.CostEstimate(
             flops=30 * sites + 200 * 3 * depth * width * lanes,
             transcendentals=0,

time: 36.6 us -> 37.1 us (1.014)
  Pallas kernels: 4.17 us -> 4.56 us
    pallas_call x1, Pallas kernels: 4.17 us -> 4.56 us  [run_local(): pl.pallas_call(body, out_shape=(jax.ShapeDtypeStruct((3, depth, slab_rows...]
where the time goes in v17:
time: 37.1 us; the launch traced here: 36.7 us
  waiting for transfers between devices  11.8 us (32%)
  starting transfers between devices  10.4 us (28%)
  other arithmetic  4.65 us (13%)
  Pallas kernels  4.56 us (12%)
  local copies, waits for them, and re-layouts  4.49 us (12%)
  between operations  0.73 us (2%)
    ppermute x5, starting transfers between devices, shifted(): lax.ppermute(array, axis, [(i, (i - shift) % size) for i in range(size)])  9.58 us
    ppermute x4, waiting for transfers between devices, butterfly_sum(): lax.ppermute(value, axis, [(i, i ^ step) for i in range(size)])  9.03 us
    pallas_call x1, Pallas kernels, run_local(): pl.pallas_call(body, out_shape=(jax.ShapeDtypeStruct((3, depth, slab_rows...  4.56 us
    unnamed x17, local copies, waits for them, and re-layouts  3.06 us
    ppermute x5, waiting for transfers between devices, shifted(): lax.ppermute(array, axis, [(i, (i - shift) % size) for i in range(size)])  2.81 us
    dynamic_slice x1, local copies, waits for them, and re-layouts, shards(): lax.dynamic_slice_in_dim(relaxed, group * block_y, block_y, -1)  1.43 us
    ppermute x4, starting transfers between devices, butterfly_sum(): lax.ppermute(value, axis, [(i, i ^ step) for i in range(size)])  0.87 us
    mul x1, other arithmetic, make_probes(): waves = jnp.stack([jnp.cos(angle) * ramp, jnp.sin(angle) * ramp], 1)  0.85 us
  transfers between devices with their start and end apart: 9, of which 6 were waited for; matrix products, arithmetic and copies ran while one was open for 15% of the time, Pallas kernels for 0%

profile of v17, /device:TPU:0, one launch (start us, length us, event | category | flops | bytes accessed | tf_op | source)
XLA Modules:
  0.0 36.7 jit_solution(4354703935514144378)
XLA Ops:
  0.7 0.8 %convert_element_type.38 = f32[3,4,4,64]{3,2,1,0:T(4,128)S(1)} convert(s32[3,4,4,64]{3,2,1,0:T(4,128)} %param.7) | non-fusion elementwise | flops 3072 | bytes 24576 | tf_op jit(solution)/shard_map/convert_element_type | solution.py:280
  1.4 3.0 %collective-permute-start = (f32[5,4,4,64]{3,2,1,0:T(4,128)S(1)}, f32[5,4,4,64]{3,2,1,0:T(4,128)S(1)}, u32[]{:S(2)}, u32[]{:S(2)}) collective-permute-start(f32[5,4,4,64]{3,2,1,0:T(4,128)S(1)} %pad_maximum_fusion), channel_id=1, source_target_pairs={{0,16},{16,0},{1,17},{17,1},{2,18},{18,2},{3,19},{19,3},{4,20},{20... | collective-permute-start | bytes 61448 | tf_op jit(solution)/shard_map/ppermute | solution.py:25
  4.5 0.7 %copy-done.7 = s32[8,3]{0,1:T(4,128)S(1)} copy-done((s32[8,3]{0,1:T(4,128)S(1)}, s32[8,3]{0,1:T(4,128)}, u32[]{:S(2)}) %copy-start.7) | copy-done | bytes 120
  5.3 0.1 fusion.8
  5.4 0.8 %cosine_multiply_fusion = (f32[8,1,4,12,128]{4,0,2,1,3:T(8,128)S(1)}, f32[8,1,4,12,128]{4,0,2,1,3:T(8,128)S(1)}) fusion(f32[12]{0:T(128)S(1)} %add_sqrt_fusion, f32[8,128]{1,0:T(8,128)S(1)} %fusion.12, f32[8,4,12]{0,1,2:T(4,128)S(1)} %broadcast_add_fusion), kind=kLoop, calls=%fused_computation.2 | loop fusion | flops 196608 | bytes 398896 | tf_op jit(solution)/shard_map/mul | solution.py:81
  6.2 0.6 %fusion.19.refs_6_ = f32[3,8]{1,0:T(4,128)} fusion(s32[8]{0:T(128)S(1)} %and_select_fusion), kind=kLoop, calls=%fused_computation.49 | loop fusion | flops 48 | bytes 128 | tf_op jit(solution)/shard_map/convert_element_type | solution.py:82
  6.8 0.2 fusion.4.refs_2_
  7.0 1.7 %collective-permute-start.1 = (f32[5,4,4,128]{3,2,1,0:T(4,128)S(1)}, f32[5,4,4,128]{3,2,1,0:T(4,128)S(1)}, u32[]{:S(2)}, u32[]{:S(2)}) collective-permute-start(f32[5,4,4,128]{3,2,1,0:T(4,128)S(1)} %fusion.4.refs_2_), channel_id=1, source_target_pairs={{0,2},{1,3},{2,4},{3,5},{4,6},{5,7},{6,8},{7,9},{8,10},{9,11},{10,... | collective-permute-start | bytes 122888 | tf_op jit(solution)/shard_map/ppermute | solution.py:25
  8.7 4.4 %collective-permute-start.3 = (f32[5,4,4,128]{3,2,1,0:T(4,128)S(1)}, f32[5,4,4,128]{3,2,1,0:T(4,128)S(1)}, u32[]{:S(2)}, u32[]{:S(2)}) collective-permute-start(f32[5,4,4,128]{3,2,1,0:T(4,128)S(1)} %fusion.4.refs_2_), channel_id=1, source_target_pairs={{0,15},{1,0},{2,1},{3,2},{4,3},{5,4},{6,5},{7,6},{8,7},{9,8},{10,9... | collective-permute-start | bytes 122888 | tf_op jit(solution)/shard_map/ppermute | solution.py:25
  13.2 0.4 %collective-permute-start.4 = (f32[5,4,4,128]{3,2,1,0:T(4,128)S(1)}, f32[5,4,4,128]{3,2,1,0:T(4,128)S(1)}, u32[]{:S(2)}, u32[]{:S(2)}) collective-permute-start(f32[5,4,4,128]{3,2,1,0:T(4,128)S(1)} %fusion.4.refs_2_), channel_id=1, source_target_pairs={{0,14},{1,15},{2,0},{3,1},{4,2},{5,3},{6,4},{7,5},{8,6},{9,7},{10,... | collective-permute-start | bytes 122888 | tf_op jit(solution)/shard_map/ppermute | solution.py:25
  13.6 0.8 %maximum_bitcast_fusion.refs_5_ = f32[12,2,4,8,128]{4,3,2,1,0:T(8,128)} fusion(f32[8,1,4,12,128]{4,0,2,1,3:T(8,128)S(1)} %get-tuple-element.13, f32[8,1,4,12,128]{4,0,2,1,3:T(8,128)S(1)} %get-tuple-element.12), kind=kLoop, calls=%fused_computation | loop fusion | flops 98304 | bytes 786432 | tf_op jit(solution)/shard_map/transpose | solution.py:295
  14.4 0.5 %collective-permute-done.2.refs_1_ = f32[5,4,4,128]{3,2,1,0:T(4,128)S(1)} collective-permute-done((f32[5,4,4,128]{3,2,1,0:T(4,128)S(1)}, f32[5,4,4,128]{3,2,1,0:T(4,128)S(1)}, u32[]{:S(2)}, u32[]{:S(2)}) %collective-permute-start.2) | collective-permute-done | bytes 40992 | tf_op jit(solution)/shard_map/ppermute | solution.py:25
  14.9 2.3 %collective-permute-done.4.refs_4_ = f32[5,4,4,128]{3,2,1,0:T(4,128)S(1)} collective-permute-done((f32[5,4,4,128]{3,2,1,0:T(4,128)S(1)}, f32[5,4,4,128]{3,2,1,0:T(4,128)S(1)}, u32[]{:S(2)}, u32[]{:S(2)}) %collective-permute-start.4) | collective-permute-done | bytes 40992 | tf_op jit(solution)/shard_map/ppermute | solution.py:25
  17.2 0.6 %copy-done.4 = f32[5,4,4,128]{3,2,1,0:T(4,128)} copy-done((f32[5,4,4,128]{3,2,1,0:T(4,128)}, f32[5,4,4,128]{3,2,1,0:T(4,128)S(1)}, u32[]{:S(2)}) %copy-start.4) | copy-done | bytes 40984
  17.8 4.6 %shard_map.76 = (f32[3,4,4,128]{3,2,1,0:T(4,128)}, bf16[4,2,3,4,8,128]{5,4,3,2,1,0:T(8,128)(2,1)}, f32[4,8]{1,0:T(4,128)}) custom-call(f32[5,4,4,128]{3,2,1,0:T(4,128)} %copy-done.1, f32[5,4,4,128]{3,2,1,0:T(4,128)} %copy-done.2, f32[5,4,4,128]{3,2,1,0:T(4,128)} %copy-done, f32[5,4,4,128]{3,2,1,0:T(4,128)} %copy-done.3, f32[5,4,4,128]{3,2,1,0:T(4,128)} %copy-done.4, ...), custom_call_target="tpu_custom_call" | custom-call | flops 14991360 | bytes 1032192 | tf_op jit(solution)/shard_map/pallas_call | solution.py:239
  22.4 1.4 %collective-permute-done.5 = f32[4,8]{1,0:T(4,128)S(1)} collective-permute-done((f32[4,8]{1,0:T(4,128)}, f32[4,8]{1,0:T(4,128)S(1)}, u32[]{:S(2)}, u32[]{:S(2)}) %collective-permute-start.5) | collective-permute-done | bytes 160 | tf_op jit(solution)/shard_map/ppermute | solution.py:94
  23.8 0.7 %add.172 = f32[4,8]{1,0:T(4,128)S(1)} add(f32[4,8]{1,0:T(4,128)} %get-tuple-element.8, f32[4,8]{1,0:T(4,128)S(1)} %collective-permute-done.5) | non-fusion elementwise | flops 32 | bytes 384 | tf_op jit(solution)/shard_map/add | solution.py:94
  24.5 3.6 %collective-permute-done.6 = f32[4,8]{1,0:T(4,128)S(1)} collective-permute-done((f32[4,8]{1,0:T(4,128)S(1)}, f32[4,8]{1,0:T(4,128)S(1)}, u32[]{:S(2)}, u32[]{:S(2)}) %collective-permute-start.6) | collective-permute-done | bytes 160 | tf_op jit(solution)/shard_map/ppermute | solution.py:94
  28.1 1.4 %constant_dynamic-slice_fusion = f32[3,4,4,64]{3,2,1,0:T(4,128)} fusion(f32[3,4,4,128]{3,2,1,0:T(4,128)} %get-tuple-element.6, s32[]{:T(128)S(6)} %select_n.77), kind=kLoop, calls=%fused_computation.41 | loop fusion | bytes 24580 | tf_op jit(solution)/shard_map/dynamic_slice | solution.py:299
  29.5 2.2 %collective-permute-done.7 = f32[4,8]{1,0:T(4,128)S(1)} collective-permute-done((f32[4,8]{1,0:T(4,128)S(1)}, f32[4,8]{1,0:T(4,128)S(1)}, u32[]{:S(2)}, u32[]{:S(2)}) %collective-permute-start.7) | collective-permute-done | bytes 160 | tf_op jit(solution)/shard_map/ppermute | solution.py:94
  31.7 0.8 %collective-permute-start.8 = (f32[4,8]{1,0:T(4,128)S(1)}, f32[4,8]{1,0:T(4,128)S(1)}, u32[]{:S(2)}, u32[]{:S(2)}) collective-permute-start(f32[4,8]{1,0:T(4,128)S(1)} %add.174), channel_id=1, source_target_pairs={{0,8},{1,9},{2,10},{3,11},{4,12},{5,13},{6,14},{7,15},{8,0},{9,1},... | collective-permute-start | bytes 392 | tf_op jit(solution)/shard_map/ppermute | solution.py:94
  32.5 1.8 %copy.8 = bf16[8,2,3,4,4,128]{5,4,3,2,1,0:T(4,128)(2,1)} copy(bf16[8,2,3,4,4,128]{5,0,3,2,1,4:T(8,128)(2,1)} %bitcast.13) | data formatting | bytes 393216
  34.2 1.9 %collective-permute-done.8 = f32[4,8]{1,0:T(4,128)S(1)} collective-permute-done((f32[4,8]{1,0:T(4,128)S(1)}, f32[4,8]{1,0:T(4,128)S(1)}, u32[]{:S(2)}, u32[]{:S(2)}) %collective-permute-start.8) | collective-permute-done | bytes 160 | tf_op jit(solution)/shard_map/ppermute | solution.py:94
  36.1 0.6 %multiply_bitcast_fusion = f32[8,4]{0,1:T(4,128)} fusion(f32[4,8]{1,0:T(4,128)S(1)} %add.174, f32[4,8]{1,0:T(4,128)S(1)} %collective-permute-done.8), kind=kLoop, calls=%fused_computation.47 | loop fusion | flops 64 | bytes 384 | tf_op jit(solution)/shard_map/transpose | solution.py:302
  (31 shorter events, 0.3 us)
Async XLA Ops:
  0.6 0.8 %copy-start.5 = (f32[4,4,64]{2,1,0:T(4,128)S(1)}, f32[4,4,64]{2,1,0:T(4,128)}, u32[]{:S(2)}) copy-start(f32[4,4,64]{2,1,0:T(4,128)} %param.5) | copy-start | bytes 12292
  0.6 0.8 %copy-start.6 = (f32[4,4,64]{2,1,0:T(4,128)S(1)}, f32[4,4,64]{2,1,0:T(4,128)}, u32[]{:S(2)}) copy-start(f32[4,4,64]{2,1,0:T(4,128)} %param.6) | copy-start | bytes 12292
  1.4 5.4 %collective-permute-start = (f32[5,4,4,64]{3,2,1,0:T(4,128)S(1)}, f32[5,4,4,64]{3,2,1,0:T(4,128)S(1)}, u32[]{:S(2)}, u32[]{:S(2)}) collective-permute-start(f32[5,4,4,64]{3,2,1,0:T(4,128)S(1)} %pad_maximum_fusion), channel_id=1, source_target_pairs={{0,16},{16,0},{1,17},{17,1},{2,18},{18,2},{3,19},{19,3},{4,20},{20... | collective-permute-start | bytes 61448 | tf_op jit(solution)/shard_map/ppermute | solution.py:25
  4.5 0.7 %copy-start.7 = (s32[8,3]{0,1:T(4,128)S(1)}, s32[8,3]{0,1:T(4,128)}, u32[]{:S(2)}) copy-start(s32[8,3]{0,1:T(4,128)} %param.9) | copy-start | bytes 292
  7.0 7.4 %copy-start = (f32[5,4,4,128]{3,2,1,0:T(4,128)}, f32[5,4,4,128]{3,2,1,0:T(4,128)S(1)}, u32[]{:S(2)}) copy-start(f32[5,4,4,128]{3,2,1,0:T(4,128)S(1)} %fusion.4.refs_2_) | copy-start | bytes 122884
  7.0 7.4 %collective-permute-start.1 = (f32[5,4,4,128]{3,2,1,0:T(4,128)S(1)}, f32[5,4,4,128]{3,2,1,0:T(4,128)S(1)}, u32[]{:S(2)}, u32[]{:S(2)}) collective-permute-start(f32[5,4,4,128]{3,2,1,0:T(4,128)S(1)} %fusion.4.refs_2_), channel_id=1, source_target_pairs={{0,2},{1,3},{2,4},{3,5},{4,6},{5,7},{6,8},{7,9},{8,10},{9,11},{10,... | collective-permute-start | bytes 122888 | tf_op jit(solution)/shard_map/ppermute | solution.py:25
  8.7 6.1 %collective-permute-start.2 = (f32[5,4,4,128]{3,2,1,0:T(4,128)S(1)}, f32[5,4,4,128]{3,2,1,0:T(4,128)S(1)}, u32[]{:S(2)}, u32[]{:S(2)}) collective-permute-start(f32[5,4,4,128]{3,2,1,0:T(4,128)S(1)} %fusion.4.refs_2_), channel_id=1, source_target_pairs={{0,1},{1,2},{2,3},{3,4},{4,5},{5,6},{6,7},{7,8},{8,9},{9,10},{10,1... | collective-permute-start | bytes 122888 | tf_op jit(solution)/shard_map/ppermute | solution.py:25
  8.7 6.1 %collective-permute-start.3 = (f32[5,4,4,128]{3,2,1,0:T(4,128)S(1)}, f32[5,4,4,128]{3,2,1,0:T(4,128)S(1)}, u32[]{:S(2)}, u32[]{:S(2)}) collective-permute-start(f32[5,4,4,128]{3,2,1,0:T(4,128)S(1)} %fusion.4.refs_2_), channel_id=1, source_target_pairs={{0,15},{1,0},{2,1},{3,2},{4,3},{5,4},{6,5},{7,6},{8,7},{9,8},{10,9... | collective-permute-start | bytes 122888 | tf_op jit(solution)/shard_map/ppermute | solution.py:25
  13.2 4.0 %collective-permute-start.4 = (f32[5,4,4,128]{3,2,1,0:T(4,128)S(1)}, f32[5,4,4,128]{3,2,1,0:T(4,128)S(1)}, u32[]{:S(2)}, u32[]{:S(2)}) collective-permute-start(f32[5,4,4,128]{3,2,1,0:T(4,128)S(1)} %fusion.4.refs_2_), channel_id=1, source_target_pairs={{0,14},{1,15},{2,0},{3,1},{4,2},{5,3},{6,4},{7,5},{8,6},{9,7},{10,... | collective-permute-start | bytes 122888 | tf_op jit(solution)/shard_map/ppermute | solution.py:25
  14.4 2.8 %copy-start.1 = (f32[5,4,4,128]{3,2,1,0:T(4,128)}, f32[5,4,4,128]{3,2,1,0:T(4,128)S(1)}, u32[]{:S(2)}) copy-start(f32[5,4,4,128]{3,2,1,0:T(4,128)S(1)} %collective-permute-done.1.refs_0_) | copy-start | bytes 122884
  14.8 2.3 %copy-start.2 = (f32[5,4,4,128]{3,2,1,0:T(4,128)}, f32[5,4,4,128]{3,2,1,0:T(4,128)S(1)}, u32[]{:S(2)}) copy-start(f32[5,4,4,128]{3,2,1,0:T(4,128)S(1)} %collective-permute-done.2.refs_1_) | copy-start | bytes 122884
  14.9 2.3 %copy-start.3 = (f32[5,4,4,128]{3,2,1,0:T(4,128)}, f32[5,4,4,128]{3,2,1,0:T(4,128)S(1)}, u32[]{:S(2)}) copy-start(f32[5,4,4,128]{3,2,1,0:T(4,128)S(1)} %collective-permute-done.3.refs_3_) | copy-start | bytes 122884
  17.2 0.6 %copy-start.4 = (f32[5,4,4,128]{3,2,1,0:T(4,128)}, f32[5,4,4,128]{3,2,1,0:T(4,128)S(1)}, u32[]{:S(2)}) copy-start(f32[5,4,4,128]{3,2,1,0:T(4,128)S(1)} %collective-permute-done.4.refs_4_) | copy-start | bytes 122884
  22.4 1.4 %collective-permute-start.5 = (f32[4,8]{1,0:T(4,128)}, f32[4,8]{1,0:T(4,128)S(1)}, u32[]{:S(2)}, u32[]{:S(2)}) collective-permute-start(f32[4,8]{1,0:T(4,128)} %get-tuple-element.8), channel_id=1, source_target_pairs={{0,1},{1,0},{2,3},{3,2},{4,5},{5,4},{6,7},{7,6},{8,9},{9,8},{10,11... | collective-permute-start | bytes 392 | tf_op jit(solution)/shard_map/ppermute | solution.py:94
  24.5 3.6 %collective-permute-start.6 = (f32[4,8]{1,0:T(4,128)S(1)}, f32[4,8]{1,0:T(4,128)S(1)}, u32[]{:S(2)}, u32[]{:S(2)}) collective-permute-start(f32[4,8]{1,0:T(4,128)S(1)} %add.172), channel_id=1, source_target_pairs={{0,2},{1,3},{2,0},{3,1},{4,6},{5,7},{6,4},{7,5},{8,10},{9,11},{10,... | collective-permute-start | bytes 392 | tf_op jit(solution)/shard_map/ppermute | solution.py:94
  28.1 3.6 %collective-permute-start.7 = (f32[4,8]{1,0:T(4,128)S(1)}, f32[4,8]{1,0:T(4,128)S(1)}, u32[]{:S(2)}, u32[]{:S(2)}) collective-permute-start(f32[4,8]{1,0:T(4,128)S(1)} %add.173), channel_id=1, source_target_pairs={{0,4},{1,5},{2,6},{3,7},{4,0},{5,1},{6,2},{7,3},{8,12},{9,13},{10,... | collective-permute-start | bytes 392 | tf_op jit(solution)/shard_map/ppermute | solution.py:94
  31.7 4.5 %collective-permute-start.8 = (f32[4,8]{1,0:T(4,128)S(1)}, f32[4,8]{1,0:T(4,128)S(1)}, u32[]{:S(2)}, u32[]{:S(2)}) collective-permute-start(f32[4,8]{1,0:T(4,128)S(1)} %add.174), channel_id=1, source_target_pairs={{0,8},{1,9},{2,10},{3,11},{4,12},{5,13},{6,14},{7,15},{8,0},{9,1},... | collective-permute-start | bytes 392 | tf_op jit(solution)/shard_map/ppermute | solution.py:94

commit v18 on v14

--- a/solution.py
+++ b/solution.py
@@ -169,7 +169,7 @@
         bonds_zr[xr] = z_roll(site[2], 1)
     for xr in range(n_start - 2):
         w = first + 1 + xr
-        spins_b[xr] = jnp.broadcast_to(sweep_b[:, :, w - base_b:w - base_b + 1, :], (3, depth, probes, lanes))
+        spins_b[xr] = jnp.broadcast_to(sweep_b[:, :, w - base_b:w - base_b + 1, :] * (-2.0 * precess_scale), (3, depth, probes, lanes))
 
     polar = [polar_ref[j] for j in range(3)]
 
@@ -200,10 +200,10 @@
                     spin[2] * polar[0] - spin[0] * polar[2],
                     spin[0] * polar[1] - spin[1] * polar[0],
                 )
-                advanced = jnp.stack([total * turn[j] for j in range(3)], 1) * -precess_scale
+                advanced = jnp.stack([total * turn[j] for j in range(3)], 1) * 0.5
             else:
                 previous = start_row(i + 2) if order == 1 else t_refs[order - 1][i + 2]
-                advanced = cross_product(spins_b[b - 1], total) * (-2.0 * precess_scale) - previous
+                advanced = cross_product(spins_b[b - 1], total) - previous
             target[i] = advanced.astype(target.dtype)
             if halo <= w < halo + slab_rows:
                 squares = advanced * advanced

time: 36.6 us -> 36.6 us (level)
  no operation moved by 1% of the time
where the time goes in v18:
time: 36.6 us; the launch traced here: 36.2 us
  waiting for transfers between devices  12 us (33%)
  starting transfers between devices  10.8 us (30%)
  local copies, waits for them, and re-layouts  4.56 us (12%)
  other arithmetic  4.08 us (11%)
  Pallas kernels  4.07 us (11%)
  between operations  0.73 us (2%)
    ppermute x5, starting transfers between devices, shifted(): lax.ppermute(array, axis, [(i, (i - shift) % size) for i in range(size)])  9.95 us
    ppermute x4, waiting for transfers between devices, butterfly_sum(): lax.ppermute(value, axis, [(i, i ^ step) for i in range(size)])  9.04 us
    pallas_call x1, Pallas kernels, run_local(): pl.pallas_call(body, out_shape=(jax.ShapeDtypeStruct((3, depth, slab_rows...  4.07 us
    ppermute x5, waiting for transfers between devices, shifted(): lax.ppermute(array, axis, [(i, (i - shift) % size) for i in range(size)])  2.99 us
    unnamed x17, local copies, waits for them, and re-layouts  2.46 us
    dynamic_slice x1, local copies, waits for them, and re-layouts, shards(): lax.dynamic_slice_in_dim(relaxed, group * block_y, block_y, -1)  1.43 us
    mul x1, other arithmetic, make_probes(): waves = jnp.stack([jnp.cos(angle) * ramp, jnp.sin(angle) * ramp], 1)  0.85 us
    ppermute x4, starting transfers between devices, butterfly_sum(): lax.ppermute(value, axis, [(i, i ^ step) for i in range(size)])  0.8 us
  transfers between devices with their start and end apart: 9, of which 7 were waited for; matrix products, arithmetic and copies ran while one was open for 14% of the time, Pallas kernels for 0%

profile of v18, /device:TPU:0, one launch (start us, length us, event | category | flops | bytes accessed | tf_op | source)
XLA Modules:
  0.0 36.2 jit_solution(13510892927454774780)
XLA Ops:
  0.7 0.8 %convert_element_type.42 = f32[3,4,4,64]{3,2,1,0:T(4,128)S(1)} convert(s32[3,4,4,64]{3,2,1,0:T(4,128)} %param.7) | non-fusion elementwise | flops 3072 | bytes 24576 | tf_op jit(solution)/shard_map/convert_element_type | solution.py:266
  1.4 3.0 %collective-permute-start = (f32[5,4,4,64]{3,2,1,0:T(4,128)S(1)}, f32[5,4,4,64]{3,2,1,0:T(4,128)S(1)}, u32[]{:S(2)}, u32[]{:S(2)}) collective-permute-start(f32[5,4,4,64]{3,2,1,0:T(4,128)S(1)} %pad_maximum_fusion), channel_id=1, source_target_pairs={{0,16},{16,0},{1,17},{17,1},{2,18},{18,2},{3,19},{19,3},{4,20},{20... | collective-permute-start | bytes 61448 | tf_op jit(solution)/shard_map/ppermute | solution.py:25
  4.5 0.7 %copy-done.7 = s32[8,3]{0,1:T(4,128)S(1)} copy-done((s32[8,3]{0,1:T(4,128)S(1)}, s32[8,3]{0,1:T(4,128)}, u32[]{:S(2)}) %copy-start.7) | copy-done | bytes 120
  5.3 0.1 fusion.8
  5.4 0.8 %cosine_multiply_fusion = (f32[8,1,4,12,128]{4,0,2,1,3:T(8,128)S(1)}, f32[8,1,4,12,128]{4,0,2,1,3:T(8,128)S(1)}) fusion(f32[12]{0:T(128)S(1)} %add_sqrt_fusion, f32[8,128]{1,0:T(8,128)S(1)} %fusion.12, f32[8,4,12]{0,1,2:T(4,128)S(1)} %broadcast_add_fusion), kind=kLoop, calls=%fused_computation.2 | loop fusion | flops 196608 | bytes 398896 | tf_op jit(solution)/shard_map/mul | solution.py:81
  6.2 0.2 collective-permute-done
  6.4 0.2 fusion.4.refs_2_
  6.6 2.1 %collective-permute-start.1 = (f32[5,4,4,128]{3,2,1,0:T(4,128)S(1)}, f32[5,4,4,128]{3,2,1,0:T(4,128)S(1)}, u32[]{:S(2)}, u32[]{:S(2)}) collective-permute-start(f32[5,4,4,128]{3,2,1,0:T(4,128)S(1)} %fusion.4.refs_2_), channel_id=1, source_target_pairs={{0,2},{1,3},{2,4},{3,5},{4,6},{5,7},{6,8},{7,9},{8,10},{9,11},{10,... | collective-permute-start | bytes 122888 | tf_op jit(solution)/shard_map/ppermute | solution.py:25
  8.7 4.4 %collective-permute-start.3 = (f32[5,4,4,128]{3,2,1,0:T(4,128)S(1)}, f32[5,4,4,128]{3,2,1,0:T(4,128)S(1)}, u32[]{:S(2)}, u32[]{:S(2)}) collective-permute-start(f32[5,4,4,128]{3,2,1,0:T(4,128)S(1)} %fusion.4.refs_2_), channel_id=1, source_target_pairs={{0,15},{1,0},{2,1},{3,2},{4,3},{5,4},{6,5},{7,6},{8,7},{9,8},{10,9... | collective-permute-start | bytes 122888 | tf_op jit(solution)/shard_map/ppermute | solution.py:25
  13.2 0.4 %collective-permute-start.4 = (f32[5,4,4,128]{3,2,1,0:T(4,128)S(1)}, f32[5,4,4,128]{3,2,1,0:T(4,128)S(1)}, u32[]{:S(2)}, u32[]{:S(2)}) collective-permute-start(f32[5,4,4,128]{3,2,1,0:T(4,128)S(1)} %fusion.4.refs_2_), channel_id=1, source_target_pairs={{0,14},{1,15},{2,0},{3,1},{4,2},{5,3},{6,4},{7,5},{8,6},{9,7},{10,... | collective-permute-start | bytes 122888 | tf_op jit(solution)/shard_map/ppermute | solution.py:25
  13.6 0.8 %maximum_bitcast_fusion.refs_5_ = f32[12,2,4,8,128]{4,3,2,1,0:T(8,128)} fusion(f32[8,1,4,12,128]{4,0,2,1,3:T(8,128)S(1)} %get-tuple-element.13, f32[8,1,4,12,128]{4,0,2,1,3:T(8,128)S(1)} %get-tuple-element.12), kind=kLoop, calls=%fused_computation | loop fusion | flops 98304 | bytes 786432 | tf_op jit(solution)/shard_map/transpose | solution.py:281
  14.4 0.5 %collective-permute-done.2.refs_1_ = f32[5,4,4,128]{3,2,1,0:T(4,128)S(1)} collective-permute-done((f32[5,4,4,128]{3,2,1,0:T(4,128)S(1)}, f32[5,4,4,128]{3,2,1,0:T(4,128)S(1)}, u32[]{:S(2)}, u32[]{:S(2)}) %collective-permute-start.2) | collective-permute-done | bytes 40992 | tf_op jit(solution)/shard_map/ppermute | solution.py:25
  14.9 2.3 %collective-permute-done.4.refs_4_ = f32[5,4,4,128]{3,2,1,0:T(4,128)S(1)} collective-permute-done((f32[5,4,4,128]{3,2,1,0:T(4,128)S(1)}, f32[5,4,4,128]{3,2,1,0:T(4,128)S(1)}, u32[]{:S(2)}, u32[]{:S(2)}) %collective-permute-start.4) | collective-permute-done | bytes 40992 | tf_op jit(solution)/shard_map/ppermute | solution.py:25
  17.2 0.7 %broadcast_in_dim.8.refs_6_ = f32[3,8,128]{2,1,0:T(8,128)} broadcast(f32[3,8]{1,0:T(4,128)S(1)} %fusion.19), dimensions={0,1} | broadcast | bytes 12384 | tf_op jit(solution)/shard_map/broadcast_in_dim | solution.py:282
  17.9 4.1 %shard_map.76 = (f32[3,4,4,128]{3,2,1,0:T(4,128)}, bf16[4,2,3,4,8,128]{5,4,3,2,1,0:T(8,128)(2,1)}, f32[4,8]{1,0:T(4,128)}) custom-call(f32[5,4,4,128]{3,2,1,0:T(4,128)} %copy-done.1, f32[5,4,4,128]{3,2,1,0:T(4,128)} %copy-done.2, f32[5,4,4,128]{3,2,1,0:T(4,128)} %copy-done, f32[5,4,4,128]{3,2,1,0:T(4,128)} %copy-done.3, f32[5,4,4,128]{3,2,1,0:T(4,128)} %copy-done.4, ...), custom_call_target="tpu_custom_call" | custom-call | flops 14991360 | bytes 1032192 | tf_op jit(solution)/shard_map/pallas_call | solution.py:227
  21.9 1.4 %collective-permute-done.5 = f32[4,8]{1,0:T(4,128)S(1)} collective-permute-done((f32[4,8]{1,0:T(4,128)}, f32[4,8]{1,0:T(4,128)S(1)}, u32[]{:S(2)}, u32[]{:S(2)}) %collective-permute-start.5) | collective-permute-done | bytes 160 | tf_op jit(solution)/shard_map/ppermute | solution.py:94
  23.3 0.7 %add.172 = f32[4,8]{1,0:T(4,128)S(1)} add(f32[4,8]{1,0:T(4,128)} %get-tuple-element.8, f32[4,8]{1,0:T(4,128)S(1)} %collective-permute-done.5) | non-fusion elementwise | flops 32 | bytes 384 | tf_op jit(solution)/shard_map/add | solution.py:94
  24.0 3.6 %collective-permute-done.6 = f32[4,8]{1,0:T(4,128)S(1)} collective-permute-done((f32[4,8]{1,0:T(4,128)S(1)}, f32[4,8]{1,0:T(4,128)S(1)}, u32[]{:S(2)}, u32[]{:S(2)}) %collective-permute-start.6) | collective-permute-done | bytes 160 | tf_op jit(solution)/shard_map/ppermute | solution.py:94
  27.6 1.4 %constant_dynamic-slice_fusion = f32[3,4,4,64]{3,2,1,0:T(4,128)} fusion(f32[3,4,4,128]{3,2,1,0:T(4,128)} %get-tuple-element.6, s32[]{:T(128)S(6)} %select_n.77), kind=kLoop, calls=%fused_computation.41 | loop fusion | bytes 24580 | tf_op jit(solution)/shard_map/dynamic_slice | solution.py:285
  29.0 2.2 %collective-permute-done.7 = f32[4,8]{1,0:T(4,128)S(1)} collective-permute-done((f32[4,8]{1,0:T(4,128)S(1)}, f32[4,8]{1,0:T(4,128)S(1)}, u32[]{:S(2)}, u32[]{:S(2)}) %collective-permute-start.7) | collective-permute-done | bytes 160 | tf_op jit(solution)/shard_map/ppermute | solution.py:94
  31.2 0.8 %collective-permute-start.8 = (f32[4,8]{1,0:T(4,128)S(1)}, f32[4,8]{1,0:T(4,128)S(1)}, u32[]{:S(2)}, u32[]{:S(2)}) collective-permute-start(f32[4,8]{1,0:T(4,128)S(1)} %add.174), channel_id=1, source_target_pairs={{0,8},{1,9},{2,10},{3,11},{4,12},{5,13},{6,14},{7,15},{8,0},{9,1},... | collective-permute-start | bytes 392 | tf_op jit(solution)/shard_map/ppermute | solution.py:94
  31.9 1.8 %copy.8 = bf16[8,2,3,4,4,128]{5,4,3,2,1,0:T(4,128)(2,1)} copy(bf16[8,2,3,4,4,128]{5,0,3,2,1,4:T(8,128)(2,1)} %bitcast.13) | data formatting | bytes 393216
  33.7 1.9 %collective-permute-done.8 = f32[4,8]{1,0:T(4,128)S(1)} collective-permute-done((f32[4,8]{1,0:T(4,128)S(1)}, f32[4,8]{1,0:T(4,128)S(1)}, u32[]{:S(2)}, u32[]{:S(2)}) %collective-permute-start.8) | collective-permute-done | bytes 160 | tf_op jit(solution)/shard_map/ppermute | solution.py:94
  35.6 0.6 %multiply_bitcast_fusion = f32[8,4]{0,1:T(4,128)} fusion(f32[4,8]{1,0:T(4,128)S(1)} %add.174, f32[4,8]{1,0:T(4,128)S(1)} %collective-permute-done.8), kind=kLoop, calls=%fused_computation.47 | loop fusion | flops 64 | bytes 384 | tf_op jit(solution)/shard_map/transpose | solution.py:288
  (32 shorter events, 0.2 us)
Async XLA Ops:
  0.6 0.8 %copy-start.5 = (f32[4,4,64]{2,1,0:T(4,128)S(1)}, f32[4,4,64]{2,1,0:T(4,128)}, u32[]{:S(2)}) copy-start(f32[4,4,64]{2,1,0:T(4,128)} %param.5) | copy-start | bytes 12292
  0.6 0.8 %copy-start.6 = (f32[4,4,64]{2,1,0:T(4,128)S(1)}, f32[4,4,64]{2,1,0:T(4,128)}, u32[]{:S(2)}) copy-start(f32[4,4,64]{2,1,0:T(4,128)} %param.6) | copy-start | bytes 12292
  1.4 5.0 %collective-permute-start = (f32[5,4,4,64]{3,2,1,0:T(4,128)S(1)}, f32[5,4,4,64]{3,2,1,0:T(4,128)S(1)}, u32[]{:S(2)}, u32[]{:S(2)}) collective-permute-start(f32[5,4,4,64]{3,2,1,0:T(4,128)S(1)} %pad_maximum_fusion), channel_id=1, source_target_pairs={{0,16},{16,0},{1,17},{17,1},{2,18},{18,2},{3,19},{19,3},{4,20},{20... | collective-permute-start | bytes 61448 | tf_op jit(solution)/shard_map/ppermute | solution.py:25
  4.5 0.7 %copy-start.7 = (s32[8,3]{0,1:T(4,128)S(1)}, s32[8,3]{0,1:T(4,128)}, u32[]{:S(2)}) copy-start(s32[8,3]{0,1:T(4,128)} %param.9) | copy-start | bytes 292
  6.6 7.7 %copy-start = (f32[5,4,4,128]{3,2,1,0:T(4,128)}, f32[5,4,4,128]{3,2,1,0:T(4,128)S(1)}, u32[]{:S(2)}) copy-start(f32[5,4,4,128]{3,2,1,0:T(4,128)S(1)} %fusion.4.refs_2_) | copy-start | bytes 122884
  6.6 7.7 %collective-permute-start.1 = (f32[5,4,4,128]{3,2,1,0:T(4,128)S(1)}, f32[5,4,4,128]{3,2,1,0:T(4,128)S(1)}, u32[]{:S(2)}, u32[]{:S(2)}) collective-permute-start(f32[5,4,4,128]{3,2,1,0:T(4,128)S(1)} %fusion.4.refs_2_), channel_id=1, source_target_pairs={{0,2},{1,3},{2,4},{3,5},{4,6},{5,7},{6,8},{7,9},{8,10},{9,11},{10,... | collective-permute-start | bytes 122888 | tf_op jit(solution)/shard_map/ppermute | solution.py:25
  8.7 6.1 %collective-permute-start.2 = (f32[5,4,4,128]{3,2,1,0:T(4,128)S(1)}, f32[5,4,4,128]{3,2,1,0:T(4,128)S(1)}, u32[]{:S(2)}, u32[]{:S(2)}) collective-permute-start(f32[5,4,4,128]{3,2,1,0:T(4,128)S(1)} %fusion.4.refs_2_), channel_id=1, source_target_pairs={{0,1},{1,2},{2,3},{3,4},{4,5},{5,6},{6,7},{7,8},{8,9},{9,10},{10,1... | collective-permute-start | bytes 122888 | tf_op jit(solution)/shard_map/ppermute | solution.py:25
  8.7 6.1 %collective-permute-start.3 = (f32[5,4,4,128]{3,2,1,0:T(4,128)S(1)}, f32[5,4,4,128]{3,2,1,0:T(4,128)S(1)}, u32[]{:S(2)}, u32[]{:S(2)}) collective-permute-start(f32[5,4,4,128]{3,2,1,0:T(4,128)S(1)} %fusion.4.refs_2_), channel_id=1, source_target_pairs={{0,15},{1,0},{2,1},{3,2},{4,3},{5,4},{6,5},{7,6},{8,7},{9,8},{10,9... | collective-permute-start | bytes 122888 | tf_op jit(solution)/shard_map/ppermute | solution.py:25
  13.2 4.0 %collective-permute-start.4 = (f32[5,4,4,128]{3,2,1,0:T(4,128)S(1)}, f32[5,4,4,128]{3,2,1,0:T(4,128)S(1)}, u32[]{:S(2)}, u32[]{:S(2)}) collective-permute-start(f32[5,4,4,128]{3,2,1,0:T(4,128)S(1)} %fusion.4.refs_2_), channel_id=1, source_target_pairs={{0,14},{1,15},{2,0},{3,1},{4,2},{5,3},{6,4},{7,5},{8,6},{9,7},{10,... | collective-permute-start | bytes 122888 | tf_op jit(solution)/shard_map/ppermute | solution.py:25
  14.4 3.5 %copy-start.1 = (f32[5,4,4,128]{3,2,1,0:T(4,128)}, f32[5,4,4,128]{3,2,1,0:T(4,128)S(1)}, u32[]{:S(2)}) copy-start(f32[5,4,4,128]{3,2,1,0:T(4,128)S(1)} %collective-permute-done.1.refs_0_) | copy-start | bytes 122884
  14.8 3.0 %copy-start.2 = (f32[5,4,4,128]{3,2,1,0:T(4,128)}, f32[5,4,4,128]{3,2,1,0:T(4,128)S(1)}, u32[]{:S(2)}) copy-start(f32[5,4,4,128]{3,2,1,0:T(4,128)S(1)} %collective-permute-done.2.refs_1_) | copy-start | bytes 122884
  14.9 3.0 %copy-start.3 = (f32[5,4,4,128]{3,2,1,0:T(4,128)}, f32[5,4,4,128]{3,2,1,0:T(4,128)S(1)}, u32[]{:S(2)}) copy-start(f32[5,4,4,128]{3,2,1,0:T(4,128)S(1)} %collective-permute-done.3.refs_3_) | copy-start | bytes 122884
  17.2 0.7 %copy-start.4 = (f32[5,4,4,128]{3,2,1,0:T(4,128)}, f32[5,4,4,128]{3,2,1,0:T(4,128)S(1)}, u32[]{:S(2)}) copy-start(f32[5,4,4,128]{3,2,1,0:T(4,128)S(1)} %collective-permute-done.4.refs_4_) | copy-start | bytes 122884
  21.9 1.4 %collective-permute-start.5 = (f32[4,8]{1,0:T(4,128)}, f32[4,8]{1,0:T(4,128)S(1)}, u32[]{:S(2)}, u32[]{:S(2)}) collective-permute-start(f32[4,8]{1,0:T(4,128)} %get-tuple-element.8), channel_id=1, source_target_pairs={{0,1},{1,0},{2,3},{3,2},{4,5},{5,4},{6,7},{7,6},{8,9},{9,8},{10,11... | collective-permute-start | bytes 392 | tf_op jit(solution)/shard_map/ppermute | solution.py:94
  24.0 3.6 %collective-permute-start.6 = (f32[4,8]{1,0:T(4,128)S(1)}, f32[4,8]{1,0:T(4,128)S(1)}, u32[]{:S(2)}, u32[]{:S(2)}) collective-permute-start(f32[4,8]{1,0:T(4,128)S(1)} %add.172), channel_id=1, source_target_pairs={{0,2},{1,3},{2,0},{3,1},{4,6},{5,7},{6,4},{7,5},{8,10},{9,11},{10,... | collective-permute-start | bytes 392 | tf_op jit(solution)/shard_map/ppermute | solution.py:94
  27.6 3.6 %collective-permute-start.7 = (f32[4,8]{1,0:T(4,128)S(1)}, f32[4,8]{1,0:T(4,128)S(1)}, u32[]{:S(2)}, u32[]{:S(2)}) collective-permute-start(f32[4,8]{1,0:T(4,128)S(1)} %add.173), channel_id=1, source_target_pairs={{0,4},{1,5},{2,6},{3,7},{4,0},{5,1},{6,2},{7,3},{8,12},{9,13},{10,... | collective-permute-start | bytes 392 | tf_op jit(solution)/shard_map/ppermute | solution.py:94
  31.2 4.5 %collective-permute-start.8 = (f32[4,8]{1,0:T(4,128)S(1)}, f32[4,8]{1,0:T(4,128)S(1)}, u32[]{:S(2)}, u32[]{:S(2)}) collective-permute-start(f32[4,8]{1,0:T(4,128)S(1)} %add.174), channel_id=1, source_target_pairs={{0,8},{1,9},{2,10},{3,11},{4,12},{5,13},{6,14},{7,15},{8,0},{9,1},... | collective-permute-start | bytes 392 | tf_op jit(solution)/shard_map/ppermute | solution.py:94
